TPU v7x, 256 devices: a whole 4x4x8 slice. The times are simulated.
256 devices in a mesh: row: 16 (over y, z_hi, core), col: 16 (over x, z_lo).
Axes of the slice: x: 4, y: 4, z: 8 (z_hi: 2, z_lo: 4; z = z_hi * 4 + z_lo), core: 2. Of those that a mesh axis runs over, the one named last changes fastest.
Arguments:
- features: bfloat16 [32768, 256], P(('row', 'col')), may hold values from -6 to 6
- w_in: bfloat16 [256, 256], replicated, may hold values from -0.375 to 0.375
- bias: float32 [256], replicated, may hold values from -3 to 3
- w_out: bfloat16 [256, 172], replicated, may hold values from -1.5 to 1.5
- tiles: bfloat16 [16, 16, 128, 128, 128], P('row', 'col'), may hold values from 0 to 1.2630181
- tile_rows: int32 [16, 16, 128], P('row', 'col'), may hold values from 0 to 15, as said below
- tile_cols: int32 [16, 16, 128], P('row', 'col'), may hold values from 0 to 15
- tile_count: int32 [16, 16], P('row', 'col'), may hold values from 32 to 128, as said below
- labels: int32 [32768], P(('col', 'row')), may hold values from 0 to 171
Outputs:
- loss: float32 [], replicated
- grad_x: bfloat16 [32768, 256], P(('row', 'col'))
- grad_w_in: float32 [256, 256], replicated
- grad_w_out: float32 [256, 172], replicated
- grad_bias: float32 [256], replicated
Inputs may be any that keep to these rules, and one draw needn't show every extreme that they name: `tile_rows`: on each grid entry the pairs of tile row and tile column of all slots are distinct. `tile_count`: some grid entry holds exactly 128 live tiles.
All inputs are finite; a program needn't handle non-finite values.
Results may differ from a plain program's by a relative error of at most 0.0041.
The roundings to bfloat16 on the way count: a program that leaves them out, or rounds other values in their place, can miss the bound.
Values may be sent and summed in bfloat16 or wider, within the bound.
No kernel may reach another device: no remote copies, remote signals or barrier semaphores. Data moves between devices by JAX's collectives and lax.ppermute only.
A program may use at most 128 MiB of HBM per device.

v0:
```python
import math

import jax
import jax.numpy as jnp
from jax import lax
from jax.sharding import PartitionSpec as P

TILE = 128


def forward_tiles(tile_block, row_ids, col_ids, live_count, source, row_count):
    width = source.shape[1]
    pieces = source.reshape(-1, TILE, width)[col_ids]
    products = jnp.einsum("tab,tbf->taf", tile_block, pieces, preferred_element_type=jnp.float32)
    live = (jnp.arange(row_ids.shape[0], dtype=jnp.int32) < live_count).astype(jnp.float32)
    products = products * live[:, None, None]
    summed = jnp.zeros((row_count, TILE, width), jnp.float32).at[row_ids].add(products)
    return summed.reshape(row_count * TILE, width)


def backward_tiles(tile_block, row_ids, col_ids, live_count, grads, col_count):
    width = grads.shape[1]
    pieces = grads.reshape(-1, TILE, width)[row_ids]
    products = jnp.einsum("tab,taf->tbf", tile_block, pieces, preferred_element_type=jnp.float32)
    live = (jnp.arange(col_ids.shape[0], dtype=jnp.int32) < live_count).astype(jnp.float32)
    products = products * live[:, None, None]
    summed = jnp.zeros((col_count, TILE, width), jnp.float32).at[col_ids].add(products)
    return summed.reshape(col_count * TILE, width)


def head_block(agg, bias, w_out, node_labels):
    pre_act = agg + bias[None, :]
    squash = jax.nn.sigmoid(pre_act)
    hidden = (pre_act * squash).astype(jnp.bfloat16)
    logits = jnp.dot(hidden, w_out, preferred_element_type=jnp.float32)
    top_val = jnp.max(logits, axis=1)
    lse = top_val + jnp.log(jnp.sum(jnp.exp(logits - top_val[:, None]), axis=1))
    onehot = (jnp.arange(w_out.shape[1], dtype=jnp.int32)[None, :] == node_labels[:, None]).astype(
        jnp.float32
    )
    picked = jnp.sum(logits * onehot, axis=1)
    loss_sum = jnp.sum(lse - picked)
    dlog = (jnp.exp(logits - lse[:, None]) - onehot).astype(jnp.bfloat16)
    out_term = jnp.einsum("nf,nc->fc", hidden, dlog, preferred_element_type=jnp.float32)
    d_hidden = jnp.einsum("nc,fc->nf", dlog, w_out, preferred_element_type=jnp.float32)
    grad_z = (d_hidden * squash * (1.0 + pre_act * (1.0 - squash))).astype(jnp.bfloat16)
    bias_term = jnp.sum(grad_z.astype(jnp.float32), axis=0)
    return (loss_sum, out_term, bias_term, grad_z)


def backward_part(features, tile_block, row_ids, col_ids, live_count, grad_block, col_tiles):
    back_part = backward_tiles(tile_block, row_ids, col_ids, live_count, grad_block, col_tiles)
    grad_proj = lax.psum_scatter(back_part, "col", scatter_dimension=0, tiled=True).astype(
        jnp.bfloat16
    )
    in_term = jnp.einsum("nf,ng->fg", features, grad_proj, preferred_element_type=jnp.float32)
    return (grad_proj, in_term)


def weight_total(in_term):
    return lax.psum(in_term, ("row", "col"))


def body(features, w_in, bias, w_out, tiles, tile_rows, tile_cols, tile_count, labels):
    row_devices = lax.axis_size("row")
    col_devices = lax.axis_size("col")
    rows_here = features.shape[0]
    nodes = rows_here * row_devices * col_devices
    scale = 1.0 / math.sqrt(rows_here)
    row_tiles = row_devices * rows_here // TILE
    col_tiles = col_devices * rows_here // TILE
    tile_block = tiles[0, 0]
    row_ids = tile_rows[0, 0]
    col_ids = tile_cols[0, 0]
    live_count = tile_count[0, 0]
    proj = jnp.dot(features, w_in, preferred_element_type=jnp.float32).astype(jnp.bfloat16)
    source = lax.all_gather(proj, "col", axis=0, tiled=True)
    partial_value = forward_tiles(tile_block, row_ids, col_ids, live_count, source, row_tiles)
    agg = lax.psum_scatter(partial_value, "row", scatter_dimension=0, tiled=True)
    loss_sum, out_term, bias_term, grad_z = head_block(agg, bias, w_out, labels)
    grad_block = lax.all_gather(grad_z, "row", axis=0, tiled=True)
    loss_sum, out_term, bias_term = lax.psum((loss_sum, out_term, bias_term), ("row", "col"))
    grad_proj, in_term = backward_part(
        features, tile_block, row_ids, col_ids, live_count, grad_block, col_tiles
    )
    in_total = weight_total(in_term)
    grad_w_in = in_total * scale
    grad_x = jnp.einsum("ng,fg->nf", grad_proj, w_in, preferred_element_type=jnp.float32).astype(
        jnp.bfloat16
    )
    return (loss_sum / nodes, grad_x, grad_w_in, out_term * scale, bias_term * scale)


def solution(mesh):
    placed = (
        P(("row", "col"), None),
        P(),
        P(),
        P(),
        P("row", "col", None, None, None),
        P("row", "col", None),
        P("row", "col", None),
        P("row", "col"),
        P(("col", "row")),
    )
    return jax.shard_map(
        body,
        mesh=mesh,
        in_specs=placed,
        out_specs=(P(), P(("row", "col"), None), P(), P(), P()),
        check_vma=False,
    )
```

profile of v0, /device:TPU:1, one launch (start us, length us, event | category | flops | bytes accessed | tf_op | source)
XLA Modules:
  0.0 722.1 jit_solution(3918829927751231485)
XLA Ops:
  7.2 0.0 copy-start
  7.2 0.0 all-gather.3.cloned.1.call-start
  7.2 0.8 copy-done
  8.1 1.6 convolution_convert_fusion.1
  9.7 0.0 all-gather.3.cloned.1.call-update
  9.7 0.0 reduce-scatter.3.cloned.1.call-start
  10.4 0.7 fusion.8
  11.1 0.7 fusion.7
  11.8 74.5 %all-gather.3.cloned.1.call-done = bf16[2048,256]{1,0:T(8,128)(2,1)} async-done(((bf16[128,256]{1,0:T(8,128)(2,1)}), bf16[2048,256]{1,0:T(8,128)(2,1)}) %all-gather.3.cloned.1.call-update) | async-done | bytes 1048592 | tf_op jit(solution)/shard_map/all_gather | solution.py:77
  86.3 7.8 %gather_fusion = bf16[128,128,256]{2,1,0:T(8,128)(2,1)} fusion(bf16[16,128,256]{2,1,0:T(8,128)(2,1)} %bitcast.35, s32[1024]{0:T(1024)S(1)} %pad_clamp_fusion.1), kind=kCustom, calls=%fused_computation | custom fusion | bytes 16777728 | tf_op jit(solution)/shard_map/gather | solution.py:13
  94.1 12.9 %multiply_bitcast_fusion.1 = f32[128,128,256]{1,2,0:T(8,128)} fusion(bf16[128,128,256]{2,1,0:T(8,128)(2,1)} %gather_fusion, f32[128]{0:T(128)S(1)} %compare_convert_fusion, bf16[1,1,128,128,128]{4,3,2,1,0:T(8,128)(2,1)} %param.13), kind=kOutput, calls=%fused_computation.5 | convolution fusion | flops 1077936128 | bytes 29360640 | tf_op jit(solution)/shard_map/tab,tbf->taf/dot_general | solution.py:14
  107.0 17.5 %copy.18 = f32[128,128,256]{2,1,0:T(8,128)} copy(f32[128,128,256]{1,2,0:T(8,128)} %multiply_bitcast_fusion.1) | data formatting | bytes 33554432 | tf_op jit(solution)/shard_map/mul | solution.py:16
  124.4 0.2 broadcast.52.clone
  124.6 0.0 copy-start.6
  124.7 0.0 copy-start.7
  124.7 0.0 copy-start.4
  124.7 24.3 %scatter_fusion = f32[16,128,256]{2,1,0:T(8,128)S(1)} fusion(f32[16,128,256]{2,1,0:T(8,128)S(1)} %broadcast.52.clone, s32[128]{0:T(128)S(1)} %fusion.7, f32[128,128,256]{2,1,0:T(8,128)} %copy.18), kind=kCustom, calls=%fused_computation.2 | custom fusion | flops 4194304 | bytes 50332160 | tf_op jit(solution)/shard_map/scatter-add | solution.py:17
  149.0 0.0 copy-start.2
  149.0 1.3 copy-done.2
  150.4 0.0 reduce-scatter.3.cloned.1.call-update
  150.4 0.0 all-gather.5.cloned.1.call-start
  150.4 94.1 %reduce-scatter.3.cloned.1.call-done = f32[128,256]{1,0:T(8,128)} async-done(((f32[2048,256]{1,0:T(8,128)}), f32[128,256]{1,0:T(8,128)}) %reduce-scatter.3.cloned.1.call-update) | async-done | bytes 131088 | tf_op jit(solution)/shard_map/reduce_scatter | solution.py:79
  244.5 0.0 copy-done.6
  244.5 0.0 copy-done.7
  244.5 1.1 fusion.10
  245.7 0.0 copy-done.4
  245.7 0.1 select_reduce_fusion
  245.7 0.6 subtract_reduce_fusion
  246.3 1.8 convert_reduce_fusion
  248.1 0.0 all-gather.5.cloned.1.call-update
  248.1 0.2 reduce-scatter.5.cloned.1.call-start
  248.4 54.0 %all-gather.5.cloned.1.call-done = bf16[2048,256]{1,0:T(8,128)(2,1)} async-done(((bf16[128,256]{1,0:T(8,128)(2,1)}), bf16[2048,256]{1,0:T(8,128)(2,1)}) %all-gather.5.cloned.1.call-update) | async-done | bytes 1048592 | tf_op jit(solution)/shard_map/all_gather | solution.py:81
  302.3 7.8 %gather_fusion.1 = bf16[128,128,256]{2,1,0:T(8,128)(2,1)} fusion(bf16[16,128,256]{2,1,0:T(8,128)(2,1)} %bitcast.36, s32[1024]{0:T(1024)S(1)} %pad_clamp_fusion), kind=kCustom, calls=%fused_computation.1 | custom fusion | bytes 16777728 | tf_op jit(solution)/shard_map/gather | solution.py:23
  310.1 13.7 %multiply_bitcast_fusion = f32[128,128,256]{1,2,0:T(8,128)} fusion(bf16[128,128,256]{2,1,0:T(8,128)(2,1)} %gather_fusion.1, f32[128]{0:T(128)S(1)} %compare_convert_fusion, bf16[1,1,128,128,128]{4,3,2,1,0:T(8,128)(2,1)} %param.13), kind=kOutput, calls=%fused_computation.4 | convolution fusion | flops 1077936128 | bytes 29360640 | tf_op jit(solution)/shard_map/tab,taf->tbf/dot_general | solution.py:24
  323.8 17.5 %copy.20 = f32[128,128,256]{2,1,0:T(8,128)} copy(f32[128,128,256]{1,2,0:T(8,128)} %multiply_bitcast_fusion) | data formatting | bytes 33554432 | tf_op jit(solution)/shard_map/mul | solution.py:26
  341.2 0.2 broadcast.52
  341.4 0.0 copy-start.5
  341.4 0.0 copy-start.3
  341.5 24.3 %scatter_fusion.1 = f32[16,128,256]{2,1,0:T(8,128)S(1)} fusion(f32[16,128,256]{2,1,0:T(8,128)S(1)} %broadcast.52, s32[128]{0:T(128)S(1)} %fusion.8, f32[128,128,256]{2,1,0:T(8,128)} %copy.20), kind=kCustom, calls=%fused_computation.3 | custom fusion | flops 4194304 | bytes 50332160 | tf_op jit(solution)/shard_map/scatter-add | solution.py:27
  365.8 0.0 copy-start.1
  365.8 1.3 copy-done.1
  367.1 0.0 reduce-scatter.5.cloned.1.call-update
  367.2 0.0 all-reduce.4.cloned.1.call-start
  367.2 76.4 %all-reduce = (f32[]{:T(128)}, f32[256]{0:T(256)S(1)}) all-reduce(f32[]{:T(128)} %get-tuple-element.21, f32[256]{0:T(256)S(1)} %get-tuple-element.25), channel_id=1, replica_groups=mesh['row'=16,'col'=16] {'row','col'}, use_global_device_ids=true, to_apply=%region_6.0 | all-reduce | flops 257 | bytes 2056 | tf_op jit(solution)/shard_map/psum | solution.py:82
  444.3 0.6 broadcast_multiply_fusion.2
  444.8 0.0 copy-done.5
  444.8 0.9 fusion.6
  445.7 0.0 reduce-scatter.5.cloned.1.call-done
  445.7 0.0 copy-done.3
  445.7 1.8 convolution_bitcast_fusion
  447.5 0.0 all-reduce.4.cloned.1.call-update
  447.6 1.7 convolution_convert_fusion
  449.3 261.7 %all-reduce.4.cloned.1.call-done = (f32[256,256]{0,1:T(8,128)}, f32[256,172]{0,1:T(8,128)}) async-done(((f32[256,256]{0,1:T(8,128)}, f32[256,172]{0,1:T(8,128)}), (f32[256,256]{0,1:T(8,128)}, f32[256,172]{0,1:T(8,128)})) %all-reduce.4.cloned.1.call-update) | async-done | bytes 438288 | tf_op jit(solution)/shard_map/psum | solution.py:61
  711.0 1.0 broadcast_multiply_fusion
  712.0 0.8 copy.21
  712.8 1.6 broadcast_multiply_fusion.1
  (3 shorter events, 0.0 us)
Async XLA Ops:
  7.2 0.9 copy-start
  7.2 79.1 %all-gather.3.cloned.1.call-start = ((), (), s32[]{:S(2)}) async-start(), calls=%async_computation.2 | async-start | bytes 1114112 | tf_op jit(solution)/shard_map/all_gather | solution.py:77
  9.7 234.8 %reduce-scatter.3.cloned.1.call-start = ((), (), s32[]{:S(2)}) async-start(), calls=%async_computation.3 | async-start | bytes 2228224 | tf_op jit(solution)/shard_map/reduce_scatter | solution.py:79
  124.6 119.9 %copy-start.6 = (bf16[256,172]{0,1:T(8,128)(2,1)S(1)}, bf16[256,172]{0,1:T(8,128)(2,1)}, u32[]{:S(2)}) copy-start(bf16[256,172]{0,1:T(8,128)(2,1)} %param.12) | copy-start | bytes 264196
  124.7 119.9 %copy-start.7 = (f32[256]{0:T(256)S(1)}, f32[256]{0:T(256)}, u32[]{:S(2)}) copy-start(f32[256]{0:T(256)} %param.11) | copy-start | bytes 3076
  124.7 121.0 %copy-start.4 = (s32[128]{0:T(128)S(1)}, s32[128]{0:T(128)}, u32[]{:S(2)}) copy-start(s32[128]{0:T(128)} %param.17) | copy-start | bytes 1540
  149.0 1.4 copy-start.2
  150.4 151.9 %all-gather.5.cloned.1.call-start = ((), (), s32[]{:S(2)}) async-start(), calls=%async_computation.4 | async-start | bytes 1114112 | tf_op jit(solution)/shard_map/all_gather | solution.py:81
  248.1 197.6 %reduce-scatter.5.cloned.1.call-start = ((), (), s32[]{:S(2)}) async-start(), calls=%async_computation.5 | async-start | bytes 2228224 | tf_op jit(solution)/shard_map/reduce_scatter | solution.py:53
  341.4 103.4 %copy-start.5 = (f32[128,256]{1,0:T(8,128)S(1)}, f32[128,256]{1,0:T(8,128)}, u32[]{:S(2)}) copy-start(f32[128,256]{1,0:T(8,128)} %reduce-scatter.3.cloned.1.call-done) | copy-start | bytes 393220
  341.4 104.3 %copy-start.3 = (bf16[128,256]{1,0:T(8,128)(2,1)S(1)}, bf16[128,256]{1,0:T(8,128)(2,1)}, u32[]{:S(2)}) copy-start(bf16[128,256]{1,0:T(8,128)(2,1)} %param.9) | copy-start | bytes 196612
  365.8 1.4 copy-start.1
  367.2 343.9 %all-reduce.4.cloned.1.call-start = ((), (), s32[]{:S(2)}) async-start(), calls=%async_computation.6 | async-start | bytes 884736 | tf_op jit(solution)/shard_map/psum | solution.py:61
Sparse Core Ops, SparseCore 0:
  10.3 75.9 all-gather.2
  150.5 93.9 reduce-scatter.2
  248.2 54.0 all-gather.4
  367.3 76.8 reduce-scatter.4
  450.1 260.8 all-reduce.3
where the time goes:
time: 723 us; the launch traced here: 722 us
  waiting for transfers between devices  484 us (67%)
  blocking collectives  76.4 us (11%)
  local copies, waits for them, and re-layouts  55.3 us (8%)
  other arithmetic  53.8 us (7%)
  matrix products  35.5 us (5%)
  between operations  16.3 us (2%)
    psum x1, waiting for transfers between devices, weight_total(): return lax.psum(in_term, ('row', 'col'))  262 us
    reduce_scatter x1, waiting for transfers between devices, body(): lax.psum_scatter(partial_value, 'row', scatter_dimension=0, tiled=True)  94.1 us
    psum x1, blocking collectives, body(): lax.psum((loss_sum, out_term, bias_term), ('row', 'col'))  76.4 us
    all_gather x1, waiting for transfers between devices, body(): source = lax.all_gather(proj, 'col', axis=0, tiled=True)  74.5 us
    all_gather x1, waiting for transfers between devices, body(): grad_block = lax.all_gather(grad_z, 'row', axis=0, tiled=True)  54 us
    scatter-add x1, other arithmetic, backward_tiles(): jnp.zeros((col_count, TILE, width), jnp.float32).at[col_ids].add(products)  24.3 us
    scatter-add x1, other arithmetic, forward_tiles(): jnp.zeros((row_count, TILE, width), jnp.float32).at[row_ids].add(products)  24.3 us
    mul x1, local copies, waits for them, and re-layouts, forward_tiles(): products = products * live[:, None, None]  17.5 us
  transfers between devices with their start and end apart: 5, of which 4 were waited for; matrix products, arithmetic and copies ran while one was open for 1% of the time, Pallas kernels for 0%

commit v1 on v0

v1 whole, which is shorter than its diff:
```python
import math

import jax
import jax.numpy as jnp
from jax import lax
from jax.experimental import pallas as pl
from jax.experimental.pallas import tpu as pltpu
from jax.sharding import PartitionSpec as P

TILE = 128
CHUNK = 8


def _tile_kernel(transpose, rows_ref, cols_ref, count_ref, tiles_ref, src_ref, out_ref):
    step = pl.program_id(0)
    count = count_ref[0]

    @pl.when(step == 0)
    def _():
        out_ref[...] = jnp.zeros_like(out_ref)

    for j in range(CHUNK):
        slot = step * CHUNK + j

        @pl.when(slot < count)
        def _():
            if transpose:
                src_at = rows_ref[slot]
                dst_at = cols_ref[slot]
            else:
                src_at = cols_ref[slot]
                dst_at = rows_ref[slot]
            src = src_ref[pl.ds(pl.multiple_of(src_at * TILE, TILE), TILE), :]
            tile = tiles_ref[j]
            if transpose:
                part = lax.dot_general(
                    tile, src, (((0,), (0,)), ((), ())), preferred_element_type=jnp.float32
                )
            else:
                part = jnp.dot(tile, src, preferred_element_type=jnp.float32)
            dst = pl.ds(pl.multiple_of(dst_at * TILE, TILE), TILE)
            out_ref[dst, :] += part


def tile_product(tile_block, row_ids, col_ids, live_count, source, out_tiles, transpose):
    slots = tile_block.shape[0]
    width = source.shape[1]
    steps = slots // CHUNK

    def tiles_map(i, rows, cols, count):
        last = jnp.maximum(count[0] - 1, 0) // CHUNK
        return (jnp.minimum(i, last), 0, 0)

    grid_spec = pltpu.PrefetchScalarGridSpec(
        num_scalar_prefetch=3,
        grid=(steps,),
        in_specs=[
            pl.BlockSpec((CHUNK, TILE, TILE), tiles_map),
            pl.BlockSpec(source.shape, lambda i, rows, cols, count: (0, 0)),
        ],
        out_specs=pl.BlockSpec((out_tiles * TILE, width), lambda i, rows, cols, count: (0, 0)),
    )
    return pl.pallas_call(
        lambda *refs: _tile_kernel(transpose, *refs),
        grid_spec=grid_spec,
        out_shape=jax.ShapeDtypeStruct((out_tiles * TILE, width), jnp.float32),
        compiler_params=pltpu.CompilerParams(dimension_semantics=("arbitrary",)),
    )(row_ids, col_ids, live_count.reshape(1), tile_block, source)


def head_block(agg, bias, w_out, node_labels):
    pre_act = agg + bias[None, :]
    squash = jax.nn.sigmoid(pre_act)
    hidden = (pre_act * squash).astype(jnp.bfloat16)
    logits = jnp.dot(hidden, w_out, preferred_element_type=jnp.float32)
    top_val = jnp.max(logits, axis=1)
    lse = top_val + jnp.log(jnp.sum(jnp.exp(logits - top_val[:, None]), axis=1))
    onehot = (jnp.arange(w_out.shape[1], dtype=jnp.int32)[None, :] == node_labels[:, None]).astype(
        jnp.float32
    )
    picked = jnp.sum(logits * onehot, axis=1)
    loss_sum = jnp.sum(lse - picked)
    dlog = (jnp.exp(logits - lse[:, None]) - onehot).astype(jnp.bfloat16)
    out_term = jnp.einsum("nf,nc->fc", hidden, dlog, preferred_element_type=jnp.float32)
    d_hidden = jnp.einsum("nc,fc->nf", dlog, w_out, preferred_element_type=jnp.float32)
    grad_z = (d_hidden * squash * (1.0 + pre_act * (1.0 - squash))).astype(jnp.bfloat16)
    bias_term = jnp.sum(grad_z.astype(jnp.float32), axis=0)
    return (loss_sum, out_term, bias_term, grad_z)


def body(features, w_in, bias, w_out, tiles, tile_rows, tile_cols, tile_count, labels):
    row_devices = lax.axis_size("row")
    col_devices = lax.axis_size("col")
    rows_here = features.shape[0]
    feat = features.shape[1]
    classes = w_out.shape[1]
    nodes = rows_here * row_devices * col_devices
    scale = 1.0 / math.sqrt(rows_here)
    row_tiles = row_devices * rows_here // TILE
    col_tiles = col_devices * rows_here // TILE
    tile_block = tiles[0, 0]
    row_ids = tile_rows[0, 0]
    col_ids = tile_cols[0, 0]
    live_count = tile_count[0, 0]
    proj = jnp.dot(features, w_in, preferred_element_type=jnp.float32).astype(jnp.bfloat16)
    source = lax.all_gather(proj, "col", axis=0, tiled=True)
    partial_value = tile_product(tile_block, row_ids, col_ids, live_count, source, row_tiles, False)
    agg = lax.psum_scatter(partial_value, "row", scatter_dimension=0, tiled=True)
    loss_sum, out_term, bias_term, grad_z = head_block(agg, bias, w_out, labels)
    grad_block = lax.all_gather(grad_z, "row", axis=0, tiled=True)
    back_part = tile_product(tile_block, row_ids, col_ids, live_count, grad_block, col_tiles, True)
    grad_proj = lax.psum_scatter(back_part, "col", scatter_dimension=0, tiled=True).astype(
        jnp.bfloat16
    )
    in_term = jnp.einsum("nf,ng->fg", features, grad_proj, preferred_element_type=jnp.float32)
    extra = jnp.zeros((feat, 2), jnp.float32)
    extra = extra.at[:, 0].set(bias_term).at[0, 1].set(loss_sum)
    packed = jnp.concatenate([in_term, out_term, extra], axis=1)
    packed = lax.psum(packed, ("row", "col"))
    grad_w_in = packed[:, :feat] * scale
    grad_w_out = packed[:, feat : feat + classes] * scale
    grad_bias = packed[:, feat + classes] * scale
    loss = packed[0, feat + classes + 1] / nodes
    grad_x = jnp.einsum("ng,fg->nf", grad_proj, w_in, preferred_element_type=jnp.float32).astype(
        jnp.bfloat16
    )
    return (loss, grad_x, grad_w_in, grad_w_out, grad_bias)


def solution(mesh):
    placed = (
        P(("row", "col"), None),
        P(),
        P(),
        P(),
        P("row", "col", None, None, None),
        P("row", "col", None),
        P("row", "col", None),
        P("row", "col"),
        P(("col", "row")),
    )
    return jax.shard_map(
        body,
        mesh=mesh,
        in_specs=placed,
        out_specs=(P(), P(("row", "col"), None), P(), P(), P()),
        check_vma=False,
    )
```

time: 723 us -> 646 us (0.89)
  waiting for transfers between devices: 484 us -> 567 us
  blocking collectives: 76.4 us -> 0 us
  local copies, waits for them, and re-layouts: 55.3 us -> 5.48 us
  other arithmetic: 53.8 us -> 5.31 us
  Pallas kernels: 0 us -> 44 us
  matrix products: 35.5 us -> 7.54 us
    reduce_scatter x1, waiting for transfers between devices: 0.01 us -> 78.8 us  [body(): lax.psum_scatter(back_part, 'col', scatter_dimension=0, tiled=True)]
    psum x1 -> x0, blocking collectives: 76.4 us -> none  [body(): lax.psum((loss_sum, out_term, bias_term), ('row', 'col'))]
    scatter-add x2 -> x0, other arithmetic: 48.6 us -> none  [the longest x1 24.3 us: backward_tiles(): jnp.zeros((col_count, TILE, width), jnp.float32).at[col_ids].add(products)]
    pallas_call x0 -> x2, Pallas kernels: none -> 44 us  [tile_product(): pl.pallas_call(lambda *refs: _tile_kernel(transpose, *refs), grid_spec=gr...]
    mul x2 -> x0, local copies, waits for them, and re-layouts: 34.9 us -> none  [the longest x1 17.5 us: forward_tiles(): products = products * live[:, None, None]]
    dot_general x3 -> x1, matrix products: 28.4 us -> 1.11 us  [body(): jnp.einsum('nf,ng->fg', features, grad_proj, preferred_element_type=jnp.f...]
    gather x2 -> x0, local copies, waits for them, and re-layouts: 15.5 us -> none  [the longest x1 7.78 us: backward_tiles(): pieces = grads.reshape(-1, TILE, width)[row_ids]]
  transfers between devices with their start and end apart: 5 -> 5, of which waited for: 4 -> 5; matrix products, arithmetic and copies ran while one was open for 1% -> 1% of each run, Pallas kernels for 0% -> 0%
where the time goes in v1:
time: 646 us
  waiting for transfers between devices  567 us (88%)
  Pallas kernels  44 us (7%)
  between operations  16.3 us (3%)
  matrix products  7.54 us (1%)
    psum x1, waiting for transfers between devices, body(): packed = lax.psum(packed, ('row', 'col'))  262 us
    reduce_scatter x1, waiting for transfers between devices, body(): lax.psum_scatter(partial_value, 'row', scatter_dimension=0, tiled=True)  96.6 us
    reduce_scatter x1, waiting for transfers between devices, body(): lax.psum_scatter(back_part, 'col', scatter_dimension=0, tiled=True)  78.8 us
    all_gather x1, waiting for transfers between devices, body(): source = lax.all_gather(proj, 'col', axis=0, tiled=True)  75.9 us
    all_gather x1, waiting for transfers between devices, body(): grad_block = lax.all_gather(grad_z, 'row', axis=0, tiled=True)  54.1 us
    pallas_call x2, Pallas kernels, tile_product(): pl.pallas_call(lambda *refs: _tile_kernel(transpose, *refs), grid_spec=gr...  44 us
  transfers between devices with their start and end apart: 5, of which 5 were waited for; matrix products, arithmetic and copies ran while one was open for 1% of the time, Pallas kernels for 0%

profile of v1, /device:TPU:1, one launch (start us, length us, event | category | flops | bytes accessed | tf_op | source)
XLA Modules:
  0.0 646.0 jit_solution(6126753787275990125)
XLA Ops:
  7.2 0.0 copy-start
  7.2 0.0 all-gather.3.cloned.1.call-start
  7.2 0.8 copy-done
  8.1 1.6 convolution_convert_fusion.1
  9.7 0.0 all-gather.3.cloned.1.call-update
  9.7 0.0 reduce-scatter.3.cloned.1.call-start
  10.4 75.9 %all-gather.3.cloned.1.call-done.refs_4_ = bf16[2048,256]{1,0:T(8,128)(2,1)} async-done(((bf16[128,256]{1,0:T(8,128)(2,1)}), bf16[2048,256]{1,0:T(8,128)(2,1)}) %all-gather.3.cloned.1.call-update) | async-done | bytes 1048592 | tf_op jit(solution)/shard_map/all_gather | solution.py:106
  86.3 19.6 %shard_map.128 = f32[2048,256]{1,0:T(8,128)} custom-call(s32[128]{0:T(128)} %bitcast.22, s32[128]{0:T(128)} %bitcast.24, s32[1]{0:T(128)} %bitcast.18.refs_2_, bf16[128,128,128]{2,1,0:T(8,128)(2,1)} %bitcast.20, bf16[2048,256]{1,0:T(8,128)(2,1)} %all-gather.3.cloned.1.call-done.refs_4_), custom_call_target="tpu_custom_call" | custom-call | tf_op jit(solution)/shard_map/pallas_call | solution.py:63
  105.9 0.0 copy-start.4
  105.9 0.0 copy-start.5
  105.9 0.0 copy-start.2
  105.9 0.0 reduce-scatter.3.cloned.1.call-update
  106.0 0.0 all-gather.5.cloned.1.call-start
  106.0 96.6 %reduce-scatter.3.cloned.1.call-done = f32[128,256]{1,0:T(8,128)} async-done(((f32[2048,256]{1,0:T(8,128)}), f32[128,256]{1,0:T(8,128)}) %reduce-scatter.3.cloned.1.call-update) | async-done | bytes 131088 | tf_op jit(solution)/shard_map/reduce_scatter | solution.py:108
  202.6 0.0 copy-done.4
  202.6 0.0 copy-done.5
  202.6 1.1 fusion.7
  203.7 0.0 copy-done.2
  203.7 0.1 select_reduce_fusion
  203.8 0.6 subtract_reduce_fusion
  204.4 1.8 convert_reduce_fusion
  206.1 0.0 all-gather.5.cloned.1.call-update
  206.2 0.0 reduce-scatter.5.cloned.1.call-start
  206.2 54.1 %all-gather.5.cloned.1.call-done.refs_4_ = bf16[2048,256]{1,0:T(8,128)(2,1)} async-done(((bf16[128,256]{1,0:T(8,128)(2,1)}), bf16[2048,256]{1,0:T(8,128)(2,1)}) %all-gather.5.cloned.1.call-update) | async-done | bytes 1048592 | tf_op jit(solution)/shard_map/all_gather | solution.py:110
  260.3 24.4 %shard_map.129 = f32[2048,256]{1,0:T(8,128)} custom-call(s32[128]{0:T(128)} %bitcast.23, s32[128]{0:T(128)} %bitcast.25, s32[1]{0:T(128)} %bitcast.19.refs_2_, bf16[128,128,128]{2,1,0:T(8,128)(2,1)} %bitcast.21, bf16[2048,256]{1,0:T(8,128)(2,1)} %all-gather.5.cloned.1.call-done.refs_4_), custom_call_target="tpu_custom_call" | custom-call | tf_op jit(solution)/shard_map/pallas_call | solution.py:63
  284.7 0.0 copy-start.3
  284.7 0.0 copy-start.1
  284.7 0.0 reduce-scatter.5.cloned.1.call-update
  284.7 0.0 all-reduce.3.cloned.1.call-start
  284.8 0.6 fusion.6
  285.4 2.0 scatter.9
  287.4 0.0 copy-done.3
  287.4 0.2 fusion.4
  287.6 78.8 %reduce-scatter.5.cloned.1.call-done = f32[128,256]{1,0:T(8,128)} async-done(((f32[2048,256]{1,0:T(8,128)}), f32[128,256]{1,0:T(8,128)}) %reduce-scatter.5.cloned.1.call-update) | async-done | bytes 131088 | tf_op jit(solution)/shard_map/reduce_scatter | solution.py:112
  366.4 0.0 copy-done.1
  366.4 1.1 convolution_bitcast_fusion
  367.5 0.8 pad_maximum_fusion
  368.3 0.0 all-reduce.3.cloned.1.call-update
  368.3 1.7 convolution_convert_fusion
  370.1 261.7 %all-reduce.3.cloned.1.call-done = f32[256,430]{0,1:T(8,128)} async-done(((f32[256,430]{0,1:T(8,128)}), f32[256,430]{0,1:T(8,128)}) %all-reduce.3.cloned.1.call-update) | async-done | bytes 440336 | tf_op jit(solution)/shard_map/psum | solution.py:119
  631.8 1.0 slice_multiply_fusion
  632.7 0.8 copy.14
  633.6 1.2 slice.53
  635.4 1.3 slice_multiply_fusion.2
  636.7 1.6 slice_multiply_fusion.1
  (2 shorter events, 0.0 us)
Async XLA Ops:
  7.2 0.9 copy-start
  7.2 79.1 %all-gather.3.cloned.1.call-start = ((), (), s32[]{:S(2)}) async-start(), calls=%async_computation.2 | async-start | bytes 1114112 | tf_op jit(solution)/shard_map/all_gather | solution.py:106
  9.7 192.8 %reduce-scatter.3.cloned.1.call-start = ((), (), s32[]{:S(2)}) async-start(), calls=%async_computation.3 | async-start | bytes 2228224 | tf_op jit(solution)/shard_map/reduce_scatter | solution.py:108
  105.9 96.7 %copy-start.4 = (bf16[256,172]{0,1:T(8,128)(2,1)S(1)}, bf16[256,172]{0,1:T(8,128)(2,1)}, u32[]{:S(2)}) copy-start(bf16[256,172]{0,1:T(8,128)(2,1)} %param.16) | copy-start | bytes 264196
  105.9 96.7 %copy-start.5 = (f32[256]{0:T(256)S(1)}, f32[256]{0:T(256)}, u32[]{:S(2)}) copy-start(f32[256]{0:T(256)} %param.15) | copy-start | bytes 3076
  105.9 97.8 %copy-start.2 = (s32[128]{0:T(128)S(1)}, s32[128]{0:T(128)}, u32[]{:S(2)}) copy-start(s32[128]{0:T(128)} %param.21) | copy-start | bytes 1540
  106.0 154.4 %all-gather.5.cloned.1.call-start = ((), (), s32[]{:S(2)}) async-start(), calls=%async_computation.4 | async-start | bytes 1114112 | tf_op jit(solution)/shard_map/all_gather | solution.py:110
  206.2 160.2 %reduce-scatter.5.cloned.1.call-start = ((), (), s32[]{:S(2)}) async-start(), calls=%async_computation.5 | async-start | bytes 2228224 | tf_op jit(solution)/shard_map/reduce_scatter | solution.py:112
  284.7 2.7 copy-start.3
  284.7 81.7 %copy-start.1 = (bf16[128,256]{1,0:T(8,128)(2,1)S(1)}, bf16[128,256]{1,0:T(8,128)(2,1)}, u32[]{:S(2)}) copy-start(bf16[128,256]{1,0:T(8,128)(2,1)} %param.13) | copy-start | bytes 196612
  284.7 347.0 %all-reduce.3.cloned.1.call-start = ((), (), s32[]{:S(2)}) async-start(), calls=%async_computation.6 | async-start | bytes 884736 | tf_op jit(solution)/shard_map/psum | solution.py:119
Sparse Core Ops, SparseCore 0:
  10.3 75.9 all-gather.2
  106.1 96.4 reduce-scatter.2
  206.3 54.0 all-gather.4
  284.9 81.4 reduce-scatter.4
  371.7 259.9 all-reduce.2

commit v2 on v1

--- a/solution.py
+++ b/solution.py
@@ -68,6 +68,28 @@
     )(row_ids, col_ids, live_count.reshape(1), tile_block, source)
 
 
+def gather_rows(x, axis):
+    n = lax.axis_size(axis)
+    spread = jnp.broadcast_to(x[None], (n,) + x.shape)
+    got = lax.all_to_all(spread, axis, 0, 0, tiled=False)
+    return got.reshape(n * x.shape[0], x.shape[1])
+
+
+def scatter_rows(x, axis):
+    n = lax.axis_size(axis)
+    got = lax.all_to_all(x.reshape(n, -1, x.shape[1]), axis, 0, 0, tiled=False)
+    return jnp.sum(got, axis=0)
+
+
+def reduce_all(x, axes):
+    n = lax.psum(1, axes)
+    got = lax.all_to_all(x.reshape(n, -1, x.shape[1]), axes, 0, 0, tiled=False)
+    mine = jnp.sum(got, axis=0)
+    spread = jnp.broadcast_to(mine[None], (n,) + mine.shape)
+    back = lax.all_to_all(spread, axes, 0, 0, tiled=False)
+    return back.reshape(x.shape)
+
+
 def head_block(agg, bias, w_out, node_labels):
     pre_act = agg + bias[None, :]
     squash = jax.nn.sigmoid(pre_act)
@@ -103,20 +125,18 @@
     col_ids = tile_cols[0, 0]
     live_count = tile_count[0, 0]
     proj = jnp.dot(features, w_in, preferred_element_type=jnp.float32).astype(jnp.bfloat16)
-    source = lax.all_gather(proj, "col", axis=0, tiled=True)
+    source = gather_rows(proj, "col")
     partial_value = tile_product(tile_block, row_ids, col_ids, live_count, source, row_tiles, False)
-    agg = lax.psum_scatter(partial_value, "row", scatter_dimension=0, tiled=True)
+    agg = scatter_rows(partial_value, "row")
     loss_sum, out_term, bias_term, grad_z = head_block(agg, bias, w_out, labels)
-    grad_block = lax.all_gather(grad_z, "row", axis=0, tiled=True)
+    grad_block = gather_rows(grad_z, "row")
     back_part = tile_product(tile_block, row_ids, col_ids, live_count, grad_block, col_tiles, True)
-    grad_proj = lax.psum_scatter(back_part, "col", scatter_dimension=0, tiled=True).astype(
-        jnp.bfloat16
-    )
+    grad_proj = scatter_rows(back_part, "col").astype(jnp.bfloat16)
     in_term = jnp.einsum("nf,ng->fg", features, grad_proj, preferred_element_type=jnp.float32)
     extra = jnp.zeros((feat, 2), jnp.float32)
     extra = extra.at[:, 0].set(bias_term).at[0, 1].set(loss_sum)
     packed = jnp.concatenate([in_term, out_term, extra], axis=1)
-    packed = lax.psum(packed, ("row", "col"))
+    packed = reduce_all(packed, ("row", "col"))
     grad_w_in = packed[:, :feat] * scale
     grad_w_out = packed[:, feat : feat + classes] * scale
     grad_bias = packed[:, feat + classes] * scale

time: 646 us -> 303 us (0.47)
  waiting for transfers between devices: 567 us -> 93.9 us
  blocking collectives: 0 us -> 125 us
  starting transfers between devices: 0.21 us -> 40.7 us
  Pallas kernels: 44 us -> 26.5 us
  between operations: 16.3 us -> 3.19 us
    psum x1 -> x0, waiting for transfers between devices: 262 us -> none  [body(): packed = lax.psum(packed, ('row', 'col'))]
    reduce_scatter x2 -> x0, waiting for transfers between devices: 175 us -> none  [the longest x1 96.6 us: body(): lax.psum_scatter(partial_value, 'row', scatter_dimension=0, tiled=True)]
    all_gather x2 -> x0, waiting for transfers between devices: 130 us -> none  [the longest x1 75.9 us: body(): source = lax.all_gather(proj, 'col', axis=0, tiled=True)]
    all_to_all x0 -> x3, blocking collectives: none -> 125 us  [the longest x1 60 us: scatter_rows(): got = lax.all_to_all(x.reshape(n, -1, x.shape[1]), axis, 0, 0, tiled=False)]
    all_to_all x0 -> x3, waiting for transfers between devices: none -> 93.9 us  [the longest x1 47 us: scatter_rows(): got = lax.all_to_all(x.reshape(n, -1, x.shape[1]), axis, 0, 0, tiled=False)]
    all_to_all x0 -> x3, starting transfers between devices: none -> 40.7 us  [the longest x1 26.2 us: scatter_rows(): got = lax.all_to_all(x.reshape(n, -1, x.shape[1]), axis, 0, 0, tiled=False)]
    pallas_call x2, Pallas kernels: 44 us -> 26.5 us  [tile_product(): pl.pallas_call(lambda *refs: _tile_kernel(transpose, *refs), grid_spec=gr...]
  transfers between devices with their start and end apart: 5 -> 3, of which waited for: 5 -> 3; matrix products, arithmetic and copies ran while one was open for 1% -> 1% of each run, Pallas kernels for 0% -> 0%
where the time goes in v2:
time: 303 us; the launch traced here: 304 us
  blocking collectives  125 us (41%)
  waiting for transfers between devices  93.9 us (31%)
  starting transfers between devices  40.7 us (13%)
  Pallas kernels  26.5 us (9%)
  local copies, waits for them, and re-layouts  9.55 us (3%)
  between operations  3.19 us (1%)
    all_to_all x1, blocking collectives, scatter_rows(): got = lax.all_to_all(x.reshape(n, -1, x.shape[1]), axis, 0, 0, tiled=False)  60 us
    all_to_all x1, waiting for transfers between devices, scatter_rows(): got = lax.all_to_all(x.reshape(n, -1, x.shape[1]), axis, 0, 0, tiled=False)  47 us
    all_to_all x1, blocking collectives, gather_rows(): got = lax.all_to_all(spread, axis, 0, 0, tiled=False)  33.7 us
    all_to_all x1, blocking collectives, reduce_all(): got = lax.all_to_all(x.reshape(n, -1, x.shape[1]), axes, 0, 0, tiled=False)  31.6 us
    pallas_call x2, Pallas kernels, tile_product(): pl.pallas_call(lambda *refs: _tile_kernel(transpose, *refs), grid_spec=gr...  26.5 us
    all_to_all x1, waiting for transfers between devices, gather_rows(): got = lax.all_to_all(spread, axis, 0, 0, tiled=False)  26.4 us
    all_to_all x1, starting transfers between devices, scatter_rows(): got = lax.all_to_all(x.reshape(n, -1, x.shape[1]), axis, 0, 0, tiled=False)  26.2 us
    all_to_all x1, waiting for transfers between devices, reduce_all(): back = lax.all_to_all(spread, axes, 0, 0, tiled=False)  20.5 us
  transfers between devices with their start and end apart: 3, of which 3 were waited for; matrix products, arithmetic and copies ran while one was open for 1% of the time, Pallas kernels for 0%

profile of v2, /device:TPU:1, one launch (start us, length us, event | category | flops | bytes accessed | tf_op | source)
XLA Modules:
  0.0 304.4 jit_solution(2648517113774302806)
XLA Ops:
  0.6 0.0 copy-start
  0.6 0.9 copy-done
  1.5 1.0 convolution_convert_fusion.1
  2.5 1.1 broadcast_in_dim.6
  3.6 9.0 %all-to-all-start = ((bf16[16,128,256]{2,1,0:T(8,128)(2,1)}), bf16[16,128,256]{2,1,0:T(8,128)(2,1)S(1)}, u32[]{:S(2)}, u32[]{:S(2)}) async-start(bf16[16,128,256]{2,1,0:T(8,128)(2,1)} %broadcast_in_dim.6), calls=%async_computation | async-start | bytes 2097152 | tf_op jit(solution)/shard_map/all_to_all | solution.py:74
  13.3 26.4 %all-to-all-done = bf16[16,128,256]{2,1,0:T(8,128)(2,1)S(1)} async-done(((bf16[16,128,256]{2,1,0:T(8,128)(2,1)}), bf16[16,128,256]{2,1,0:T(8,128)(2,1)S(1)}, u32[]{:S(2)}, u32[]{:S(2)}) %all-to-all-start) | async-done | bytes 1048608 | tf_op jit(solution)/shard_map/all_to_all | solution.py:74
  39.7 0.0 copy-start.1
  39.7 1.0 copy-done.1
  40.7 12.1 %shard_map.128 = f32[2048,256]{1,0:T(8,128)} custom-call(s32[128]{0:T(128)} %bitcast.39, s32[128]{0:T(128)} %bitcast.41, s32[1]{0:T(128)} %bitcast.27.refs_2_, bf16[128,128,128]{2,1,0:T(8,128)(2,1)} %bitcast.29, bf16[2048,256]{1,0:T(8,128)(2,1)} %bitcast.33), custom_call_target="tpu_custom_call" | custom-call | tf_op jit(solution)/shard_map/pallas_call | solution.py:63
  52.8 60.0 %all_to_all.30 = f32[16,128,256]{2,1,0:T(8,128)S(1)} all-to-all(f32[16,128,256]{2,1,0:T(8,128)} %bitcast.32), channel_id=1, replica_groups=mesh['row'=16,'col'=16] {'row'}, dimensions={0} | all-to-all | bytes 4194304 | tf_op jit(solution)/shard_map/all_to_all | solution.py:80
  112.7 0.0 copy-start.4
  112.7 0.0 copy-start.5
  112.7 0.0 copy-start.3
  112.7 0.1 reduce_sum.63
  112.9 0.8 copy-done.4
  113.6 0.0 copy-done.5
  113.6 0.2 fusion.7
  113.8 0.0 copy-done.3
  113.9 0.1 select_reduce_fusion
  113.9 0.6 subtract_reduce_fusion
  114.5 0.2 convert_reduce_fusion
  114.7 0.1 broadcast_in_dim.7
  114.9 33.7 %all_to_all.31 = bf16[16,128,256]{2,1,0:T(8,128)(2,1)} all-to-all(bf16[16,128,256]{2,1,0:T(8,128)(2,1)S(1)} %broadcast_in_dim.7), channel_id=1, replica_groups=mesh['row'=16,'col'=16] {'row'}, dimensions={0} | all-to-all | bytes 2097152 | tf_op jit(solution)/shard_map/all_to_all | solution.py:74
  148.5 14.4 %shard_map.129 = f32[2048,256]{1,0:T(8,128)} custom-call(s32[128]{0:T(128)} %bitcast.40, s32[128]{0:T(128)} %bitcast.42, s32[1]{0:T(128)} %bitcast.28.refs_2_, bf16[128,128,128]{2,1,0:T(8,128)(2,1)} %bitcast.30, bf16[2048,256]{1,0:T(8,128)(2,1)} %bitcast.34), custom_call_target="tpu_custom_call" | custom-call | tf_op jit(solution)/shard_map/pallas_call | solution.py:63
  163.0 26.2 %all-to-all-start.3 = ((f32[16,128,256]{2,1,0:T(8,128)}), f32[16,128,256]{2,1,0:T(8,128)S(1)}, u32[]{:S(2)}, u32[]{:S(2)}) async-start(f32[16,128,256]{2,1,0:T(8,128)} %bitcast.31), calls=%async_computation.3 | async-start | bytes 4194304 | tf_op jit(solution)/shard_map/all_to_all | solution.py:80
  189.1 0.0 copy-start.2
  189.1 0.6 fusion.6
  189.7 2.0 scatter.9
  191.7 0.2 fusion.4
  191.9 47.0 %all-to-all-done.3 = f32[16,128,256]{2,1,0:T(8,128)S(1)} async-done(((f32[16,128,256]{2,1,0:T(8,128)}), f32[16,128,256]{2,1,0:T(8,128)S(1)}, u32[]{:S(2)}, u32[]{:S(2)}) %all-to-all-start.3) | async-done | bytes 2097184 | tf_op jit(solution)/shard_map/all_to_all | solution.py:80
  238.9 0.1 reduce_sum.65
  239.1 0.0 copy-done.2
  239.1 0.2 convolution_bitcast_fusion
  239.3 0.4 copy.17
  239.7 31.6 %all_to_all.32 = f32[256,1,430]{2,1,0:T(1,128)S(1)} all-to-all(f32[256,1,430]{2,1,0:T(1,128)S(1)} %copy.17), channel_id=1, replica_groups=mesh['row'=16,'col'=16] {'row','col'}, dimensions={0} | all-to-all | bytes 880640 | tf_op jit(solution)/shard_map/all_to_all | solution.py:86
  271.3 0.4 reduce_sum.69
  271.7 1.1 broadcast_in_dim.8
  272.7 5.6 %all-to-all-start.5 = ((f32[256,1,430]{2,1,0:T(1,128)}), f32[256,1,430]{2,1,0:T(1,128)S(1)}, u32[]{:S(2)}, u32[]{:S(2)}) async-start(f32[256,1,430]{2,1,0:T(1,128)} %broadcast_in_dim.8), calls=%async_computation.5 | async-start | bytes 1048576 | tf_op jit(solution)/shard_map/all_to_all | solution.py:89
  278.3 0.8 convolution_convert_fusion
  279.1 20.5 %all-to-all-done.5 = f32[256,1,430]{2,1,0:T(1,128)S(1)} async-done(((f32[256,1,430]{2,1,0:T(1,128)}), f32[256,1,430]{2,1,0:T(1,128)S(1)}, u32[]{:S(2)}, u32[]{:S(2)}) %all-to-all-start.5) | async-done | bytes 440352 | tf_op jit(solution)/shard_map/all_to_all | solution.py:89
  299.7 0.3 copy.18
  300.0 0.5 slice.53
  300.5 0.6 slice_multiply_fusion.2
  301.1 0.7 slice_multiply_fusion.1
  301.8 0.8 copy.19
  (4 shorter events, 0.1 us)
Async XLA Ops:
  0.6 0.9 copy-start
  3.6 36.1 %all-to-all-start = ((bf16[16,128,256]{2,1,0:T(8,128)(2,1)}), bf16[16,128,256]{2,1,0:T(8,128)(2,1)S(1)}, u32[]{:S(2)}, u32[]{:S(2)}) async-start(bf16[16,128,256]{2,1,0:T(8,128)(2,1)} %broadcast_in_dim.6), calls=%async_computation | async-start | bytes 2097152 | tf_op jit(solution)/shard_map/all_to_all | solution.py:74
  39.7 1.0 copy-start.1
  112.7 0.9 copy-start.4
  112.7 0.9 copy-start.5
  112.7 1.1 copy-start.3
  163.0 76.0 %all-to-all-start.3 = ((f32[16,128,256]{2,1,0:T(8,128)}), f32[16,128,256]{2,1,0:T(8,128)S(1)}, u32[]{:S(2)}, u32[]{:S(2)}) async-start(f32[16,128,256]{2,1,0:T(8,128)} %bitcast.31), calls=%async_computation.3 | async-start | bytes 4194304 | tf_op jit(solution)/shard_map/all_to_all | solution.py:80
  189.1 49.9 %copy-start.2 = (bf16[128,256]{1,0:T(8,128)(2,1)S(1)}, bf16[128,256]{1,0:T(8,128)(2,1)}, u32[]{:S(2)}) copy-start(bf16[128,256]{1,0:T(8,128)(2,1)} %param.13) | copy-start | bytes 196612
  272.7 26.9 %all-to-all-start.5 = ((f32[256,1,430]{2,1,0:T(1,128)}), f32[256,1,430]{2,1,0:T(1,128)S(1)}, u32[]{:S(2)}, u32[]{:S(2)}) async-start(f32[256,1,430]{2,1,0:T(1,128)} %broadcast_in_dim.8), calls=%async_computation.5 | async-start | bytes 1048576 | tf_op jit(solution)/shard_map/all_to_all | solution.py:89

commit v3 on v2

--- a/solution.py
+++ b/solution.py
@@ -5,7 +5,7 @@
 from jax import lax
 from jax.experimental import pallas as pl
 from jax.experimental.pallas import tpu as pltpu
-from jax.sharding import PartitionSpec as P
+from jax.sharding import Mesh, PartitionSpec as P
 
 TILE = 128
 CHUNK = 8
@@ -69,26 +69,31 @@
 
 
 def gather_rows(x, axis):
-    n = lax.axis_size(axis)
+    n = lax.psum(1, axis)
     spread = jnp.broadcast_to(x[None], (n,) + x.shape)
     got = lax.all_to_all(spread, axis, 0, 0, tiled=False)
     return got.reshape(n * x.shape[0], x.shape[1])
 
 
 def scatter_rows(x, axis):
-    n = lax.axis_size(axis)
+    n = lax.psum(1, axis)
     got = lax.all_to_all(x.reshape(n, -1, x.shape[1]), axis, 0, 0, tiled=False)
     return jnp.sum(got, axis=0)
 
 
+def swap_core(x):
+    return lax.ppermute(x, "core", [(0, 1), (1, 0)])
+
+
 def reduce_all(x, axes):
-    n = lax.psum(1, axes)
-    got = lax.all_to_all(x.reshape(n, -1, x.shape[1]), axes, 0, 0, tiled=False)
-    mine = jnp.sum(got, axis=0)
-    spread = jnp.broadcast_to(mine[None], (n,) + mine.shape)
-    back = lax.all_to_all(spread, axes, 0, 0, tiled=False)
-    return back.reshape(x.shape)
-
+    half = x.shape[0] // 2
+    first = lax.axis_index("core") == 0
+    mine = jnp.where(first, x[:half], x[half:])
+    other = jnp.where(first, x[half:], x[:half])
+    summed = mine + swap_core(other)
+    summed = gather_rows(scatter_rows(summed, axes), axes)
+    partner = swap_core(summed)
+    return jnp.where(first, jnp.concatenate([summed, partner]), jnp.concatenate([partner, summed]))
 
 def head_block(agg, bias, w_out, node_labels):
     pre_act = agg + bias[None, :]
@@ -111,8 +116,8 @@
 
 
 def body(features, w_in, bias, w_out, tiles, tile_rows, tile_cols, tile_count, labels):
-    row_devices = lax.axis_size("row")
-    col_devices = lax.axis_size("col")
+    row_devices = lax.psum(1, ("rh", "core"))
+    col_devices = lax.psum(1, ("cx", "cz"))
     rows_here = features.shape[0]
     feat = features.shape[1]
     classes = w_out.shape[1]
@@ -124,19 +129,24 @@
     row_ids = tile_rows[0, 0]
     col_ids = tile_cols[0, 0]
     live_count = tile_count[0, 0]
+    row_hi = row_ids // 2
+    row_pos = jnp.where(row_ids % 2 == lax.axis_index("core"), row_hi, row_hi + row_tiles // 2)
     proj = jnp.dot(features, w_in, preferred_element_type=jnp.float32).astype(jnp.bfloat16)
-    source = gather_rows(proj, "col")
-    partial_value = tile_product(tile_block, row_ids, col_ids, live_count, source, row_tiles, False)
-    agg = scatter_rows(partial_value, "row")
+    source = gather_rows(gather_rows(proj, "cz"), "cx")
+    partial_value = tile_product(tile_block, row_pos, col_ids, live_count, source, row_tiles, False)
+    half = partial_value.shape[0] // 2
+    summed = partial_value[:half] + swap_core(partial_value[half:])
+    agg = scatter_rows(summed, "rh")
     loss_sum, out_term, bias_term, grad_z = head_block(agg, bias, w_out, labels)
-    grad_block = gather_rows(grad_z, "row")
-    back_part = tile_product(tile_block, row_ids, col_ids, live_count, grad_block, col_tiles, True)
-    grad_proj = scatter_rows(back_part, "col").astype(jnp.bfloat16)
+    gathered = gather_rows(grad_z, "rh")
+    grad_block = jnp.concatenate([gathered, swap_core(gathered)])
+    back_part = tile_product(tile_block, row_pos, col_ids, live_count, grad_block, col_tiles, True)
+    grad_proj = scatter_rows(scatter_rows(back_part, "cx"), "cz").astype(jnp.bfloat16)
     in_term = jnp.einsum("nf,ng->fg", features, grad_proj, preferred_element_type=jnp.float32)
     extra = jnp.zeros((feat, 2), jnp.float32)
     extra = extra.at[:, 0].set(bias_term).at[0, 1].set(loss_sum)
     packed = jnp.concatenate([in_term, out_term, extra], axis=1)
-    packed = reduce_all(packed, ("row", "col"))
+    packed = reduce_all(packed, ("rh", "cx", "cz"))
     grad_w_in = packed[:, :feat] * scale
     grad_w_out = packed[:, feat : feat + classes] * scale
     grad_bias = packed[:, feat + classes] * scale
@@ -148,21 +158,27 @@
 
 
 def solution(mesh):
+    row_size, col_size = mesh.shape["row"], mesh.shape["col"]
+    cz = 4 if col_size % 4 == 0 else 1
+    fine = Mesh(
+        mesh.devices.reshape(row_size // 2, 2, col_size // cz, cz), ("rh", "core", "cx", "cz")
+    )
+    row, col = ("rh", "core"), ("cx", "cz")
     placed = (
-        P(("row", "col"), None),
+        P(row + col, None),
         P(),
         P(),
         P(),
-        P("row", "col", None, None, None),
-        P("row", "col", None),
-        P("row", "col", None),
-        P("row", "col"),
-        P(("col", "row")),
+        P(row, col, None, None, None),
+        P(row, col, None),
+        P(row, col, None),
+        P(row, col),
+        P(col + row),
     )
     return jax.shard_map(
         body,
-        mesh=mesh,
+        mesh=fine,
         in_specs=placed,
-        out_specs=(P(), P(("row", "col"), None), P(), P(), P()),
+        out_specs=(P(), P(row + col, None), P(), P(), P()),
         check_vma=False,
     )

time: 303 us -> 250 us (0.83); the launches traced: 304 us -> 248 us
  waiting for transfers between devices: 93.9 us -> 24.3 us
  starting transfers between devices: 40.7 us -> 49.8 us
    all_to_all x1, waiting for transfers between devices: 47 us -> 8.69 us  [scatter_rows(): got = lax.all_to_all(x.reshape(n, -1, x.shape[1]), axis, 0, 0, tiled=False)]
    all_to_all x1 -> x0, blocking collectives: 31.6 us -> none  [reduce_all(): got = lax.all_to_all(x.reshape(n, -1, x.shape[1]), axes, 0, 0, tiled=False)]
    ppermute x0 -> x4, starting transfers between devices: none -> 30.6 us  [swap_core(): return lax.ppermute(x, 'core', [(0, 1), (1, 0)])]
    all_to_all x1 -> x0, waiting for transfers between devices: 20.5 us -> none  [reduce_all(): back = lax.all_to_all(spread, axes, 0, 0, tiled=False)]
    all_to_all x1 -> x3, blocking collectives: 60 us -> 79.3 us  [scatter_rows(): got = lax.all_to_all(x.reshape(n, -1, x.shape[1]), axis, 0, 0, tiled=False)]
    all_to_all x1, waiting for transfers between devices: 26.4 us -> 10.4 us  [gather_rows(): got = lax.all_to_all(spread, axis, 0, 0, tiled=False)]
    all_to_all x1 -> x3, blocking collectives: 33.7 us -> 46.1 us  [gather_rows(): got = lax.all_to_all(spread, axis, 0, 0, tiled=False)]
    all_to_all x1, starting transfers between devices: 26.2 us -> 15.2 us  [scatter_rows(): got = lax.all_to_all(x.reshape(n, -1, x.shape[1]), axis, 0, 0, tiled=False)]
  transfers between devices with their start and end apart: 3 -> 6, of which waited for: 3 -> 6; matrix products, arithmetic and copies ran while one was open for 1% -> 2% of each run, Pallas kernels for 0% -> 0%
where the time goes in v3:
time: 250 us; the launch traced here: 248 us
  blocking collectives  125 us (50%)
  starting transfers between devices  49.8 us (20%)
  Pallas kernels  28.5 us (11%)
  waiting for transfers between devices  24.3 us (10%)
  local copies, waits for them, and re-layouts  8.82 us (4%)
  other arithmetic  5.1 us (2%)
  between operations  3.25 us (1%)
  matrix products  2.66 us (1%)
    all_to_all x3, blocking collectives, scatter_rows(): got = lax.all_to_all(x.reshape(n, -1, x.shape[1]), axis, 0, 0, tiled=False)  79.3 us
    all_to_all x3, blocking collectives, gather_rows(): got = lax.all_to_all(spread, axis, 0, 0, tiled=False)  46.1 us
    ppermute x4, starting transfers between devices, swap_core(): return lax.ppermute(x, 'core', [(0, 1), (1, 0)])  30.6 us
    pallas_call x2, Pallas kernels, tile_product(): pl.pallas_call(lambda *refs: _tile_kernel(transpose, *refs), grid_spec=gr...  28.5 us
    all_to_all x1, starting transfers between devices, scatter_rows(): got = lax.all_to_all(x.reshape(n, -1, x.shape[1]), axis, 0, 0, tiled=False)  15.2 us
    all_to_all x1, waiting for transfers between devices, gather_rows(): got = lax.all_to_all(spread, axis, 0, 0, tiled=False)  10.4 us
    all_to_all x1, waiting for transfers between devices, scatter_rows(): got = lax.all_to_all(x.reshape(n, -1, x.shape[1]), axis, 0, 0, tiled=False)  8.69 us
    ppermute x4, waiting for transfers between devices, swap_core(): return lax.ppermute(x, 'core', [(0, 1), (1, 0)])  5.2 us
  transfers between devices with their start and end apart: 6, of which 6 were waited for; matrix products, arithmetic and copies ran while one was open for 2% of the time, Pallas kernels for 0%

profile of v3, /device:TPU:1, one launch (start us, length us, event | category | flops | bytes accessed | tf_op | source)
XLA Modules:
  0.0 247.9 jit_solution(18222078939574687898)
XLA Ops:
  0.6 0.0 copy-start
  0.6 0.9 copy-done
  1.5 1.0 convolution_convert_fusion.1
  2.5 0.0 copy-start.7
  2.6 13.1 %all_to_all.40 = bf16[4,128,256]{2,1,0:T(8,128)(2,1)S(1)} all-to-all(bf16[4,128,256]{2,1,0:T(8,128)(2,1)S(1)} %broadcast_in_dim.10), channel_id=1, replica_groups=mesh['rh'=8,'core'=2,'cx'=4,'cz'=4] {'cz'}, dimensions={0} | all-to-all | bytes 524288 | tf_op jit(solution)/shard_map/all_to_all | solution.py:74
  15.6 1.1 broadcast_in_dim.12
  16.7 4.0 %all-to-all-start.1 = ((bf16[4,512,256]{2,1,0:T(8,128)(2,1)}), bf16[4,512,256]{2,1,0:T(8,128)(2,1)S(1)}, u32[]{:S(2)}, u32[]{:S(2)}) async-start(bf16[4,512,256]{2,1,0:T(8,128)(2,1)} %broadcast_in_dim.12), calls=%async_computation.1 | async-start | bytes 2097152 | tf_op jit(solution)/shard_map/all_to_all | solution.py:74
  21.4 0.0 copy-done.7
  21.4 0.5 compare_select_fusion.refs_0_
  21.9 10.4 %all-to-all-done.1 = bf16[4,512,256]{2,1,0:T(8,128)(2,1)S(1)} async-done(((bf16[4,512,256]{2,1,0:T(8,128)(2,1)}), bf16[4,512,256]{2,1,0:T(8,128)(2,1)S(1)}, u32[]{:S(2)}, u32[]{:S(2)}) %all-to-all-start.1) | async-done | bytes 1048608 | tf_op jit(solution)/shard_map/all_to_all | solution.py:74
  32.3 0.0 copy-start.2
  32.3 1.0 copy-done.2
  33.3 12.9 %shard_map.128 = f32[2048,256]{1,0:T(8,128)} custom-call(s32[128]{0:T(128)} %compare_select_fusion.refs_0_, s32[128]{0:T(128)} %bitcast.48, s32[1]{0:T(128)} %bitcast.36.refs_2_, bf16[128,128,128]{2,1,0:T(8,128)(2,1)} %bitcast.38, bf16[2048,256]{1,0:T(8,128)(2,1)} %bitcast.42), custom_call_target="tpu_custom_call" | custom-call | tf_op jit(solution)/shard_map/pallas_call | solution.py:63
  46.3 0.0 copy-start.1
  46.3 1.4 slice.72
  47.7 14.1 %collective-permute-start = (f32[1024,256]{1,0:T(8,128)S(1)}, f32[1024,256]{1,0:T(8,128)S(1)}, u32[]{:S(2)}, u32[]{:S(2)}) collective-permute-start(f32[1024,256]{1,0:T(8,128)S(1)} %slice.72), channel_id=1, source_target_pairs={{0,16},{16,0},{1,17},{17,1},{2,18},{18,2},{3,19},{19,3},{4,20},{20... | collective-permute-start | bytes 3145736 | tf_op jit(solution)/shard_map/ppermute | solution.py:85
  61.8 2.3 collective-permute-done
  64.1 0.0 copy-done.1
  64.1 0.1 slice_add_fusion
  64.2 0.0 copy-start.5
  64.3 0.0 copy-start.6
  64.3 0.0 copy-start.4
  64.3 23.7 %all_to_all.41 = f32[8,128,256]{2,1,0:T(8,128)S(1)} all-to-all(f32[8,128,256]{2,1,0:T(8,128)S(1)} %bitcast.41), channel_id=1, replica_groups=mesh['rh'=8,'core'=2,'cx'=4,'cz'=4] {'rh'}, dimensions={0} | all-to-all | bytes 2097152 | tf_op jit(solution)/shard_map/all_to_all | solution.py:80
  88.0 0.1 reduce_sum.72
  88.0 0.0 copy-done.5
  88.1 0.0 copy-done.6
  88.1 0.2 fusion.7
  88.3 0.0 copy-done.4
  88.3 0.1 select_reduce_fusion
  88.3 0.6 subtract_reduce_fusion
  89.0 0.2 convert_reduce_fusion
  89.2 13.9 %all_to_all.42 = bf16[8,128,256]{2,1,0:T(8,128)(2,1)S(1)} all-to-all(bf16[8,128,256]{2,1,0:T(8,128)(2,1)S(1)} %broadcast_in_dim.13), channel_id=1, replica_groups=mesh['rh'=8,'core'=2,'cx'=4,'cz'=4] {'rh'}, dimensions={0} | all-to-all | bytes 1048576 | tf_op jit(solution)/shard_map/all_to_all | solution.py:74
  103.1 9.3 %collective-permute-start.1 = (bf16[1024,256]{1,0:T(8,128)(2,1)S(1)}, bf16[1024,256]{1,0:T(8,128)(2,1)S(1)}, u32[]{:S(2)}, u32[]{:S(2)}) collective-permute-start(bf16[1024,256]{1,0:T(8,128)(2,1)S(1)} %bitcast.43), channel_id=1, source_target_pairs={{0,16},{16,0},{1,17},{17,1},{2,18},{18,2},{3,19},{19,3},{4,20},{20... | collective-permute-start | bytes 1572872 | tf_op jit(solution)/shard_map/ppermute | solution.py:85
  112.4 1.5 collective-permute-done.1
  113.9 1.1 pad_maximum_fusion.refs_4_
  115.0 15.6 %shard_map.129 = f32[2048,256]{1,0:T(8,128)} custom-call(s32[128]{0:T(128)} %compare_select_fusion.refs_0_, s32[128]{0:T(128)} %bitcast.49, s32[1]{0:T(128)} %bitcast.37.refs_2_, bf16[128,128,128]{2,1,0:T(8,128)(2,1)} %bitcast.39, bf16[2048,256]{1,0:T(8,128)(2,1)} %pad_maximum_fusion.refs_4_), custom_call_target="tpu_custom_call" | custom-call | tf_op jit(solution)/shard_map/pallas_call | solution.py:63
  130.6 32.8 %all_to_all.43 = f32[4,512,256]{2,1,0:T(8,128)S(1)} all-to-all(f32[4,512,256]{2,1,0:T(8,128)} %bitcast.40), channel_id=1, replica_groups=mesh['rh'=8,'core'=2,'cx'=4,'cz'=4] {'cx'}, dimensions={0} | all-to-all | bytes 4194304 | tf_op jit(solution)/shard_map/all_to_all | solution.py:80
  163.4 0.0 copy-start.3
  163.4 1.0 reduce_sum.74
  164.3 15.2 %all-to-all-start.5 = ((f32[4,128,256]{2,1,0:T(8,128)}), f32[4,128,256]{2,1,0:T(8,128)S(1)}, u32[]{:S(2)}, u32[]{:S(2)}) async-start(f32[4,128,256]{2,1,0:T(8,128)} %bitcast.9), calls=%async_computation.5 | async-start | bytes 1048576 | tf_op jit(solution)/shard_map/all_to_all | solution.py:80
  179.6 0.6 fusion.6
  180.2 2.0 scatter.9
  182.1 0.2 fusion.4
  182.3 8.7 %all-to-all-done.5 = f32[4,128,256]{2,1,0:T(8,128)S(1)} async-done(((f32[4,128,256]{2,1,0:T(8,128)}), f32[4,128,256]{2,1,0:T(8,128)S(1)}, u32[]{:S(2)}, u32[]{:S(2)}) %all-to-all-start.5) | async-done | bytes 524320 | tf_op jit(solution)/shard_map/all_to_all | solution.py:80
  191.1 0.0 copy-done.3
  191.1 0.2 convolution_bitcast_fusion
  191.4 4.1 %collective-permute-start.2 = (f32[128,430]{0,1:T(8,128)S(1)}, f32[128,430]{0,1:T(8,128)S(1)}, u32[]{:S(2)}, u32[]{:S(2)}) collective-permute-start(f32[128,430]{0,1:T(8,128)S(1)} %slice_select_fusion), channel_id=1, source_target_pairs={{0,16},{16,0},{1,17},{17,1},{2,18},{18,2},{3,19},{19,3},{4,20},{20... | collective-permute-start | bytes 660488 | tf_op jit(solution)/shard_map/ppermute | solution.py:85
  195.4 1.1 collective-permute-done.2
  196.6 0.1 copy.20
  196.7 22.8 %all_to_all.44 = f32[128,1,430]{2,1,0:T(1,128)S(1)} all-to-all(f32[128,1,430]{2,1,0:T(1,128)S(1)} %copy.20), channel_id=1, replica_groups=mesh['rh'=8,'core'=2,'cx'=4,'cz'=4] {'rh','cx','cz'}, dimensions={0} | all-to-all | bytes 440320 | tf_op jit(solution)/shard_map/all_to_all | solution.py:80
  219.5 0.2 reduce_sum.79
  219.8 0.1 broadcast_in_dim.14
  219.9 19.2 %all_to_all.45 = f32[128,1,430]{2,1,0:T(1,128)S(1)} all-to-all(f32[128,1,430]{2,1,0:T(1,128)S(1)} %broadcast_in_dim.14), channel_id=1, replica_groups=mesh['rh'=8,'core'=2,'cx'=4,'cz'=4] {'rh','cx','cz'}, dimensions={0} | all-to-all | bytes 440320 | tf_op jit(solution)/shard_map/all_to_all | solution.py:74
  239.1 0.1 copy.21
  239.2 3.2 %collective-permute-start.3 = (f32[128,430]{0,1:T(8,128)S(1)}, f32[128,430]{0,1:T(8,128)S(1)}, u32[]{:S(2)}, u32[]{:S(2)}) collective-permute-start(f32[128,430]{0,1:T(8,128)S(1)} %bitcast.46), channel_id=1, source_target_pairs={{0,16},{16,0},{1,17},{17,1},{2,18},{18,2},{3,19},{19,3},{4,20},{20... | collective-permute-start | bytes 660488 | tf_op jit(solution)/shard_map/ppermute | solution.py:85
  242.4 0.8 convolution_convert_fusion
  243.2 0.3 collective-permute-done.3
  243.5 0.1 maximum_select_fusion
  243.5 0.5 slice.75
  244.0 0.6 slice_multiply_fusion.2
  244.6 0.7 slice_multiply_fusion.1
  245.3 0.8 copy.22
  (9 shorter events, 0.2 us)
Async XLA Ops:
  0.6 0.9 copy-start
  2.5 18.8 %copy-start.7 = (s32[1,1,128]{2,1,0:T(1,128)S(1)}, s32[1,1,128]{2,1,0:T(1,128)}, u32[]{:S(2)}) copy-start(s32[1,1,128]{2,1,0:T(1,128)} %param.18) | copy-start | bytes 1540
  16.7 15.6 %all-to-all-start.1 = ((bf16[4,512,256]{2,1,0:T(8,128)(2,1)}), bf16[4,512,256]{2,1,0:T(8,128)(2,1)S(1)}, u32[]{:S(2)}, u32[]{:S(2)}) async-start(bf16[4,512,256]{2,1,0:T(8,128)(2,1)} %broadcast_in_dim.12), calls=%async_computation.1 | async-start | bytes 2097152 | tf_op jit(solution)/shard_map/all_to_all | solution.py:74
  32.3 1.0 copy-start.2
  46.3 17.8 %copy-start.1 = (f32[2048,256]{1,0:T(8,128)S(1)}, f32[2048,256]{1,0:T(8,128)}, u32[]{:S(2)}) copy-start(f32[2048,256]{1,0:T(8,128)} %shard_map.128) | copy-start | bytes 6291460
  47.7 16.4 %collective-permute-start = (f32[1024,256]{1,0:T(8,128)S(1)}, f32[1024,256]{1,0:T(8,128)S(1)}, u32[]{:S(2)}, u32[]{:S(2)}) collective-permute-start(f32[1024,256]{1,0:T(8,128)S(1)} %slice.72), channel_id=1, source_target_pairs={{0,16},{16,0},{1,17},{17,1},{2,18},{18,2},{3,19},{19,3},{4,20},{20... | collective-permute-start | bytes 3145736 | tf_op jit(solution)/shard_map/ppermute | solution.py:85
  64.2 23.8 %copy-start.5 = (bf16[256,172]{0,1:T(8,128)(2,1)S(1)}, bf16[256,172]{0,1:T(8,128)(2,1)}, u32[]{:S(2)}) copy-start(bf16[256,172]{0,1:T(8,128)(2,1)} %param.16) | copy-start | bytes 264196
  64.3 23.8 %copy-start.6 = (f32[256]{0:T(256)S(1)}, f32[256]{0:T(256)}, u32[]{:S(2)}) copy-start(f32[256]{0:T(256)} %param.15) | copy-start | bytes 3076
  64.3 24.0 %copy-start.4 = (s32[128]{0:T(128)S(1)}, s32[128]{0:T(128)}, u32[]{:S(2)}) copy-start(s32[128]{0:T(128)} %param.21) | copy-start | bytes 1540
  103.1 10.8 %collective-permute-start.1 = (bf16[1024,256]{1,0:T(8,128)(2,1)S(1)}, bf16[1024,256]{1,0:T(8,128)(2,1)S(1)}, u32[]{:S(2)}, u32[]{:S(2)}) collective-permute-start(bf16[1024,256]{1,0:T(8,128)(2,1)S(1)} %bitcast.43), channel_id=1, source_target_pairs={{0,16},{16,0},{1,17},{17,1},{2,18},{18,2},{3,19},{19,3},{4,20},{20... | collective-permute-start | bytes 1572872 | tf_op jit(solution)/shard_map/ppermute | solution.py:85
  163.4 27.7 %copy-start.3 = (bf16[128,256]{1,0:T(8,128)(2,1)S(1)}, bf16[128,256]{1,0:T(8,128)(2,1)}, u32[]{:S(2)}) copy-start(bf16[128,256]{1,0:T(8,128)(2,1)} %param.13) | copy-start | bytes 196612
  164.3 26.7 %all-to-all-start.5 = ((f32[4,128,256]{2,1,0:T(8,128)}), f32[4,128,256]{2,1,0:T(8,128)S(1)}, u32[]{:S(2)}, u32[]{:S(2)}) async-start(f32[4,128,256]{2,1,0:T(8,128)} %bitcast.9), calls=%async_computation.5 | async-start | bytes 1048576 | tf_op jit(solution)/shard_map/all_to_all | solution.py:80
  191.4 5.2 %collective-permute-start.2 = (f32[128,430]{0,1:T(8,128)S(1)}, f32[128,430]{0,1:T(8,128)S(1)}, u32[]{:S(2)}, u32[]{:S(2)}) collective-permute-start(f32[128,430]{0,1:T(8,128)S(1)} %slice_select_fusion), channel_id=1, source_target_pairs={{0,16},{16,0},{1,17},{17,1},{2,18},{18,2},{3,19},{19,3},{4,20},{20... | collective-permute-start | bytes 660488 | tf_op jit(solution)/shard_map/ppermute | solution.py:85
  239.2 4.3 %collective-permute-start.3 = (f32[128,430]{0,1:T(8,128)S(1)}, f32[128,430]{0,1:T(8,128)S(1)}, u32[]{:S(2)}, u32[]{:S(2)}) collective-permute-start(f32[128,430]{0,1:T(8,128)S(1)} %bitcast.46), channel_id=1, source_target_pairs={{0,16},{16,0},{1,17},{17,1},{2,18},{18,2},{3,19},{19,3},{4,20},{20... | collective-permute-start | bytes 660488 | tf_op jit(solution)/shard_map/ppermute | solution.py:85

commit v4 on v3

--- a/solution.py
+++ b/solution.py
@@ -11,41 +11,43 @@
 CHUNK = 8
 
 
-def _tile_kernel(transpose, rows_ref, cols_ref, count_ref, tiles_ref, src_ref, out_ref):
+def _dense_kernel(transpose, rows_ref, cols_ref, count_ref, tiles_ref, src_ref, out_ref, dense_ref):
     step = pl.program_id(0)
     count = count_ref[0]
 
     @pl.when(step == 0)
     def _():
-        out_ref[...] = jnp.zeros_like(out_ref)
+        dense_ref[...] = jnp.zeros_like(dense_ref)
 
     for j in range(CHUNK):
         slot = step * CHUNK + j
 
         @pl.when(slot < count)
         def _():
-            if transpose:
-                src_at = rows_ref[slot]
-                dst_at = cols_ref[slot]
-            else:
-                src_at = cols_ref[slot]
-                dst_at = rows_ref[slot]
-            src = src_ref[pl.ds(pl.multiple_of(src_at * TILE, TILE), TILE), :]
-            tile = tiles_ref[j]
-            if transpose:
-                part = lax.dot_general(
-                    tile, src, (((0,), (0,)), ((), ())), preferred_element_type=jnp.float32
-                )
-            else:
-                part = jnp.dot(tile, src, preferred_element_type=jnp.float32)
-            dst = pl.ds(pl.multiple_of(dst_at * TILE, TILE), TILE)
-            out_ref[dst, :] += part
+            at_row = pl.multiple_of(rows_ref[slot] * TILE, TILE)
+            at_col = pl.multiple_of(cols_ref[slot] * TILE, TILE)
+            dense_ref[pl.ds(at_row, TILE), pl.ds(at_col, TILE)] = tiles_ref[j]
+
+    @pl.when(step == pl.num_programs(0) - 1)
+    def _():
+        if transpose:
+            out_ref[...] = jnp.dot(src_ref[...], dense_ref[...], preferred_element_type=jnp.float32)
+        else:
+            out_ref[...] = jnp.dot(dense_ref[...], src_ref[...], preferred_element_type=jnp.float32)
 
 
 def tile_product(tile_block, row_ids, col_ids, live_count, source, out_tiles, transpose):
     slots = tile_block.shape[0]
     width = source.shape[1]
     steps = slots // CHUNK
+    src_tiles = source.shape[0] // TILE
+    dense_shape = (out_tiles * TILE, src_tiles * TILE)
+    if transpose:
+        source = source.T
+        dense_shape = (src_tiles * TILE, out_tiles * TILE)
+        out_shape = (width, out_tiles * TILE)
+    else:
+        out_shape = (out_tiles * TILE, width)
 
     def tiles_map(i, rows, cols, count):
         last = jnp.maximum(count[0] - 1, 0) // CHUNK
@@ -58,14 +60,16 @@
             pl.BlockSpec((CHUNK, TILE, TILE), tiles_map),
             pl.BlockSpec(source.shape, lambda i, rows, cols, count: (0, 0)),
         ],
-        out_specs=pl.BlockSpec((out_tiles * TILE, width), lambda i, rows, cols, count: (0, 0)),
+        out_specs=pl.BlockSpec(out_shape, lambda i, rows, cols, count: (0, 0)),
+        scratch_shapes=[pltpu.VMEM(dense_shape, jnp.bfloat16)],
     )
-    return pl.pallas_call(
-        lambda *refs: _tile_kernel(transpose, *refs),
+    result = pl.pallas_call(
+        lambda *refs: _dense_kernel(transpose, *refs),
         grid_spec=grid_spec,
-        out_shape=jax.ShapeDtypeStruct((out_tiles * TILE, width), jnp.float32),
+        out_shape=jax.ShapeDtypeStruct(out_shape, jnp.float32),
         compiler_params=pltpu.CompilerParams(dimension_semantics=("arbitrary",)),
     )(row_ids, col_ids, live_count.reshape(1), tile_block, source)
+    return result.T if transpose else result
 
 
 def gather_rows(x, axis):

time: 250 us -> 231 us (0.924)
  starting transfers between devices: 49.8 us -> 34.2 us
  Pallas kernels: 28.5 us -> 18.8 us
  blocking collectives: 125 us -> 128 us
  local copies, waits for them, and re-layouts: 8.82 us -> 11.6 us
  waiting for transfers between devices: 24.3 us -> 26.9 us
    pallas_call x2, Pallas kernels: 28.5 us -> 18.8 us  [tile_product(): pl.pallas_call(lambda *refs: _dense_kernel(transpose, *refs), grid_spec=g...]
    all_to_all x1, starting transfers between devices: 15.2 us -> 7.24 us  [scatter_rows(): got = lax.all_to_all(x.reshape(n, -1, x.shape[1]), axis, 0, 0, tiled=False)]
    ppermute x4, starting transfers between devices: 30.6 us -> 22.9 us  [swap_core(): return lax.ppermute(x, 'core', [(0, 1), (1, 0)])]
    all_to_all x3, blocking collectives: 79.3 us -> 82.1 us  [scatter_rows(): got = lax.all_to_all(x.reshape(n, -1, x.shape[1]), axis, 0, 0, tiled=False)]
    reshape x1 -> x3, local copies, waits for them, and re-layouts: 0.15 us -> 2.75 us  [scatter_rows(): got = lax.all_to_all(x.reshape(n, -1, x.shape[1]), axis, 0, 0, tiled=False)]
    all_to_all x1, waiting for transfers between devices: 8.69 us -> 11.3 us  [scatter_rows(): got = lax.all_to_all(x.reshape(n, -1, x.shape[1]), axis, 0, 0, tiled=False)]
where the time goes in v4:
time: 231 us; the launch traced here: 230 us
  blocking collectives  128 us (55%)
  starting transfers between devices  34.2 us (15%)
  waiting for transfers between devices  26.9 us (12%)
  Pallas kernels  18.8 us (8%)
  local copies, waits for them, and re-layouts  11.6 us (5%)
  other arithmetic  4.41 us (2%)
  between operations  3.29 us (1%)
  matrix products  2.62 us (1%)
    all_to_all x3, blocking collectives, scatter_rows(): got = lax.all_to_all(x.reshape(n, -1, x.shape[1]), axis, 0, 0, tiled=False)  82.1 us
    all_to_all x3, blocking collectives, gather_rows(): got = lax.all_to_all(spread, axis, 0, 0, tiled=False)  46.3 us
    ppermute x4, starting transfers between devices, swap_core(): return lax.ppermute(x, 'core', [(0, 1), (1, 0)])  22.9 us
    pallas_call x2, Pallas kernels, tile_product(): pl.pallas_call(lambda *refs: _dense_kernel(transpose, *refs), grid_spec=g...  18.8 us
    all_to_all x1, waiting for transfers between devices, scatter_rows(): got = lax.all_to_all(x.reshape(n, -1, x.shape[1]), axis, 0, 0, tiled=False)  11.3 us
    all_to_all x1, waiting for transfers between devices, gather_rows(): got = lax.all_to_all(spread, axis, 0, 0, tiled=False)  10.4 us
    all_to_all x1, starting transfers between devices, scatter_rows(): got = lax.all_to_all(x.reshape(n, -1, x.shape[1]), axis, 0, 0, tiled=False)  7.24 us
    ppermute x4, waiting for transfers between devices, swap_core(): return lax.ppermute(x, 'core', [(0, 1), (1, 0)])  5.2 us
  transfers between devices with their start and end apart: 6, of which 6 were waited for; matrix products, arithmetic and copies ran while one was open for 2% of the time, Pallas kernels for 0%

profile of v4, /device:TPU:1, one launch (start us, length us, event | category | flops | bytes accessed | tf_op | source)
XLA Modules:
  0.0 230.2 jit_solution(7095713846720195343)
XLA Ops:
  0.6 0.0 copy-start
  0.6 0.9 copy-done
  1.5 1.0 convolution_convert_fusion.1
  2.5 0.0 copy-start.7
  2.6 13.1 %all_to_all.40 = bf16[4,128,256]{2,1,0:T(8,128)(2,1)S(1)} all-to-all(bf16[4,128,256]{2,1,0:T(8,128)(2,1)S(1)} %broadcast_in_dim.10), channel_id=1, replica_groups=mesh['rh'=8,'core'=2,'cx'=4,'cz'=4] {'cz'}, dimensions={0} | all-to-all | bytes 524288 | tf_op jit(solution)/shard_map/all_to_all | solution.py:78
  15.6 1.1 broadcast_in_dim.12
  16.7 4.0 %all-to-all-start.1 = ((bf16[4,512,256]{2,1,0:T(8,128)(2,1)}), bf16[4,512,256]{2,1,0:T(8,128)(2,1)S(1)}, u32[]{:S(2)}, u32[]{:S(2)}) async-start(bf16[4,512,256]{2,1,0:T(8,128)(2,1)} %broadcast_in_dim.12), calls=%async_computation.1 | async-start | bytes 2097152 | tf_op jit(solution)/shard_map/all_to_all | solution.py:78
  21.4 0.0 copy-done.7
  21.4 0.5 compare_select_fusion.refs_0_
  21.9 10.4 %all-to-all-done.1 = bf16[4,512,256]{2,1,0:T(8,128)(2,1)S(1)} async-done(((bf16[4,512,256]{2,1,0:T(8,128)(2,1)}), bf16[4,512,256]{2,1,0:T(8,128)(2,1)S(1)}, u32[]{:S(2)}, u32[]{:S(2)}) %all-to-all-start.1) | async-done | bytes 1048608 | tf_op jit(solution)/shard_map/all_to_all | solution.py:78
  32.3 1.0 copy-done.2
  33.3 9.4 %shard_map.128 = f32[2048,256]{1,0:T(8,128)} custom-call(s32[128]{0:T(128)} %compare_select_fusion.refs_0_, s32[128]{0:T(128)} %bitcast.61, s32[1]{0:T(128)} %bitcast.50.refs_2_, bf16[128,128,128]{2,1,0:T(8,128)(2,1)} %bitcast.52, bf16[2048,256]{1,0:T(8,128)(2,1)} %bitcast.57), custom_call_target="tpu_custom_call" | custom-call | tf_op jit(solution)/shard_map/pallas_call | solution.py:66
  42.7 1.4 slice.72
  44.2 6.3 %collective-permute-start = (f32[1024,256]{1,0:T(8,128)S(1)}, f32[1024,256]{1,0:T(8,128)S(1)}, u32[]{:S(2)}, u32[]{:S(2)}) collective-permute-start(f32[1024,256]{1,0:T(8,128)S(1)} %slice.72), channel_id=1, source_target_pairs={{0,16},{16,0},{1,17},{17,1},{2,18},{18,2},{3,19},{19,3},{4,20},{20... | collective-permute-start | bytes 3145736 | tf_op jit(solution)/shard_map/ppermute | solution.py:89
  50.5 2.3 collective-permute-done
  52.7 0.0 copy-done.1
  52.7 0.1 slice_add_fusion
  52.9 0.0 copy-start.5
  52.9 0.0 copy-start.6
  52.9 0.0 copy-start.4
  52.9 28.9 %all_to_all.41 = f32[8,128,256]{2,1,0:T(8,128)S(1)} all-to-all(f32[8,128,256]{2,1,0:T(8,128)S(1)} %bitcast.56), channel_id=1, replica_groups=mesh['rh'=8,'core'=2,'cx'=4,'cz'=4] {'rh'}, dimensions={0} | all-to-all | bytes 2097152 | tf_op jit(solution)/shard_map/all_to_all | solution.py:84
  81.9 0.1 reduce_sum.72
  81.9 0.0 copy-done.5
  82.0 0.0 copy-done.6
  82.0 0.2 fusion.7
  82.2 0.1 select_reduce_fusion
  82.2 0.6 subtract_reduce_fusion
  82.9 0.2 convert_reduce_fusion
  83.1 0.1 copy.29
  83.2 0.1 broadcast_in_dim.13
  83.3 14.1 %all_to_all.42 = bf16[8,128,256]{1,2,0:T(8,128)(2,1)S(1)} all-to-all(bf16[8,128,256]{1,2,0:T(8,128)(2,1)S(1)} %broadcast_in_dim.13), channel_id=1, replica_groups=mesh['rh'=8,'core'=2,'cx'=4,'cz'=4] {'rh'}, dimensions={0} | all-to-all | bytes 1048576 | tf_op jit(solution)/shard_map/all_to_all | solution.py:78
  97.4 0.1 copy_bitcast_fusion.1
  97.4 12.0 %collective-permute-start.1 = (bf16[1024,256]{0,1:T(8,128)(2,1)S(1)}, bf16[1024,256]{0,1:T(8,128)(2,1)S(1)}, u32[]{:S(2)}, u32[]{:S(2)}) collective-permute-start(bf16[1024,256]{0,1:T(8,128)(2,1)S(1)} %copy_bitcast_fusion.1), channel_id=1, source_target_pairs={{0,16},{16,0},{1,17},{17,1},{2,18},{18,2},{3,19},{19,3},{4,20},{20... | collective-permute-start | bytes 1572872 | tf_op jit(solution)/shard_map/ppermute | solution.py:89
  109.4 1.5 collective-permute-done.1
  111.0 1.1 maximum_bitcast_fusion.refs_4_
  112.0 9.4 %shard_map.129 = f32[256,2048]{1,0:T(8,128)} custom-call(s32[128]{0:T(128)} %compare_select_fusion.refs_0_, s32[128]{0:T(128)} %bitcast.62, s32[1]{0:T(128)} %bitcast.51.refs_2_, bf16[128,128,128]{2,1,0:T(8,128)(2,1)} %bitcast.53, bf16[256,2048]{1,0:T(8,128)(2,1)} %maximum_bitcast_fusion.refs_4_), custom_call_target="tpu_custom_call" | custom-call | tf_op jit(solution)/shard_map/pallas_call | solution.py:66
  121.4 1.8 copy.46
  123.2 31.8 %all_to_all.43 = f32[4,512,256]{1,2,0:T(8,128)S(1)} all-to-all(f32[4,512,256]{1,2,0:T(8,128)S(1)} %bitcast.54), channel_id=1, replica_groups=mesh['rh'=8,'core'=2,'cx'=4,'cz'=4] {'cx'}, dimensions={0} | all-to-all | bytes 4194304 | tf_op jit(solution)/shard_map/all_to_all | solution.py:84
  155.0 0.2 reduce_sum.74
  155.3 0.0 copy-start.3
  155.3 0.8 copy_bitcast_fusion.2
  156.1 7.2 %all-to-all-start.5 = ((f32[4,128,256]{1,2,0:T(8,128)}), f32[4,128,256]{1,2,0:T(8,128)S(1)}, u32[]{:S(2)}, u32[]{:S(2)}) async-start(f32[4,128,256]{1,2,0:T(8,128)} %copy_bitcast_fusion.2), calls=%async_computation.5 | async-start | bytes 1048576 | tf_op jit(solution)/shard_map/all_to_all | solution.py:84
  163.3 0.6 fusion.6
  163.9 2.0 scatter.9
  165.9 0.2 fusion.4
  166.1 11.3 %all-to-all-done.5 = f32[4,128,256]{1,2,0:T(8,128)S(1)} async-done(((f32[4,128,256]{1,2,0:T(8,128)}), f32[4,128,256]{1,2,0:T(8,128)S(1)}, u32[]{:S(2)}, u32[]{:S(2)}) %all-to-all-start.5) | async-done | bytes 524320 | tf_op jit(solution)/shard_map/all_to_all | solution.py:84
  177.4 0.0 copy-done.3
  177.4 0.2 convolution_bitcast_fusion
  177.7 1.5 collective-permute-start.2
  179.2 1.1 collective-permute-done.2
  180.3 0.1 copy.35
  180.5 21.4 %all_to_all.44 = f32[128,1,430]{2,1,0:T(1,128)S(1)} all-to-all(f32[128,1,430]{2,1,0:T(1,128)S(1)} %copy.35), channel_id=1, replica_groups=mesh['rh'=8,'core'=2,'cx'=4,'cz'=4] {'rh','cx','cz'}, dimensions={0} | all-to-all | bytes 440320 | tf_op jit(solution)/shard_map/all_to_all | solution.py:84
  201.8 0.2 reduce_sum.79
  202.1 0.1 broadcast_in_dim.14
  202.2 19.2 %all_to_all.45 = f32[128,1,430]{2,1,0:T(1,128)S(1)} all-to-all(f32[128,1,430]{2,1,0:T(1,128)S(1)} %broadcast_in_dim.14), channel_id=1, replica_groups=mesh['rh'=8,'core'=2,'cx'=4,'cz'=4] {'rh','cx','cz'}, dimensions={0} | all-to-all | bytes 440320 | tf_op jit(solution)/shard_map/all_to_all | solution.py:78
  221.4 0.1 copy.36
  221.5 3.2 %collective-permute-start.3 = (f32[128,430]{0,1:T(8,128)S(1)}, f32[128,430]{0,1:T(8,128)S(1)}, u32[]{:S(2)}, u32[]{:S(2)}) collective-permute-start(f32[128,430]{0,1:T(8,128)S(1)} %bitcast.59), channel_id=1, source_target_pairs={{0,16},{16,0},{1,17},{17,1},{2,18},{18,2},{3,19},{19,3},{4,20},{20... | collective-permute-start | bytes 660488 | tf_op jit(solution)/shard_map/ppermute | solution.py:89
  224.7 0.8 convolution_convert_fusion
  225.5 0.3 collective-permute-done.3
  225.8 0.1 maximum_select_fusion
  225.8 0.5 slice.75
  226.3 0.6 slice_multiply_fusion.2
  226.9 0.7 slice_multiply_fusion.1
  227.6 0.8 copy.37
  (11 shorter events, 0.2 us)
Async XLA Ops:
  0.6 0.9 copy-start
  2.5 18.8 %copy-start.7 = (s32[1,1,128]{2,1,0:T(1,128)S(1)}, s32[1,1,128]{2,1,0:T(1,128)}, u32[]{:S(2)}) copy-start(s32[1,1,128]{2,1,0:T(1,128)} %param.18) | copy-start | bytes 1540
  16.7 15.6 %all-to-all-start.1 = ((bf16[4,512,256]{2,1,0:T(8,128)(2,1)}), bf16[4,512,256]{2,1,0:T(8,128)(2,1)S(1)}, u32[]{:S(2)}, u32[]{:S(2)}) async-start(bf16[4,512,256]{2,1,0:T(8,128)(2,1)} %broadcast_in_dim.12), calls=%async_computation.1 | async-start | bytes 2097152 | tf_op jit(solution)/shard_map/all_to_all | solution.py:78
  32.3 1.0 copy-start.2
  42.7 10.0 %copy-start.1 = (f32[2048,256]{1,0:T(8,128)S(1)}, f32[2048,256]{1,0:T(8,128)}, u32[]{:S(2)}) copy-start(f32[2048,256]{1,0:T(8,128)} %shard_map.128) | copy-start | bytes 6291460
  44.2 8.6 %collective-permute-start = (f32[1024,256]{1,0:T(8,128)S(1)}, f32[1024,256]{1,0:T(8,128)S(1)}, u32[]{:S(2)}, u32[]{:S(2)}) collective-permute-start(f32[1024,256]{1,0:T(8,128)S(1)} %slice.72), channel_id=1, source_target_pairs={{0,16},{16,0},{1,17},{17,1},{2,18},{18,2},{3,19},{19,3},{4,20},{20... | collective-permute-start | bytes 3145736 | tf_op jit(solution)/shard_map/ppermute | solution.py:89
  52.9 29.1 %copy-start.5 = (bf16[256,172]{0,1:T(8,128)(2,1)S(1)}, bf16[256,172]{0,1:T(8,128)(2,1)}, u32[]{:S(2)}) copy-start(bf16[256,172]{0,1:T(8,128)(2,1)} %param.16) | copy-start | bytes 264196
  52.9 29.1 %copy-start.6 = (f32[256]{0:T(256)S(1)}, f32[256]{0:T(256)}, u32[]{:S(2)}) copy-start(f32[256]{0:T(256)} %param.15) | copy-start | bytes 3076
  52.9 29.3 %copy-start.4 = (s32[128]{0:T(128)S(1)}, s32[128]{0:T(128)}, u32[]{:S(2)}) copy-start(s32[128]{0:T(128)} %param.21) | copy-start | bytes 1540
  97.4 13.5 %collective-permute-start.1 = (bf16[1024,256]{0,1:T(8,128)(2,1)S(1)}, bf16[1024,256]{0,1:T(8,128)(2,1)S(1)}, u32[]{:S(2)}, u32[]{:S(2)}) collective-permute-start(bf16[1024,256]{0,1:T(8,128)(2,1)S(1)} %copy_bitcast_fusion.1), channel_id=1, source_target_pairs={{0,16},{16,0},{1,17},{17,1},{2,18},{18,2},{3,19},{19,3},{4,20},{20... | collective-permute-start | bytes 1572872 | tf_op jit(solution)/shard_map/ppermute | solution.py:89
  155.3 22.2 %copy-start.3 = (bf16[128,256]{1,0:T(8,128)(2,1)S(1)}, bf16[128,256]{1,0:T(8,128)(2,1)}, u32[]{:S(2)}) copy-start(bf16[128,256]{1,0:T(8,128)(2,1)} %param.13) | copy-start | bytes 196612
  156.1 21.3 %all-to-all-start.5 = ((f32[4,128,256]{1,2,0:T(8,128)}), f32[4,128,256]{1,2,0:T(8,128)S(1)}, u32[]{:S(2)}, u32[]{:S(2)}) async-start(f32[4,128,256]{1,2,0:T(8,128)} %copy_bitcast_fusion.2), calls=%async_computation.5 | async-start | bytes 1048576 | tf_op jit(solution)/shard_map/all_to_all | solution.py:84
  177.7 2.6 %collective-permute-start.2 = (f32[128,430]{0,1:T(8,128)S(1)}, f32[128,430]{0,1:T(8,128)S(1)}, u32[]{:S(2)}, u32[]{:S(2)}) collective-permute-start(f32[128,430]{0,1:T(8,128)S(1)} %slice_select_fusion), channel_id=1, source_target_pairs={{0,16},{16,0},{1,17},{17,1},{2,18},{18,2},{3,19},{19,3},{4,20},{20... | collective-permute-start | bytes 660488 | tf_op jit(solution)/shard_map/ppermute | solution.py:89
  221.5 4.3 %collective-permute-start.3 = (f32[128,430]{0,1:T(8,128)S(1)}, f32[128,430]{0,1:T(8,128)S(1)}, u32[]{:S(2)}, u32[]{:S(2)}) collective-permute-start(f32[128,430]{0,1:T(8,128)S(1)} %bitcast.59), channel_id=1, source_target_pairs={{0,16},{16,0},{1,17},{17,1},{2,18},{18,2},{3,19},{19,3},{4,20},{20... | collective-permute-start | bytes 660488 | tf_op jit(solution)/shard_map/ppermute | solution.py:89

commit v5 on v4

--- a/solution.py
+++ b/solution.py
@@ -120,7 +120,7 @@
 
 
 def body(features, w_in, bias, w_out, tiles, tile_rows, tile_cols, tile_count, labels):
-    row_devices = lax.psum(1, ("rh", "core"))
+    row_devices = lax.psum(1, ("y", "zh", "core"))
     col_devices = lax.psum(1, ("cx", "cz"))
     rows_here = features.shape[0]
     feat = features.shape[1]
@@ -140,9 +140,9 @@
     partial_value = tile_product(tile_block, row_pos, col_ids, live_count, source, row_tiles, False)
     half = partial_value.shape[0] // 2
     summed = partial_value[:half] + swap_core(partial_value[half:])
-    agg = scatter_rows(summed, "rh")
+    agg = scatter_rows(scatter_rows(summed, "y"), "zh")
     loss_sum, out_term, bias_term, grad_z = head_block(agg, bias, w_out, labels)
-    gathered = gather_rows(grad_z, "rh")
+    gathered = gather_rows(grad_z, ("y", "zh"))
     grad_block = jnp.concatenate([gathered, swap_core(gathered)])
     back_part = tile_product(tile_block, row_pos, col_ids, live_count, grad_block, col_tiles, True)
     grad_proj = scatter_rows(scatter_rows(back_part, "cx"), "cz").astype(jnp.bfloat16)
@@ -150,7 +150,7 @@
     extra = jnp.zeros((feat, 2), jnp.float32)
     extra = extra.at[:, 0].set(bias_term).at[0, 1].set(loss_sum)
     packed = jnp.concatenate([in_term, out_term, extra], axis=1)
-    packed = reduce_all(packed, ("rh", "cx", "cz"))
+    packed = reduce_all(packed, ("y", "zh", "cx", "cz"))
     grad_w_in = packed[:, :feat] * scale
     grad_w_out = packed[:, feat : feat + classes] * scale
     grad_bias = packed[:, feat + classes] * scale
@@ -165,9 +165,10 @@
     row_size, col_size = mesh.shape["row"], mesh.shape["col"]
     cz = 4 if col_size % 4 == 0 else 1
     fine = Mesh(
-        mesh.devices.reshape(row_size // 2, 2, col_size // cz, cz), ("rh", "core", "cx", "cz")
+        mesh.devices.reshape(row_size // 4, 2, 2, col_size // cz, cz),
+        ("y", "zh", "core", "cx", "cz"),
     )
-    row, col = ("rh", "core"), ("cx", "cz")
+    row, col = ("y", "zh", "core"), ("cx", "cz")
     placed = (
         P(row + col, None),
         P(),

time: 231 us -> 229 us (level)
  blocking collectives: 128 us -> 136 us
  starting transfers between devices: 34.2 us -> 27.1 us
  waiting for transfers between devices: 26.9 us -> 24.3 us
    ppermute x4, starting transfers between devices: 22.9 us -> 15.3 us  [swap_core(): return lax.ppermute(x, 'core', [(0, 1), (1, 0)])]
    all_to_all x3 -> x4, blocking collectives: 82.1 us -> 86.9 us  [scatter_rows(): got = lax.all_to_all(x.reshape(n, -1, x.shape[1]), axis, 0, 0, tiled=False)]
    all_to_all x3, blocking collectives: 46.3 us -> 49.2 us  [gather_rows(): got = lax.all_to_all(spread, axis, 0, 0, tiled=False)]
    all_to_all x1, waiting for transfers between devices: 11.3 us -> 8.66 us  [scatter_rows(): got = lax.all_to_all(x.reshape(n, -1, x.shape[1]), axis, 0, 0, tiled=False)]
where the time goes in v5:
time: 229 us; the launch traced here: 228 us
  blocking collectives  136 us (59%)
  starting transfers between devices  27.1 us (12%)
  waiting for transfers between devices  24.3 us (11%)
  Pallas kernels  18.8 us (8%)
  local copies, waits for them, and re-layouts  11.6 us (5%)
  other arithmetic  4.43 us (2%)
  between operations  3.29 us (1%)
  matrix products  2.62 us (1%)
    all_to_all x4, blocking collectives, scatter_rows(): got = lax.all_to_all(x.reshape(n, -1, x.shape[1]), axis, 0, 0, tiled=False)  86.9 us
    all_to_all x3, blocking collectives, gather_rows(): got = lax.all_to_all(spread, axis, 0, 0, tiled=False)  49.2 us
    pallas_call x2, Pallas kernels, tile_product(): pl.pallas_call(lambda *refs: _dense_kernel(transpose, *refs), grid_spec=g...  18.8 us
    ppermute x4, starting transfers between devices, swap_core(): return lax.ppermute(x, 'core', [(0, 1), (1, 0)])  15.3 us
    all_to_all x1, waiting for transfers between devices, gather_rows(): got = lax.all_to_all(spread, axis, 0, 0, tiled=False)  10.4 us
    all_to_all x1, waiting for transfers between devices, scatter_rows(): got = lax.all_to_all(x.reshape(n, -1, x.shape[1]), axis, 0, 0, tiled=False)  8.66 us
    all_to_all x1, starting transfers between devices, scatter_rows(): got = lax.all_to_all(x.reshape(n, -1, x.shape[1]), axis, 0, 0, tiled=False)  7.81 us
    ppermute x4, waiting for transfers between devices, swap_core(): return lax.ppermute(x, 'core', [(0, 1), (1, 0)])  5.2 us
  transfers between devices with their start and end apart: 6, of which 6 were waited for; matrix products, arithmetic and copies ran while one was open for 2% of the time, Pallas kernels for 0%

profile of v5, /device:TPU:1, one launch (start us, length us, event | category | flops | bytes accessed | tf_op | source)
XLA Modules:
  0.0 228.3 jit_solution(10496966462769441007)
XLA Ops:
  0.6 0.0 copy-start
  0.6 0.9 copy-done
  1.5 1.0 convolution_convert_fusion.1
  2.5 0.0 copy-start.7
  2.6 13.1 %all_to_all.45 = bf16[4,128,256]{2,1,0:T(8,128)(2,1)S(1)} all-to-all(bf16[4,128,256]{2,1,0:T(8,128)(2,1)S(1)} %broadcast_in_dim.10), channel_id=1, replica_groups=mesh['y'=4,'zh'=2,'core'=2,'cx'=4,'cz'=4] {'cz'}, dimensions={0} | all-to-all | bytes 524288 | tf_op jit(solution)/shard_map/all_to_all | solution.py:78
  15.6 1.1 broadcast_in_dim.12
  16.7 4.0 %all-to-all-start.1 = ((bf16[4,512,256]{2,1,0:T(8,128)(2,1)}), bf16[4,512,256]{2,1,0:T(8,128)(2,1)S(1)}, u32[]{:S(2)}, u32[]{:S(2)}) async-start(bf16[4,512,256]{2,1,0:T(8,128)(2,1)} %broadcast_in_dim.12), calls=%async_computation.1 | async-start | bytes 2097152 | tf_op jit(solution)/shard_map/all_to_all | solution.py:78
  21.4 0.0 copy-done.7
  21.4 0.5 compare_select_fusion.refs_0_
  21.9 10.4 %all-to-all-done.1 = bf16[4,512,256]{2,1,0:T(8,128)(2,1)S(1)} async-done(((bf16[4,512,256]{2,1,0:T(8,128)(2,1)}), bf16[4,512,256]{2,1,0:T(8,128)(2,1)S(1)}, u32[]{:S(2)}, u32[]{:S(2)}) %all-to-all-start.1) | async-done | bytes 1048608 | tf_op jit(solution)/shard_map/all_to_all | solution.py:78
  32.3 1.0 copy-done.2
  33.3 9.4 %shard_map.128 = f32[2048,256]{1,0:T(8,128)} custom-call(s32[128]{0:T(128)} %compare_select_fusion.refs_0_, s32[128]{0:T(128)} %bitcast.63, s32[1]{0:T(128)} %bitcast.51.refs_2_, bf16[128,128,128]{2,1,0:T(8,128)(2,1)} %bitcast.53, bf16[2048,256]{1,0:T(8,128)(2,1)} %bitcast.58), custom_call_target="tpu_custom_call" | custom-call | tf_op jit(solution)/shard_map/pallas_call | solution.py:66
  42.7 1.4 slice.72
  44.2 4.4 %collective-permute-start = (f32[1024,256]{1,0:T(8,128)S(1)}, f32[1024,256]{1,0:T(8,128)S(1)}, u32[]{:S(2)}, u32[]{:S(2)}) collective-permute-start(f32[1024,256]{1,0:T(8,128)S(1)} %slice.72), channel_id=1, source_target_pairs={{0,16},{16,0},{1,17},{17,1},{2,18},{18,2},{3,19},{19,3},{4,20},{20... | collective-permute-start | bytes 3145736 | tf_op jit(solution)/shard_map/ppermute | solution.py:89
  48.6 2.3 %collective-permute-done = f32[1024,256]{1,0:T(8,128)S(1)} collective-permute-done((f32[1024,256]{1,0:T(8,128)S(1)}, f32[1024,256]{1,0:T(8,128)S(1)}, u32[]{:S(2)}, u32[]{:S(2)}) %collective-permute-start) | collective-permute-done | bytes 1048608 | tf_op jit(solution)/shard_map/ppermute | solution.py:89
  50.9 0.0 copy-done.1
  50.9 0.1 slice_add_fusion
  51.0 0.0 copy-start.5
  51.1 0.0 copy-start.6
  51.1 0.0 copy-start.4
  51.1 21.9 %all_to_all.46 = f32[4,256,256]{2,1,0:T(8,128)S(1)} all-to-all(f32[4,256,256]{2,1,0:T(8,128)S(1)} %bitcast.57), channel_id=1, replica_groups=mesh['y'=4,'zh'=2,'core'=2,'cx'=4,'cz'=4] {'y'}, dimensions={0} | all-to-all | bytes 2097152 | tf_op jit(solution)/shard_map/all_to_all | solution.py:84
  72.9 0.1 reduce_sum.81
  73.0 13.4 %all_to_all.47 = f32[2,128,256]{2,1,0:T(8,128)S(1)} all-to-all(f32[2,128,256]{2,1,0:T(8,128)S(1)} %bitcast.60), channel_id=1, replica_groups=mesh['y'=4,'zh'=2,'core'=2,'cx'=4,'cz'=4] {'zh'}, dimensions={0} | all-to-all | bytes 524288 | tf_op jit(solution)/shard_map/all_to_all | solution.py:84
  86.5 0.0 copy-done.5
  86.5 0.2 fusion.7
  86.7 0.1 select_reduce_fusion
  86.8 0.6 subtract_reduce_fusion
  87.4 0.2 convert_reduce_fusion
  87.6 0.1 copy.38
  87.7 0.1 broadcast_in_dim.13
  87.8 17.0 %all_to_all.48 = bf16[8,128,256]{1,2,0:T(8,128)(2,1)S(1)} all-to-all(bf16[8,128,256]{1,2,0:T(8,128)(2,1)S(1)} %broadcast_in_dim.13), channel_id=1, replica_groups=mesh['y'=4,'zh'=2,'core'=2,'cx'=4,'cz'=4] {'y','zh'}, dimensions={0} | all-to-all | bytes 1048576 | tf_op jit(solution)/shard_map/all_to_all | solution.py:78
  104.8 0.1 copy_bitcast_fusion.1
  104.9 3.6 %collective-permute-start.1 = (bf16[1024,256]{0,1:T(8,128)(2,1)S(1)}, bf16[1024,256]{0,1:T(8,128)(2,1)S(1)}, u32[]{:S(2)}, u32[]{:S(2)}) collective-permute-start(bf16[1024,256]{0,1:T(8,128)(2,1)S(1)} %copy_bitcast_fusion.1), channel_id=1, source_target_pairs={{0,16},{16,0},{1,17},{17,1},{2,18},{18,2},{3,19},{19,3},{4,20},{20... | collective-permute-start | bytes 1572872 | tf_op jit(solution)/shard_map/ppermute | solution.py:89
  108.5 1.5 collective-permute-done.1
  110.1 1.1 maximum_bitcast_fusion.refs_4_
  111.1 9.4 %shard_map.129 = f32[256,2048]{1,0:T(8,128)} custom-call(s32[128]{0:T(128)} %compare_select_fusion.refs_0_, s32[128]{0:T(128)} %bitcast.64, s32[1]{0:T(128)} %bitcast.52.refs_2_, bf16[128,128,128]{2,1,0:T(8,128)(2,1)} %bitcast.54, bf16[256,2048]{1,0:T(8,128)(2,1)} %maximum_bitcast_fusion.refs_4_), custom_call_target="tpu_custom_call" | custom-call | tf_op jit(solution)/shard_map/pallas_call | solution.py:66
  120.5 1.8 copy.55
  122.3 27.4 %all_to_all.49 = f32[4,512,256]{1,2,0:T(8,128)S(1)} all-to-all(f32[4,512,256]{1,2,0:T(8,128)S(1)} %bitcast.55), channel_id=1, replica_groups=mesh['y'=4,'zh'=2,'core'=2,'cx'=4,'cz'=4] {'cx'}, dimensions={0} | all-to-all | bytes 4194304 | tf_op jit(solution)/shard_map/all_to_all | solution.py:84
  149.7 0.2 reduce_sum.84
  150.0 0.0 copy-start.3
  150.0 0.8 copy_bitcast_fusion.2
  150.8 7.8 %all-to-all-start.6 = ((f32[4,128,256]{1,2,0:T(8,128)}), f32[4,128,256]{1,2,0:T(8,128)S(1)}, u32[]{:S(2)}, u32[]{:S(2)}) async-start(f32[4,128,256]{1,2,0:T(8,128)} %copy_bitcast_fusion.2), calls=%async_computation.6 | async-start | bytes 1048576 | tf_op jit(solution)/shard_map/all_to_all | solution.py:84
  158.6 0.6 fusion.6
  159.2 2.0 scatter.9
  161.2 0.2 fusion.4
  161.4 8.7 %all-to-all-done.6 = f32[4,128,256]{1,2,0:T(8,128)S(1)} async-done(((f32[4,128,256]{1,2,0:T(8,128)}), f32[4,128,256]{1,2,0:T(8,128)S(1)}, u32[]{:S(2)}, u32[]{:S(2)}) %all-to-all-start.6) | async-done | bytes 524320 | tf_op jit(solution)/shard_map/all_to_all | solution.py:84
  170.1 0.0 copy-done.3
  170.1 0.2 convolution_bitcast_fusion
  170.3 4.1 %collective-permute-start.2 = (f32[128,430]{0,1:T(8,128)S(1)}, f32[128,430]{0,1:T(8,128)S(1)}, u32[]{:S(2)}, u32[]{:S(2)}) collective-permute-start(f32[128,430]{0,1:T(8,128)S(1)} %slice_select_fusion), channel_id=1, source_target_pairs={{0,16},{16,0},{1,17},{17,1},{2,18},{18,2},{3,19},{19,3},{4,20},{20... | collective-permute-start | bytes 660488 | tf_op jit(solution)/shard_map/ppermute | solution.py:89
  174.4 1.1 collective-permute-done.2
  175.6 0.1 copy.44
  175.7 24.1 %all_to_all.50 = f32[128,1,430]{2,1,0:T(1,128)S(1)} all-to-all(f32[128,1,430]{2,1,0:T(1,128)S(1)} %copy.44), channel_id=1, replica_groups=mesh['y'=4,'zh'=2,'core'=2,'cx'=4,'cz'=4] {'y','zh','cx','cz'}, dimensions={0} | all-to-all | bytes 440320 | tf_op jit(solution)/shard_map/all_to_all | solution.py:84
  199.9 0.2 reduce_sum.89
  200.1 0.1 broadcast_in_dim.14
  200.3 19.2 %all_to_all.51 = f32[128,1,430]{2,1,0:T(1,128)S(1)} all-to-all(f32[128,1,430]{2,1,0:T(1,128)S(1)} %broadcast_in_dim.14), channel_id=1, replica_groups=mesh['y'=4,'zh'=2,'core'=2,'cx'=4,'cz'=4] {'y','zh','cx','cz'}, dimensions={0} | all-to-all | bytes 440320 | tf_op jit(solution)/shard_map/all_to_all | solution.py:78
  219.4 0.1 copy.45
  219.6 3.2 %collective-permute-start.3 = (f32[128,430]{0,1:T(8,128)S(1)}, f32[128,430]{0,1:T(8,128)S(1)}, u32[]{:S(2)}, u32[]{:S(2)}) collective-permute-start(f32[128,430]{0,1:T(8,128)S(1)} %bitcast.61), channel_id=1, source_target_pairs={{0,16},{16,0},{1,17},{17,1},{2,18},{18,2},{3,19},{19,3},{4,20},{20... | collective-permute-start | bytes 660488 | tf_op jit(solution)/shard_map/ppermute | solution.py:89
  222.7 0.8 convolution_convert_fusion
  223.6 0.3 collective-permute-done.3
  223.8 0.1 maximum_select_fusion
  223.9 0.5 slice.75
  224.4 0.6 slice_multiply_fusion.2
  225.0 0.7 slice_multiply_fusion.1
  225.7 0.8 copy.46
  (13 shorter events, 0.2 us)
Async XLA Ops:
  0.6 0.9 copy-start
  2.5 18.8 %copy-start.7 = (s32[1,1,128]{2,1,0:T(1,128)S(1)}, s32[1,1,128]{2,1,0:T(1,128)}, u32[]{:S(2)}) copy-start(s32[1,1,128]{2,1,0:T(1,128)} %param.18) | copy-start | bytes 1540
  16.7 15.6 %all-to-all-start.1 = ((bf16[4,512,256]{2,1,0:T(8,128)(2,1)}), bf16[4,512,256]{2,1,0:T(8,128)(2,1)S(1)}, u32[]{:S(2)}, u32[]{:S(2)}) async-start(bf16[4,512,256]{2,1,0:T(8,128)(2,1)} %broadcast_in_dim.12), calls=%async_computation.1 | async-start | bytes 2097152 | tf_op jit(solution)/shard_map/all_to_all | solution.py:78
  32.3 1.0 copy-start.2
  42.7 8.2 %copy-start.1 = (f32[2048,256]{1,0:T(8,128)S(1)}, f32[2048,256]{1,0:T(8,128)}, u32[]{:S(2)}) copy-start(f32[2048,256]{1,0:T(8,128)} %shard_map.128) | copy-start | bytes 6291460
  44.2 6.7 %collective-permute-start = (f32[1024,256]{1,0:T(8,128)S(1)}, f32[1024,256]{1,0:T(8,128)S(1)}, u32[]{:S(2)}, u32[]{:S(2)}) collective-permute-start(f32[1024,256]{1,0:T(8,128)S(1)} %slice.72), channel_id=1, source_target_pairs={{0,16},{16,0},{1,17},{17,1},{2,18},{18,2},{3,19},{19,3},{4,20},{20... | collective-permute-start | bytes 3145736 | tf_op jit(solution)/shard_map/ppermute | solution.py:89
  51.0 35.4 %copy-start.5 = (bf16[256,172]{0,1:T(8,128)(2,1)S(1)}, bf16[256,172]{0,1:T(8,128)(2,1)}, u32[]{:S(2)}) copy-start(bf16[256,172]{0,1:T(8,128)(2,1)} %param.16) | copy-start | bytes 264196
  51.1 35.4 %copy-start.6 = (f32[256]{0:T(256)S(1)}, f32[256]{0:T(256)}, u32[]{:S(2)}) copy-start(f32[256]{0:T(256)} %param.15) | copy-start | bytes 3076
  51.1 35.6 %copy-start.4 = (s32[128]{0:T(128)S(1)}, s32[128]{0:T(128)}, u32[]{:S(2)}) copy-start(s32[128]{0:T(128)} %param.21) | copy-start | bytes 1540
  104.9 5.2 %collective-permute-start.1 = (bf16[1024,256]{0,1:T(8,128)(2,1)S(1)}, bf16[1024,256]{0,1:T(8,128)(2,1)S(1)}, u32[]{:S(2)}, u32[]{:S(2)}) collective-permute-start(bf16[1024,256]{0,1:T(8,128)(2,1)S(1)} %copy_bitcast_fusion.1), channel_id=1, source_target_pairs={{0,16},{16,0},{1,17},{17,1},{2,18},{18,2},{3,19},{19,3},{4,20},{20... | collective-permute-start | bytes 1572872 | tf_op jit(solution)/shard_map/ppermute | solution.py:89
  150.0 20.1 %copy-start.3 = (bf16[128,256]{1,0:T(8,128)(2,1)S(1)}, bf16[128,256]{1,0:T(8,128)(2,1)}, u32[]{:S(2)}) copy-start(bf16[128,256]{1,0:T(8,128)(2,1)} %param.13) | copy-start | bytes 196612
  150.8 19.2 %all-to-all-start.6 = ((f32[4,128,256]{1,2,0:T(8,128)}), f32[4,128,256]{1,2,0:T(8,128)S(1)}, u32[]{:S(2)}, u32[]{:S(2)}) async-start(f32[4,128,256]{1,2,0:T(8,128)} %copy_bitcast_fusion.2), calls=%async_computation.6 | async-start | bytes 1048576 | tf_op jit(solution)/shard_map/all_to_all | solution.py:84
  170.3 5.2 %collective-permute-start.2 = (f32[128,430]{0,1:T(8,128)S(1)}, f32[128,430]{0,1:T(8,128)S(1)}, u32[]{:S(2)}, u32[]{:S(2)}) collective-permute-start(f32[128,430]{0,1:T(8,128)S(1)} %slice_select_fusion), channel_id=1, source_target_pairs={{0,16},{16,0},{1,17},{17,1},{2,18},{18,2},{3,19},{19,3},{4,20},{20... | collective-permute-start | bytes 660488 | tf_op jit(solution)/shard_map/ppermute | solution.py:89
  219.6 4.3 %collective-permute-start.3 = (f32[128,430]{0,1:T(8,128)S(1)}, f32[128,430]{0,1:T(8,128)S(1)}, u32[]{:S(2)}, u32[]{:S(2)}) collective-permute-start(f32[128,430]{0,1:T(8,128)S(1)} %bitcast.61), channel_id=1, source_target_pairs={{0,16},{16,0},{1,17},{17,1},{2,18},{18,2},{3,19},{19,3},{4,20},{20... | collective-permute-start | bytes 660488 | tf_op jit(solution)/shard_map/ppermute | solution.py:89

commit v6 on v5

--- a/solution.py
+++ b/solution.py
@@ -79,10 +79,13 @@
     return got.reshape(n * x.shape[0], x.shape[1])
 
 
-def scatter_rows(x, axis):
+def scatter_rows(x, axis, kind=None):
     n = lax.psum(1, axis)
-    got = lax.all_to_all(x.reshape(n, -1, x.shape[1]), axis, 0, 0, tiled=False)
-    return jnp.sum(got, axis=0)
+    sent = x.reshape(n, -1, x.shape[1])
+    if kind is not None:
+        sent = sent.astype(kind)
+    got = lax.all_to_all(sent, axis, 0, 0, tiled=False)
+    return jnp.sum(got.astype(jnp.float32), axis=0)
 
 
 def swap_core(x):
@@ -140,12 +143,12 @@
     partial_value = tile_product(tile_block, row_pos, col_ids, live_count, source, row_tiles, False)
     half = partial_value.shape[0] // 2
     summed = partial_value[:half] + swap_core(partial_value[half:])
-    agg = scatter_rows(scatter_rows(summed, "y"), "zh")
+    agg = scatter_rows(scatter_rows(summed, "y", jnp.bfloat16), "zh")
     loss_sum, out_term, bias_term, grad_z = head_block(agg, bias, w_out, labels)
     gathered = gather_rows(grad_z, ("y", "zh"))
     grad_block = jnp.concatenate([gathered, swap_core(gathered)])
     back_part = tile_product(tile_block, row_pos, col_ids, live_count, grad_block, col_tiles, True)
-    grad_proj = scatter_rows(scatter_rows(back_part, "cx"), "cz").astype(jnp.bfloat16)
+    grad_proj = scatter_rows(scatter_rows(back_part, "cx", jnp.bfloat16), "cz").astype(jnp.bfloat16)
     in_term = jnp.einsum("nf,ng->fg", features, grad_proj, preferred_element_type=jnp.float32)
     extra = jnp.zeros((feat, 2), jnp.float32)
     extra = extra.at[:, 0].set(bias_term).at[0, 1].set(loss_sum)

time: 229 us -> 213 us (0.930)
  blocking collectives: 136 us -> 109 us
  Pallas kernels: 18.8 us -> 28 us
  waiting for transfers between devices: 24.3 us -> 26.9 us
    all_to_all x4, blocking collectives: 86.9 us -> 62.8 us  [scatter_rows(): got = lax.all_to_all(sent, axis, 0, 0, tiled=False)]
    pallas_call x2, Pallas kernels: 18.8 us -> 28 us  [tile_product(): pl.pallas_call(lambda *refs: _dense_kernel(transpose, *refs), grid_spec=g...]
    all_to_all x3, blocking collectives: 49.2 us -> 46.2 us  [gather_rows(): got = lax.all_to_all(spread, axis, 0, 0, tiled=False)]
    all_to_all x1, waiting for transfers between devices: 8.66 us -> 11.3 us  [scatter_rows(): got = lax.all_to_all(sent, axis, 0, 0, tiled=False)]
    ppermute x4, starting transfers between devices: 15.3 us -> 12.9 us  [swap_core(): return lax.ppermute(x, 'core', [(0, 1), (1, 0)])]
where the time goes in v6:
time: 213 us; the launch traced here: 211 us
  blocking collectives  109 us (51%)
  Pallas kernels  28 us (13%)
  waiting for transfers between devices  26.9 us (13%)
  starting transfers between devices  25 us (12%)
  local copies, waits for them, and re-layouts  9.93 us (5%)
  other arithmetic  6.08 us (3%)
  between operations  3.29 us (2%)
  matrix products  2.61 us (1%)
    all_to_all x4, blocking collectives, scatter_rows(): got = lax.all_to_all(sent, axis, 0, 0, tiled=False)  62.8 us
    all_to_all x3, blocking collectives, gather_rows(): got = lax.all_to_all(spread, axis, 0, 0, tiled=False)  46.2 us
    pallas_call x2, Pallas kernels, tile_product(): pl.pallas_call(lambda *refs: _dense_kernel(transpose, *refs), grid_spec=g...  28 us
    ppermute x4, starting transfers between devices, swap_core(): return lax.ppermute(x, 'core', [(0, 1), (1, 0)])  12.9 us
    all_to_all x1, waiting for transfers between devices, scatter_rows(): got = lax.all_to_all(sent, axis, 0, 0, tiled=False)  11.3 us
    all_to_all x1, waiting for transfers between devices, gather_rows(): got = lax.all_to_all(spread, axis, 0, 0, tiled=False)  10.4 us
    all_to_all x1, starting transfers between devices, scatter_rows(): got = lax.all_to_all(sent, axis, 0, 0, tiled=False)  8.11 us
    ppermute x4, waiting for transfers between devices, swap_core(): return lax.ppermute(x, 'core', [(0, 1), (1, 0)])  5.2 us
  transfers between devices with their start and end apart: 6, of which 6 were waited for; matrix products, arithmetic and copies ran while one was open for 2% of the time, Pallas kernels for 0%

profile of v6, /device:TPU:1, one launch (start us, length us, event | category | flops | bytes accessed | tf_op | source)
XLA Modules:
  0.0 210.9 jit_solution(6764854723247493641)
XLA Ops:
  0.6 0.0 copy-start
  0.6 0.9 copy-done
  1.5 1.0 convolution_convert_fusion.1
  2.5 0.0 copy-start.7
  2.6 13.1 %all_to_all.45 = bf16[4,128,256]{2,1,0:T(8,128)(2,1)S(1)} all-to-all(bf16[4,128,256]{2,1,0:T(8,128)(2,1)S(1)} %broadcast_in_dim.10), channel_id=1, replica_groups=mesh['y'=4,'zh'=2,'core'=2,'cx'=4,'cz'=4] {'cz'}, dimensions={0} | all-to-all | bytes 524288 | tf_op jit(solution)/shard_map/all_to_all | solution.py:78
  15.6 1.1 broadcast_in_dim.12
  16.7 4.0 %all-to-all-start.1 = ((bf16[4,512,256]{2,1,0:T(8,128)(2,1)}), bf16[4,512,256]{2,1,0:T(8,128)(2,1)S(1)}, u32[]{:S(2)}, u32[]{:S(2)}) async-start(bf16[4,512,256]{2,1,0:T(8,128)(2,1)} %broadcast_in_dim.12), calls=%async_computation.1 | async-start | bytes 2097152 | tf_op jit(solution)/shard_map/all_to_all | solution.py:78
  21.4 0.0 copy-done.7
  21.4 0.5 compare_select_fusion.refs_0_
  21.9 10.4 %all-to-all-done.1 = bf16[4,512,256]{2,1,0:T(8,128)(2,1)S(1)} async-done(((bf16[4,512,256]{2,1,0:T(8,128)(2,1)}), bf16[4,512,256]{2,1,0:T(8,128)(2,1)S(1)}, u32[]{:S(2)}, u32[]{:S(2)}) %all-to-all-start.1) | async-done | bytes 1048608 | tf_op jit(solution)/shard_map/all_to_all | solution.py:78
  32.3 1.0 copy-done.2
  33.3 14.0 %shard_map.128 = f32[2048,256]{1,0:T(8,128)} custom-call(s32[128]{0:T(128)} %compare_select_fusion.refs_0_, s32[128]{0:T(128)} %bitcast.63, s32[1]{0:T(128)} %bitcast.51.refs_2_, bf16[128,128,128]{2,1,0:T(8,128)(2,1)} %bitcast.53, bf16[2048,256]{1,0:T(8,128)(2,1)} %bitcast.57), custom_call_target="tpu_custom_call" | custom-call | tf_op jit(solution)/shard_map/pallas_call | solution.py:66
  47.4 1.4 slice.72
  48.8 0.0 copy-start.5
  48.8 0.0 copy-start.6
  48.8 3.6 %collective-permute-start = (f32[1024,256]{1,0:T(8,128)S(1)}, f32[1024,256]{1,0:T(8,128)S(1)}, u32[]{:S(2)}, u32[]{:S(2)}) collective-permute-start(f32[1024,256]{1,0:T(8,128)S(1)} %slice.72), channel_id=1, source_target_pairs={{0,16},{16,0},{1,17},{17,1},{2,18},{18,2},{3,19},{19,3},{4,20},{20... | collective-permute-start | bytes 3145736 | tf_op jit(solution)/shard_map/ppermute | solution.py:92
  52.4 2.3 %collective-permute-done = f32[1024,256]{1,0:T(8,128)S(1)} collective-permute-done((f32[1024,256]{1,0:T(8,128)S(1)}, f32[1024,256]{1,0:T(8,128)S(1)}, u32[]{:S(2)}, u32[]{:S(2)}) %collective-permute-start) | collective-permute-done | bytes 1048608 | tf_op jit(solution)/shard_map/ppermute | solution.py:92
  54.7 0.0 copy-done.1
  54.7 0.2 fusion.2
  54.8 0.0 copy-start.4
  54.9 11.0 %all_to_all.46 = bf16[4,256,256]{2,1,0:T(8,128)(2,1)S(1)} all-to-all(bf16[4,256,256]{2,1,0:T(8,128)(2,1)S(1)} %bitcast.58), channel_id=1, replica_groups=mesh['y'=4,'zh'=2,'core'=2,'cx'=4,'cz'=4] {'y'}, dimensions={0} | all-to-all | bytes 1048576 | tf_op jit(solution)/shard_map/all_to_all | solution.py:87
  65.9 0.1 convert_reduce_fusion.1
  66.0 15.7 %all_to_all.47 = f32[2,128,256]{2,1,0:T(8,128)S(1)} all-to-all(f32[2,128,256]{2,1,0:T(8,128)S(1)} %bitcast.60), channel_id=1, replica_groups=mesh['y'=4,'zh'=2,'core'=2,'cx'=4,'cz'=4] {'zh'}, dimensions={0} | all-to-all | bytes 524288 | tf_op jit(solution)/shard_map/all_to_all | solution.py:87
  81.7 0.0 copy-done.5
  81.7 0.0 copy-done.6
  81.7 0.2 fusion.8
  81.9 0.1 select_reduce_fusion
  82.0 0.6 subtract_reduce_fusion
  82.6 0.2 convert_reduce_fusion.2
  82.8 0.1 copy.38
  83.0 0.1 broadcast_in_dim.13
  83.0 14.0 %all_to_all.48 = bf16[8,128,256]{1,2,0:T(8,128)(2,1)S(1)} all-to-all(bf16[8,128,256]{1,2,0:T(8,128)(2,1)S(1)} %broadcast_in_dim.13), channel_id=1, replica_groups=mesh['y'=4,'zh'=2,'core'=2,'cx'=4,'cz'=4] {'y','zh'}, dimensions={0} | all-to-all | bytes 1048576 | tf_op jit(solution)/shard_map/all_to_all | solution.py:78
  97.0 0.1 copy_bitcast_fusion.1
  97.1 4.7 %collective-permute-start.1 = (bf16[1024,256]{0,1:T(8,128)(2,1)S(1)}, bf16[1024,256]{0,1:T(8,128)(2,1)S(1)}, u32[]{:S(2)}, u32[]{:S(2)}) collective-permute-start(bf16[1024,256]{0,1:T(8,128)(2,1)S(1)} %copy_bitcast_fusion.1), channel_id=1, source_target_pairs={{0,16},{16,0},{1,17},{17,1},{2,18},{18,2},{3,19},{19,3},{4,20},{20... | collective-permute-start | bytes 1572872 | tf_op jit(solution)/shard_map/ppermute | solution.py:92
  101.8 1.5 collective-permute-done.1
  103.3 1.1 maximum_bitcast_fusion.refs_4_
  104.4 14.0 %shard_map.129 = f32[256,2048]{1,0:T(8,128)} custom-call(s32[128]{0:T(128)} %compare_select_fusion.refs_0_, s32[128]{0:T(128)} %bitcast.64, s32[1]{0:T(128)} %bitcast.52.refs_2_, bf16[128,128,128]{2,1,0:T(8,128)(2,1)} %bitcast.54, bf16[256,2048]{1,0:T(8,128)(2,1)} %maximum_bitcast_fusion.refs_4_), custom_call_target="tpu_custom_call" | custom-call | tf_op jit(solution)/shard_map/pallas_call | solution.py:66
  118.4 1.7 convert_element_type.53
  120.1 0.1 copy.55
  120.2 15.1 %all_to_all.49 = bf16[4,512,256]{1,2,0:T(8,128)(2,1)S(1)} all-to-all(bf16[4,512,256]{1,2,0:T(8,128)(2,1)S(1)} %bitcast.56), channel_id=1, replica_groups=mesh['y'=4,'zh'=2,'core'=2,'cx'=4,'cz'=4] {'cx'}, dimensions={0} | all-to-all | bytes 2097152 | tf_op jit(solution)/shard_map/all_to_all | solution.py:87
  135.3 0.1 convert_reduce_fusion
  135.5 0.8 copy_bitcast_fusion.2
  136.3 8.1 %all-to-all-start.6 = ((f32[4,128,256]{1,2,0:T(8,128)}), f32[4,128,256]{1,2,0:T(8,128)S(1)}, u32[]{:S(2)}, u32[]{:S(2)}) async-start(f32[4,128,256]{1,2,0:T(8,128)} %copy_bitcast_fusion.2), calls=%async_computation.6 | async-start | bytes 1048576 | tf_op jit(solution)/shard_map/all_to_all | solution.py:87
  144.4 0.6 fusion.7
  145.0 2.0 scatter.9
  147.0 0.2 fusion.5
  147.2 11.3 %all-to-all-done.6 = f32[4,128,256]{1,2,0:T(8,128)S(1)} async-done(((f32[4,128,256]{1,2,0:T(8,128)}), f32[4,128,256]{1,2,0:T(8,128)S(1)}, u32[]{:S(2)}, u32[]{:S(2)}) %all-to-all-start.6) | async-done | bytes 524320 | tf_op jit(solution)/shard_map/all_to_all | solution.py:87
  158.5 0.2 convolution_bitcast_fusion
  158.7 1.5 collective-permute-start.2
  160.2 1.1 collective-permute-done.2
  161.4 0.1 copy.44
  161.5 21.0 %all_to_all.50 = f32[128,1,430]{2,1,0:T(1,128)S(1)} all-to-all(f32[128,1,430]{2,1,0:T(1,128)S(1)} %copy.44), channel_id=1, replica_groups=mesh['y'=4,'zh'=2,'core'=2,'cx'=4,'cz'=4] {'y','zh','cx','cz'}, dimensions={0} | all-to-all | bytes 440320 | tf_op jit(solution)/shard_map/all_to_all | solution.py:87
  182.5 0.2 reduce_sum.89
  182.7 0.1 broadcast_in_dim.14
  182.9 19.2 %all_to_all.51 = f32[128,1,430]{2,1,0:T(1,128)S(1)} all-to-all(f32[128,1,430]{2,1,0:T(1,128)S(1)} %broadcast_in_dim.14), channel_id=1, replica_groups=mesh['y'=4,'zh'=2,'core'=2,'cx'=4,'cz'=4] {'y','zh','cx','cz'}, dimensions={0} | all-to-all | bytes 440320 | tf_op jit(solution)/shard_map/all_to_all | solution.py:78
  202.0 0.1 copy.45
  202.2 3.2 %collective-permute-start.3 = (f32[128,430]{0,1:T(8,128)S(1)}, f32[128,430]{0,1:T(8,128)S(1)}, u32[]{:S(2)}, u32[]{:S(2)}) collective-permute-start(f32[128,430]{0,1:T(8,128)S(1)} %bitcast.61), channel_id=1, source_target_pairs={{0,16},{16,0},{1,17},{17,1},{2,18},{18,2},{3,19},{19,3},{4,20},{20... | collective-permute-start | bytes 660488 | tf_op jit(solution)/shard_map/ppermute | solution.py:92
  205.3 0.8 convolution_convert_fusion
  206.2 0.3 collective-permute-done.3
  206.4 0.1 maximum_select_fusion
  206.5 0.7 slice_multiply_fusion.1
  207.2 0.5 slice.75
  207.7 0.6 slice_multiply_fusion.2
  208.3 0.8 copy.46
  (14 shorter events, 0.2 us)
Async XLA Ops:
  0.6 0.9 copy-start
  2.5 18.8 %copy-start.7 = (s32[1,1,128]{2,1,0:T(1,128)S(1)}, s32[1,1,128]{2,1,0:T(1,128)}, u32[]{:S(2)}) copy-start(s32[1,1,128]{2,1,0:T(1,128)} %param.18) | copy-start | bytes 1540
  16.7 15.6 %all-to-all-start.1 = ((bf16[4,512,256]{2,1,0:T(8,128)(2,1)}), bf16[4,512,256]{2,1,0:T(8,128)(2,1)S(1)}, u32[]{:S(2)}, u32[]{:S(2)}) async-start(bf16[4,512,256]{2,1,0:T(8,128)(2,1)} %broadcast_in_dim.12), calls=%async_computation.1 | async-start | bytes 2097152 | tf_op jit(solution)/shard_map/all_to_all | solution.py:78
  32.3 1.0 copy-start.2
  47.3 7.3 %copy-start.1 = (f32[2048,256]{1,0:T(8,128)S(1)}, f32[2048,256]{1,0:T(8,128)}, u32[]{:S(2)}) copy-start(f32[2048,256]{1,0:T(8,128)} %shard_map.128) | copy-start | bytes 6291460
  48.8 32.9 %copy-start.5 = (bf16[256,172]{0,1:T(8,128)(2,1)S(1)}, bf16[256,172]{0,1:T(8,128)(2,1)}, u32[]{:S(2)}) copy-start(bf16[256,172]{0,1:T(8,128)(2,1)} %param.16) | copy-start | bytes 264196
  48.8 32.9 %copy-start.6 = (f32[256]{0:T(256)S(1)}, f32[256]{0:T(256)}, u32[]{:S(2)}) copy-start(f32[256]{0:T(256)} %param.15) | copy-start | bytes 3076
  48.8 5.9 %collective-permute-start = (f32[1024,256]{1,0:T(8,128)S(1)}, f32[1024,256]{1,0:T(8,128)S(1)}, u32[]{:S(2)}, u32[]{:S(2)}) collective-permute-start(f32[1024,256]{1,0:T(8,128)S(1)} %slice.72), channel_id=1, source_target_pairs={{0,16},{16,0},{1,17},{17,1},{2,18},{18,2},{3,19},{19,3},{4,20},{20... | collective-permute-start | bytes 3145736 | tf_op jit(solution)/shard_map/ppermute | solution.py:92
  54.8 27.1 %copy-start.4 = (s32[128]{0:T(128)S(1)}, s32[128]{0:T(128)}, u32[]{:S(2)}) copy-start(s32[128]{0:T(128)} %param.21) | copy-start | bytes 1540
  97.1 6.2 %collective-permute-start.1 = (bf16[1024,256]{0,1:T(8,128)(2,1)S(1)}, bf16[1024,256]{0,1:T(8,128)(2,1)S(1)}, u32[]{:S(2)}, u32[]{:S(2)}) collective-permute-start(bf16[1024,256]{0,1:T(8,128)(2,1)S(1)} %copy_bitcast_fusion.1), channel_id=1, source_target_pairs={{0,16},{16,0},{1,17},{17,1},{2,18},{18,2},{3,19},{19,3},{4,20},{20... | collective-permute-start | bytes 1572872 | tf_op jit(solution)/shard_map/ppermute | solution.py:92
  135.3 23.2 %copy-start.3 = (bf16[128,256]{1,0:T(8,128)(2,1)S(1)}, bf16[128,256]{1,0:T(8,128)(2,1)}, u32[]{:S(2)}) copy-start(bf16[128,256]{1,0:T(8,128)(2,1)} %param.13) | copy-start | bytes 196612
  136.3 22.2 %all-to-all-start.6 = ((f32[4,128,256]{1,2,0:T(8,128)}), f32[4,128,256]{1,2,0:T(8,128)S(1)}, u32[]{:S(2)}, u32[]{:S(2)}) async-start(f32[4,128,256]{1,2,0:T(8,128)} %copy_bitcast_fusion.2), calls=%async_computation.6 | async-start | bytes 1048576 | tf_op jit(solution)/shard_map/all_to_all | solution.py:87
  158.7 2.6 %collective-permute-start.2 = (f32[128,430]{0,1:T(8,128)S(1)}, f32[128,430]{0,1:T(8,128)S(1)}, u32[]{:S(2)}, u32[]{:S(2)}) collective-permute-start(f32[128,430]{0,1:T(8,128)S(1)} %slice_select_fusion), channel_id=1, source_target_pairs={{0,16},{16,0},{1,17},{17,1},{2,18},{18,2},{3,19},{19,3},{4,20},{20... | collective-permute-start | bytes 660488 | tf_op jit(solution)/shard_map/ppermute | solution.py:92
  202.2 4.3 %collective-permute-start.3 = (f32[128,430]{0,1:T(8,128)S(1)}, f32[128,430]{0,1:T(8,128)S(1)}, u32[]{:S(2)}, u32[]{:S(2)}) collective-permute-start(f32[128,430]{0,1:T(8,128)S(1)} %bitcast.61), channel_id=1, source_target_pairs={{0,16},{16,0},{1,17},{17,1},{2,18},{18,2},{3,19},{19,3},{4,20},{20... | collective-permute-start | bytes 660488 | tf_op jit(solution)/shard_map/ppermute | solution.py:92

commit v7 on v5

--- a/solution.py
+++ b/solution.py
@@ -8,10 +8,10 @@
 from jax.sharding import Mesh, PartitionSpec as P
 
 TILE = 128
-CHUNK = 8
+CHUNK = 32
 
 
-def _dense_kernel(transpose, rows_ref, cols_ref, count_ref, tiles_ref, src_ref, out_ref, dense_ref):
+def _dense_kernel(transpose, rows_ref, cols_ref, count_ref, tiles_ref, src_a, src_b, out_a, out_b, dense_ref):
     step = pl.program_id(0)
     count = count_ref[0]
 
@@ -30,46 +30,55 @@
 
     @pl.when(step == pl.num_programs(0) - 1)
     def _():
+        half = dense_ref.shape[0] // 2
         if transpose:
-            out_ref[...] = jnp.dot(src_ref[...], dense_ref[...], preferred_element_type=jnp.float32)
+            dims = (((0,), (0,)), ((), ()))
+            res = lax.dot_general(src_a[...], dense_ref[:half, :], dims, preferred_element_type=jnp.float32)
+            res += lax.dot_general(src_b[...], dense_ref[half:, :], dims, preferred_element_type=jnp.float32)
+            out_a[...] = res
         else:
-            out_ref[...] = jnp.dot(dense_ref[...], src_ref[...], preferred_element_type=jnp.float32)
+            src = src_a[...]
+            out_a[...] = jnp.dot(dense_ref[:half, :], src, preferred_element_type=jnp.float32)
+            out_b[...] = jnp.dot(dense_ref[half:, :], src, preferred_element_type=jnp.float32)
 
 
-def tile_product(tile_block, row_ids, col_ids, live_count, source, out_tiles, transpose):
+def tile_product(tile_block, row_ids, col_ids, live_count, sources, out_tiles, transpose):
     slots = tile_block.shape[0]
-    width = source.shape[1]
+    width = sources[0].shape[1]
     steps = slots // CHUNK
-    src_tiles = source.shape[0] // TILE
-    dense_shape = (out_tiles * TILE, src_tiles * TILE)
     if transpose:
-        source = source.T
+        src_tiles = 2 * sources[0].shape[0] // TILE
         dense_shape = (src_tiles * TILE, out_tiles * TILE)
-        out_shape = (width, out_tiles * TILE)
+        out_shapes = [(width, out_tiles * TILE), (8, 128)]
     else:
-        out_shape = (out_tiles * TILE, width)
+        sources = (sources[0], jnp.zeros((8, 128), sources[0].dtype))
+        src_tiles = sources[0].shape[0] // TILE
+        dense_shape = (out_tiles * TILE, src_tiles * TILE)
+        out_shapes = [(out_tiles * TILE // 2, width)] * 2
 
     def tiles_map(i, rows, cols, count):
         last = jnp.maximum(count[0] - 1, 0) // CHUNK
         return (jnp.minimum(i, last), 0, 0)
 
+    def whole(shape):
+        return pl.BlockSpec(shape, lambda i, rows, cols, count: (0, 0))
+
     grid_spec = pltpu.PrefetchScalarGridSpec(
         num_scalar_prefetch=3,
         grid=(steps,),
-        in_specs=[
-            pl.BlockSpec((CHUNK, TILE, TILE), tiles_map),
-            pl.BlockSpec(source.shape, lambda i, rows, cols, count: (0, 0)),
-        ],
-        out_specs=pl.BlockSpec(out_shape, lambda i, rows, cols, count: (0, 0)),
+        in_specs=[pl.BlockSpec((CHUNK, TILE, TILE), tiles_map)] + [whole(x.shape) for x in sources],
+        out_specs=[whole(shape) for shape in out_shapes],
         scratch_shapes=[pltpu.VMEM(dense_shape, jnp.bfloat16)],
     )
-    result = pl.pallas_call(
+    first, second = pl.pallas_call(
         lambda *refs: _dense_kernel(transpose, *refs),
         grid_spec=grid_spec,
-        out_shape=jax.ShapeDtypeStruct(out_shape, jnp.float32),
+        out_shape=[jax.ShapeDtypeStruct(shape, jnp.float32) for shape in out_shapes],
         compiler_params=pltpu.CompilerParams(dimension_semantics=("arbitrary",)),
-    )(row_ids, col_ids, live_count.reshape(1), tile_block, source)
-    return result.T if transpose else result
+    )(row_ids, col_ids, live_count.reshape(1), tile_block, *sources)
+    if transpose:
+        return first.T
+    return first, second
 
 
 def gather_rows(x, axis):
@@ -137,14 +146,13 @@
     row_pos = jnp.where(row_ids % 2 == lax.axis_index("core"), row_hi, row_hi + row_tiles // 2)
     proj = jnp.dot(features, w_in, preferred_element_type=jnp.float32).astype(jnp.bfloat16)
     source = gather_rows(gather_rows(proj, "cz"), "cx")
-    partial_value = tile_product(tile_block, row_pos, col_ids, live_count, source, row_tiles, False)
-    half = partial_value.shape[0] // 2
-    summed = partial_value[:half] + swap_core(partial_value[half:])
+    mine, other = tile_product(tile_block, row_pos, col_ids, live_count, (source,), row_tiles, False)
+    summed = mine + swap_core(other)
     agg = scatter_rows(scatter_rows(summed, "y"), "zh")
     loss_sum, out_term, bias_term, grad_z = head_block(agg, bias, w_out, labels)
     gathered = gather_rows(grad_z, ("y", "zh"))
-    grad_block = jnp.concatenate([gathered, swap_core(gathered)])
-    back_part = tile_product(tile_block, row_pos, col_ids, live_count, grad_block, col_tiles, True)
+    sources = (gathered, swap_core(gathered))
+    back_part = tile_product(tile_block, row_pos, col_ids, live_count, sources, col_tiles, True)
     grad_proj = scatter_rows(scatter_rows(back_part, "cx"), "cz").astype(jnp.bfloat16)
     in_term = jnp.einsum("nf,ng->fg", features, grad_proj, preferred_element_type=jnp.float32)
     extra = jnp.zeros((feat, 2), jnp.float32)

time: 229 us -> 219 us (0.956)
  blocking collectives: 136 us -> 129 us
  starting transfers between devices: 27.1 us -> 24.1 us
  waiting for transfers between devices: 24.3 us -> 26.9 us
    all_to_all x4, blocking collectives: 86.9 us -> 82.4 us  [scatter_rows(): got = lax.all_to_all(x.reshape(n, -1, x.shape[1]), axis, 0, 0, tiled=False)]
    all_to_all x3, blocking collectives: 49.2 us -> 46.2 us  [gather_rows(): got = lax.all_to_all(spread, axis, 0, 0, tiled=False)]
    all_to_all x1, waiting for transfers between devices: 8.66 us -> 11.1 us  [scatter_rows(): got = lax.all_to_all(x.reshape(n, -1, x.shape[1]), axis, 0, 0, tiled=False)]
where the time goes in v7:
time: 219 us; the launch traced here: 218 us
  blocking collectives  129 us (59%)
  waiting for transfers between devices  26.9 us (12%)
  starting transfers between devices  24.1 us (11%)
  Pallas kernels  17.2 us (8%)
  local copies, waits for them, and re-layouts  10.8 us (5%)
  other arithmetic  4.56 us (2%)
  between operations  3.28 us (1%)
  matrix products  2.62 us (1%)
    all_to_all x4, blocking collectives, scatter_rows(): got = lax.all_to_all(x.reshape(n, -1, x.shape[1]), axis, 0, 0, tiled=False)  82.4 us
    all_to_all x3, blocking collectives, gather_rows(): got = lax.all_to_all(spread, axis, 0, 0, tiled=False)  46.2 us
    pallas_call x2, Pallas kernels, tile_product(): pl.pallas_call(lambda *refs: _dense_kernel(transpose, *refs), grid_spec=g...  17.2 us
    ppermute x4, starting transfers between devices, swap_core(): return lax.ppermute(x, 'core', [(0, 1), (1, 0)])  13.8 us
    all_to_all x1, waiting for transfers between devices, scatter_rows(): got = lax.all_to_all(x.reshape(n, -1, x.shape[1]), axis, 0, 0, tiled=False)  11.1 us
    all_to_all x1, waiting for transfers between devices, gather_rows(): got = lax.all_to_all(spread, axis, 0, 0, tiled=False)  10.4 us
    all_to_all x1, starting transfers between devices, scatter_rows(): got = lax.all_to_all(x.reshape(n, -1, x.shape[1]), axis, 0, 0, tiled=False)  6.29 us
    ppermute x4, waiting for transfers between devices, swap_core(): return lax.ppermute(x, 'core', [(0, 1), (1, 0)])  5.41 us
  transfers between devices with their start and end apart: 6, of which 6 were waited for; matrix products, arithmetic and copies ran while one was open for 2% of the time, Pallas kernels for 0%

profile of v7, /device:TPU:1, one launch (start us, length us, event | category | flops | bytes accessed | tf_op | source)
XLA Modules:
  0.0 218.1 jit_solution(7094604289311915187)
XLA Ops:
  0.6 0.0 copy-start
  0.6 0.9 copy-done
  1.5 1.0 convolution_convert_fusion.1
  2.5 0.0 copy-start.8
  2.6 13.1 %all_to_all.45 = bf16[4,128,256]{2,1,0:T(8,128)(2,1)S(1)} all-to-all(bf16[4,128,256]{2,1,0:T(8,128)(2,1)S(1)} %broadcast_in_dim.12), channel_id=1, replica_groups=mesh['y'=4,'zh'=2,'core'=2,'cx'=4,'cz'=4] {'cz'}, dimensions={0} | all-to-all | bytes 524288 | tf_op jit(solution)/shard_map/all_to_all | solution.py:87
  15.6 1.1 broadcast_in_dim.14
  16.7 4.0 %all-to-all-start.1 = ((bf16[4,512,256]{2,1,0:T(8,128)(2,1)}), bf16[4,512,256]{2,1,0:T(8,128)(2,1)S(1)}, u32[]{:S(2)}, u32[]{:S(2)}) async-start(bf16[4,512,256]{2,1,0:T(8,128)(2,1)} %broadcast_in_dim.14), calls=%async_computation.1 | async-start | bytes 2097152 | tf_op jit(solution)/shard_map/all_to_all | solution.py:87
  21.4 0.0 copy-done.8
  21.4 0.5 compare_select_fusion.refs_0_
  21.9 10.4 %all-to-all-done.1 = bf16[4,512,256]{2,1,0:T(8,128)(2,1)S(1)} async-done(((bf16[4,512,256]{2,1,0:T(8,128)(2,1)}), bf16[4,512,256]{2,1,0:T(8,128)(2,1)S(1)}, u32[]{:S(2)}, u32[]{:S(2)}) %all-to-all-start.1) | async-done | bytes 1048608 | tf_op jit(solution)/shard_map/all_to_all | solution.py:87
  32.3 0.0 copy-start.1
  32.3 0.6 broadcast_in_dim.15.refs_5_
  33.0 0.4 copy-done.1
  33.3 8.6 %shard_map.128 = (f32[1024,256]{1,0:T(8,128)}, f32[1024,256]{1,0:T(8,128)}) custom-call(s32[128]{0:T(128)} %compare_select_fusion.refs_0_, s32[128]{0:T(128)} %bitcast.59, s32[1]{0:T(128)} %bitcast.45.refs_2_, bf16[128,128,128]{2,1,0:T(8,128)(2,1)} %bitcast.47, bf16[2048,256]{1,0:T(8,128)(2,1)} %bitcast.51, bf16[8,128]{1,0:T(8,128)(2,1)} %broadcast_in_dim.15.refs_5_), custom_call_target="tpu_custom_call" | custom-call | tf_op jit(solution)/shard_map/pallas_call | solution.py:73
  41.9 4.5 %collective-permute-start = (f32[1024,256]{1,0:T(8,128)}, f32[1024,256]{1,0:T(8,128)S(1)}, u32[]{:S(2)}, u32[]{:S(2)}) collective-permute-start(f32[1024,256]{1,0:T(8,128)} %get-tuple-element.33), channel_id=1, source_target_pairs={{0,16},{16,0},{1,17},{17,1},{2,18},{18,2},{3,19},{19,3},{4,20},{20... | collective-permute-start | bytes 3145736 | tf_op jit(solution)/shard_map/ppermute | solution.py:98
  46.4 2.5 %collective-permute-done = f32[1024,256]{1,0:T(8,128)S(1)} collective-permute-done((f32[1024,256]{1,0:T(8,128)}, f32[1024,256]{1,0:T(8,128)S(1)}, u32[]{:S(2)}, u32[]{:S(2)}) %collective-permute-start) | collective-permute-done | bytes 1048608 | tf_op jit(solution)/shard_map/ppermute | solution.py:98
  48.9 1.4 add.49
  50.3 0.0 copy-start.6
  50.3 0.0 copy-start.7
  50.3 0.0 copy-start.5
  50.3 18.2 %all_to_all.46 = f32[4,256,256]{2,1,0:T(8,128)S(1)} all-to-all(f32[4,256,256]{2,1,0:T(8,128)S(1)} %bitcast.50), channel_id=1, replica_groups=mesh['y'=4,'zh'=2,'core'=2,'cx'=4,'cz'=4] {'y'}, dimensions={0} | all-to-all | bytes 2097152 | tf_op jit(solution)/shard_map/all_to_all | solution.py:93
  68.5 0.1 reduce_sum.81
  68.6 14.7 %all_to_all.47 = f32[2,128,256]{2,1,0:T(8,128)S(1)} all-to-all(f32[2,128,256]{2,1,0:T(8,128)S(1)} %bitcast.56), channel_id=1, replica_groups=mesh['y'=4,'zh'=2,'core'=2,'cx'=4,'cz'=4] {'zh'}, dimensions={0} | all-to-all | bytes 524288 | tf_op jit(solution)/shard_map/all_to_all | solution.py:93
  83.3 0.0 copy-done.6
  83.3 0.0 copy-done.7
  83.3 0.2 fusion.7
  83.5 0.0 copy-done.5
  83.5 0.1 select_reduce_fusion
  83.6 0.6 subtract_reduce_fusion
  84.2 0.2 convert_reduce_fusion
  84.5 14.0 %all_to_all.48 = bf16[8,128,256]{2,1,0:T(8,128)(2,1)S(1)} all-to-all(bf16[8,128,256]{2,1,0:T(8,128)(2,1)S(1)} %broadcast_in_dim.16), channel_id=1, replica_groups=mesh['y'=4,'zh'=2,'core'=2,'cx'=4,'cz'=4] {'y','zh'}, dimensions={0} | all-to-all | bytes 1048576 | tf_op jit(solution)/shard_map/all_to_all | solution.py:87
  98.4 0.0 copy-start.2
  98.4 4.5 %collective-permute-start.1 = (bf16[1024,256]{1,0:T(8,128)(2,1)S(1)}, bf16[1024,256]{1,0:T(8,128)(2,1)S(1)}, u32[]{:S(2)}, u32[]{:S(2)}) collective-permute-start(bf16[1024,256]{1,0:T(8,128)(2,1)S(1)} %bitcast.52), channel_id=1, source_target_pairs={{0,16},{16,0},{1,17},{17,1},{2,18},{18,2},{3,19},{19,3},{4,20},{20... | collective-permute-start | bytes 1572872 | tf_op jit(solution)/shard_map/ppermute | solution.py:98
  102.9 1.5 collective-permute-done.1.refs_5_
  104.4 0.0 copy-done.2
  104.4 0.8 copy-done.3
  105.3 8.6 %shard_map.129 = (f32[256,2048]{1,0:T(8,128)}, f32[8,128]{1,0:T(8,128)}) custom-call(s32[128]{0:T(128)} %compare_select_fusion.refs_0_, s32[128]{0:T(128)} %bitcast.60, s32[1]{0:T(128)} %bitcast.46.refs_2_, bf16[128,128,128]{2,1,0:T(8,128)(2,1)} %bitcast.48, bf16[1024,256]{1,0:T(8,128)(2,1)} %bitcast.53, bf16[1024,256]{1,0:T(8,128)(2,1)} %copy-done.3), custom_call_target="tpu_custom_call" | custom-call | tf_op jit(solution)/shard_map/pallas_call | solution.py:73
  113.9 1.8 copy.44
  115.6 28.4 %all_to_all.49 = f32[4,512,256]{1,2,0:T(8,128)S(1)} all-to-all(f32[4,512,256]{1,2,0:T(8,128)S(1)} %bitcast.49), channel_id=1, replica_groups=mesh['y'=4,'zh'=2,'core'=2,'cx'=4,'cz'=4] {'cx'}, dimensions={0} | all-to-all | bytes 4194304 | tf_op jit(solution)/shard_map/all_to_all | solution.py:93
  144.1 0.2 reduce_sum.84
  144.3 0.0 copy-start.4
  144.3 0.8 copy_bitcast_fusion.1
  145.2 6.3 %all-to-all-start.6 = ((f32[4,128,256]{1,2,0:T(8,128)}), f32[4,128,256]{1,2,0:T(8,128)S(1)}, u32[]{:S(2)}, u32[]{:S(2)}) async-start(f32[4,128,256]{1,2,0:T(8,128)} %copy_bitcast_fusion.1), calls=%async_computation.6 | async-start | bytes 1048576 | tf_op jit(solution)/shard_map/all_to_all | solution.py:93
  151.5 0.6 fusion.6
  152.1 2.0 scatter.9
  154.0 0.2 fusion.4
  154.2 11.1 %all-to-all-done.6 = f32[4,128,256]{1,2,0:T(8,128)S(1)} async-done(((f32[4,128,256]{1,2,0:T(8,128)}), f32[4,128,256]{1,2,0:T(8,128)S(1)}, u32[]{:S(2)}, u32[]{:S(2)}) %all-to-all-start.6) | async-done | bytes 524320 | tf_op jit(solution)/shard_map/all_to_all | solution.py:93
  165.4 0.0 copy-done.4
  165.4 0.2 convolution_bitcast_fusion
  165.6 1.7 collective-permute-start.2
  167.3 1.1 collective-permute-done.2
  168.4 0.1 copy.35
  168.6 21.1 %all_to_all.50 = f32[128,1,430]{2,1,0:T(1,128)S(1)} all-to-all(f32[128,1,430]{2,1,0:T(1,128)S(1)} %copy.35), channel_id=1, replica_groups=mesh['y'=4,'zh'=2,'core'=2,'cx'=4,'cz'=4] {'y','zh','cx','cz'}, dimensions={0} | all-to-all | bytes 440320 | tf_op jit(solution)/shard_map/all_to_all | solution.py:93
  189.7 0.2 reduce_sum.89
  189.9 0.1 broadcast_in_dim.17
  190.1 19.2 %all_to_all.51 = f32[128,1,430]{2,1,0:T(1,128)S(1)} all-to-all(f32[128,1,430]{2,1,0:T(1,128)S(1)} %broadcast_in_dim.17), channel_id=1, replica_groups=mesh['y'=4,'zh'=2,'core'=2,'cx'=4,'cz'=4] {'y','zh','cx','cz'}, dimensions={0} | all-to-all | bytes 440320 | tf_op jit(solution)/shard_map/all_to_all | solution.py:87
  209.3 0.1 copy.36
  209.4 3.2 %collective-permute-start.3 = (f32[128,430]{0,1:T(8,128)S(1)}, f32[128,430]{0,1:T(8,128)S(1)}, u32[]{:S(2)}, u32[]{:S(2)}) collective-permute-start(f32[128,430]{0,1:T(8,128)S(1)} %bitcast.57), channel_id=1, source_target_pairs={{0,16},{16,0},{1,17},{17,1},{2,18},{18,2},{3,19},{19,3},{4,20},{20... | collective-permute-start | bytes 660488 | tf_op jit(solution)/shard_map/ppermute | solution.py:98
  212.5 0.8 convolution_convert_fusion
  213.4 0.3 collective-permute-done.3
  213.7 0.5 slice.65
  214.2 0.6 slice_multiply_fusion.2
  214.8 0.7 slice_multiply_fusion.1
  215.5 0.8 copy.37
  (12 shorter events, 0.3 us)
Async XLA Ops:
  0.6 0.9 copy-start
  2.5 18.8 %copy-start.8 = (s32[1,1,128]{2,1,0:T(1,128)S(1)}, s32[1,1,128]{2,1,0:T(1,128)}, u32[]{:S(2)}) copy-start(s32[1,1,128]{2,1,0:T(1,128)} %param.18) | copy-start | bytes 1540
  16.7 15.6 %all-to-all-start.1 = ((bf16[4,512,256]{2,1,0:T(8,128)(2,1)}), bf16[4,512,256]{2,1,0:T(8,128)(2,1)S(1)}, u32[]{:S(2)}, u32[]{:S(2)}) async-start(bf16[4,512,256]{2,1,0:T(8,128)(2,1)} %broadcast_in_dim.14), calls=%async_computation.1 | async-start | bytes 2097152 | tf_op jit(solution)/shard_map/all_to_all | solution.py:87
  32.3 1.0 copy-start.1
  41.9 7.0 %collective-permute-start = (f32[1024,256]{1,0:T(8,128)}, f32[1024,256]{1,0:T(8,128)S(1)}, u32[]{:S(2)}, u32[]{:S(2)}) collective-permute-start(f32[1024,256]{1,0:T(8,128)} %get-tuple-element.33), channel_id=1, source_target_pairs={{0,16},{16,0},{1,17},{17,1},{2,18},{18,2},{3,19},{19,3},{4,20},{20... | collective-permute-start | bytes 3145736 | tf_op jit(solution)/shard_map/ppermute | solution.py:98
  50.3 33.0 %copy-start.6 = (bf16[256,172]{0,1:T(8,128)(2,1)S(1)}, bf16[256,172]{0,1:T(8,128)(2,1)}, u32[]{:S(2)}) copy-start(bf16[256,172]{0,1:T(8,128)(2,1)} %param.16) | copy-start | bytes 264196
  50.3 33.0 %copy-start.7 = (f32[256]{0:T(256)S(1)}, f32[256]{0:T(256)}, u32[]{:S(2)}) copy-start(f32[256]{0:T(256)} %param.15) | copy-start | bytes 3076
  50.3 33.2 %copy-start.5 = (s32[128]{0:T(128)S(1)}, s32[128]{0:T(128)}, u32[]{:S(2)}) copy-start(s32[128]{0:T(128)} %param.21) | copy-start | bytes 1540
  98.4 6.0 %copy-start.2 = (bf16[8,128,256]{2,1,0:T(8,128)(2,1)}, bf16[8,128,256]{2,1,0:T(8,128)(2,1)S(1)}, u32[]{:S(2)}) copy-start(bf16[8,128,256]{2,1,0:T(8,128)(2,1)S(1)} %all_to_all.48) | copy-start | bytes 1572868
  98.4 6.0 %collective-permute-start.1 = (bf16[1024,256]{1,0:T(8,128)(2,1)S(1)}, bf16[1024,256]{1,0:T(8,128)(2,1)S(1)}, u32[]{:S(2)}, u32[]{:S(2)}) collective-permute-start(bf16[1024,256]{1,0:T(8,128)(2,1)S(1)} %bitcast.52), channel_id=1, source_target_pairs={{0,16},{16,0},{1,17},{17,1},{2,18},{18,2},{3,19},{19,3},{4,20},{20... | collective-permute-start | bytes 1572872 | tf_op jit(solution)/shard_map/ppermute | solution.py:98
  104.4 0.8 copy-start.3
  144.3 21.0 %copy-start.4 = (bf16[128,256]{1,0:T(8,128)(2,1)S(1)}, bf16[128,256]{1,0:T(8,128)(2,1)}, u32[]{:S(2)}) copy-start(bf16[128,256]{1,0:T(8,128)(2,1)} %param.13) | copy-start | bytes 196612
  145.2 20.2 %all-to-all-start.6 = ((f32[4,128,256]{1,2,0:T(8,128)}), f32[4,128,256]{1,2,0:T(8,128)S(1)}, u32[]{:S(2)}, u32[]{:S(2)}) async-start(f32[4,128,256]{1,2,0:T(8,128)} %copy_bitcast_fusion.1), calls=%async_computation.6 | async-start | bytes 1048576 | tf_op jit(solution)/shard_map/all_to_all | solution.py:93
  165.6 2.8 %collective-permute-start.2 = (f32[128,430]{0,1:T(8,128)S(1)}, f32[128,430]{0,1:T(8,128)S(1)}, u32[]{:S(2)}, u32[]{:S(2)}) collective-permute-start(f32[128,430]{0,1:T(8,128)S(1)} %slice_select_fusion), channel_id=1, source_target_pairs={{0,16},{16,0},{1,17},{17,1},{2,18},{18,2},{3,19},{19,3},{4,20},{20... | collective-permute-start | bytes 660488 | tf_op jit(solution)/shard_map/ppermute | solution.py:98
  209.4 4.3 %collective-permute-start.3 = (f32[128,430]{0,1:T(8,128)S(1)}, f32[128,430]{0,1:T(8,128)S(1)}, u32[]{:S(2)}, u32[]{:S(2)}) collective-permute-start(f32[128,430]{0,1:T(8,128)S(1)} %bitcast.57), channel_id=1, source_target_pairs={{0,16},{16,0},{1,17},{17,1},{2,18},{18,2},{3,19},{19,3},{4,20},{20... | collective-permute-start | bytes 660488 | tf_op jit(solution)/shard_map/ppermute | solution.py:98

commit v8 on v7

--- a/solution.py
+++ b/solution.py
@@ -94,8 +94,22 @@
     return jnp.sum(got, axis=0)
 
 
-def swap_core(x):
-    return lax.ppermute(x, "core", [(0, 1), (1, 0)])
+def swap_core(x, axis="core"):
+    return lax.ppermute(x, axis, [(0, 1), (1, 0)])
+
+
+def pair_scatter(x, axis):
+    half = x.shape[0] // 2
+    me = lax.axis_index(axis)
+    mine = lax.dynamic_slice_in_dim(x, me * half, half, 0)
+    other = lax.dynamic_slice_in_dim(x, (1 - me) * half, half, 0)
+    return mine + swap_core(other, axis)
+
+
+def pair_gather(x, axis):
+    other = swap_core(x, axis)
+    first = lax.axis_index(axis) == 0
+    return jnp.where(first, jnp.concatenate([x, other]), jnp.concatenate([other, x]))
 
 
 def reduce_all(x, axes):
@@ -148,9 +162,9 @@
     source = gather_rows(gather_rows(proj, "cz"), "cx")
     mine, other = tile_product(tile_block, row_pos, col_ids, live_count, (source,), row_tiles, False)
     summed = mine + swap_core(other)
-    agg = scatter_rows(scatter_rows(summed, "y"), "zh")
+    agg = pair_scatter(scatter_rows(summed, "y"), "zh")
     loss_sum, out_term, bias_term, grad_z = head_block(agg, bias, w_out, labels)
-    gathered = gather_rows(grad_z, ("y", "zh"))
+    gathered = gather_rows(pair_gather(grad_z, "zh"), "y")
     sources = (gathered, swap_core(gathered))
     back_part = tile_product(tile_block, row_pos, col_ids, live_count, sources, col_tiles, True)
     grad_proj = scatter_rows(scatter_rows(back_part, "cx"), "cz").astype(jnp.bfloat16)

time: 219 us -> 218 us (level)
  blocking collectives: 129 us -> 95.5 us
  waiting for transfers between devices: 26.9 us -> 47.8 us
  starting transfers between devices: 24.1 us -> 36.2 us
    all_to_all x4 -> x2, blocking collectives: 82.4 us -> 53.9 us  [scatter_rows(): got = lax.all_to_all(x.reshape(n, -1, x.shape[1]), axis, 0, 0, tiled=False)]
    all_to_all x1 -> x2, waiting for transfers between devices: 11.1 us -> 25.7 us  [scatter_rows(): got = lax.all_to_all(x.reshape(n, -1, x.shape[1]), axis, 0, 0, tiled=False)]
    ppermute x4 -> x6, starting transfers between devices: 13.8 us -> 24.2 us  [swap_core(): return lax.ppermute(x, axis, [(0, 1), (1, 0)])]
    ppermute x4 -> x6, waiting for transfers between devices: 5.41 us -> 11.6 us  [swap_core(): return lax.ppermute(x, axis, [(0, 1), (1, 0)])]
    all_to_all x3, blocking collectives: 46.2 us -> 41.6 us  [gather_rows(): got = lax.all_to_all(spread, axis, 0, 0, tiled=False)]
    all_to_all x1 -> x2, starting transfers between devices: 6.29 us -> 8.01 us  [scatter_rows(): got = lax.all_to_all(x.reshape(n, -1, x.shape[1]), axis, 0, 0, tiled=False)]
  transfers between devices with their start and end apart: 6 -> 9, of which waited for: 6 -> 9; matrix products, arithmetic and copies ran while one was open for 2% -> 2% of each run, Pallas kernels for 0% -> 0%
where the time goes in v8:
time: 218 us; the launch traced here: 217 us
  blocking collectives  95.5 us (44%)
  waiting for transfers between devices  47.8 us (22%)
  starting transfers between devices  36.2 us (17%)
  Pallas kernels  15.2 us (7%)
  local copies, waits for them, and re-layouts  10.8 us (5%)
  other arithmetic  5.65 us (3%)
  between operations  3.27 us (2%)
  matrix products  2.56 us (1%)
    all_to_all x2, blocking collectives, scatter_rows(): got = lax.all_to_all(x.reshape(n, -1, x.shape[1]), axis, 0, 0, tiled=False)  53.9 us
    all_to_all x3, blocking collectives, gather_rows(): got = lax.all_to_all(spread, axis, 0, 0, tiled=False)  41.6 us
    all_to_all x2, waiting for transfers between devices, scatter_rows(): got = lax.all_to_all(x.reshape(n, -1, x.shape[1]), axis, 0, 0, tiled=False)  25.7 us
    ppermute x6, starting transfers between devices, swap_core(): return lax.ppermute(x, axis, [(0, 1), (1, 0)])  24.2 us
    pallas_call x2, Pallas kernels, tile_product(): pl.pallas_call(lambda *refs: _dense_kernel(transpose, *refs), grid_spec=g...  15.2 us
    ppermute x6, waiting for transfers between devices, swap_core(): return lax.ppermute(x, axis, [(0, 1), (1, 0)])  11.6 us
    all_to_all x1, waiting for transfers between devices, gather_rows(): got = lax.all_to_all(spread, axis, 0, 0, tiled=False)  10.4 us
    all_to_all x2, starting transfers between devices, scatter_rows(): got = lax.all_to_all(x.reshape(n, -1, x.shape[1]), axis, 0, 0, tiled=False)  8.01 us
  transfers between devices with their start and end apart: 9, of which 9 were waited for; matrix products, arithmetic and copies ran while one was open for 2% of the time, Pallas kernels for 0%

profile of v8, /device:TPU:1, one launch (start us, length us, event | category | flops | bytes accessed | tf_op | source)
XLA Modules:
  0.0 216.9 jit_solution(12354418963187144028)
XLA Ops:
  0.6 0.0 copy-start
  0.6 0.9 copy-done
  1.5 1.0 convolution_convert_fusion.1
  2.5 0.0 copy-start.8
  2.6 13.1 %all_to_all.40 = bf16[4,128,256]{2,1,0:T(8,128)(2,1)S(1)} all-to-all(bf16[4,128,256]{2,1,0:T(8,128)(2,1)S(1)} %broadcast_in_dim.12), channel_id=1, replica_groups=mesh['y'=4,'zh'=2,'core'=2,'cx'=4,'cz'=4] {'cz'}, dimensions={0} | all-to-all | bytes 524288 | tf_op jit(solution)/shard_map/all_to_all | solution.py:87
  15.6 1.0 broadcast_in_dim.14
  16.7 4.0 %all-to-all-start.1 = ((bf16[4,512,256]{2,1,0:T(8,128)(2,1)}), bf16[4,512,256]{2,1,0:T(8,128)(2,1)S(1)}, u32[]{:S(2)}, u32[]{:S(2)}) async-start(bf16[4,512,256]{2,1,0:T(8,128)(2,1)} %broadcast_in_dim.14), calls=%async_computation.1 | async-start | bytes 2097152 | tf_op jit(solution)/shard_map/all_to_all | solution.py:87
  21.4 0.0 copy-done.8
  21.4 0.5 compare_select_fusion.refs_0_
  21.9 10.4 %all-to-all-done.1 = bf16[4,512,256]{2,1,0:T(8,128)(2,1)S(1)} async-done(((bf16[4,512,256]{2,1,0:T(8,128)(2,1)}), bf16[4,512,256]{2,1,0:T(8,128)(2,1)S(1)}, u32[]{:S(2)}, u32[]{:S(2)}) %all-to-all-start.1) | async-done | bytes 1048608 | tf_op jit(solution)/shard_map/all_to_all | solution.py:87
  32.3 0.6 broadcast_in_dim.15.refs_5_
  32.9 0.4 copy-done.1
  33.3 7.6 %shard_map.128 = (f32[1024,256]{1,0:T(8,128)}, f32[1024,256]{1,0:T(8,128)}) custom-call(s32[128]{0:T(128)} %compare_select_fusion.refs_0_, s32[128]{0:T(128)} %bitcast.58, s32[1]{0:T(128)} %bitcast.46.refs_2_, bf16[128,128,128]{2,1,0:T(8,128)(2,1)} %bitcast.48, bf16[2048,256]{1,0:T(8,128)(2,1)} %bitcast.51, bf16[8,128]{1,0:T(8,128)(2,1)} %broadcast_in_dim.15.refs_5_), custom_call_target="tpu_custom_call" | custom-call | tf_op jit(solution)/shard_map/pallas_call | solution.py:73
  40.9 5.5 %collective-permute-start = (f32[1024,256]{1,0:T(8,128)}, f32[1024,256]{1,0:T(8,128)S(1)}, u32[]{:S(2)}, u32[]{:S(2)}) collective-permute-start(f32[1024,256]{1,0:T(8,128)} %get-tuple-element.33), channel_id=1, source_target_pairs={{0,16},{16,0},{1,17},{17,1},{2,18},{18,2},{3,19},{19,3},{4,20},{20... | collective-permute-start | bytes 3145736 | tf_op jit(solution)/shard_map/ppermute | solution.py:98
  46.4 2.5 %collective-permute-done = f32[1024,256]{1,0:T(8,128)S(1)} collective-permute-done((f32[1024,256]{1,0:T(8,128)}, f32[1024,256]{1,0:T(8,128)S(1)}, u32[]{:S(2)}, u32[]{:S(2)}) %collective-permute-start) | collective-permute-done | bytes 1048608 | tf_op jit(solution)/shard_map/ppermute | solution.py:98
  48.9 2.4 %add.58 = f32[1024,256]{1,0:T(8,128)} add(f32[1024,256]{1,0:T(8,128)} %get-tuple-element.32, f32[1024,256]{1,0:T(8,128)S(1)} %collective-permute-done) | non-fusion elementwise | flops 262144 | bytes 3145728 | tf_op jit(solution)/shard_map/add | solution.py:164
  51.3 4.4 %all-to-all-start.2 = ((f32[4,256,256]{2,1,0:T(8,128)}), f32[4,256,256]{2,1,0:T(8,128)S(1)}, u32[]{:S(2)}, u32[]{:S(2)}) async-start(f32[4,256,256]{2,1,0:T(8,128)} %bitcast.6), calls=%async_computation.2 | async-start | bytes 2097152 | tf_op jit(solution)/shard_map/all_to_all | solution.py:93
  55.6 14.5 %all-to-all-done.2 = f32[4,256,256]{2,1,0:T(8,128)S(1)} async-done(((f32[4,256,256]{2,1,0:T(8,128)}), f32[4,256,256]{2,1,0:T(8,128)S(1)}, u32[]{:S(2)}, u32[]{:S(2)}) %all-to-all-start.2) | async-done | bytes 1048608 | tf_op jit(solution)/shard_map/all_to_all | solution.py:93
  70.2 0.1 reduce_sum.72
  70.3 3.9 %collective-permute-start.1 = (f32[128,256]{1,0:T(8,128)S(1)}, f32[128,256]{1,0:T(8,128)S(1)}, u32[]{:S(2)}, u32[]{:S(2)}) collective-permute-start(f32[128,256]{1,0:T(8,128)S(1)} %constant_dynamic-slice_fusion), channel_id=1, source_target_pairs={{0,32},{32,0},{1,33},{33,1},{2,34},{34,2},{3,35},{35,3},{4,36},{36... | collective-permute-start | bytes 393224 | tf_op jit(solution)/shard_map/ppermute | solution.py:98
  74.2 4.0 %collective-permute-done.1 = f32[128,256]{1,0:T(8,128)S(1)} collective-permute-done((f32[128,256]{1,0:T(8,128)S(1)}, f32[128,256]{1,0:T(8,128)S(1)}, u32[]{:S(2)}, u32[]{:S(2)}) %collective-permute-start.1) | collective-permute-done | bytes 131104 | tf_op jit(solution)/shard_map/ppermute | solution.py:98
  78.2 0.0 copy-done.7
  78.2 0.1 multiply_convert_fusion.1
  78.3 0.0 copy-done.5
  78.3 0.2 fusion.4
  78.5 0.0 copy-done.6
  78.5 0.1 select_reduce_fusion
  78.5 0.6 subtract_reduce_fusion
  79.1 0.2 convert_reduce_fusion
  79.4 5.0 %collective-permute-start.2 = (bf16[128,256]{1,0:T(8,128)(2,1)S(1)}, bf16[128,256]{1,0:T(8,128)(2,1)S(1)}, u32[]{:S(2)}, u32[]{:S(2)}) collective-permute-start(bf16[128,256]{1,0:T(8,128)(2,1)S(1)} %get-tuple-element.64), channel_id=1, source_target_pairs={{0,32},{32,0},{1,33},{33,1},{2,34},{34,2},{3,35},{35,3},{4,36},{36... | collective-permute-start | bytes 196616 | tf_op jit(solution)/shard_map/ppermute | solution.py:98
  84.4 2.2 %collective-permute-done.2 = bf16[128,256]{1,0:T(8,128)(2,1)S(1)} collective-permute-done((bf16[128,256]{1,0:T(8,128)(2,1)S(1)}, bf16[128,256]{1,0:T(8,128)(2,1)S(1)}, u32[]{:S(2)}, u32[]{:S(2)}) %collective-permute-start.2) | collective-permute-done | bytes 65568 | tf_op jit(solution)/shard_map/ppermute | solution.py:98
  86.7 9.3 %all_to_all.41 = bf16[4,256,256]{2,1,0:T(8,128)(2,1)S(1)} all-to-all(bf16[4,256,256]{2,1,0:T(8,128)(2,1)S(1)} %broadcast_in_dim.16), channel_id=1, replica_groups=mesh['y'=4,'zh'=2,'core'=2,'cx'=4,'cz'=4] {'y'}, dimensions={0} | all-to-all | bytes 1048576 | tf_op jit(solution)/shard_map/all_to_all | solution.py:87
  96.0 5.0 %collective-permute-start.3 = (bf16[1024,256]{1,0:T(8,128)(2,1)S(1)}, bf16[1024,256]{1,0:T(8,128)(2,1)S(1)}, u32[]{:S(2)}, u32[]{:S(2)}) collective-permute-start(bf16[1024,256]{1,0:T(8,128)(2,1)S(1)} %bitcast.52), channel_id=1, source_target_pairs={{0,16},{16,0},{1,17},{17,1},{2,18},{18,2},{3,19},{19,3},{4,20},{20... | collective-permute-start | bytes 1572872 | tf_op jit(solution)/shard_map/ppermute | solution.py:98
  101.0 1.5 collective-permute-done.3.refs_5_
  102.5 0.0 copy-done.2
  102.5 0.8 copy-done.3
  103.3 7.6 %shard_map.129 = (f32[256,2048]{1,0:T(8,128)}, f32[8,128]{1,0:T(8,128)}) custom-call(s32[128]{0:T(128)} %compare_select_fusion.refs_0_, s32[128]{0:T(128)} %bitcast.59, s32[1]{0:T(128)} %bitcast.47.refs_2_, bf16[128,128,128]{2,1,0:T(8,128)(2,1)} %bitcast.49, bf16[1024,256]{1,0:T(8,128)(2,1)} %bitcast.53, bf16[1024,256]{1,0:T(8,128)(2,1)} %copy-done.3), custom_call_target="tpu_custom_call" | custom-call | tf_op jit(solution)/shard_map/pallas_call | solution.py:73
  110.9 1.8 copy.37
  112.7 31.2 %all_to_all.42 = f32[4,512,256]{1,2,0:T(8,128)S(1)} all-to-all(f32[4,512,256]{1,2,0:T(8,128)S(1)} %bitcast.50), channel_id=1, replica_groups=mesh['y'=4,'zh'=2,'core'=2,'cx'=4,'cz'=4] {'cx'}, dimensions={0} | all-to-all | bytes 4194304 | tf_op jit(solution)/shard_map/all_to_all | solution.py:93
  143.9 0.2 reduce_sum.74
  144.1 0.0 copy-start.4
  144.1 0.8 copy_bitcast_fusion.1
  144.9 3.7 %all-to-all-start.5 = ((f32[4,128,256]{1,2,0:T(8,128)}), f32[4,128,256]{1,2,0:T(8,128)S(1)}, u32[]{:S(2)}, u32[]{:S(2)}) async-start(f32[4,128,256]{1,2,0:T(8,128)} %copy_bitcast_fusion.1), calls=%async_computation.5 | async-start | bytes 1048576 | tf_op jit(solution)/shard_map/all_to_all | solution.py:93
  148.6 0.6 fusion.3
  149.2 2.0 scatter.9
  151.2 0.2 fusion.2
  151.3 11.2 %all-to-all-done.5 = f32[4,128,256]{1,2,0:T(8,128)S(1)} async-done(((f32[4,128,256]{1,2,0:T(8,128)}), f32[4,128,256]{1,2,0:T(8,128)S(1)}, u32[]{:S(2)}, u32[]{:S(2)}) %all-to-all-start.5) | async-done | bytes 524320 | tf_op jit(solution)/shard_map/all_to_all | solution.py:93
  162.5 0.0 copy-done.4
  162.6 0.2 convolution_bitcast_fusion
  162.8 1.6 collective-permute-start.4
  164.4 1.1 collective-permute-done.4
  165.6 0.1 copy.28
  165.7 22.7 %all_to_all.43 = f32[128,1,430]{2,1,0:T(1,128)S(1)} all-to-all(f32[128,1,430]{2,1,0:T(1,128)S(1)} %copy.28), channel_id=1, replica_groups=mesh['y'=4,'zh'=2,'core'=2,'cx'=4,'cz'=4] {'y','zh','cx','cz'}, dimensions={0} | all-to-all | bytes 440320 | tf_op jit(solution)/shard_map/all_to_all | solution.py:93
  188.5 0.2 reduce_sum.79
  188.7 0.1 broadcast_in_dim.17
  188.9 19.2 %all_to_all.44 = f32[128,1,430]{2,1,0:T(1,128)S(1)} all-to-all(f32[128,1,430]{2,1,0:T(1,128)S(1)} %broadcast_in_dim.17), channel_id=1, replica_groups=mesh['y'=4,'zh'=2,'core'=2,'cx'=4,'cz'=4] {'y','zh','cx','cz'}, dimensions={0} | all-to-all | bytes 440320 | tf_op jit(solution)/shard_map/all_to_all | solution.py:87
  208.0 0.1 copy.29
  208.2 3.2 %collective-permute-start.5 = (f32[128,430]{0,1:T(8,128)S(1)}, f32[128,430]{0,1:T(8,128)S(1)}, u32[]{:S(2)}, u32[]{:S(2)}) collective-permute-start(f32[128,430]{0,1:T(8,128)S(1)} %bitcast.56), channel_id=1, source_target_pairs={{0,16},{16,0},{1,17},{17,1},{2,18},{18,2},{3,19},{19,3},{4,20},{20... | collective-permute-start | bytes 660488 | tf_op jit(solution)/shard_map/ppermute | solution.py:98
  211.3 0.8 convolution_convert_fusion
  212.1 0.3 collective-permute-done.5
  212.5 0.7 slice_multiply_fusion.1
  213.2 0.5 slice.65
  213.7 0.6 slice_multiply_fusion.2
  214.3 0.8 copy.30
  (18 shorter events, 0.3 us)
Async XLA Ops:
  0.6 0.9 copy-start
  2.5 18.8 %copy-start.8 = (s32[1,1,128]{2,1,0:T(1,128)S(1)}, s32[1,1,128]{2,1,0:T(1,128)}, u32[]{:S(2)}) copy-start(s32[1,1,128]{2,1,0:T(1,128)} %param.18) | copy-start | bytes 1540
  16.7 15.6 %all-to-all-start.1 = ((bf16[4,512,256]{2,1,0:T(8,128)(2,1)}), bf16[4,512,256]{2,1,0:T(8,128)(2,1)S(1)}, u32[]{:S(2)}, u32[]{:S(2)}) async-start(bf16[4,512,256]{2,1,0:T(8,128)(2,1)} %broadcast_in_dim.14), calls=%async_computation.1 | async-start | bytes 2097152 | tf_op jit(solution)/shard_map/all_to_all | solution.py:87
  32.3 1.0 copy-start.1
  40.9 8.0 %collective-permute-start = (f32[1024,256]{1,0:T(8,128)}, f32[1024,256]{1,0:T(8,128)S(1)}, u32[]{:S(2)}, u32[]{:S(2)}) collective-permute-start(f32[1024,256]{1,0:T(8,128)} %get-tuple-element.33), channel_id=1, source_target_pairs={{0,16},{16,0},{1,17},{17,1},{2,18},{18,2},{3,19},{19,3},{4,20},{20... | collective-permute-start | bytes 3145736 | tf_op jit(solution)/shard_map/ppermute | solution.py:98
  51.3 26.9 %copy-start.7 = (f32[256]{0:T(256)S(1)}, f32[256]{0:T(256)}, u32[]{:S(2)}) copy-start(f32[256]{0:T(256)} %param.15) | copy-start | bytes 3076
  51.3 27.0 %copy-start.5 = (bf16[256,172]{0,1:T(8,128)(2,1)S(1)}, bf16[256,172]{0,1:T(8,128)(2,1)}, u32[]{:S(2)}) copy-start(bf16[256,172]{0,1:T(8,128)(2,1)} %param.16) | copy-start | bytes 264196
  51.3 27.2 %copy-start.6 = (s32[128]{0:T(128)S(1)}, s32[128]{0:T(128)}, u32[]{:S(2)}) copy-start(s32[128]{0:T(128)} %param.21) | copy-start | bytes 1540
  51.3 18.9 %all-to-all-start.2 = ((f32[4,256,256]{2,1,0:T(8,128)}), f32[4,256,256]{2,1,0:T(8,128)S(1)}, u32[]{:S(2)}, u32[]{:S(2)}) async-start(f32[4,256,256]{2,1,0:T(8,128)} %bitcast.6), calls=%async_computation.2 | async-start | bytes 2097152 | tf_op jit(solution)/shard_map/all_to_all | solution.py:93
  70.3 7.9 %collective-permute-start.1 = (f32[128,256]{1,0:T(8,128)S(1)}, f32[128,256]{1,0:T(8,128)S(1)}, u32[]{:S(2)}, u32[]{:S(2)}) collective-permute-start(f32[128,256]{1,0:T(8,128)S(1)} %constant_dynamic-slice_fusion), channel_id=1, source_target_pairs={{0,32},{32,0},{1,33},{33,1},{2,34},{34,2},{3,35},{35,3},{4,36},{36... | collective-permute-start | bytes 393224 | tf_op jit(solution)/shard_map/ppermute | solution.py:98
  79.4 7.2 %collective-permute-start.2 = (bf16[128,256]{1,0:T(8,128)(2,1)S(1)}, bf16[128,256]{1,0:T(8,128)(2,1)S(1)}, u32[]{:S(2)}, u32[]{:S(2)}) collective-permute-start(bf16[128,256]{1,0:T(8,128)(2,1)S(1)} %get-tuple-element.64), channel_id=1, source_target_pairs={{0,32},{32,0},{1,33},{33,1},{2,34},{34,2},{3,35},{35,3},{4,36},{36... | collective-permute-start | bytes 196616 | tf_op jit(solution)/shard_map/ppermute | solution.py:98
  96.0 6.5 %copy-start.2 = (bf16[4,256,256]{2,1,0:T(8,128)(2,1)}, bf16[4,256,256]{2,1,0:T(8,128)(2,1)S(1)}, u32[]{:S(2)}) copy-start(bf16[4,256,256]{2,1,0:T(8,128)(2,1)S(1)} %all_to_all.41) | copy-start | bytes 1572868
  96.0 6.5 %collective-permute-start.3 = (bf16[1024,256]{1,0:T(8,128)(2,1)S(1)}, bf16[1024,256]{1,0:T(8,128)(2,1)S(1)}, u32[]{:S(2)}, u32[]{:S(2)}) collective-permute-start(bf16[1024,256]{1,0:T(8,128)(2,1)S(1)} %bitcast.52), channel_id=1, source_target_pairs={{0,16},{16,0},{1,17},{17,1},{2,18},{18,2},{3,19},{19,3},{4,20},{20... | collective-permute-start | bytes 1572872 | tf_op jit(solution)/shard_map/ppermute | solution.py:98
  102.5 0.8 copy-start.3
  144.1 18.4 %copy-start.4 = (bf16[128,256]{1,0:T(8,128)(2,1)S(1)}, bf16[128,256]{1,0:T(8,128)(2,1)}, u32[]{:S(2)}) copy-start(bf16[128,256]{1,0:T(8,128)(2,1)} %param.13) | copy-start | bytes 196612
  144.9 17.6 %all-to-all-start.5 = ((f32[4,128,256]{1,2,0:T(8,128)}), f32[4,128,256]{1,2,0:T(8,128)S(1)}, u32[]{:S(2)}, u32[]{:S(2)}) async-start(f32[4,128,256]{1,2,0:T(8,128)} %copy_bitcast_fusion.1), calls=%async_computation.5 | async-start | bytes 1048576 | tf_op jit(solution)/shard_map/all_to_all | solution.py:93
  162.8 2.7 %collective-permute-start.4 = (f32[128,430]{0,1:T(8,128)S(1)}, f32[128,430]{0,1:T(8,128)S(1)}, u32[]{:S(2)}, u32[]{:S(2)}) collective-permute-start(f32[128,430]{0,1:T(8,128)S(1)} %slice_select_fusion), channel_id=1, source_target_pairs={{0,16},{16,0},{1,17},{17,1},{2,18},{18,2},{3,19},{19,3},{4,20},{20... | collective-permute-start | bytes 660488 | tf_op jit(solution)/shard_map/ppermute | solution.py:98
  208.2 4.3 %collective-permute-start.5 = (f32[128,430]{0,1:T(8,128)S(1)}, f32[128,430]{0,1:T(8,128)S(1)}, u32[]{:S(2)}, u32[]{:S(2)}) collective-permute-start(f32[128,430]{0,1:T(8,128)S(1)} %bitcast.56), channel_id=1, source_target_pairs={{0,16},{16,0},{1,17},{17,1},{2,18},{18,2},{3,19},{19,3},{4,20},{20... | collective-permute-start | bytes 660488 | tf_op jit(solution)/shard_map/ppermute | solution.py:98

commit v9 on v8

--- a/solution.py
+++ b/solution.py
@@ -164,7 +164,7 @@
     summed = mine + swap_core(other)
     agg = pair_scatter(scatter_rows(summed, "y"), "zh")
     loss_sum, out_term, bias_term, grad_z = head_block(agg, bias, w_out, labels)
-    gathered = gather_rows(pair_gather(grad_z, "zh"), "y")
+    gathered = gather_rows(grad_z, ("y", "zh"))
     sources = (gathered, swap_core(gathered))
     back_part = tile_product(tile_block, row_pos, col_ids, live_count, sources, col_tiles, True)
     grad_proj = scatter_rows(scatter_rows(back_part, "cx"), "cz").astype(jnp.bfloat16)

time: 218 us -> 219 us (level)
  blocking collectives: 95.5 us -> 103 us
  waiting for transfers between devices: 47.8 us -> 44.3 us
  starting transfers between devices: 36.2 us -> 33.2 us
    all_to_all x3, blocking collectives: 41.6 us -> 50.6 us  [gather_rows(): got = lax.all_to_all(spread, axis, 0, 0, tiled=False)]
    ppermute x6 -> x5, starting transfers between devices: 24.2 us -> 19.4 us  [swap_core(): return lax.ppermute(x, axis, [(0, 1), (1, 0)])]
    ppermute x6 -> x5, waiting for transfers between devices: 11.6 us -> 8.24 us  [swap_core(): return lax.ppermute(x, axis, [(0, 1), (1, 0)])]
  transfers between devices with their start and end apart: 9 -> 8, of which waited for: 9 -> 8; matrix products, arithmetic and copies ran while one was open for 2% -> 2% of each run, Pallas kernels for 0% -> 0%
where the time goes in v9:
time: 219 us; the launch traced here: 218 us
  blocking collectives  103 us (47%)
  waiting for transfers between devices  44.3 us (20%)
  starting transfers between devices  33.2 us (15%)
  Pallas kernels  15.2 us (7%)
  local copies, waits for them, and re-layouts  10.8 us (5%)
  other arithmetic  5.63 us (3%)
  between operations  3.26 us (1%)
  matrix products  2.57 us (1%)
    all_to_all x2, blocking collectives, scatter_rows(): got = lax.all_to_all(x.reshape(n, -1, x.shape[1]), axis, 0, 0, tiled=False)  52.4 us
    all_to_all x3, blocking collectives, gather_rows(): got = lax.all_to_all(spread, axis, 0, 0, tiled=False)  50.6 us
    all_to_all x2, waiting for transfers between devices, scatter_rows(): got = lax.all_to_all(x.reshape(n, -1, x.shape[1]), axis, 0, 0, tiled=False)  25.6 us
    ppermute x5, starting transfers between devices, swap_core(): return lax.ppermute(x, axis, [(0, 1), (1, 0)])  19.4 us
    pallas_call x2, Pallas kernels, tile_product(): pl.pallas_call(lambda *refs: _dense_kernel(transpose, *refs), grid_spec=g...  15.2 us
    all_to_all x1, waiting for transfers between devices, gather_rows(): got = lax.all_to_all(spread, axis, 0, 0, tiled=False)  10.4 us
    all_to_all x2, starting transfers between devices, scatter_rows(): got = lax.all_to_all(x.reshape(n, -1, x.shape[1]), axis, 0, 0, tiled=False)  9.76 us
    ppermute x5, waiting for transfers between devices, swap_core(): return lax.ppermute(x, axis, [(0, 1), (1, 0)])  8.24 us
  transfers between devices with their start and end apart: 8, of which 8 were waited for; matrix products, arithmetic and copies ran while one was open for 2% of the time, Pallas kernels for 0%

profile of v9, /device:TPU:1, one launch (start us, length us, event | category | flops | bytes accessed | tf_op | source)
XLA Modules:
  0.0 218.0 jit_solution(4161940672382013048)
XLA Ops:
  0.6 0.0 copy-start
  0.6 0.9 copy-done
  1.5 1.0 convolution_convert_fusion.1
  2.5 0.0 copy-start.8
  2.6 13.1 %all_to_all.40 = bf16[4,128,256]{2,1,0:T(8,128)(2,1)S(1)} all-to-all(bf16[4,128,256]{2,1,0:T(8,128)(2,1)S(1)} %broadcast_in_dim.12), channel_id=1, replica_groups=mesh['y'=4,'zh'=2,'core'=2,'cx'=4,'cz'=4] {'cz'}, dimensions={0} | all-to-all | bytes 524288 | tf_op jit(solution)/shard_map/all_to_all | solution.py:87
  15.6 1.1 broadcast_in_dim.14
  16.7 4.0 %all-to-all-start.1 = ((bf16[4,512,256]{2,1,0:T(8,128)(2,1)}), bf16[4,512,256]{2,1,0:T(8,128)(2,1)S(1)}, u32[]{:S(2)}, u32[]{:S(2)}) async-start(bf16[4,512,256]{2,1,0:T(8,128)(2,1)} %broadcast_in_dim.14), calls=%async_computation.1 | async-start | bytes 2097152 | tf_op jit(solution)/shard_map/all_to_all | solution.py:87
  21.4 0.0 copy-done.8
  21.4 0.5 compare_select_fusion.refs_0_
  21.9 10.4 %all-to-all-done.1 = bf16[4,512,256]{2,1,0:T(8,128)(2,1)S(1)} async-done(((bf16[4,512,256]{2,1,0:T(8,128)(2,1)}), bf16[4,512,256]{2,1,0:T(8,128)(2,1)S(1)}, u32[]{:S(2)}, u32[]{:S(2)}) %all-to-all-start.1) | async-done | bytes 1048608 | tf_op jit(solution)/shard_map/all_to_all | solution.py:87
  32.3 0.0 copy-start.1
  32.3 0.6 broadcast_in_dim.15.refs_5_
  33.0 0.4 copy-done.1
  33.4 7.6 %shard_map.128 = (f32[1024,256]{1,0:T(8,128)}, f32[1024,256]{1,0:T(8,128)}) custom-call(s32[128]{0:T(128)} %compare_select_fusion.refs_0_, s32[128]{0:T(128)} %bitcast.58, s32[1]{0:T(128)} %bitcast.46.refs_2_, bf16[128,128,128]{2,1,0:T(8,128)(2,1)} %bitcast.48, bf16[2048,256]{1,0:T(8,128)(2,1)} %bitcast.51, bf16[8,128]{1,0:T(8,128)(2,1)} %broadcast_in_dim.15.refs_5_), custom_call_target="tpu_custom_call" | custom-call | tf_op jit(solution)/shard_map/pallas_call | solution.py:73
  41.0 5.4 %collective-permute-start = (f32[1024,256]{1,0:T(8,128)}, f32[1024,256]{1,0:T(8,128)S(1)}, u32[]{:S(2)}, u32[]{:S(2)}) collective-permute-start(f32[1024,256]{1,0:T(8,128)} %get-tuple-element.33), channel_id=1, source_target_pairs={{0,16},{16,0},{1,17},{17,1},{2,18},{18,2},{3,19},{19,3},{4,20},{20... | collective-permute-start | bytes 3145736 | tf_op jit(solution)/shard_map/ppermute | solution.py:98
  46.3 2.5 %collective-permute-done = f32[1024,256]{1,0:T(8,128)S(1)} collective-permute-done((f32[1024,256]{1,0:T(8,128)}, f32[1024,256]{1,0:T(8,128)S(1)}, u32[]{:S(2)}, u32[]{:S(2)}) %collective-permute-start) | collective-permute-done | bytes 1048608 | tf_op jit(solution)/shard_map/ppermute | solution.py:98
  48.8 2.4 %add.58 = f32[1024,256]{1,0:T(8,128)} add(f32[1024,256]{1,0:T(8,128)} %get-tuple-element.32, f32[1024,256]{1,0:T(8,128)S(1)} %collective-permute-done) | non-fusion elementwise | flops 262144 | bytes 3145728 | tf_op jit(solution)/shard_map/add | solution.py:164
  51.2 0.0 copy-start.7
  51.2 3.9 %all-to-all-start.2 = ((f32[4,256,256]{2,1,0:T(8,128)}), f32[4,256,256]{2,1,0:T(8,128)S(1)}, u32[]{:S(2)}, u32[]{:S(2)}) async-start(f32[4,256,256]{2,1,0:T(8,128)} %bitcast.6), calls=%async_computation.2 | async-start | bytes 2097152 | tf_op jit(solution)/shard_map/all_to_all | solution.py:93
  55.1 14.5 %all-to-all-done.2 = f32[4,256,256]{2,1,0:T(8,128)S(1)} async-done(((f32[4,256,256]{2,1,0:T(8,128)}), f32[4,256,256]{2,1,0:T(8,128)S(1)}, u32[]{:S(2)}, u32[]{:S(2)}) %all-to-all-start.2) | async-done | bytes 1048608 | tf_op jit(solution)/shard_map/all_to_all | solution.py:93
  69.6 0.1 reduce_sum.72
  69.7 5.1 %collective-permute-start.1 = (f32[128,256]{1,0:T(8,128)S(1)}, f32[128,256]{1,0:T(8,128)S(1)}, u32[]{:S(2)}, u32[]{:S(2)}) collective-permute-start(f32[128,256]{1,0:T(8,128)S(1)} %constant_dynamic-slice_fusion), channel_id=1, source_target_pairs={{0,32},{32,0},{1,33},{33,1},{2,34},{34,2},{3,35},{35,3},{4,36},{36... | collective-permute-start | bytes 393224 | tf_op jit(solution)/shard_map/ppermute | solution.py:98
  74.8 2.8 %collective-permute-done.1 = f32[128,256]{1,0:T(8,128)S(1)} collective-permute-done((f32[128,256]{1,0:T(8,128)S(1)}, f32[128,256]{1,0:T(8,128)S(1)}, u32[]{:S(2)}, u32[]{:S(2)}) %collective-permute-start.1) | collective-permute-done | bytes 131104 | tf_op jit(solution)/shard_map/ppermute | solution.py:98
  77.6 0.0 copy-done.7
  77.6 0.1 multiply_convert_fusion.1
  77.7 0.0 copy-done.5
  77.7 0.2 fusion.4
  77.9 0.0 copy-done.6
  77.9 0.1 select_reduce_fusion
  78.0 0.6 subtract_reduce_fusion
  78.6 0.2 convert_reduce_fusion
  78.9 18.4 %all_to_all.41 = bf16[8,128,256]{2,1,0:T(8,128)(2,1)S(1)} all-to-all(bf16[8,128,256]{2,1,0:T(8,128)(2,1)S(1)} %broadcast_in_dim.16), channel_id=1, replica_groups=mesh['y'=4,'zh'=2,'core'=2,'cx'=4,'cz'=4] {'y','zh'}, dimensions={0} | all-to-all | bytes 1048576 | tf_op jit(solution)/shard_map/all_to_all | solution.py:87
  97.2 4.1 %collective-permute-start.2 = (bf16[1024,256]{1,0:T(8,128)(2,1)S(1)}, bf16[1024,256]{1,0:T(8,128)(2,1)S(1)}, u32[]{:S(2)}, u32[]{:S(2)}) collective-permute-start(bf16[1024,256]{1,0:T(8,128)(2,1)S(1)} %bitcast.52), channel_id=1, source_target_pairs={{0,16},{16,0},{1,17},{17,1},{2,18},{18,2},{3,19},{19,3},{4,20},{20... | collective-permute-start | bytes 1572872 | tf_op jit(solution)/shard_map/ppermute | solution.py:98
  101.3 1.5 collective-permute-done.2.refs_5_
  102.9 0.0 copy-done.2
  102.9 0.8 copy-done.3
  103.7 7.6 %shard_map.129 = (f32[256,2048]{1,0:T(8,128)}, f32[8,128]{1,0:T(8,128)}) custom-call(s32[128]{0:T(128)} %compare_select_fusion.refs_0_, s32[128]{0:T(128)} %bitcast.59, s32[1]{0:T(128)} %bitcast.47.refs_2_, bf16[128,128,128]{2,1,0:T(8,128)(2,1)} %bitcast.49, bf16[1024,256]{1,0:T(8,128)(2,1)} %bitcast.53, bf16[1024,256]{1,0:T(8,128)(2,1)} %copy-done.3), custom_call_target="tpu_custom_call" | custom-call | tf_op jit(solution)/shard_map/pallas_call | solution.py:73
  111.3 1.8 copy.37
  113.1 31.3 %all_to_all.42 = f32[4,512,256]{1,2,0:T(8,128)S(1)} all-to-all(f32[4,512,256]{1,2,0:T(8,128)S(1)} %bitcast.50), channel_id=1, replica_groups=mesh['y'=4,'zh'=2,'core'=2,'cx'=4,'cz'=4] {'cx'}, dimensions={0} | all-to-all | bytes 4194304 | tf_op jit(solution)/shard_map/all_to_all | solution.py:93
  144.3 0.2 reduce_sum.74
  144.6 0.0 copy-start.4
  144.6 0.8 copy_bitcast_fusion.1
  145.4 5.9 %all-to-all-start.5 = ((f32[4,128,256]{1,2,0:T(8,128)}), f32[4,128,256]{1,2,0:T(8,128)S(1)}, u32[]{:S(2)}, u32[]{:S(2)}) async-start(f32[4,128,256]{1,2,0:T(8,128)} %copy_bitcast_fusion.1), calls=%async_computation.5 | async-start | bytes 1048576 | tf_op jit(solution)/shard_map/all_to_all | solution.py:93
  151.3 0.6 fusion.3
  151.9 2.0 scatter.9
  153.9 0.2 fusion.2
  154.1 11.1 %all-to-all-done.5 = f32[4,128,256]{1,2,0:T(8,128)S(1)} async-done(((f32[4,128,256]{1,2,0:T(8,128)}), f32[4,128,256]{1,2,0:T(8,128)S(1)}, u32[]{:S(2)}, u32[]{:S(2)}) %all-to-all-start.5) | async-done | bytes 524320 | tf_op jit(solution)/shard_map/all_to_all | solution.py:93
  165.2 0.0 copy-done.4
  165.2 0.2 convolution_bitcast_fusion
  165.4 1.7 collective-permute-start.3
  167.1 1.1 collective-permute-done.3
  168.3 0.1 copy.28
  168.4 21.1 %all_to_all.43 = f32[128,1,430]{2,1,0:T(1,128)S(1)} all-to-all(f32[128,1,430]{2,1,0:T(1,128)S(1)} %copy.28), channel_id=1, replica_groups=mesh['y'=4,'zh'=2,'core'=2,'cx'=4,'cz'=4] {'y','zh','cx','cz'}, dimensions={0} | all-to-all | bytes 440320 | tf_op jit(solution)/shard_map/all_to_all | solution.py:93
  189.6 0.2 reduce_sum.79
  189.8 0.1 broadcast_in_dim.17
  189.9 19.2 %all_to_all.44 = f32[128,1,430]{2,1,0:T(1,128)S(1)} all-to-all(f32[128,1,430]{2,1,0:T(1,128)S(1)} %broadcast_in_dim.17), channel_id=1, replica_groups=mesh['y'=4,'zh'=2,'core'=2,'cx'=4,'cz'=4] {'y','zh','cx','cz'}, dimensions={0} | all-to-all | bytes 440320 | tf_op jit(solution)/shard_map/all_to_all | solution.py:87
  209.1 0.1 copy.29
  209.2 3.2 %collective-permute-start.4 = (f32[128,430]{0,1:T(8,128)S(1)}, f32[128,430]{0,1:T(8,128)S(1)}, u32[]{:S(2)}, u32[]{:S(2)}) collective-permute-start(f32[128,430]{0,1:T(8,128)S(1)} %bitcast.56), channel_id=1, source_target_pairs={{0,16},{16,0},{1,17},{17,1},{2,18},{18,2},{3,19},{19,3},{4,20},{20... | collective-permute-start | bytes 660488 | tf_op jit(solution)/shard_map/ppermute | solution.py:98
  212.4 0.8 convolution_convert_fusion
  213.2 0.3 collective-permute-done.4
  213.6 0.7 slice_multiply_fusion.1
  214.3 0.5 slice.65
  214.8 0.6 slice_multiply_fusion.2
  215.3 0.8 copy.30
  (15 shorter events, 0.3 us)
Async XLA Ops:
  0.6 0.9 copy-start
  2.5 18.8 %copy-start.8 = (s32[1,1,128]{2,1,0:T(1,128)S(1)}, s32[1,1,128]{2,1,0:T(1,128)}, u32[]{:S(2)}) copy-start(s32[1,1,128]{2,1,0:T(1,128)} %param.18) | copy-start | bytes 1540
  16.7 15.6 %all-to-all-start.1 = ((bf16[4,512,256]{2,1,0:T(8,128)(2,1)}), bf16[4,512,256]{2,1,0:T(8,128)(2,1)S(1)}, u32[]{:S(2)}, u32[]{:S(2)}) async-start(bf16[4,512,256]{2,1,0:T(8,128)(2,1)} %broadcast_in_dim.14), calls=%async_computation.1 | async-start | bytes 2097152 | tf_op jit(solution)/shard_map/all_to_all | solution.py:87
  32.3 1.0 copy-start.1
  41.0 7.9 %collective-permute-start = (f32[1024,256]{1,0:T(8,128)}, f32[1024,256]{1,0:T(8,128)S(1)}, u32[]{:S(2)}, u32[]{:S(2)}) collective-permute-start(f32[1024,256]{1,0:T(8,128)} %get-tuple-element.33), channel_id=1, source_target_pairs={{0,16},{16,0},{1,17},{17,1},{2,18},{18,2},{3,19},{19,3},{4,20},{20... | collective-permute-start | bytes 3145736 | tf_op jit(solution)/shard_map/ppermute | solution.py:98
  51.2 26.4 %copy-start.7 = (f32[256]{0:T(256)S(1)}, f32[256]{0:T(256)}, u32[]{:S(2)}) copy-start(f32[256]{0:T(256)} %param.15) | copy-start | bytes 3076
  51.2 26.5 %copy-start.5 = (bf16[256,172]{0,1:T(8,128)(2,1)S(1)}, bf16[256,172]{0,1:T(8,128)(2,1)}, u32[]{:S(2)}) copy-start(bf16[256,172]{0,1:T(8,128)(2,1)} %param.16) | copy-start | bytes 264196
  51.2 26.7 %copy-start.6 = (s32[128]{0:T(128)S(1)}, s32[128]{0:T(128)}, u32[]{:S(2)}) copy-start(s32[128]{0:T(128)} %param.21) | copy-start | bytes 1540
  51.2 18.4 %all-to-all-start.2 = ((f32[4,256,256]{2,1,0:T(8,128)}), f32[4,256,256]{2,1,0:T(8,128)S(1)}, u32[]{:S(2)}, u32[]{:S(2)}) async-start(f32[4,256,256]{2,1,0:T(8,128)} %bitcast.6), calls=%async_computation.2 | async-start | bytes 2097152 | tf_op jit(solution)/shard_map/all_to_all | solution.py:93
  69.7 7.9 %collective-permute-start.1 = (f32[128,256]{1,0:T(8,128)S(1)}, f32[128,256]{1,0:T(8,128)S(1)}, u32[]{:S(2)}, u32[]{:S(2)}) collective-permute-start(f32[128,256]{1,0:T(8,128)S(1)} %constant_dynamic-slice_fusion), channel_id=1, source_target_pairs={{0,32},{32,0},{1,33},{33,1},{2,34},{34,2},{3,35},{35,3},{4,36},{36... | collective-permute-start | bytes 393224 | tf_op jit(solution)/shard_map/ppermute | solution.py:98
  97.2 5.6 %copy-start.2 = (bf16[8,128,256]{2,1,0:T(8,128)(2,1)}, bf16[8,128,256]{2,1,0:T(8,128)(2,1)S(1)}, u32[]{:S(2)}) copy-start(bf16[8,128,256]{2,1,0:T(8,128)(2,1)S(1)} %all_to_all.41) | copy-start | bytes 1572868
  97.2 5.6 %collective-permute-start.2 = (bf16[1024,256]{1,0:T(8,128)(2,1)S(1)}, bf16[1024,256]{1,0:T(8,128)(2,1)S(1)}, u32[]{:S(2)}, u32[]{:S(2)}) collective-permute-start(bf16[1024,256]{1,0:T(8,128)(2,1)S(1)} %bitcast.52), channel_id=1, source_target_pairs={{0,16},{16,0},{1,17},{17,1},{2,18},{18,2},{3,19},{19,3},{4,20},{20... | collective-permute-start | bytes 1572872 | tf_op jit(solution)/shard_map/ppermute | solution.py:98
  102.8 0.8 copy-start.3
  144.6 20.6 %copy-start.4 = (bf16[128,256]{1,0:T(8,128)(2,1)S(1)}, bf16[128,256]{1,0:T(8,128)(2,1)}, u32[]{:S(2)}) copy-start(bf16[128,256]{1,0:T(8,128)(2,1)} %param.13) | copy-start | bytes 196612
  145.4 19.7 %all-to-all-start.5 = ((f32[4,128,256]{1,2,0:T(8,128)}), f32[4,128,256]{1,2,0:T(8,128)S(1)}, u32[]{:S(2)}, u32[]{:S(2)}) async-start(f32[4,128,256]{1,2,0:T(8,128)} %copy_bitcast_fusion.1), calls=%async_computation.5 | async-start | bytes 1048576 | tf_op jit(solution)/shard_map/all_to_all | solution.py:93
  165.4 2.8 %collective-permute-start.3 = (f32[128,430]{0,1:T(8,128)S(1)}, f32[128,430]{0,1:T(8,128)S(1)}, u32[]{:S(2)}, u32[]{:S(2)}) collective-permute-start(f32[128,430]{0,1:T(8,128)S(1)} %slice_select_fusion), channel_id=1, source_target_pairs={{0,16},{16,0},{1,17},{17,1},{2,18},{18,2},{3,19},{19,3},{4,20},{20... | collective-permute-start | bytes 660488 | tf_op jit(solution)/shard_map/ppermute | solution.py:98
  209.2 4.3 %collective-permute-start.4 = (f32[128,430]{0,1:T(8,128)S(1)}, f32[128,430]{0,1:T(8,128)S(1)}, u32[]{:S(2)}, u32[]{:S(2)}) collective-permute-start(f32[128,430]{0,1:T(8,128)S(1)} %bitcast.56), channel_id=1, source_target_pairs={{0,16},{16,0},{1,17},{17,1},{2,18},{18,2},{3,19},{19,3},{4,20},{20... | collective-permute-start | bytes 660488 | tf_op jit(solution)/shard_map/ppermute | solution.py:98

commit v10 on v9

--- a/solution.py
+++ b/solution.py
@@ -88,10 +88,13 @@
     return got.reshape(n * x.shape[0], x.shape[1])
 
 
-def scatter_rows(x, axis):
+def scatter_rows(x, axis, kind=None):
     n = lax.psum(1, axis)
-    got = lax.all_to_all(x.reshape(n, -1, x.shape[1]), axis, 0, 0, tiled=False)
-    return jnp.sum(got, axis=0)
+    sent = x.reshape(n, -1, x.shape[1])
+    if kind is not None:
+        sent = sent.astype(kind)
+    got = lax.all_to_all(sent, axis, 0, 0, tiled=False)
+    return jnp.sum(got.astype(jnp.float32), axis=0)
 
 
 def swap_core(x, axis="core"):
@@ -162,7 +165,7 @@
     source = gather_rows(gather_rows(proj, "cz"), "cx")
     mine, other = tile_product(tile_block, row_pos, col_ids, live_count, (source,), row_tiles, False)
     summed = mine + swap_core(other)
-    agg = pair_scatter(scatter_rows(summed, "y"), "zh")
+    agg = pair_scatter(scatter_rows(summed, "y", jnp.bfloat16), "zh")
     loss_sum, out_term, bias_term, grad_z = head_block(agg, bias, w_out, labels)
     gathered = gather_rows(grad_z, ("y", "zh"))
     sources = (gathered, swap_core(gathered))

time: 219 us -> 213 us (0.973)
  waiting for transfers between devices: 44.3 us -> 39.9 us
  starting transfers between devices: 33.2 us -> 29.7 us
    all_to_all x2, waiting for transfers between devices: 25.6 us -> 20.2 us  [scatter_rows(): got = lax.all_to_all(sent, axis, 0, 0, tiled=False)]
    all_to_all x3, blocking collectives: 50.6 us -> 55.1 us  [gather_rows(): got = lax.all_to_all(spread, axis, 0, 0, tiled=False)]
    ppermute x5, starting transfers between devices: 19.4 us -> 16.1 us  [swap_core(): return lax.ppermute(x, axis, [(0, 1), (1, 0)])]
    all_to_all x2, blocking collectives: 52.4 us -> 49.7 us  [scatter_rows(): got = lax.all_to_all(sent, axis, 0, 0, tiled=False)]
    add x1 -> x0, other arithmetic: 2.39 us -> none  [body(): summed = mine + swap_core(other)]
where the time goes in v10:
time: 213 us; the launch traced here: 212 us
  blocking collectives  105 us (49%)
  waiting for transfers between devices  39.9 us (19%)
  starting transfers between devices  29.7 us (14%)
  Pallas kernels  15.3 us (7%)
  local copies, waits for them, and re-layouts  10.8 us (5%)
  other arithmetic  5.4 us (3%)
  between operations  3.26 us (2%)
  matrix products  2.57 us (1%)
    all_to_all x3, blocking collectives, gather_rows(): got = lax.all_to_all(spread, axis, 0, 0, tiled=False)  55.1 us
    all_to_all x2, blocking collectives, scatter_rows(): got = lax.all_to_all(sent, axis, 0, 0, tiled=False)  49.7 us
    all_to_all x2, waiting for transfers between devices, scatter_rows(): got = lax.all_to_all(sent, axis, 0, 0, tiled=False)  20.2 us
    ppermute x5, starting transfers between devices, swap_core(): return lax.ppermute(x, axis, [(0, 1), (1, 0)])  16.1 us
    pallas_call x2, Pallas kernels, tile_product(): pl.pallas_call(lambda *refs: _dense_kernel(transpose, *refs), grid_spec=g...  15.3 us
    all_to_all x1, waiting for transfers between devices, gather_rows(): got = lax.all_to_all(spread, axis, 0, 0, tiled=False)  10.4 us
    all_to_all x2, starting transfers between devices, scatter_rows(): got = lax.all_to_all(sent, axis, 0, 0, tiled=False)  9.63 us
    ppermute x5, waiting for transfers between devices, swap_core(): return lax.ppermute(x, axis, [(0, 1), (1, 0)])  9.25 us
  transfers between devices with their start and end apart: 8, of which 8 were waited for; matrix products, arithmetic and copies ran while one was open for 2% of the time, Pallas kernels for 0%

profile of v10, /device:TPU:1, one launch (start us, length us, event | category | flops | bytes accessed | tf_op | source)
XLA Modules:
  0.0 211.8 jit_solution(14356372775845252626)
XLA Ops:
  0.6 0.0 copy-start
  0.6 0.9 copy-done
  1.5 1.0 convolution_convert_fusion.1
  2.5 0.0 copy-start.8
  2.6 13.1 %all_to_all.40 = bf16[4,128,256]{2,1,0:T(8,128)(2,1)S(1)} all-to-all(bf16[4,128,256]{2,1,0:T(8,128)(2,1)S(1)} %broadcast_in_dim.12), channel_id=1, replica_groups=mesh['y'=4,'zh'=2,'core'=2,'cx'=4,'cz'=4] {'cz'}, dimensions={0} | all-to-all | bytes 524288 | tf_op jit(solution)/shard_map/all_to_all | solution.py:87
  15.6 1.1 broadcast_in_dim.14
  16.7 4.0 %all-to-all-start.1 = ((bf16[4,512,256]{2,1,0:T(8,128)(2,1)}), bf16[4,512,256]{2,1,0:T(8,128)(2,1)S(1)}, u32[]{:S(2)}, u32[]{:S(2)}) async-start(bf16[4,512,256]{2,1,0:T(8,128)(2,1)} %broadcast_in_dim.14), calls=%async_computation.1 | async-start | bytes 2097152 | tf_op jit(solution)/shard_map/all_to_all | solution.py:87
  21.4 0.0 copy-done.8
  21.4 0.5 compare_select_fusion.refs_0_
  21.9 10.4 %all-to-all-done.1 = bf16[4,512,256]{2,1,0:T(8,128)(2,1)S(1)} async-done(((bf16[4,512,256]{2,1,0:T(8,128)(2,1)}), bf16[4,512,256]{2,1,0:T(8,128)(2,1)S(1)}, u32[]{:S(2)}, u32[]{:S(2)}) %all-to-all-start.1) | async-done | bytes 1048608 | tf_op jit(solution)/shard_map/all_to_all | solution.py:87
  32.3 0.0 copy-start.1
  32.3 0.6 broadcast_in_dim.15.refs_5_
  33.0 0.4 copy-done.1
  33.4 7.7 %shard_map.128 = (f32[1024,256]{1,0:T(8,128)}, f32[1024,256]{1,0:T(8,128)}) custom-call(s32[128]{0:T(128)} %compare_select_fusion.refs_0_, s32[128]{0:T(128)} %bitcast.58, s32[1]{0:T(128)} %bitcast.46.refs_2_, bf16[128,128,128]{2,1,0:T(8,128)(2,1)} %bitcast.48, bf16[2048,256]{1,0:T(8,128)(2,1)} %bitcast.51, bf16[8,128]{1,0:T(8,128)(2,1)} %broadcast_in_dim.15.refs_5_), custom_call_target="tpu_custom_call" | custom-call | tf_op jit(solution)/shard_map/pallas_call | solution.py:73
  41.0 4.3 %collective-permute-start = (f32[1024,256]{1,0:T(8,128)}, f32[1024,256]{1,0:T(8,128)S(1)}, u32[]{:S(2)}, u32[]{:S(2)}) collective-permute-start(f32[1024,256]{1,0:T(8,128)} %get-tuple-element.33), channel_id=1, source_target_pairs={{0,16},{16,0},{1,17},{17,1},{2,18},{18,2},{3,19},{19,3},{4,20},{20... | collective-permute-start | bytes 3145736 | tf_op jit(solution)/shard_map/ppermute | solution.py:101
  45.3 2.5 %collective-permute-done = f32[1024,256]{1,0:T(8,128)S(1)} collective-permute-done((f32[1024,256]{1,0:T(8,128)}, f32[1024,256]{1,0:T(8,128)S(1)}, u32[]{:S(2)}, u32[]{:S(2)}) %collective-permute-start) | collective-permute-done | bytes 1048608 | tf_op jit(solution)/shard_map/ppermute | solution.py:101
  47.8 0.0 copy-start.7
  47.8 2.2 %add_convert_fusion = bf16[1024,256]{1,0:T(8,128)(2,1)} fusion(f32[1024,256]{1,0:T(8,128)} %get-tuple-element.32, f32[1024,256]{1,0:T(8,128)S(1)} %collective-permute-done), kind=kLoop, calls=%fused_computation.6 | loop fusion | flops 524288 | bytes 2621440 | tf_op jit(solution)/shard_map/convert_element_type | solution.py:95
  50.0 5.6 %all-to-all-start.2 = ((bf16[4,256,256]{2,1,0:T(8,128)(2,1)}), bf16[4,256,256]{2,1,0:T(8,128)(2,1)S(1)}, u32[]{:S(2)}, u32[]{:S(2)}) async-start(bf16[4,256,256]{2,1,0:T(8,128)(2,1)} %bitcast.6), calls=%async_computation.2 | async-start | bytes 1048576 | tf_op jit(solution)/shard_map/all_to_all | solution.py:96
  55.6 8.9 %all-to-all-done.2 = bf16[4,256,256]{2,1,0:T(8,128)(2,1)S(1)} async-done(((bf16[4,256,256]{2,1,0:T(8,128)(2,1)}), bf16[4,256,256]{2,1,0:T(8,128)(2,1)S(1)}, u32[]{:S(2)}, u32[]{:S(2)}) %all-to-all-start.2) | async-done | bytes 524320 | tf_op jit(solution)/shard_map/all_to_all | solution.py:96
  64.5 0.1 convert_reduce_fusion
  64.6 4.1 %collective-permute-start.1 = (f32[128,256]{1,0:T(8,128)S(1)}, f32[128,256]{1,0:T(8,128)S(1)}, u32[]{:S(2)}, u32[]{:S(2)}) collective-permute-start(f32[128,256]{1,0:T(8,128)S(1)} %constant_dynamic-slice_fusion), channel_id=1, source_target_pairs={{0,32},{32,0},{1,33},{33,1},{2,34},{34,2},{3,35},{35,3},{4,36},{36... | collective-permute-start | bytes 393224 | tf_op jit(solution)/shard_map/ppermute | solution.py:101
  68.7 3.8 %collective-permute-done.1 = f32[128,256]{1,0:T(8,128)S(1)} collective-permute-done((f32[128,256]{1,0:T(8,128)S(1)}, f32[128,256]{1,0:T(8,128)S(1)}, u32[]{:S(2)}, u32[]{:S(2)}) %collective-permute-start.1) | collective-permute-done | bytes 131104 | tf_op jit(solution)/shard_map/ppermute | solution.py:101
  72.5 0.0 copy-done.7
  72.5 0.1 multiply_convert_fusion.1
  72.6 0.0 copy-done.5
  72.6 0.2 fusion.4
  72.8 0.0 copy-done.6
  72.8 0.1 select_reduce_fusion
  72.9 0.6 subtract_reduce_fusion
  73.5 0.2 convert_reduce_fusion.1
  73.7 22.9 %all_to_all.41 = bf16[8,128,256]{2,1,0:T(8,128)(2,1)S(1)} all-to-all(bf16[8,128,256]{2,1,0:T(8,128)(2,1)S(1)} %broadcast_in_dim.16), channel_id=1, replica_groups=mesh['y'=4,'zh'=2,'core'=2,'cx'=4,'cz'=4] {'y','zh'}, dimensions={0} | all-to-all | bytes 1048576 | tf_op jit(solution)/shard_map/all_to_all | solution.py:87
  96.6 3.1 %collective-permute-start.2 = (bf16[1024,256]{1,0:T(8,128)(2,1)S(1)}, bf16[1024,256]{1,0:T(8,128)(2,1)S(1)}, u32[]{:S(2)}, u32[]{:S(2)}) collective-permute-start(bf16[1024,256]{1,0:T(8,128)(2,1)S(1)} %bitcast.52), channel_id=1, source_target_pairs={{0,16},{16,0},{1,17},{17,1},{2,18},{18,2},{3,19},{19,3},{4,20},{20... | collective-permute-start | bytes 1572872 | tf_op jit(solution)/shard_map/ppermute | solution.py:101
  99.7 1.5 collective-permute-done.2.refs_5_
  101.3 0.0 copy-done.2
  101.3 0.8 copy-done.3
  102.1 7.7 %shard_map.129 = (f32[256,2048]{1,0:T(8,128)}, f32[8,128]{1,0:T(8,128)}) custom-call(s32[128]{0:T(128)} %compare_select_fusion.refs_0_, s32[128]{0:T(128)} %bitcast.59, s32[1]{0:T(128)} %bitcast.47.refs_2_, bf16[128,128,128]{2,1,0:T(8,128)(2,1)} %bitcast.49, bf16[1024,256]{1,0:T(8,128)(2,1)} %bitcast.53, bf16[1024,256]{1,0:T(8,128)(2,1)} %copy-done.3), custom_call_target="tpu_custom_call" | custom-call | tf_op jit(solution)/shard_map/pallas_call | solution.py:73
  109.8 1.8 copy.37
  111.5 28.6 %all_to_all.42 = f32[4,512,256]{1,2,0:T(8,128)S(1)} all-to-all(f32[4,512,256]{1,2,0:T(8,128)S(1)} %bitcast.50), channel_id=1, replica_groups=mesh['y'=4,'zh'=2,'core'=2,'cx'=4,'cz'=4] {'cx'}, dimensions={0} | all-to-all | bytes 4194304 | tf_op jit(solution)/shard_map/all_to_all | solution.py:96
  140.2 0.2 reduce_sum.74
  140.4 0.0 copy-start.4
  140.4 0.8 copy_bitcast_fusion.1
  141.2 4.0 %all-to-all-start.5 = ((f32[4,128,256]{1,2,0:T(8,128)}), f32[4,128,256]{1,2,0:T(8,128)S(1)}, u32[]{:S(2)}, u32[]{:S(2)}) async-start(f32[4,128,256]{1,2,0:T(8,128)} %copy_bitcast_fusion.1), calls=%async_computation.5 | async-start | bytes 1048576 | tf_op jit(solution)/shard_map/all_to_all | solution.py:96
  145.3 0.6 fusion.3
  145.8 2.0 scatter.9
  147.8 0.2 fusion.2
  148.0 11.3 %all-to-all-done.5 = f32[4,128,256]{1,2,0:T(8,128)S(1)} async-done(((f32[4,128,256]{1,2,0:T(8,128)}), f32[4,128,256]{1,2,0:T(8,128)S(1)}, u32[]{:S(2)}, u32[]{:S(2)}) %all-to-all-start.5) | async-done | bytes 524320 | tf_op jit(solution)/shard_map/all_to_all | solution.py:96
  159.3 0.0 copy-done.4
  159.3 0.2 convolution_bitcast_fusion
  159.6 1.5 collective-permute-start.3
  161.1 1.1 collective-permute-done.3
  162.2 0.1 copy.28
  162.4 21.0 %all_to_all.43 = f32[128,1,430]{2,1,0:T(1,128)S(1)} all-to-all(f32[128,1,430]{2,1,0:T(1,128)S(1)} %copy.28), channel_id=1, replica_groups=mesh['y'=4,'zh'=2,'core'=2,'cx'=4,'cz'=4] {'y','zh','cx','cz'}, dimensions={0} | all-to-all | bytes 440320 | tf_op jit(solution)/shard_map/all_to_all | solution.py:96
  183.4 0.2 reduce_sum.79
  183.6 0.1 broadcast_in_dim.17
  183.8 19.2 %all_to_all.44 = f32[128,1,430]{2,1,0:T(1,128)S(1)} all-to-all(f32[128,1,430]{2,1,0:T(1,128)S(1)} %broadcast_in_dim.17), channel_id=1, replica_groups=mesh['y'=4,'zh'=2,'core'=2,'cx'=4,'cz'=4] {'y','zh','cx','cz'}, dimensions={0} | all-to-all | bytes 440320 | tf_op jit(solution)/shard_map/all_to_all | solution.py:87
  203.0 0.1 copy.29
  203.1 3.2 %collective-permute-start.4 = (f32[128,430]{0,1:T(8,128)S(1)}, f32[128,430]{0,1:T(8,128)S(1)}, u32[]{:S(2)}, u32[]{:S(2)}) collective-permute-start(f32[128,430]{0,1:T(8,128)S(1)} %bitcast.56), channel_id=1, source_target_pairs={{0,16},{16,0},{1,17},{17,1},{2,18},{18,2},{3,19},{19,3},{4,20},{20... | collective-permute-start | bytes 660488 | tf_op jit(solution)/shard_map/ppermute | solution.py:101
  206.3 0.8 convolution_convert_fusion
  207.1 0.3 collective-permute-done.4
  207.4 0.7 slice_multiply_fusion.1
  208.1 0.5 slice.65
  208.6 0.6 slice_multiply_fusion.2
  209.2 0.8 copy.30
  (15 shorter events, 0.3 us)
Async XLA Ops:
  0.6 0.9 copy-start
  2.5 18.8 %copy-start.8 = (s32[1,1,128]{2,1,0:T(1,128)S(1)}, s32[1,1,128]{2,1,0:T(1,128)}, u32[]{:S(2)}) copy-start(s32[1,1,128]{2,1,0:T(1,128)} %param.18) | copy-start | bytes 1540
  16.7 15.6 %all-to-all-start.1 = ((bf16[4,512,256]{2,1,0:T(8,128)(2,1)}), bf16[4,512,256]{2,1,0:T(8,128)(2,1)S(1)}, u32[]{:S(2)}, u32[]{:S(2)}) async-start(bf16[4,512,256]{2,1,0:T(8,128)(2,1)} %broadcast_in_dim.14), calls=%async_computation.1 | async-start | bytes 2097152 | tf_op jit(solution)/shard_map/all_to_all | solution.py:87
  32.3 1.0 copy-start.1
  41.0 6.8 %collective-permute-start = (f32[1024,256]{1,0:T(8,128)}, f32[1024,256]{1,0:T(8,128)S(1)}, u32[]{:S(2)}, u32[]{:S(2)}) collective-permute-start(f32[1024,256]{1,0:T(8,128)} %get-tuple-element.33), channel_id=1, source_target_pairs={{0,16},{16,0},{1,17},{17,1},{2,18},{18,2},{3,19},{19,3},{4,20},{20... | collective-permute-start | bytes 3145736 | tf_op jit(solution)/shard_map/ppermute | solution.py:101
  47.8 24.7 %copy-start.7 = (f32[256]{0:T(256)S(1)}, f32[256]{0:T(256)}, u32[]{:S(2)}) copy-start(f32[256]{0:T(256)} %param.15) | copy-start | bytes 3076
  47.8 24.8 %copy-start.5 = (bf16[256,172]{0,1:T(8,128)(2,1)S(1)}, bf16[256,172]{0,1:T(8,128)(2,1)}, u32[]{:S(2)}) copy-start(bf16[256,172]{0,1:T(8,128)(2,1)} %param.16) | copy-start | bytes 264196
  47.8 25.0 %copy-start.6 = (s32[128]{0:T(128)S(1)}, s32[128]{0:T(128)}, u32[]{:S(2)}) copy-start(s32[128]{0:T(128)} %param.21) | copy-start | bytes 1540
  50.0 14.5 %all-to-all-start.2 = ((bf16[4,256,256]{2,1,0:T(8,128)(2,1)}), bf16[4,256,256]{2,1,0:T(8,128)(2,1)S(1)}, u32[]{:S(2)}, u32[]{:S(2)}) async-start(bf16[4,256,256]{2,1,0:T(8,128)(2,1)} %bitcast.6), calls=%async_computation.2 | async-start | bytes 1048576 | tf_op jit(solution)/shard_map/all_to_all | solution.py:96
  64.6 7.9 %collective-permute-start.1 = (f32[128,256]{1,0:T(8,128)S(1)}, f32[128,256]{1,0:T(8,128)S(1)}, u32[]{:S(2)}, u32[]{:S(2)}) collective-permute-start(f32[128,256]{1,0:T(8,128)S(1)} %constant_dynamic-slice_fusion), channel_id=1, source_target_pairs={{0,32},{32,0},{1,33},{33,1},{2,34},{34,2},{3,35},{35,3},{4,36},{36... | collective-permute-start | bytes 393224 | tf_op jit(solution)/shard_map/ppermute | solution.py:101
  96.6 4.7 %copy-start.2 = (bf16[8,128,256]{2,1,0:T(8,128)(2,1)}, bf16[8,128,256]{2,1,0:T(8,128)(2,1)S(1)}, u32[]{:S(2)}) copy-start(bf16[8,128,256]{2,1,0:T(8,128)(2,1)S(1)} %all_to_all.41) | copy-start | bytes 1572868
  96.6 4.7 %collective-permute-start.2 = (bf16[1024,256]{1,0:T(8,128)(2,1)S(1)}, bf16[1024,256]{1,0:T(8,128)(2,1)S(1)}, u32[]{:S(2)}, u32[]{:S(2)}) collective-permute-start(bf16[1024,256]{1,0:T(8,128)(2,1)S(1)} %bitcast.52), channel_id=1, source_target_pairs={{0,16},{16,0},{1,17},{17,1},{2,18},{18,2},{3,19},{19,3},{4,20},{20... | collective-permute-start | bytes 1572872 | tf_op jit(solution)/shard_map/ppermute | solution.py:101
  101.3 0.8 copy-start.3
  140.4 18.9 %copy-start.4 = (bf16[128,256]{1,0:T(8,128)(2,1)S(1)}, bf16[128,256]{1,0:T(8,128)(2,1)}, u32[]{:S(2)}) copy-start(bf16[128,256]{1,0:T(8,128)(2,1)} %param.13) | copy-start | bytes 196612
  141.2 18.1 %all-to-all-start.5 = ((f32[4,128,256]{1,2,0:T(8,128)}), f32[4,128,256]{1,2,0:T(8,128)S(1)}, u32[]{:S(2)}, u32[]{:S(2)}) async-start(f32[4,128,256]{1,2,0:T(8,128)} %copy_bitcast_fusion.1), calls=%async_computation.5 | async-start | bytes 1048576 | tf_op jit(solution)/shard_map/all_to_all | solution.py:96
  159.6 2.6 %collective-permute-start.3 = (f32[128,430]{0,1:T(8,128)S(1)}, f32[128,430]{0,1:T(8,128)S(1)}, u32[]{:S(2)}, u32[]{:S(2)}) collective-permute-start(f32[128,430]{0,1:T(8,128)S(1)} %slice_select_fusion), channel_id=1, source_target_pairs={{0,16},{16,0},{1,17},{17,1},{2,18},{18,2},{3,19},{19,3},{4,20},{20... | collective-permute-start | bytes 660488 | tf_op jit(solution)/shard_map/ppermute | solution.py:101
  203.1 4.3 %collective-permute-start.4 = (f32[128,430]{0,1:T(8,128)S(1)}, f32[128,430]{0,1:T(8,128)S(1)}, u32[]{:S(2)}, u32[]{:S(2)}) collective-permute-start(f32[128,430]{0,1:T(8,128)S(1)} %bitcast.56), channel_id=1, source_target_pairs={{0,16},{16,0},{1,17},{17,1},{2,18},{18,2},{3,19},{19,3},{4,20},{20... | collective-permute-start | bytes 660488 | tf_op jit(solution)/shard_map/ppermute | solution.py:101

commit v11 on v9

--- a/solution.py
+++ b/solution.py
@@ -96,6 +96,25 @@
 
 def swap_core(x, axis="core"):
     return lax.ppermute(x, axis, [(0, 1), (1, 0)])
+
+
+def ring_gather(x, axis):
+    n = lax.psum(1, axis)
+    me = lax.axis_index(axis)
+    parts = [x] + [lax.ppermute(x, axis, [(i, (i + k) % n) for i in range(n)]) for k in range(1, n)]
+    stacked = jnp.stack(parts[::-1])
+    return jnp.roll(stacked, me + 1, axis=0).reshape(n * x.shape[0], x.shape[1])
+
+
+def ring_scatter(x, axis):
+    n = lax.psum(1, axis)
+    me = lax.axis_index(axis)
+    size = x.shape[0] // n
+    total = lax.dynamic_slice_in_dim(x, me * size, size, 0)
+    for k in range(1, n):
+        piece = lax.dynamic_slice_in_dim(x, ((me + k) % n) * size, size, 0)
+        total = total + lax.ppermute(piece, axis, [(i, (i + k) % n) for i in range(n)])
+    return total
 
 
 def pair_scatter(x, axis):
@@ -159,7 +178,7 @@
     row_hi = row_ids // 2
     row_pos = jnp.where(row_ids % 2 == lax.axis_index("core"), row_hi, row_hi + row_tiles // 2)
     proj = jnp.dot(features, w_in, preferred_element_type=jnp.float32).astype(jnp.bfloat16)
-    source = gather_rows(gather_rows(proj, "cz"), "cx")
+    source = ring_gather(ring_gather(proj, "cz"), "cx")
     mine, other = tile_product(tile_block, row_pos, col_ids, live_count, (source,), row_tiles, False)
     summed = mine + swap_core(other)
     agg = pair_scatter(scatter_rows(summed, "y"), "zh")
@@ -167,7 +186,7 @@
     gathered = gather_rows(grad_z, ("y", "zh"))
     sources = (gathered, swap_core(gathered))
     back_part = tile_product(tile_block, row_pos, col_ids, live_count, sources, col_tiles, True)
-    grad_proj = scatter_rows(scatter_rows(back_part, "cx"), "cz").astype(jnp.bfloat16)
+    grad_proj = ring_scatter(ring_scatter(back_part, "cx"), "cz").astype(jnp.bfloat16)
     in_term = jnp.einsum("nf,ng->fg", features, grad_proj, preferred_element_type=jnp.float32)
     extra = jnp.zeros((feat, 2), jnp.float32)
     extra = extra.at[:, 0].set(bias_term).at[0, 1].set(loss_sum)

time: 219 us -> 209 us (0.954)
  blocking collectives: 103 us -> 60.4 us
  waiting for transfers between devices: 44.3 us -> 67.7 us
  starting transfers between devices: 33.2 us -> 42.9 us
    ppermute x0 -> x12, waiting for transfers between devices: none -> 44.6 us  [the longest x6 26.5 us: ring_scatter(): lax.ppermute(piece, axis, [(i, (i + k) % n) for i in range(n)])]
    all_to_all x2 -> x1, blocking collectives: 52.4 us -> 23.3 us  [scatter_rows(): got = lax.all_to_all(x.reshape(n, -1, x.shape[1]), axis, 0, 0, tiled=False)]
    ppermute x0 -> x12, starting transfers between devices: none -> 21.4 us  [the longest x6 13.2 us: ring_scatter(): lax.ppermute(piece, axis, [(i, (i + k) % n) for i in range(n)])]
    all_to_all x3 -> x2, blocking collectives: 50.6 us -> 37.1 us  [gather_rows(): got = lax.all_to_all(spread, axis, 0, 0, tiled=False)]
    all_to_all x2 -> x1, waiting for transfers between devices: 25.6 us -> 14.5 us  [scatter_rows(): got = lax.all_to_all(x.reshape(n, -1, x.shape[1]), axis, 0, 0, tiled=False)]
    all_to_all x1 -> x0, waiting for transfers between devices: 10.4 us -> none  [gather_rows(): got = lax.all_to_all(spread, axis, 0, 0, tiled=False)]
    all_to_all x2 -> x1, starting transfers between devices: 9.76 us -> 5.46 us  [scatter_rows(): got = lax.all_to_all(x.reshape(n, -1, x.shape[1]), axis, 0, 0, tiled=False)]
    all_to_all x1 -> x0, starting transfers between devices: 4.01 us -> none  [gather_rows(): got = lax.all_to_all(spread, axis, 0, 0, tiled=False)]
  transfers between devices with their start and end apart: 8 -> 18, of which waited for: 8 -> 15; matrix products, arithmetic and copies ran while one was open for 2% -> 2% of each run, Pallas kernels for 0% -> 0%
where the time goes in v11:
time: 209 us
  waiting for transfers between devices  67.7 us (32%)
  blocking collectives  60.4 us (29%)
  starting transfers between devices  42.9 us (21%)
  Pallas kernels  15.3 us (7%)
  local copies, waits for them, and re-layouts  9.54 us (5%)
  other arithmetic  7.28 us (3%)
  between operations  3.37 us (2%)
  matrix products  2.57 us (1%)
    all_to_all x2, blocking collectives, gather_rows(): got = lax.all_to_all(spread, axis, 0, 0, tiled=False)  37.1 us
    ppermute x6, waiting for transfers between devices, ring_scatter(): lax.ppermute(piece, axis, [(i, (i + k) % n) for i in range(n)])  26.5 us
    all_to_all x1, blocking collectives, scatter_rows(): got = lax.all_to_all(x.reshape(n, -1, x.shape[1]), axis, 0, 0, tiled=False)  23.3 us
    ppermute x6, waiting for transfers between devices, ring_gather(): lax.ppermute(x, axis, [(i, (i + k) % n) for i in range(n)])  18.1 us
    ppermute x5, starting transfers between devices, swap_core(): return lax.ppermute(x, axis, [(0, 1), (1, 0)])  16 us
    pallas_call x2, Pallas kernels, tile_product(): pl.pallas_call(lambda *refs: _dense_kernel(transpose, *refs), grid_spec=g...  15.3 us
    all_to_all x1, waiting for transfers between devices, scatter_rows(): got = lax.all_to_all(x.reshape(n, -1, x.shape[1]), axis, 0, 0, tiled=False)  14.5 us
    ppermute x6, starting transfers between devices, ring_scatter(): lax.ppermute(piece, axis, [(i, (i + k) % n) for i in range(n)])  13.2 us
  transfers between devices with their start and end apart: 18, of which 15 were waited for; matrix products, arithmetic and copies ran while one was open for 2% of the time, Pallas kernels for 0%

profile of v11, /device:TPU:1, one launch (start us, length us, event | category | flops | bytes accessed | tf_op | source)
XLA Modules:
  0.0 209.0 jit_solution(284029803258608435)
XLA Ops:
  0.6 0.9 copy-done
  1.5 1.0 convolution_convert_fusion.1
  2.5 5.2 %collective-permute-start = (bf16[128,256]{1,0:T(8,128)(2,1)S(1)}, bf16[128,256]{1,0:T(8,128)(2,1)S(1)}, u32[]{:S(2)}, u32[]{:S(2)}) collective-permute-start(bf16[128,256]{1,0:T(8,128)(2,1)S(1)} %convolution_convert_fusion.1), channel_id=1, source_target_pairs={{0,3},{1,0},{2,1},{3,2},{4,7},{5,4},{6,5},{7,6},{8,11},{9,8},{10,9... | collective-permute-start | bytes 196616 | tf_op jit(solution)/shard_map/ppermute | solution.py:104
  7.8 0.4 collective-permute-start.2
  8.2 0.9 collective-permute-done
  9.1 5.5 %collective-permute-done.1 = bf16[128,256]{1,0:T(8,128)(2,1)S(1)} collective-permute-done((bf16[128,256]{1,0:T(8,128)(2,1)S(1)}, bf16[128,256]{1,0:T(8,128)(2,1)S(1)}, u32[]{:S(2)}, u32[]{:S(2)}) %collective-permute-start.1) | collective-permute-done | bytes 65568 | tf_op jit(solution)/shard_map/ppermute | solution.py:104
  14.8 1.4 collective-permute-start.3
  16.2 0.5 collective-permute-start.4
  16.7 1.2 compare_select_fusion.refs_0_
  18.5 0.7 collective-permute-start.5
  19.2 2.8 %collective-permute-done.3 = bf16[512,256]{1,0:T(8,128)(2,1)S(1)} collective-permute-done((bf16[512,256]{1,0:T(8,128)(2,1)S(1)}, bf16[512,256]{1,0:T(8,128)(2,1)S(1)}, u32[]{:S(2)}, u32[]{:S(2)}) %collective-permute-start.3) | collective-permute-done | bytes 262176 | tf_op jit(solution)/shard_map/ppermute | solution.py:104
  22.1 1.6 collective-permute-done.4
  23.7 7.2 %collective-permute-done.5 = bf16[512,256]{1,0:T(8,128)(2,1)S(1)} collective-permute-done((bf16[512,256]{1,0:T(8,128)(2,1)S(1)}, bf16[512,256]{1,0:T(8,128)(2,1)S(1)}, u32[]{:S(2)}, u32[]{:S(2)}) %collective-permute-start.5) | collective-permute-done | bytes 262176 | tf_op jit(solution)/shard_map/ppermute | solution.py:104
  31.1 1.1 constant_dynamic-slice_fusion.4
  32.2 0.6 broadcast_in_dim.6.refs_5_
  32.8 7.6 %shard_map.128 = (f32[1024,256]{1,0:T(8,128)}, f32[1024,256]{1,0:T(8,128)}) custom-call(s32[128]{0:T(128)} %compare_select_fusion.refs_0_, s32[128]{0:T(128)} %bitcast.88, s32[1]{0:T(128)} %bitcast.74.refs_2_, bf16[128,128,128]{2,1,0:T(8,128)(2,1)} %bitcast.76, bf16[2048,256]{1,0:T(8,128)(2,1)} %bitcast.78, bf16[8,128]{1,0:T(8,128)(2,1)} %broadcast_in_dim.6.refs_5_), custom_call_target="tpu_custom_call" | custom-call | tf_op jit(solution)/shard_map/pallas_call | solution.py:73
  40.4 1.0 collective-permute-start.6
  41.4 2.5 %collective-permute-done.6 = f32[1024,256]{1,0:T(8,128)S(1)} collective-permute-done((f32[1024,256]{1,0:T(8,128)}, f32[1024,256]{1,0:T(8,128)S(1)}, u32[]{:S(2)}, u32[]{:S(2)}) %collective-permute-start.6) | collective-permute-done | bytes 1048608 | tf_op jit(solution)/shard_map/ppermute | solution.py:98
  43.9 2.4 %add.160 = f32[1024,256]{1,0:T(8,128)} add(f32[1024,256]{1,0:T(8,128)} %get-tuple-element.32, f32[1024,256]{1,0:T(8,128)S(1)} %collective-permute-done.6) | non-fusion elementwise | flops 262144 | bytes 3145728 | tf_op jit(solution)/shard_map/add | solution.py:183
  46.3 5.5 %all-to-all-start = ((f32[4,256,256]{2,1,0:T(8,128)}), f32[4,256,256]{2,1,0:T(8,128)S(1)}, u32[]{:S(2)}, u32[]{:S(2)}) async-start(f32[4,256,256]{2,1,0:T(8,128)} %bitcast.14), calls=%async_computation | async-start | bytes 2097152 | tf_op jit(solution)/shard_map/all_to_all | solution.py:93
  51.7 14.5 %all-to-all-done = f32[4,256,256]{2,1,0:T(8,128)S(1)} async-done(((f32[4,256,256]{2,1,0:T(8,128)}), f32[4,256,256]{2,1,0:T(8,128)S(1)}, u32[]{:S(2)}, u32[]{:S(2)}) %all-to-all-start) | async-done | bytes 1048608 | tf_op jit(solution)/shard_map/all_to_all | solution.py:93
  66.3 0.1 reduce_sum.54
  66.4 4.8 %collective-permute-start.7 = (f32[128,256]{1,0:T(8,128)S(1)}, f32[128,256]{1,0:T(8,128)S(1)}, u32[]{:S(2)}, u32[]{:S(2)}) collective-permute-start(f32[128,256]{1,0:T(8,128)S(1)} %constant_dynamic-slice_fusion.3), channel_id=1, source_target_pairs={{0,32},{32,0},{1,33},{33,1},{2,34},{34,2},{3,35},{35,3},{4,36},{36... | collective-permute-start | bytes 393224 | tf_op jit(solution)/shard_map/ppermute | solution.py:98
  71.2 3.1 %collective-permute-done.7 = f32[128,256]{1,0:T(8,128)S(1)} collective-permute-done((f32[128,256]{1,0:T(8,128)S(1)}, f32[128,256]{1,0:T(8,128)S(1)}, u32[]{:S(2)}, u32[]{:S(2)}) %collective-permute-start.7) | collective-permute-done | bytes 131104 | tf_op jit(solution)/shard_map/ppermute | solution.py:98
  74.4 0.2 fusion.4
  74.6 0.6 subtract_reduce_fusion
  75.2 0.2 convert_reduce_fusion
  75.5 17.9 %all_to_all.20 = bf16[8,128,256]{2,1,0:T(8,128)(2,1)S(1)} all-to-all(bf16[8,128,256]{2,1,0:T(8,128)(2,1)S(1)} %broadcast_in_dim.7), channel_id=1, replica_groups=mesh['y'=4,'zh'=2,'core'=2,'cx'=4,'cz'=4] {'y','zh'}, dimensions={0} | all-to-all | bytes 1048576 | tf_op jit(solution)/shard_map/all_to_all | solution.py:87
  93.4 4.5 %collective-permute-start.8 = (bf16[1024,256]{1,0:T(8,128)(2,1)S(1)}, bf16[1024,256]{1,0:T(8,128)(2,1)S(1)}, u32[]{:S(2)}, u32[]{:S(2)}) collective-permute-start(bf16[1024,256]{1,0:T(8,128)(2,1)S(1)} %bitcast.84), channel_id=1, source_target_pairs={{0,16},{16,0},{1,17},{17,1},{2,18},{18,2},{3,19},{19,3},{4,20},{20... | collective-permute-start | bytes 1572872 | tf_op jit(solution)/shard_map/ppermute | solution.py:98
  97.9 1.5 collective-permute-done.8.refs_5_
  99.5 0.8 copy-done.2
  100.3 7.7 %shard_map.129 = (f32[256,2048]{1,0:T(8,128)}, f32[8,128]{1,0:T(8,128)}) custom-call(s32[128]{0:T(128)} %compare_select_fusion.refs_0_, s32[128]{0:T(128)} %bitcast.89, s32[1]{0:T(128)} %bitcast.75.refs_2_, bf16[128,128,128]{2,1,0:T(8,128)(2,1)} %bitcast.77, bf16[1024,256]{1,0:T(8,128)(2,1)} %bitcast.85, bf16[1024,256]{1,0:T(8,128)(2,1)} %copy-done.2), custom_call_target="tpu_custom_call" | custom-call | tf_op jit(solution)/shard_map/pallas_call | solution.py:73
  107.9 1.5 dynamic-slice_bitcast_fusion.2
  109.4 0.8 collective-permute-start.10
  110.2 1.1 collective-permute-start.11
  111.3 0.5 collective-permute-start.9
  111.8 0.6 fusion.3
  112.3 2.0 scatter.9
  114.3 9.9 %collective-permute-done.10 = f32[512,256]{0,1:T(8,128)S(1)} collective-permute-done((f32[512,256]{0,1:T(8,128)S(1)}, f32[512,256]{0,1:T(8,128)S(1)}, u32[]{:S(2)}, u32[]{:S(2)}) %collective-permute-start.10) | collective-permute-done | bytes 524320 | tf_op jit(solution)/shard_map/ppermute | solution.py:116
  124.2 10.7 %collective-permute-done.11 = f32[512,256]{0,1:T(8,128)S(1)} collective-permute-done((f32[512,256]{0,1:T(8,128)S(1)}, f32[512,256]{0,1:T(8,128)S(1)}, u32[]{:S(2)}, u32[]{:S(2)}) %collective-permute-start.11) | collective-permute-done | bytes 524320 | tf_op jit(solution)/shard_map/ppermute | solution.py:116
  134.9 1.1 collective-permute-done.9
  136.1 1.3 fusion.1
  137.3 0.1 constant_dynamic-slice_fusion.2
  137.4 7.6 %collective-permute-start.12 = (f32[128,256]{0,1:T(8,128)S(1)}, f32[128,256]{0,1:T(8,128)S(1)}, u32[]{:S(2)}, u32[]{:S(2)}) collective-permute-start(f32[128,256]{0,1:T(8,128)S(1)} %get-tuple-element.57), channel_id=1, source_target_pairs={{0,1},{1,2},{2,3},{3,0},{4,5},{5,6},{6,7},{7,4},{8,9},{9,10},{10,1... | collective-permute-start | bytes 393224 | tf_op jit(solution)/shard_map/ppermute | solution.py:116
  145.0 0.9 collective-permute-start.13
  146.0 2.3 %collective-permute-start.14 = (f32[128,256]{0,1:T(8,128)S(1)}, f32[128,256]{0,1:T(8,128)S(1)}, u32[]{:S(2)}, u32[]{:S(2)}) collective-permute-start(f32[128,256]{0,1:T(8,128)S(1)} %get-tuple-element.58), channel_id=1, source_target_pairs={{0,3},{1,0},{2,1},{3,2},{4,7},{5,4},{6,5},{7,6},{8,11},{9,8},{10,9... | collective-permute-start | bytes 393224 | tf_op jit(solution)/shard_map/ppermute | solution.py:116
  148.2 0.2 fusion.2
  148.4 4.7 %collective-permute-done.13 = f32[128,256]{0,1:T(8,128)S(1)} collective-permute-done((f32[128,256]{0,1:T(8,128)S(1)}, f32[128,256]{0,1:T(8,128)S(1)}, u32[]{:S(2)}, u32[]{:S(2)}) %collective-permute-start.13) | collective-permute-done | bytes 131104 | tf_op jit(solution)/shard_map/ppermute | solution.py:116
  153.2 0.2 convolution_bitcast_fusion
  153.4 2.5 %collective-permute-start.15 = (f32[128,430]{0,1:T(8,128)S(1)}, f32[128,430]{0,1:T(8,128)S(1)}, u32[]{:S(2)}, u32[]{:S(2)}) collective-permute-start(f32[128,430]{0,1:T(8,128)S(1)} %slice_select_fusion), channel_id=1, source_target_pairs={{0,16},{16,0},{1,17},{17,1},{2,18},{18,2},{3,19},{19,3},{4,20},{20... | collective-permute-start | bytes 660488 | tf_op jit(solution)/shard_map/ppermute | solution.py:98
  156.0 1.1 collective-permute-done.15
  157.1 0.1 copy.17
  157.3 23.3 %all_to_all.21 = f32[128,1,430]{2,1,0:T(1,128)S(1)} all-to-all(f32[128,1,430]{2,1,0:T(1,128)S(1)} %copy.17), channel_id=1, replica_groups=mesh['y'=4,'zh'=2,'core'=2,'cx'=4,'cz'=4] {'y','zh','cx','cz'}, dimensions={0} | all-to-all | bytes 440320 | tf_op jit(solution)/shard_map/all_to_all | solution.py:93
  180.6 0.2 reduce_sum.59
  180.8 0.1 broadcast_in_dim.8
  180.9 19.2 %all_to_all.22 = f32[128,1,430]{2,1,0:T(1,128)S(1)} all-to-all(f32[128,1,430]{2,1,0:T(1,128)S(1)} %broadcast_in_dim.8), channel_id=1, replica_groups=mesh['y'=4,'zh'=2,'core'=2,'cx'=4,'cz'=4] {'y','zh','cx','cz'}, dimensions={0} | all-to-all | bytes 440320 | tf_op jit(solution)/shard_map/all_to_all | solution.py:87
  200.1 0.1 copy.18
  200.2 3.2 %collective-permute-start.16 = (f32[128,430]{0,1:T(8,128)S(1)}, f32[128,430]{0,1:T(8,128)S(1)}, u32[]{:S(2)}, u32[]{:S(2)}) collective-permute-start(f32[128,430]{0,1:T(8,128)S(1)} %bitcast.86), channel_id=1, source_target_pairs={{0,16},{16,0},{1,17},{17,1},{2,18},{18,2},{3,19},{19,3},{4,20},{20... | collective-permute-start | bytes 660488 | tf_op jit(solution)/shard_map/ppermute | solution.py:98
  203.4 0.8 convolution_convert_fusion
  204.2 0.3 collective-permute-done.16
  204.6 0.7 slice_multiply_fusion.1
  205.3 0.5 slice.65
  205.8 0.6 slice_multiply_fusion.2
  206.3 0.8 copy.19
  (45 shorter events, 0.7 us)
Async XLA Ops:
  0.6 0.9 copy-start
  2.5 6.6 %collective-permute-start = (bf16[128,256]{1,0:T(8,128)(2,1)S(1)}, bf16[128,256]{1,0:T(8,128)(2,1)S(1)}, u32[]{:S(2)}, u32[]{:S(2)}) collective-permute-start(bf16[128,256]{1,0:T(8,128)(2,1)S(1)} %convolution_convert_fusion.1), channel_id=1, source_target_pairs={{0,3},{1,0},{2,1},{3,2},{4,7},{5,4},{6,5},{7,6},{8,11},{9,8},{10,9... | collective-permute-start | bytes 196616 | tf_op jit(solution)/shard_map/ppermute | solution.py:104
  7.8 6.8 %collective-permute-start.1 = (bf16[128,256]{1,0:T(8,128)(2,1)S(1)}, bf16[128,256]{1,0:T(8,128)(2,1)S(1)}, u32[]{:S(2)}, u32[]{:S(2)}) collective-permute-start(bf16[128,256]{1,0:T(8,128)(2,1)S(1)} %convolution_convert_fusion.1), channel_id=1, source_target_pairs={{0,2},{1,3},{2,0},{3,1},{4,6},{5,7},{6,4},{7,5},{8,10},{9,11},{10,... | collective-permute-start | bytes 196616 | tf_op jit(solution)/shard_map/ppermute | solution.py:104
  7.8 6.8 %collective-permute-start.2 = (bf16[128,256]{1,0:T(8,128)(2,1)S(1)}, bf16[128,256]{1,0:T(8,128)(2,1)S(1)}, u32[]{:S(2)}, u32[]{:S(2)}) collective-permute-start(bf16[128,256]{1,0:T(8,128)(2,1)S(1)} %convolution_convert_fusion.1), channel_id=1, source_target_pairs={{0,1},{1,2},{2,3},{3,0},{4,5},{5,6},{6,7},{7,4},{8,9},{9,10},{10,1... | collective-permute-start | bytes 196616 | tf_op jit(solution)/shard_map/ppermute | solution.py:104
  14.8 7.3 %collective-permute-start.3 = (bf16[512,256]{1,0:T(8,128)(2,1)S(1)}, bf16[512,256]{1,0:T(8,128)(2,1)S(1)}, u32[]{:S(2)}, u32[]{:S(2)}) collective-permute-start(bf16[512,256]{1,0:T(8,128)(2,1)S(1)} %bitcast.79), channel_id=1, source_target_pairs={{0,12},{4,0},{8,4},{12,8},{1,13},{5,1},{9,5},{13,9},{2,14},{6,2},{... | collective-permute-start | bytes 786440 | tf_op jit(solution)/shard_map/ppermute | solution.py:104
  16.2 7.5 %collective-permute-start.4 = (bf16[512,256]{1,0:T(8,128)(2,1)S(1)}, bf16[512,256]{1,0:T(8,128)(2,1)S(1)}, u32[]{:S(2)}, u32[]{:S(2)}) collective-permute-start(bf16[512,256]{1,0:T(8,128)(2,1)S(1)} %bitcast.80), channel_id=1, source_target_pairs={{0,8},{4,12},{8,0},{12,4},{1,9},{5,13},{9,1},{13,5},{2,10},{6,14},... | collective-permute-start | bytes 786440 | tf_op jit(solution)/shard_map/ppermute | solution.py:104
  18.5 12.4 %collective-permute-start.5 = (bf16[512,256]{1,0:T(8,128)(2,1)S(1)}, bf16[512,256]{1,0:T(8,128)(2,1)S(1)}, u32[]{:S(2)}, u32[]{:S(2)}) collective-permute-start(bf16[512,256]{1,0:T(8,128)(2,1)S(1)} %bitcast.81), channel_id=1, source_target_pairs={{0,4},{4,8},{8,12},{12,0},{1,5},{5,9},{9,13},{13,1},{2,6},{6,10},{... | collective-permute-start | bytes 786440 | tf_op jit(solution)/shard_map/ppermute | solution.py:104
  40.4 3.5 %collective-permute-start.6 = (f32[1024,256]{1,0:T(8,128)}, f32[1024,256]{1,0:T(8,128)S(1)}, u32[]{:S(2)}, u32[]{:S(2)}) collective-permute-start(f32[1024,256]{1,0:T(8,128)} %get-tuple-element.33), channel_id=1, source_target_pairs={{0,16},{16,0},{1,17},{17,1},{2,18},{18,2},{3,19},{19,3},{4,20},{20... | collective-permute-start | bytes 3145736 | tf_op jit(solution)/shard_map/ppermute | solution.py:98
  46.3 28.0 %copy-start.6 = (f32[256]{0:T(256)S(1)}, f32[256]{0:T(256)}, u32[]{:S(2)}) copy-start(f32[256]{0:T(256)} %param.15) | copy-start | bytes 3076
  46.3 28.1 %copy-start.4 = (bf16[256,172]{0,1:T(8,128)(2,1)S(1)}, bf16[256,172]{0,1:T(8,128)(2,1)}, u32[]{:S(2)}) copy-start(bf16[256,172]{0,1:T(8,128)(2,1)} %param.16) | copy-start | bytes 264196
  46.3 28.3 %copy-start.5 = (s32[128]{0:T(128)S(1)}, s32[128]{0:T(128)}, u32[]{:S(2)}) copy-start(s32[128]{0:T(128)} %param.21) | copy-start | bytes 1540
  46.3 20.0 %all-to-all-start = ((f32[4,256,256]{2,1,0:T(8,128)}), f32[4,256,256]{2,1,0:T(8,128)S(1)}, u32[]{:S(2)}, u32[]{:S(2)}) async-start(f32[4,256,256]{2,1,0:T(8,128)} %bitcast.14), calls=%async_computation | async-start | bytes 2097152 | tf_op jit(solution)/shard_map/all_to_all | solution.py:93
  66.4 7.9 %collective-permute-start.7 = (f32[128,256]{1,0:T(8,128)S(1)}, f32[128,256]{1,0:T(8,128)S(1)}, u32[]{:S(2)}, u32[]{:S(2)}) collective-permute-start(f32[128,256]{1,0:T(8,128)S(1)} %constant_dynamic-slice_fusion.3), channel_id=1, source_target_pairs={{0,32},{32,0},{1,33},{33,1},{2,34},{34,2},{3,35},{35,3},{4,36},{36... | collective-permute-start | bytes 393224 | tf_op jit(solution)/shard_map/ppermute | solution.py:98
  93.4 6.0 %copy-start.1 = (bf16[8,128,256]{2,1,0:T(8,128)(2,1)}, bf16[8,128,256]{2,1,0:T(8,128)(2,1)S(1)}, u32[]{:S(2)}) copy-start(bf16[8,128,256]{2,1,0:T(8,128)(2,1)S(1)} %all_to_all.20) | copy-start | bytes 1572868
  93.4 6.0 %collective-permute-start.8 = (bf16[1024,256]{1,0:T(8,128)(2,1)S(1)}, bf16[1024,256]{1,0:T(8,128)(2,1)S(1)}, u32[]{:S(2)}, u32[]{:S(2)}) collective-permute-start(bf16[1024,256]{1,0:T(8,128)(2,1)S(1)} %bitcast.84), channel_id=1, source_target_pairs={{0,16},{16,0},{1,17},{17,1},{2,18},{18,2},{3,19},{19,3},{4,20},{20... | collective-permute-start | bytes 1572872 | tf_op jit(solution)/shard_map/ppermute | solution.py:98
  99.5 0.8 copy-start.2
  109.4 14.8 %collective-permute-start.10 = (f32[512,256]{0,1:T(8,128)S(1)}, f32[512,256]{0,1:T(8,128)S(1)}, u32[]{:S(2)}, u32[]{:S(2)}) collective-permute-start(f32[512,256]{0,1:T(8,128)S(1)} %get-tuple-element.56), channel_id=1, source_target_pairs={{0,8},{4,12},{8,0},{12,4},{1,9},{5,13},{9,1},{13,5},{2,10},{6,14},... | collective-permute-start | bytes 1572872 | tf_op jit(solution)/shard_map/ppermute | solution.py:116
  110.2 24.8 %collective-permute-start.11 = (f32[512,256]{0,1:T(8,128)S(1)}, f32[512,256]{0,1:T(8,128)S(1)}, u32[]{:S(2)}, u32[]{:S(2)}) collective-permute-start(f32[512,256]{0,1:T(8,128)S(1)} %get-tuple-element.55), channel_id=1, source_target_pairs={{0,12},{4,0},{8,4},{12,8},{1,13},{5,1},{9,5},{13,9},{2,14},{6,2},{... | collective-permute-start | bytes 1572872 | tf_op jit(solution)/shard_map/ppermute | solution.py:116
  111.3 24.8 %collective-permute-start.9 = (f32[512,256]{0,1:T(8,128)S(1)}, f32[512,256]{0,1:T(8,128)S(1)}, u32[]{:S(2)}, u32[]{:S(2)}) collective-permute-start(f32[512,256]{0,1:T(8,128)S(1)} %get-tuple-element.54), channel_id=1, source_target_pairs={{0,4},{4,8},{8,12},{12,0},{1,5},{5,9},{9,13},{13,1},{2,6},{6,10},{... | collective-permute-start | bytes 1572872 | tf_op jit(solution)/shard_map/ppermute | solution.py:116
  114.3 38.9 %copy-start.3 = (bf16[128,256]{1,0:T(8,128)(2,1)S(1)}, bf16[128,256]{1,0:T(8,128)(2,1)}, u32[]{:S(2)}) copy-start(bf16[128,256]{1,0:T(8,128)(2,1)} %param.13) | copy-start | bytes 196612
  137.4 11.0 %collective-permute-start.12 = (f32[128,256]{0,1:T(8,128)S(1)}, f32[128,256]{0,1:T(8,128)S(1)}, u32[]{:S(2)}, u32[]{:S(2)}) collective-permute-start(f32[128,256]{0,1:T(8,128)S(1)} %get-tuple-element.57), channel_id=1, source_target_pairs={{0,1},{1,2},{2,3},{3,0},{4,5},{5,6},{6,7},{7,4},{8,9},{9,10},{10,1... | collective-permute-start | bytes 393224 | tf_op jit(solution)/shard_map/ppermute | solution.py:116
  145.0 8.1 %collective-permute-start.13 = (f32[128,256]{0,1:T(8,128)S(1)}, f32[128,256]{0,1:T(8,128)S(1)}, u32[]{:S(2)}, u32[]{:S(2)}) collective-permute-start(f32[128,256]{0,1:T(8,128)S(1)} %get-tuple-element.59), channel_id=1, source_target_pairs={{0,2},{1,3},{2,0},{3,1},{4,6},{5,7},{6,4},{7,5},{8,10},{9,11},{10,... | collective-permute-start | bytes 393224 | tf_op jit(solution)/shard_map/ppermute | solution.py:116
  146.0 7.2 %collective-permute-start.14 = (f32[128,256]{0,1:T(8,128)S(1)}, f32[128,256]{0,1:T(8,128)S(1)}, u32[]{:S(2)}, u32[]{:S(2)}) collective-permute-start(f32[128,256]{0,1:T(8,128)S(1)} %get-tuple-element.58), channel_id=1, source_target_pairs={{0,3},{1,0},{2,1},{3,2},{4,7},{5,4},{6,5},{7,6},{8,11},{9,8},{10,9... | collective-permute-start | bytes 393224 | tf_op jit(solution)/shard_map/ppermute | solution.py:116
  153.4 3.6 %collective-permute-start.15 = (f32[128,430]{0,1:T(8,128)S(1)}, f32[128,430]{0,1:T(8,128)S(1)}, u32[]{:S(2)}, u32[]{:S(2)}) collective-permute-start(f32[128,430]{0,1:T(8,128)S(1)} %slice_select_fusion), channel_id=1, source_target_pairs={{0,16},{16,0},{1,17},{17,1},{2,18},{18,2},{3,19},{19,3},{4,20},{20... | collective-permute-start | bytes 660488 | tf_op jit(solution)/shard_map/ppermute | solution.py:98
  200.2 4.3 %collective-permute-start.16 = (f32[128,430]{0,1:T(8,128)S(1)}, f32[128,430]{0,1:T(8,128)S(1)}, u32[]{:S(2)}, u32[]{:S(2)}) collective-permute-start(f32[128,430]{0,1:T(8,128)S(1)} %bitcast.86), channel_id=1, source_target_pairs={{0,16},{16,0},{1,17},{17,1},{2,18},{18,2},{3,19},{19,3},{4,20},{20... | collective-permute-start | bytes 660488 | tf_op jit(solution)/shard_map/ppermute | solution.py:98

commit v12 on v11

--- a/solution.py
+++ b/solution.py
@@ -181,9 +181,9 @@
     source = ring_gather(ring_gather(proj, "cz"), "cx")
     mine, other = tile_product(tile_block, row_pos, col_ids, live_count, (source,), row_tiles, False)
     summed = mine + swap_core(other)
-    agg = pair_scatter(scatter_rows(summed, "y"), "zh")
+    agg = pair_scatter(ring_scatter(summed, "y"), "zh")
     loss_sum, out_term, bias_term, grad_z = head_block(agg, bias, w_out, labels)
-    gathered = gather_rows(grad_z, ("y", "zh"))
+    gathered = ring_gather(ring_gather(grad_z, "zh"), "y")
     sources = (gathered, swap_core(gathered))
     back_part = tile_product(tile_block, row_pos, col_ids, live_count, sources, col_tiles, True)
     grad_proj = ring_scatter(ring_scatter(back_part, "cx"), "cz").astype(jnp.bfloat16)

time: 209 us -> 206 us (0.986)
  blocking collectives: 60.4 us -> 46.7 us
  waiting for transfers between devices: 67.7 us -> 73.7 us
  starting transfers between devices: 42.9 us -> 45 us
    all_to_all x2 -> x1, blocking collectives: 37.1 us -> 19.2 us  [gather_rows(): got = lax.all_to_all(spread, axis, 0, 0, tiled=False)]
    all_to_all x1 -> x0, waiting for transfers between devices: 14.5 us -> none  [scatter_rows(): got = lax.all_to_all(x.reshape(n, -1, x.shape[1]), axis, 0, 0, tiled=False)]
    ppermute x6 -> x9, waiting for transfers between devices: 26.5 us -> 38.2 us  [ring_scatter(): lax.ppermute(piece, axis, [(i, (i + k) % n) for i in range(n)])]
    ppermute x6 -> x10, waiting for transfers between devices: 18.1 us -> 27 us  [ring_gather(): lax.ppermute(x, axis, [(i, (i + k) % n) for i in range(n)])]
    ppermute x6 -> x10, starting transfers between devices: 8.25 us -> 16.8 us  [ring_gather(): lax.ppermute(x, axis, [(i, (i + k) % n) for i in range(n)])]
    all_to_all x1 -> x0, starting transfers between devices: 5.46 us -> none  [scatter_rows(): got = lax.all_to_all(x.reshape(n, -1, x.shape[1]), axis, 0, 0, tiled=False)]
    all_to_all x1, blocking collectives: 23.3 us -> 27.6 us  [scatter_rows(): got = lax.all_to_all(x.reshape(n, -1, x.shape[1]), axis, 0, 0, tiled=False)]
    ppermute x5, starting transfers between devices: 16 us -> 13.8 us  [swap_core(): return lax.ppermute(x, axis, [(0, 1), (1, 0)])]
  transfers between devices with their start and end apart: 18 -> 24, of which waited for: 15 -> 20; matrix products, arithmetic and copies ran while one was open for 2% -> 2% of each run, Pallas kernels for 0% -> 0%
where the time goes in v12:
time: 206 us; the launch traced here: 205 us
  waiting for transfers between devices  73.7 us (36%)
  blocking collectives  46.7 us (23%)
  starting transfers between devices  45 us (22%)
  Pallas kernels  17.3 us (8%)
  local copies, waits for them, and re-layouts  9.69 us (5%)
  other arithmetic  6.37 us (3%)
  between operations  3.47 us (2%)
  matrix products  2.56 us (1%)
    ppermute x9, waiting for transfers between devices, ring_scatter(): lax.ppermute(piece, axis, [(i, (i + k) % n) for i in range(n)])  38.2 us
    all_to_all x1, blocking collectives, scatter_rows(): got = lax.all_to_all(x.reshape(n, -1, x.shape[1]), axis, 0, 0, tiled=False)  27.6 us
    ppermute x10, waiting for transfers between devices, ring_gather(): lax.ppermute(x, axis, [(i, (i + k) % n) for i in range(n)])  27 us
    all_to_all x1, blocking collectives, gather_rows(): got = lax.all_to_all(spread, axis, 0, 0, tiled=False)  19.2 us
    pallas_call x2, Pallas kernels, tile_product(): pl.pallas_call(lambda *refs: _dense_kernel(transpose, *refs), grid_spec=g...  17.3 us
    ppermute x10, starting transfers between devices, ring_gather(): lax.ppermute(x, axis, [(i, (i + k) % n) for i in range(n)])  16.8 us
    ppermute x9, starting transfers between devices, ring_scatter(): lax.ppermute(piece, axis, [(i, (i + k) % n) for i in range(n)])  14.4 us
    ppermute x5, starting transfers between devices, swap_core(): return lax.ppermute(x, axis, [(0, 1), (1, 0)])  13.8 us
  transfers between devices with their start and end apart: 24, of which 20 were waited for; matrix products, arithmetic and copies ran while one was open for 2% of the time, Pallas kernels for 0%

profile of v12, /device:TPU:1, one launch (start us, length us, event | category | flops | bytes accessed | tf_op | source)
XLA Modules:
  0.0 204.9 jit_solution(5998988861334155317)
XLA Ops:
  0.6 0.9 copy-done
  1.5 1.0 convolution_convert_fusion.1
  2.5 5.2 %collective-permute-start = (bf16[128,256]{1,0:T(8,128)(2,1)S(1)}, bf16[128,256]{1,0:T(8,128)(2,1)S(1)}, u32[]{:S(2)}, u32[]{:S(2)}) collective-permute-start(bf16[128,256]{1,0:T(8,128)(2,1)S(1)} %convolution_convert_fusion.1), channel_id=1, source_target_pairs={{0,3},{1,0},{2,1},{3,2},{4,7},{5,4},{6,5},{7,6},{8,11},{9,8},{10,9... | collective-permute-start | bytes 196616 | tf_op jit(solution)/shard_map/ppermute | solution.py:104
  7.8 0.4 collective-permute-start.2
  8.2 0.9 collective-permute-done
  9.1 5.5 %collective-permute-done.1 = bf16[128,256]{1,0:T(8,128)(2,1)S(1)} collective-permute-done((bf16[128,256]{1,0:T(8,128)(2,1)S(1)}, bf16[128,256]{1,0:T(8,128)(2,1)S(1)}, u32[]{:S(2)}, u32[]{:S(2)}) %collective-permute-start.1) | collective-permute-done | bytes 65568 | tf_op jit(solution)/shard_map/ppermute | solution.py:104
  14.8 1.4 collective-permute-start.3
  16.2 0.5 collective-permute-start.4
  16.7 1.2 compare_select_fusion.refs_0_
  18.5 0.7 collective-permute-start.5
  19.2 2.8 %collective-permute-done.3 = bf16[512,256]{1,0:T(8,128)(2,1)S(1)} collective-permute-done((bf16[512,256]{1,0:T(8,128)(2,1)S(1)}, bf16[512,256]{1,0:T(8,128)(2,1)S(1)}, u32[]{:S(2)}, u32[]{:S(2)}) %collective-permute-start.3) | collective-permute-done | bytes 262176 | tf_op jit(solution)/shard_map/ppermute | solution.py:104
  22.1 1.6 collective-permute-done.4
  23.7 7.2 %collective-permute-done.5 = bf16[512,256]{1,0:T(8,128)(2,1)S(1)} collective-permute-done((bf16[512,256]{1,0:T(8,128)(2,1)S(1)}, bf16[512,256]{1,0:T(8,128)(2,1)S(1)}, u32[]{:S(2)}, u32[]{:S(2)}) %collective-permute-start.5) | collective-permute-done | bytes 262176 | tf_op jit(solution)/shard_map/ppermute | solution.py:104
  31.1 1.1 constant_dynamic-slice_fusion.8
  32.2 0.6 broadcast_in_dim.4.refs_5_
  32.8 8.6 %shard_map.128 = (f32[1024,256]{1,0:T(8,128)}, f32[1024,256]{1,0:T(8,128)}) custom-call(s32[128]{0:T(128)} %compare_select_fusion.refs_0_, s32[128]{0:T(128)} %bitcast.111, s32[1]{0:T(128)} %bitcast.90.refs_2_, bf16[128,128,128]{2,1,0:T(8,128)(2,1)} %bitcast.92, bf16[2048,256]{1,0:T(8,128)(2,1)} %bitcast.94, bf16[8,128]{1,0:T(8,128)(2,1)} %broadcast_in_dim.4.refs_5_), custom_call_target="tpu_custom_call" | custom-call | tf_op jit(solution)/shard_map/pallas_call | solution.py:73
  41.4 1.2 collective-permute-start.6
  42.6 2.5 %collective-permute-done.6 = f32[1024,256]{1,0:T(8,128)S(1)} collective-permute-done((f32[1024,256]{1,0:T(8,128)}, f32[1024,256]{1,0:T(8,128)S(1)}, u32[]{:S(2)}, u32[]{:S(2)}) %collective-permute-start.6) | collective-permute-done | bytes 1048608 | tf_op jit(solution)/shard_map/ppermute | solution.py:98
  45.1 1.4 add.219
  46.5 1.4 collective-permute-start.7
  47.9 2.7 %collective-permute-start.8 = (f32[256,256]{1,0:T(8,128)S(1)}, f32[256,256]{1,0:T(8,128)S(1)}, u32[]{:S(2)}, u32[]{:S(2)}) collective-permute-start(f32[256,256]{1,0:T(8,128)S(1)} %get-tuple-element.59), channel_id=1, source_target_pairs={{0,128},{64,192},{128,0},{192,64},{1,129},{65,193},{129,1},{193,65... | collective-permute-start | bytes 786440 | tf_op jit(solution)/shard_map/ppermute | solution.py:116
  50.6 0.8 collective-permute-start.9
  51.5 4.2 %collective-permute-done.7 = f32[256,256]{1,0:T(8,128)S(1)} collective-permute-done((f32[256,256]{1,0:T(8,128)S(1)}, f32[256,256]{1,0:T(8,128)S(1)}, u32[]{:S(2)}, u32[]{:S(2)}) %collective-permute-start.7) | collective-permute-done | bytes 262176 | tf_op jit(solution)/shard_map/ppermute | solution.py:116
  55.6 6.6 %collective-permute-done.8 = f32[256,256]{1,0:T(8,128)S(1)} collective-permute-done((f32[256,256]{1,0:T(8,128)S(1)}, f32[256,256]{1,0:T(8,128)S(1)}, u32[]{:S(2)}, u32[]{:S(2)}) %collective-permute-start.8) | collective-permute-done | bytes 262176 | tf_op jit(solution)/shard_map/ppermute | solution.py:116
  62.4 4.7 %collective-permute-start.10 = (f32[128,256]{1,0:T(8,128)S(1)}, f32[128,256]{1,0:T(8,128)S(1)}, u32[]{:S(2)}, u32[]{:S(2)}) collective-permute-start(f32[128,256]{1,0:T(8,128)S(1)} %constant_dynamic-slice_fusion.4), channel_id=1, source_target_pairs={{0,32},{32,0},{1,33},{33,1},{2,34},{34,2},{3,35},{35,3},{4,36},{36... | collective-permute-start | bytes 393224 | tf_op jit(solution)/shard_map/ppermute | solution.py:98
  67.1 3.2 %collective-permute-done.10 = f32[128,256]{1,0:T(8,128)S(1)} collective-permute-done((f32[128,256]{1,0:T(8,128)S(1)}, f32[128,256]{1,0:T(8,128)S(1)}, u32[]{:S(2)}, u32[]{:S(2)}) %collective-permute-start.10) | collective-permute-done | bytes 131104 | tf_op jit(solution)/shard_map/ppermute | solution.py:98
  70.6 0.6 subtract_reduce_fusion
  71.2 0.2 convert_reduce_fusion
  71.5 5.0 %collective-permute-start.11 = (bf16[128,256]{1,0:T(8,128)(2,1)S(1)}, bf16[128,256]{1,0:T(8,128)(2,1)S(1)}, u32[]{:S(2)}, u32[]{:S(2)}) collective-permute-start(bf16[128,256]{1,0:T(8,128)(2,1)S(1)} %get-tuple-element.68), channel_id=1, source_target_pairs={{0,32},{32,0},{1,33},{33,1},{2,34},{34,2},{3,35},{35,3},{4,36},{36... | collective-permute-start | bytes 196616 | tf_op jit(solution)/shard_map/ppermute | solution.py:104
  76.4 3.1 %collective-permute-done.11 = bf16[128,256]{1,0:T(8,128)(2,1)S(1)} collective-permute-done((bf16[128,256]{1,0:T(8,128)(2,1)S(1)}, bf16[128,256]{1,0:T(8,128)(2,1)S(1)}, u32[]{:S(2)}, u32[]{:S(2)}) %collective-permute-start.11) | collective-permute-done | bytes 65568 | tf_op jit(solution)/shard_map/ppermute | solution.py:104
  79.6 2.9 %collective-permute-start.12 = (bf16[256,256]{1,0:T(8,128)(2,1)S(1)}, bf16[256,256]{1,0:T(8,128)(2,1)S(1)}, u32[]{:S(2)}, u32[]{:S(2)}) collective-permute-start(bf16[256,256]{1,0:T(8,128)(2,1)S(1)} %bitcast.102), channel_id=1, source_target_pairs={{0,192},{64,0},{128,64},{192,128},{1,193},{65,1},{129,65},{193,129... | collective-permute-start | bytes 393224 | tf_op jit(solution)/shard_map/ppermute | solution.py:104
  82.6 0.7 collective-permute-start.14
  83.3 2.6 %collective-permute-done.12 = bf16[256,256]{1,0:T(8,128)(2,1)S(1)} collective-permute-done((bf16[256,256]{1,0:T(8,128)(2,1)S(1)}, bf16[256,256]{1,0:T(8,128)(2,1)S(1)}, u32[]{:S(2)}, u32[]{:S(2)}) %collective-permute-start.12) | collective-permute-done | bytes 131104 | tf_op jit(solution)/shard_map/ppermute | solution.py:104
  85.9 2.1 %collective-permute-done.13 = bf16[256,256]{1,0:T(8,128)(2,1)S(1)} collective-permute-done((bf16[256,256]{1,0:T(8,128)(2,1)S(1)}, bf16[256,256]{1,0:T(8,128)(2,1)S(1)}, u32[]{:S(2)}, u32[]{:S(2)}) %collective-permute-start.13) | collective-permute-done | bytes 131104 | tf_op jit(solution)/shard_map/ppermute | solution.py:104
  88.0 1.0 collective-permute-done.14
  89.2 4.0 %collective-permute-start.15 = (bf16[1024,256]{1,0:T(8,128)(2,1)S(1)}, bf16[1024,256]{1,0:T(8,128)(2,1)S(1)}, u32[]{:S(2)}, u32[]{:S(2)}) collective-permute-start(bf16[1024,256]{1,0:T(8,128)(2,1)S(1)} %bitcast.100), channel_id=1, source_target_pairs={{0,16},{16,0},{1,17},{17,1},{2,18},{18,2},{3,19},{19,3},{4,20},{20... | collective-permute-start | bytes 1572872 | tf_op jit(solution)/shard_map/ppermute | solution.py:98
  93.2 1.5 collective-permute-done.15.refs_5_
  94.8 0.8 copy-done.2
  95.5 8.7 %shard_map.129 = (f32[256,2048]{1,0:T(8,128)}, f32[8,128]{1,0:T(8,128)}) custom-call(s32[128]{0:T(128)} %compare_select_fusion.refs_0_, s32[128]{0:T(128)} %bitcast.112, s32[1]{0:T(128)} %bitcast.91.refs_2_, bf16[128,128,128]{2,1,0:T(8,128)(2,1)} %bitcast.93, bf16[1024,256]{1,0:T(8,128)(2,1)} %bitcast.101, bf16[1024,256]{1,0:T(8,128)(2,1)} %copy-done.2), custom_call_target="tpu_custom_call" | custom-call | tf_op jit(solution)/shard_map/pallas_call | solution.py:73
  104.2 1.5 dynamic-slice_bitcast_fusion.2
  105.8 1.0 collective-permute-start.17
  106.8 2.0 collective-permute-start.18
  108.8 0.6 fusion.6
  109.4 2.0 scatter.9
  111.4 19.9 %collective-permute-done.16 = f32[512,256]{0,1:T(8,128)S(1)} collective-permute-done((f32[512,256]{0,1:T(8,128)S(1)}, f32[512,256]{0,1:T(8,128)S(1)}, u32[]{:S(2)}, u32[]{:S(2)}) %collective-permute-start.16) | collective-permute-done | bytes 524320 | tf_op jit(solution)/shard_map/ppermute | solution.py:116
  131.3 0.4 collective-permute-done.18
  131.6 1.3 fusion.1
  133.0 3.7 %collective-permute-start.19 = (f32[128,256]{0,1:T(8,128)S(1)}, f32[128,256]{0,1:T(8,128)S(1)}, u32[]{:S(2)}, u32[]{:S(2)}) collective-permute-start(f32[128,256]{0,1:T(8,128)S(1)} %get-tuple-element.60), channel_id=1, source_target_pairs={{0,1},{1,2},{2,3},{3,0},{4,5},{5,6},{6,7},{7,4},{8,9},{9,10},{10,1... | collective-permute-start | bytes 393224 | tf_op jit(solution)/shard_map/ppermute | solution.py:116
  136.7 0.6 collective-permute-start.20
  137.3 2.0 collective-permute-start.21
  139.5 0.3 collective-permute-done.19
  139.8 6.8 %collective-permute-done.20 = f32[128,256]{0,1:T(8,128)S(1)} collective-permute-done((f32[128,256]{0,1:T(8,128)S(1)}, f32[128,256]{0,1:T(8,128)S(1)}, u32[]{:S(2)}, u32[]{:S(2)}) %collective-permute-start.20) | collective-permute-done | bytes 131104 | tf_op jit(solution)/shard_map/ppermute | solution.py:116
  146.9 0.7 collective-permute-start.22
  147.6 1.1 collective-permute-done.22
  148.9 27.6 %all_to_all.10 = f32[128,1,430]{2,1,0:T(1,128)S(1)} all-to-all(f32[128,1,430]{2,1,0:T(1,128)S(1)} %copy.17), channel_id=1, replica_groups=mesh['y'=4,'zh'=2,'core'=2,'cx'=4,'cz'=4] {'y','zh','cx','cz'}, dimensions={0} | all-to-all | bytes 440320 | tf_op jit(solution)/shard_map/all_to_all | solution.py:93
  176.5 0.2 reduce_sum.49
  176.8 19.2 %all_to_all.11 = f32[128,1,430]{2,1,0:T(1,128)S(1)} all-to-all(f32[128,1,430]{2,1,0:T(1,128)S(1)} %broadcast_in_dim.5), channel_id=1, replica_groups=mesh['y'=4,'zh'=2,'core'=2,'cx'=4,'cz'=4] {'y','zh','cx','cz'}, dimensions={0} | all-to-all | bytes 440320 | tf_op jit(solution)/shard_map/all_to_all | solution.py:87
  196.2 3.2 %collective-permute-start.23 = (f32[128,430]{0,1:T(8,128)S(1)}, f32[128,430]{0,1:T(8,128)S(1)}, u32[]{:S(2)}, u32[]{:S(2)}) collective-permute-start(f32[128,430]{0,1:T(8,128)S(1)} %bitcast.107), channel_id=1, source_target_pairs={{0,16},{16,0},{1,17},{17,1},{2,18},{18,2},{3,19},{19,3},{4,20},{20... | collective-permute-start | bytes 660488 | tf_op jit(solution)/shard_map/ppermute | solution.py:98
  199.3 0.8 convolution_convert_fusion
  200.1 0.3 collective-permute-done.23
  200.5 0.7 slice_multiply_fusion.1
  201.2 0.5 slice.65
  201.7 0.6 slice_multiply_fusion.2
  202.2 0.8 copy.19
  (66 shorter events, 2.1 us)
Async XLA Ops:
  0.6 0.9 copy-start
  2.5 6.6 %collective-permute-start = (bf16[128,256]{1,0:T(8,128)(2,1)S(1)}, bf16[128,256]{1,0:T(8,128)(2,1)S(1)}, u32[]{:S(2)}, u32[]{:S(2)}) collective-permute-start(bf16[128,256]{1,0:T(8,128)(2,1)S(1)} %convolution_convert_fusion.1), channel_id=1, source_target_pairs={{0,3},{1,0},{2,1},{3,2},{4,7},{5,4},{6,5},{7,6},{8,11},{9,8},{10,9... | collective-permute-start | bytes 196616 | tf_op jit(solution)/shard_map/ppermute | solution.py:104
  7.8 6.8 %collective-permute-start.1 = (bf16[128,256]{1,0:T(8,128)(2,1)S(1)}, bf16[128,256]{1,0:T(8,128)(2,1)S(1)}, u32[]{:S(2)}, u32[]{:S(2)}) collective-permute-start(bf16[128,256]{1,0:T(8,128)(2,1)S(1)} %convolution_convert_fusion.1), channel_id=1, source_target_pairs={{0,2},{1,3},{2,0},{3,1},{4,6},{5,7},{6,4},{7,5},{8,10},{9,11},{10,... | collective-permute-start | bytes 196616 | tf_op jit(solution)/shard_map/ppermute | solution.py:104
  7.8 6.8 %collective-permute-start.2 = (bf16[128,256]{1,0:T(8,128)(2,1)S(1)}, bf16[128,256]{1,0:T(8,128)(2,1)S(1)}, u32[]{:S(2)}, u32[]{:S(2)}) collective-permute-start(bf16[128,256]{1,0:T(8,128)(2,1)S(1)} %convolution_convert_fusion.1), channel_id=1, source_target_pairs={{0,1},{1,2},{2,3},{3,0},{4,5},{5,6},{6,7},{7,4},{8,9},{9,10},{10,1... | collective-permute-start | bytes 196616 | tf_op jit(solution)/shard_map/ppermute | solution.py:104
  14.8 7.3 %collective-permute-start.3 = (bf16[512,256]{1,0:T(8,128)(2,1)S(1)}, bf16[512,256]{1,0:T(8,128)(2,1)S(1)}, u32[]{:S(2)}, u32[]{:S(2)}) collective-permute-start(bf16[512,256]{1,0:T(8,128)(2,1)S(1)} %bitcast.95), channel_id=1, source_target_pairs={{0,12},{4,0},{8,4},{12,8},{1,13},{5,1},{9,5},{13,9},{2,14},{6,2},{... | collective-permute-start | bytes 786440 | tf_op jit(solution)/shard_map/ppermute | solution.py:104
  16.2 7.5 %collective-permute-start.4 = (bf16[512,256]{1,0:T(8,128)(2,1)S(1)}, bf16[512,256]{1,0:T(8,128)(2,1)S(1)}, u32[]{:S(2)}, u32[]{:S(2)}) collective-permute-start(bf16[512,256]{1,0:T(8,128)(2,1)S(1)} %bitcast.96), channel_id=1, source_target_pairs={{0,8},{4,12},{8,0},{12,4},{1,9},{5,13},{9,1},{13,5},{2,10},{6,14},... | collective-permute-start | bytes 786440 | tf_op jit(solution)/shard_map/ppermute | solution.py:104
  18.5 12.4 %collective-permute-start.5 = (bf16[512,256]{1,0:T(8,128)(2,1)S(1)}, bf16[512,256]{1,0:T(8,128)(2,1)S(1)}, u32[]{:S(2)}, u32[]{:S(2)}) collective-permute-start(bf16[512,256]{1,0:T(8,128)(2,1)S(1)} %bitcast.97), channel_id=1, source_target_pairs={{0,4},{4,8},{8,12},{12,0},{1,5},{5,9},{9,13},{13,1},{2,6},{6,10},{... | collective-permute-start | bytes 786440 | tf_op jit(solution)/shard_map/ppermute | solution.py:104
  41.4 3.7 %collective-permute-start.6 = (f32[1024,256]{1,0:T(8,128)}, f32[1024,256]{1,0:T(8,128)S(1)}, u32[]{:S(2)}, u32[]{:S(2)}) collective-permute-start(f32[1024,256]{1,0:T(8,128)} %get-tuple-element.33), channel_id=1, source_target_pairs={{0,16},{16,0},{1,17},{17,1},{2,18},{18,2},{3,19},{19,3},{4,20},{20... | collective-permute-start | bytes 3145736 | tf_op jit(solution)/shard_map/ppermute | solution.py:98
  46.4 23.9 %copy-start.6 = (f32[256]{0:T(256)S(1)}, f32[256]{0:T(256)}, u32[]{:S(2)}) copy-start(f32[256]{0:T(256)} %param.15) | copy-start | bytes 3076
  46.4 23.9 %copy-start.4 = (bf16[256,172]{0,1:T(8,128)(2,1)S(1)}, bf16[256,172]{0,1:T(8,128)(2,1)}, u32[]{:S(2)}) copy-start(bf16[256,172]{0,1:T(8,128)(2,1)} %param.16) | copy-start | bytes 264196
  46.5 24.1 %copy-start.5 = (s32[128]{0:T(128)S(1)}, s32[128]{0:T(128)}, u32[]{:S(2)}) copy-start(s32[128]{0:T(128)} %param.21) | copy-start | bytes 1540
  46.5 9.1 %collective-permute-start.7 = (f32[256,256]{1,0:T(8,128)S(1)}, f32[256,256]{1,0:T(8,128)S(1)}, u32[]{:S(2)}, u32[]{:S(2)}) collective-permute-start(f32[256,256]{1,0:T(8,128)S(1)} %get-tuple-element.57), channel_id=1, source_target_pairs={{0,64},{64,128},{128,192},{192,0},{1,65},{65,129},{129,193},{193,1... | collective-permute-start | bytes 786440 | tf_op jit(solution)/shard_map/ppermute | solution.py:116
  47.9 14.4 %collective-permute-start.8 = (f32[256,256]{1,0:T(8,128)S(1)}, f32[256,256]{1,0:T(8,128)S(1)}, u32[]{:S(2)}, u32[]{:S(2)}) collective-permute-start(f32[256,256]{1,0:T(8,128)S(1)} %get-tuple-element.59), channel_id=1, source_target_pairs={{0,128},{64,192},{128,0},{192,64},{1,129},{65,193},{129,1},{193,65... | collective-permute-start | bytes 786440 | tf_op jit(solution)/shard_map/ppermute | solution.py:116
  50.6 11.6 %collective-permute-start.9 = (f32[256,256]{1,0:T(8,128)S(1)}, f32[256,256]{1,0:T(8,128)S(1)}, u32[]{:S(2)}, u32[]{:S(2)}) collective-permute-start(f32[256,256]{1,0:T(8,128)S(1)} %get-tuple-element.58), channel_id=1, source_target_pairs={{0,192},{64,0},{128,64},{192,128},{1,193},{65,1},{129,65},{193,129... | collective-permute-start | bytes 786440 | tf_op jit(solution)/shard_map/ppermute | solution.py:116
  62.4 7.9 %collective-permute-start.10 = (f32[128,256]{1,0:T(8,128)S(1)}, f32[128,256]{1,0:T(8,128)S(1)}, u32[]{:S(2)}, u32[]{:S(2)}) collective-permute-start(f32[128,256]{1,0:T(8,128)S(1)} %constant_dynamic-slice_fusion.4), channel_id=1, source_target_pairs={{0,32},{32,0},{1,33},{33,1},{2,34},{34,2},{3,35},{35,3},{4,36},{36... | collective-permute-start | bytes 393224 | tf_op jit(solution)/shard_map/ppermute | solution.py:98
  71.5 8.1 %collective-permute-start.11 = (bf16[128,256]{1,0:T(8,128)(2,1)S(1)}, bf16[128,256]{1,0:T(8,128)(2,1)S(1)}, u32[]{:S(2)}, u32[]{:S(2)}) collective-permute-start(bf16[128,256]{1,0:T(8,128)(2,1)S(1)} %get-tuple-element.68), channel_id=1, source_target_pairs={{0,32},{32,0},{1,33},{33,1},{2,34},{34,2},{3,35},{35,3},{4,36},{36... | collective-permute-start | bytes 196616 | tf_op jit(solution)/shard_map/ppermute | solution.py:104
  79.6 6.3 %collective-permute-start.12 = (bf16[256,256]{1,0:T(8,128)(2,1)S(1)}, bf16[256,256]{1,0:T(8,128)(2,1)S(1)}, u32[]{:S(2)}, u32[]{:S(2)}) collective-permute-start(bf16[256,256]{1,0:T(8,128)(2,1)S(1)} %bitcast.102), channel_id=1, source_target_pairs={{0,192},{64,0},{128,64},{192,128},{1,193},{65,1},{129,65},{193,129... | collective-permute-start | bytes 393224 | tf_op jit(solution)/shard_map/ppermute | solution.py:104
  82.6 5.4 %collective-permute-start.13 = (bf16[256,256]{1,0:T(8,128)(2,1)S(1)}, bf16[256,256]{1,0:T(8,128)(2,1)S(1)}, u32[]{:S(2)}, u32[]{:S(2)}) collective-permute-start(bf16[256,256]{1,0:T(8,128)(2,1)S(1)} %bitcast.103), channel_id=1, source_target_pairs={{0,128},{64,192},{128,0},{192,64},{1,129},{65,193},{129,1},{193,65... | collective-permute-start | bytes 393224 | tf_op jit(solution)/shard_map/ppermute | solution.py:104
  82.6 6.4 %collective-permute-start.14 = (bf16[256,256]{1,0:T(8,128)(2,1)S(1)}, bf16[256,256]{1,0:T(8,128)(2,1)S(1)}, u32[]{:S(2)}, u32[]{:S(2)}) collective-permute-start(bf16[256,256]{1,0:T(8,128)(2,1)S(1)} %bitcast.104), channel_id=1, source_target_pairs={{0,64},{64,128},{128,192},{192,0},{1,65},{65,129},{129,193},{193,1... | collective-permute-start | bytes 393224 | tf_op jit(solution)/shard_map/ppermute | solution.py:104
  89.2 5.6 %copy-start.1 = (bf16[4,256,256]{2,1,0:T(8,128)(2,1)}, bf16[4,256,256]{2,1,0:T(8,128)(2,1)S(1)}, u32[]{:S(2)}) copy-start(bf16[4,256,256]{2,1,0:T(8,128)(2,1)S(1)} %constant_dynamic-slice_fusion.3) | copy-start | bytes 1572868
  89.2 5.6 %collective-permute-start.15 = (bf16[1024,256]{1,0:T(8,128)(2,1)S(1)}, bf16[1024,256]{1,0:T(8,128)(2,1)S(1)}, u32[]{:S(2)}, u32[]{:S(2)}) collective-permute-start(bf16[1024,256]{1,0:T(8,128)(2,1)S(1)} %bitcast.100), channel_id=1, source_target_pairs={{0,16},{16,0},{1,17},{17,1},{2,18},{18,2},{3,19},{19,3},{4,20},{20... | collective-permute-start | bytes 1572872 | tf_op jit(solution)/shard_map/ppermute | solution.py:98
  94.8 0.8 copy-start.2
  105.7 25.6 %collective-permute-start.16 = (f32[512,256]{0,1:T(8,128)S(1)}, f32[512,256]{0,1:T(8,128)S(1)}, u32[]{:S(2)}, u32[]{:S(2)}) collective-permute-start(f32[512,256]{0,1:T(8,128)S(1)} %get-tuple-element.54), channel_id=1, source_target_pairs={{0,4},{4,8},{8,12},{12,0},{1,5},{5,9},{9,13},{13,1},{2,6},{6,10},{... | collective-permute-start | bytes 1572872 | tf_op jit(solution)/shard_map/ppermute | solution.py:116
  105.8 25.5 %collective-permute-start.17 = (f32[512,256]{0,1:T(8,128)S(1)}, f32[512,256]{0,1:T(8,128)S(1)}, u32[]{:S(2)}, u32[]{:S(2)}) collective-permute-start(f32[512,256]{0,1:T(8,128)S(1)} %get-tuple-element.56), channel_id=1, source_target_pairs={{0,8},{4,12},{8,0},{12,4},{1,9},{5,13},{9,1},{13,5},{2,10},{6,14},... | collective-permute-start | bytes 1572872 | tf_op jit(solution)/shard_map/ppermute | solution.py:116
  106.8 24.8 %collective-permute-start.18 = (f32[512,256]{0,1:T(8,128)S(1)}, f32[512,256]{0,1:T(8,128)S(1)}, u32[]{:S(2)}, u32[]{:S(2)}) collective-permute-start(f32[512,256]{0,1:T(8,128)S(1)} %get-tuple-element.55), channel_id=1, source_target_pairs={{0,12},{4,0},{8,4},{12,8},{1,13},{5,1},{9,5},{13,9},{2,14},{6,2},{... | collective-permute-start | bytes 1572872 | tf_op jit(solution)/shard_map/ppermute | solution.py:116
  111.4 35.3 %copy-start.3 = (bf16[128,256]{1,0:T(8,128)(2,1)S(1)}, bf16[128,256]{1,0:T(8,128)(2,1)}, u32[]{:S(2)}) copy-start(bf16[128,256]{1,0:T(8,128)(2,1)} %param.13) | copy-start | bytes 196612
  133.0 6.8 %collective-permute-start.19 = (f32[128,256]{0,1:T(8,128)S(1)}, f32[128,256]{0,1:T(8,128)S(1)}, u32[]{:S(2)}, u32[]{:S(2)}) collective-permute-start(f32[128,256]{0,1:T(8,128)S(1)} %get-tuple-element.60), channel_id=1, source_target_pairs={{0,1},{1,2},{2,3},{3,0},{4,5},{5,6},{6,7},{7,4},{8,9},{9,10},{10,1... | collective-permute-start | bytes 393224 | tf_op jit(solution)/shard_map/ppermute | solution.py:116
  136.7 9.9 %collective-permute-start.20 = (f32[128,256]{0,1:T(8,128)S(1)}, f32[128,256]{0,1:T(8,128)S(1)}, u32[]{:S(2)}, u32[]{:S(2)}) collective-permute-start(f32[128,256]{0,1:T(8,128)S(1)} %get-tuple-element.62), channel_id=1, source_target_pairs={{0,2},{1,3},{2,0},{3,1},{4,6},{5,7},{6,4},{7,5},{8,10},{9,11},{10,... | collective-permute-start | bytes 393224 | tf_op jit(solution)/shard_map/ppermute | solution.py:116
  137.3 9.3 %collective-permute-start.21 = (f32[128,256]{0,1:T(8,128)S(1)}, f32[128,256]{0,1:T(8,128)S(1)}, u32[]{:S(2)}, u32[]{:S(2)}) collective-permute-start(f32[128,256]{0,1:T(8,128)S(1)} %get-tuple-element.61), channel_id=1, source_target_pairs={{0,3},{1,0},{2,1},{3,2},{4,7},{5,4},{6,5},{7,6},{8,11},{9,8},{10,9... | collective-permute-start | bytes 393224 | tf_op jit(solution)/shard_map/ppermute | solution.py:116
  146.9 1.8 collective-permute-start.22
  196.2 4.3 %collective-permute-start.23 = (f32[128,430]{0,1:T(8,128)S(1)}, f32[128,430]{0,1:T(8,128)S(1)}, u32[]{:S(2)}, u32[]{:S(2)}) collective-permute-start(f32[128,430]{0,1:T(8,128)S(1)} %bitcast.107), channel_id=1, source_target_pairs={{0,16},{16,0},{1,17},{17,1},{2,18},{18,2},{3,19},{19,3},{4,20},{20... | collective-permute-start | bytes 660488 | tf_op jit(solution)/shard_map/ppermute | solution.py:98

commit v13 on v12

--- a/solution.py
+++ b/solution.py
@@ -132,14 +132,10 @@
 
 
 def reduce_all(x, axes):
-    half = x.shape[0] // 2
-    first = lax.axis_index("core") == 0
-    mine = jnp.where(first, x[:half], x[half:])
-    other = jnp.where(first, x[half:], x[:half])
-    summed = mine + swap_core(other)
-    summed = gather_rows(scatter_rows(summed, axes), axes)
-    partner = swap_core(summed)
-    return jnp.where(first, jnp.concatenate([summed, partner]), jnp.concatenate([partner, summed]))
+    x = ring_scatter(pair_scatter(x, "core"), "cz")
+    x = gather_rows(scatter_rows(x, axes), axes)
+    return pair_gather(ring_gather(x, "cz"), "core")
+
 
 def head_block(agg, bias, w_out, node_labels):
     pre_act = agg + bias[None, :]
@@ -191,7 +187,7 @@
     extra = jnp.zeros((feat, 2), jnp.float32)
     extra = extra.at[:, 0].set(bias_term).at[0, 1].set(loss_sum)
     packed = jnp.concatenate([in_term, out_term, extra], axis=1)
-    packed = reduce_all(packed, ("y", "zh", "cx", "cz"))
+    packed = reduce_all(packed, ("y", "zh", "cx"))
     grad_w_in = packed[:, :feat] * scale
     grad_w_out = packed[:, feat : feat + classes] * scale
     grad_bias = packed[:, feat + classes] * scale

time: 206 us -> 229 us (1.11)
  waiting for transfers between devices: 73.7 us -> 96.2 us
  starting transfers between devices: 45 us -> 56.5 us
  blocking collectives: 46.7 us -> 35.8 us
    ppermute x9 -> x12, waiting for transfers between devices: 38.2 us -> 54.9 us  [ring_scatter(): lax.ppermute(piece, axis, [(i, (i + k) % n) for i in range(n)])]
    all_to_all x1, blocking collectives: 27.6 us -> 21.2 us  [scatter_rows(): got = lax.all_to_all(x.reshape(n, -1, x.shape[1]), axis, 0, 0, tiled=False)]
    ppermute x10 -> x13, starting transfers between devices: 16.8 us -> 22.8 us  [ring_gather(): lax.ppermute(x, axis, [(i, (i + k) % n) for i in range(n)])]
    ppermute x10 -> x13, waiting for transfers between devices: 27 us -> 32.1 us  [ring_gather(): lax.ppermute(x, axis, [(i, (i + k) % n) for i in range(n)])]
    all_to_all x1, blocking collectives: 19.2 us -> 14.7 us  [gather_rows(): got = lax.all_to_all(spread, axis, 0, 0, tiled=False)]
    ppermute x9 -> x12, starting transfers between devices: 14.4 us -> 18.1 us  [ring_scatter(): lax.ppermute(piece, axis, [(i, (i + k) % n) for i in range(n)])]
  transfers between devices with their start and end apart: 24 -> 30, of which waited for: 20 -> 25; matrix products, arithmetic and copies ran while one was open for 2% -> 2% of each run, Pallas kernels for 0% -> 0%
where the time goes in v13:
time: 229 us; the launch traced here: 228 us
  waiting for transfers between devices  96.2 us (42%)
  starting transfers between devices  56.5 us (25%)
  blocking collectives  35.8 us (16%)
  Pallas kernels  17.2 us (8%)
  local copies, waits for them, and re-layouts  9.81 us (4%)
  other arithmetic  6.52 us (3%)
  between operations  3.53 us (2%)
  matrix products  2.57 us (1%)
    ppermute x12, waiting for transfers between devices, ring_scatter(): lax.ppermute(piece, axis, [(i, (i + k) % n) for i in range(n)])  54.9 us
    ppermute x13, waiting for transfers between devices, ring_gather(): lax.ppermute(x, axis, [(i, (i + k) % n) for i in range(n)])  32.1 us
    ppermute x13, starting transfers between devices, ring_gather(): lax.ppermute(x, axis, [(i, (i + k) % n) for i in range(n)])  22.8 us
    all_to_all x1, blocking collectives, scatter_rows(): got = lax.all_to_all(x.reshape(n, -1, x.shape[1]), axis, 0, 0, tiled=False)  21.2 us
    ppermute x12, starting transfers between devices, ring_scatter(): lax.ppermute(piece, axis, [(i, (i + k) % n) for i in range(n)])  18.1 us
    pallas_call x2, Pallas kernels, tile_product(): pl.pallas_call(lambda *refs: _dense_kernel(transpose, *refs), grid_spec=g...  17.2 us
    ppermute x5, starting transfers between devices, swap_core(): return lax.ppermute(x, axis, [(0, 1), (1, 0)])  15.6 us
    all_to_all x1, blocking collectives, gather_rows(): got = lax.all_to_all(spread, axis, 0, 0, tiled=False)  14.7 us
  transfers between devices with their start and end apart: 30, of which 25 were waited for; matrix products, arithmetic and copies ran while one was open for 2% of the time, Pallas kernels for 0%

profile of v13, /device:TPU:1, one launch (start us, length us, event | category | flops | bytes accessed | tf_op | source)
XLA Modules:
  0.0 228.1 jit_solution(10389829584537686601)
XLA Ops:
  0.6 0.9 copy-done
  1.5 1.0 convolution_convert_fusion.1
  2.5 5.2 %collective-permute-start = (bf16[128,256]{1,0:T(8,128)(2,1)S(1)}, bf16[128,256]{1,0:T(8,128)(2,1)S(1)}, u32[]{:S(2)}, u32[]{:S(2)}) collective-permute-start(bf16[128,256]{1,0:T(8,128)(2,1)S(1)} %convolution_convert_fusion.1), channel_id=1, source_target_pairs={{0,3},{1,0},{2,1},{3,2},{4,7},{5,4},{6,5},{7,6},{8,11},{9,8},{10,9... | collective-permute-start | bytes 196616 | tf_op jit(solution)/shard_map/ppermute | solution.py:104
  8.2 0.9 collective-permute-done
  9.1 5.5 %collective-permute-done.1 = bf16[128,256]{1,0:T(8,128)(2,1)S(1)} collective-permute-done((bf16[128,256]{1,0:T(8,128)(2,1)S(1)}, bf16[128,256]{1,0:T(8,128)(2,1)S(1)}, u32[]{:S(2)}, u32[]{:S(2)}) %collective-permute-start.1) | collective-permute-done | bytes 65568 | tf_op jit(solution)/shard_map/ppermute | solution.py:104
  14.8 1.4 collective-permute-start.3
  16.7 1.2 compare_select_fusion.refs_0_
  18.5 0.7 collective-permute-start.5
  19.2 2.8 %collective-permute-done.3 = bf16[512,256]{1,0:T(8,128)(2,1)S(1)} collective-permute-done((bf16[512,256]{1,0:T(8,128)(2,1)S(1)}, bf16[512,256]{1,0:T(8,128)(2,1)S(1)}, u32[]{:S(2)}, u32[]{:S(2)}) %collective-permute-start.3) | collective-permute-done | bytes 262176 | tf_op jit(solution)/shard_map/ppermute | solution.py:104
  22.1 1.6 collective-permute-done.4
  23.7 7.2 %collective-permute-done.5 = bf16[512,256]{1,0:T(8,128)(2,1)S(1)} collective-permute-done((bf16[512,256]{1,0:T(8,128)(2,1)S(1)}, bf16[512,256]{1,0:T(8,128)(2,1)S(1)}, u32[]{:S(2)}, u32[]{:S(2)}) %collective-permute-start.5) | collective-permute-done | bytes 262176 | tf_op jit(solution)/shard_map/ppermute | solution.py:104
  31.1 1.1 constant_dynamic-slice_fusion.13
  32.8 8.6 %shard_map.128 = (f32[1024,256]{1,0:T(8,128)}, f32[1024,256]{1,0:T(8,128)}) custom-call(s32[128]{0:T(128)} %compare_select_fusion.refs_0_, s32[128]{0:T(128)} %bitcast.128, s32[1]{0:T(128)} %bitcast.104.refs_2_, bf16[128,128,128]{2,1,0:T(8,128)(2,1)} %bitcast.106, bf16[2048,256]{1,0:T(8,128)(2,1)} %bitcast.108, bf16[8,128]{1,0:T(8,128)(2,1)} %broadcast_in_dim.4.refs_5_), custom_call_target="tpu_custom_call" | custom-call | tf_op jit(solution)/shard_map/pallas_call | solution.py:73
  41.4 2.8 %collective-permute-done.6 = f32[1024,256]{1,0:T(8,128)S(1)} collective-permute-done((f32[1024,256]{1,0:T(8,128)}, f32[1024,256]{1,0:T(8,128)S(1)}, u32[]{:S(2)}, u32[]{:S(2)}) %collective-permute-start.6) | collective-permute-done | bytes 1048608 | tf_op jit(solution)/shard_map/ppermute | solution.py:98
  44.2 1.4 add.257
  45.7 1.1 collective-permute-start.7
  46.8 3.9 %collective-permute-start.8 = (f32[256,256]{1,0:T(8,128)S(1)}, f32[256,256]{1,0:T(8,128)S(1)}, u32[]{:S(2)}, u32[]{:S(2)}) collective-permute-start(f32[256,256]{1,0:T(8,128)S(1)} %get-tuple-element.64), channel_id=1, source_target_pairs={{0,128},{64,192},{128,0},{192,64},{1,129},{65,193},{129,1},{193,65... | collective-permute-start | bytes 786440 | tf_op jit(solution)/shard_map/ppermute | solution.py:116
  50.7 1.0 collective-permute-start.9
  51.7 4.1 %collective-permute-done.7 = f32[256,256]{1,0:T(8,128)S(1)} collective-permute-done((f32[256,256]{1,0:T(8,128)S(1)}, f32[256,256]{1,0:T(8,128)S(1)}, u32[]{:S(2)}, u32[]{:S(2)}) %collective-permute-start.7) | collective-permute-done | bytes 262176 | tf_op jit(solution)/shard_map/ppermute | solution.py:116
  55.8 6.5 %collective-permute-done.8 = f32[256,256]{1,0:T(8,128)S(1)} collective-permute-done((f32[256,256]{1,0:T(8,128)S(1)}, f32[256,256]{1,0:T(8,128)S(1)}, u32[]{:S(2)}, u32[]{:S(2)}) %collective-permute-start.8) | collective-permute-done | bytes 262176 | tf_op jit(solution)/shard_map/ppermute | solution.py:116
  62.4 4.5 %collective-permute-start.10 = (f32[128,256]{1,0:T(8,128)S(1)}, f32[128,256]{1,0:T(8,128)S(1)}, u32[]{:S(2)}, u32[]{:S(2)}) collective-permute-start(f32[128,256]{1,0:T(8,128)S(1)} %constant_dynamic-slice_fusion.9), channel_id=1, source_target_pairs={{0,32},{32,0},{1,33},{33,1},{2,34},{34,2},{3,35},{35,3},{4,36},{36... | collective-permute-start | bytes 393224 | tf_op jit(solution)/shard_map/ppermute | solution.py:98
  67.0 3.4 %collective-permute-done.10 = f32[128,256]{1,0:T(8,128)S(1)} collective-permute-done((f32[128,256]{1,0:T(8,128)S(1)}, f32[128,256]{1,0:T(8,128)S(1)}, u32[]{:S(2)}, u32[]{:S(2)}) %collective-permute-start.10) | collective-permute-done | bytes 131104 | tf_op jit(solution)/shard_map/ppermute | solution.py:98
  70.7 0.6 subtract_reduce_fusion
  71.5 4.5 %collective-permute-start.11 = (bf16[128,256]{1,0:T(8,128)(2,1)S(1)}, bf16[128,256]{1,0:T(8,128)(2,1)S(1)}, u32[]{:S(2)}, u32[]{:S(2)}) collective-permute-start(bf16[128,256]{1,0:T(8,128)(2,1)S(1)} %get-tuple-element.76), channel_id=1, source_target_pairs={{0,32},{32,0},{1,33},{33,1},{2,34},{34,2},{3,35},{35,3},{4,36},{36... | collective-permute-start | bytes 196616 | tf_op jit(solution)/shard_map/ppermute | solution.py:104
  76.1 3.3 %collective-permute-done.11 = bf16[128,256]{1,0:T(8,128)(2,1)S(1)} collective-permute-done((bf16[128,256]{1,0:T(8,128)(2,1)S(1)}, bf16[128,256]{1,0:T(8,128)(2,1)S(1)}, u32[]{:S(2)}, u32[]{:S(2)}) %collective-permute-start.11) | collective-permute-done | bytes 65568 | tf_op jit(solution)/shard_map/ppermute | solution.py:104
  79.4 3.1 %collective-permute-start.12 = (bf16[256,256]{1,0:T(8,128)(2,1)S(1)}, bf16[256,256]{1,0:T(8,128)(2,1)S(1)}, u32[]{:S(2)}, u32[]{:S(2)}) collective-permute-start(bf16[256,256]{1,0:T(8,128)(2,1)S(1)} %bitcast.116), channel_id=1, source_target_pairs={{0,192},{64,0},{128,64},{192,128},{1,193},{65,1},{129,65},{193,129... | collective-permute-start | bytes 393224 | tf_op jit(solution)/shard_map/ppermute | solution.py:104
  82.6 0.6 collective-permute-start.14
  83.2 2.6 %collective-permute-done.12 = bf16[256,256]{1,0:T(8,128)(2,1)S(1)} collective-permute-done((bf16[256,256]{1,0:T(8,128)(2,1)S(1)}, bf16[256,256]{1,0:T(8,128)(2,1)S(1)}, u32[]{:S(2)}, u32[]{:S(2)}) %collective-permute-start.12) | collective-permute-done | bytes 131104 | tf_op jit(solution)/shard_map/ppermute | solution.py:104
  85.8 2.1 collective-permute-done.13
  87.9 1.1 collective-permute-done.14
  89.2 5.4 %collective-permute-start.15 = (bf16[1024,256]{1,0:T(8,128)(2,1)S(1)}, bf16[1024,256]{1,0:T(8,128)(2,1)S(1)}, u32[]{:S(2)}, u32[]{:S(2)}) collective-permute-start(bf16[1024,256]{1,0:T(8,128)(2,1)S(1)} %bitcast.114), channel_id=1, source_target_pairs={{0,16},{16,0},{1,17},{17,1},{2,18},{18,2},{3,19},{19,3},{4,20},{20... | collective-permute-start | bytes 1572872 | tf_op jit(solution)/shard_map/ppermute | solution.py:98
  94.6 1.5 collective-permute-done.15.refs_5_
  96.2 0.8 copy-done.2
  97.0 8.6 %shard_map.129 = (f32[256,2048]{1,0:T(8,128)}, f32[8,128]{1,0:T(8,128)}) custom-call(s32[128]{0:T(128)} %compare_select_fusion.refs_0_, s32[128]{0:T(128)} %bitcast.129, s32[1]{0:T(128)} %bitcast.105.refs_2_, bf16[128,128,128]{2,1,0:T(8,128)(2,1)} %bitcast.107, bf16[1024,256]{1,0:T(8,128)(2,1)} %bitcast.115, bf16[1024,256]{1,0:T(8,128)(2,1)} %copy-done.2), custom_call_target="tpu_custom_call" | custom-call | tf_op jit(solution)/shard_map/pallas_call | solution.py:73
  105.6 1.5 dynamic-slice_bitcast_fusion.2
  107.3 2.5 %collective-permute-start.18 = (f32[512,256]{0,1:T(8,128)S(1)}, f32[512,256]{0,1:T(8,128)S(1)}, u32[]{:S(2)}, u32[]{:S(2)}) collective-permute-start(f32[512,256]{0,1:T(8,128)S(1)} %get-tuple-element.60), channel_id=1, source_target_pairs={{0,12},{4,0},{8,4},{12,8},{1,13},{5,1},{9,5},{13,9},{2,14},{6,2},{... | collective-permute-start | bytes 1572872 | tf_op jit(solution)/shard_map/ppermute | solution.py:116
  109.8 0.6 fusion.7
  110.4 2.0 scatter.9
  112.4 20.7 %collective-permute-done.16 = f32[512,256]{0,1:T(8,128)S(1)} collective-permute-done((f32[512,256]{0,1:T(8,128)S(1)}, f32[512,256]{0,1:T(8,128)S(1)}, u32[]{:S(2)}, u32[]{:S(2)}) %collective-permute-start.16) | collective-permute-done | bytes 524320 | tf_op jit(solution)/shard_map/ppermute | solution.py:116
  133.1 1.0 collective-permute-done.18
  134.1 1.3 fusion.1
  135.4 1.7 collective-permute-start.19
  137.2 2.3 collective-permute-start.21
  139.6 2.3 collective-permute-done.19
  141.9 6.5 %collective-permute-done.20 = f32[128,256]{0,1:T(8,128)S(1)} collective-permute-done((f32[128,256]{0,1:T(8,128)S(1)}, f32[128,256]{0,1:T(8,128)S(1)}, u32[]{:S(2)}, u32[]{:S(2)}) %collective-permute-start.20) | collective-permute-done | bytes 131104 | tf_op jit(solution)/shard_map/ppermute | solution.py:116
  148.6 0.7 collective-permute-start.22
  149.3 1.1 collective-permute-done.22
  150.7 3.1 %collective-permute-start.23 = (f32[32,430]{0,1:T(8,128)S(1)}, f32[32,430]{0,1:T(8,128)S(1)}, u32[]{:S(2)}, u32[]{:S(2)}) collective-permute-start(f32[32,430]{0,1:T(8,128)S(1)} %get-tuple-element.68), channel_id=1, source_target_pairs={{0,1},{1,2},{2,3},{3,0},{4,5},{5,6},{6,7},{7,4},{8,9},{9,10},{10,1... | collective-permute-start | bytes 165128 | tf_op jit(solution)/shard_map/ppermute | solution.py:116
  153.8 0.9 collective-permute-start.24
  154.7 1.2 collective-permute-start.25
  156.0 4.0 %collective-permute-done.23 = f32[32,430]{0,1:T(8,128)S(1)} collective-permute-done((f32[32,430]{0,1:T(8,128)S(1)}, f32[32,430]{0,1:T(8,128)S(1)}, u32[]{:S(2)}, u32[]{:S(2)}) %collective-permute-start.23) | collective-permute-done | bytes 55072 | tf_op jit(solution)/shard_map/ppermute | solution.py:116
  159.9 9.9 %collective-permute-done.24 = f32[32,430]{0,1:T(8,128)S(1)} collective-permute-done((f32[32,430]{0,1:T(8,128)S(1)}, f32[32,430]{0,1:T(8,128)S(1)}, u32[]{:S(2)}, u32[]{:S(2)}) %collective-permute-start.24) | collective-permute-done | bytes 55072 | tf_op jit(solution)/shard_map/ppermute | solution.py:116
  170.1 21.2 %all_to_all.10 = f32[32,1,430]{2,1,0:T(1,128)S(1)} all-to-all(f32[32,1,430]{2,1,0:T(1,128)S(1)} %copy.23), channel_id=1, replica_groups=mesh['y'=4,'zh'=2,'core'=2,'cx'=4,'cz'=4] {'y','zh','cx'}, dimensions={0} | all-to-all | bytes 110080 | tf_op jit(solution)/shard_map/all_to_all | solution.py:93
  191.4 14.7 %all_to_all.11 = f32[32,1,430]{2,1,0:T(1,128)S(1)} all-to-all(f32[32,1,430]{2,1,0:T(1,128)S(1)} %broadcast_in_dim.5), channel_id=1, replica_groups=mesh['y'=4,'zh'=2,'core'=2,'cx'=4,'cz'=4] {'y','zh','cx'}, dimensions={0} | all-to-all | bytes 110080 | tf_op jit(solution)/shard_map/all_to_all | solution.py:87
  206.1 4.3 %collective-permute-start.26 = (f32[32,430]{1,0:T(8,128)S(1)}, f32[32,430]{1,0:T(8,128)S(1)}, u32[]{:S(2)}, u32[]{:S(2)}) collective-permute-start(f32[32,430]{1,0:T(8,128)S(1)} %bitcast.123), channel_id=1, source_target_pairs={{0,3},{1,0},{2,1},{3,2},{4,7},{5,4},{6,5},{7,6},{8,11},{9,8},{10,9... | collective-permute-start | bytes 165128 | tf_op jit(solution)/shard_map/ppermute | solution.py:104
  210.4 1.9 collective-permute-start.27
  212.7 2.6 %collective-permute-done.27 = f32[32,430]{1,0:T(8,128)S(1)} collective-permute-done((f32[32,430]{1,0:T(8,128)S(1)}, f32[32,430]{1,0:T(8,128)S(1)}, u32[]{:S(2)}, u32[]{:S(2)}) %collective-permute-start.27) | collective-permute-done | bytes 55072 | tf_op jit(solution)/shard_map/ppermute | solution.py:104
  215.3 1.9 collective-permute-done.28
  217.3 4.9 %collective-permute-start.29 = (f32[128,430]{1,0:T(8,128)S(1)}, f32[128,430]{1,0:T(8,128)S(1)}, u32[]{:S(2)}, u32[]{:S(2)}) collective-permute-start(f32[128,430]{1,0:T(8,128)S(1)} %bitcast.121), channel_id=1, source_target_pairs={{0,16},{16,0},{1,17},{17,1},{2,18},{18,2},{3,19},{19,3},{4,20},{20... | collective-permute-start | bytes 660488 | tf_op jit(solution)/shard_map/ppermute | solution.py:98
  222.3 0.8 convolution_convert_fusion
  223.5 0.7 slice_multiply_fusion.1
  224.2 0.6 slice.53
  224.8 0.7 fusion.5
  225.6 0.8 copy.24
  (89 shorter events, 5.1 us)
Async XLA Ops:
  0.6 0.9 copy-start
  2.5 6.6 %collective-permute-start = (bf16[128,256]{1,0:T(8,128)(2,1)S(1)}, bf16[128,256]{1,0:T(8,128)(2,1)S(1)}, u32[]{:S(2)}, u32[]{:S(2)}) collective-permute-start(bf16[128,256]{1,0:T(8,128)(2,1)S(1)} %convolution_convert_fusion.1), channel_id=1, source_target_pairs={{0,3},{1,0},{2,1},{3,2},{4,7},{5,4},{6,5},{7,6},{8,11},{9,8},{10,9... | collective-permute-start | bytes 196616 | tf_op jit(solution)/shard_map/ppermute | solution.py:104
  7.8 6.8 %collective-permute-start.1 = (bf16[128,256]{1,0:T(8,128)(2,1)S(1)}, bf16[128,256]{1,0:T(8,128)(2,1)S(1)}, u32[]{:S(2)}, u32[]{:S(2)}) collective-permute-start(bf16[128,256]{1,0:T(8,128)(2,1)S(1)} %convolution_convert_fusion.1), channel_id=1, source_target_pairs={{0,2},{1,3},{2,0},{3,1},{4,6},{5,7},{6,4},{7,5},{8,10},{9,11},{10,... | collective-permute-start | bytes 196616 | tf_op jit(solution)/shard_map/ppermute | solution.py:104
  7.8 6.8 %collective-permute-start.2 = (bf16[128,256]{1,0:T(8,128)(2,1)S(1)}, bf16[128,256]{1,0:T(8,128)(2,1)S(1)}, u32[]{:S(2)}, u32[]{:S(2)}) collective-permute-start(bf16[128,256]{1,0:T(8,128)(2,1)S(1)} %convolution_convert_fusion.1), channel_id=1, source_target_pairs={{0,1},{1,2},{2,3},{3,0},{4,5},{5,6},{6,7},{7,4},{8,9},{9,10},{10,1... | collective-permute-start | bytes 196616 | tf_op jit(solution)/shard_map/ppermute | solution.py:104
  14.8 7.3 %collective-permute-start.3 = (bf16[512,256]{1,0:T(8,128)(2,1)S(1)}, bf16[512,256]{1,0:T(8,128)(2,1)S(1)}, u32[]{:S(2)}, u32[]{:S(2)}) collective-permute-start(bf16[512,256]{1,0:T(8,128)(2,1)S(1)} %bitcast.109), channel_id=1, source_target_pairs={{0,12},{4,0},{8,4},{12,8},{1,13},{5,1},{9,5},{13,9},{2,14},{6,2},{... | collective-permute-start | bytes 786440 | tf_op jit(solution)/shard_map/ppermute | solution.py:104
  16.2 7.5 %collective-permute-start.4 = (bf16[512,256]{1,0:T(8,128)(2,1)S(1)}, bf16[512,256]{1,0:T(8,128)(2,1)S(1)}, u32[]{:S(2)}, u32[]{:S(2)}) collective-permute-start(bf16[512,256]{1,0:T(8,128)(2,1)S(1)} %bitcast.110), channel_id=1, source_target_pairs={{0,8},{4,12},{8,0},{12,4},{1,9},{5,13},{9,1},{13,5},{2,10},{6,14},... | collective-permute-start | bytes 786440 | tf_op jit(solution)/shard_map/ppermute | solution.py:104
  18.5 12.4 %collective-permute-start.5 = (bf16[512,256]{1,0:T(8,128)(2,1)S(1)}, bf16[512,256]{1,0:T(8,128)(2,1)S(1)}, u32[]{:S(2)}, u32[]{:S(2)}) collective-permute-start(bf16[512,256]{1,0:T(8,128)(2,1)S(1)} %bitcast.111), channel_id=1, source_target_pairs={{0,4},{4,8},{8,12},{12,0},{1,5},{5,9},{9,13},{13,1},{2,6},{6,10},{... | collective-permute-start | bytes 786440 | tf_op jit(solution)/shard_map/ppermute | solution.py:104
  41.4 2.9 %collective-permute-start.6 = (f32[1024,256]{1,0:T(8,128)}, f32[1024,256]{1,0:T(8,128)S(1)}, u32[]{:S(2)}, u32[]{:S(2)}) collective-permute-start(f32[1024,256]{1,0:T(8,128)} %get-tuple-element.33), channel_id=1, source_target_pairs={{0,16},{16,0},{1,17},{17,1},{2,18},{18,2},{3,19},{19,3},{4,20},{20... | collective-permute-start | bytes 3145736 | tf_op jit(solution)/shard_map/ppermute | solution.py:98
  45.6 24.8 %copy-start.6 = (f32[256]{0:T(256)S(1)}, f32[256]{0:T(256)}, u32[]{:S(2)}) copy-start(f32[256]{0:T(256)} %param.15) | copy-start | bytes 3076
  45.6 24.8 %copy-start.4 = (bf16[256,172]{0,1:T(8,128)(2,1)S(1)}, bf16[256,172]{0,1:T(8,128)(2,1)}, u32[]{:S(2)}) copy-start(bf16[256,172]{0,1:T(8,128)(2,1)} %param.16) | copy-start | bytes 264196
  45.6 25.0 %copy-start.5 = (s32[128]{0:T(128)S(1)}, s32[128]{0:T(128)}, u32[]{:S(2)}) copy-start(s32[128]{0:T(128)} %param.21) | copy-start | bytes 1540
  45.7 10.1 %collective-permute-start.7 = (f32[256,256]{1,0:T(8,128)S(1)}, f32[256,256]{1,0:T(8,128)S(1)}, u32[]{:S(2)}, u32[]{:S(2)}) collective-permute-start(f32[256,256]{1,0:T(8,128)S(1)} %get-tuple-element.62), channel_id=1, source_target_pairs={{0,64},{64,128},{128,192},{192,0},{1,65},{65,129},{129,193},{193,1... | collective-permute-start | bytes 786440 | tf_op jit(solution)/shard_map/ppermute | solution.py:116
  46.8 15.6 %collective-permute-start.8 = (f32[256,256]{1,0:T(8,128)S(1)}, f32[256,256]{1,0:T(8,128)S(1)}, u32[]{:S(2)}, u32[]{:S(2)}) collective-permute-start(f32[256,256]{1,0:T(8,128)S(1)} %get-tuple-element.64), channel_id=1, source_target_pairs={{0,128},{64,192},{128,0},{192,64},{1,129},{65,193},{129,1},{193,65... | collective-permute-start | bytes 786440 | tf_op jit(solution)/shard_map/ppermute | solution.py:116
  50.7 11.6 %collective-permute-start.9 = (f32[256,256]{1,0:T(8,128)S(1)}, f32[256,256]{1,0:T(8,128)S(1)}, u32[]{:S(2)}, u32[]{:S(2)}) collective-permute-start(f32[256,256]{1,0:T(8,128)S(1)} %get-tuple-element.63), channel_id=1, source_target_pairs={{0,192},{64,0},{128,64},{192,128},{1,193},{65,1},{129,65},{193,129... | collective-permute-start | bytes 786440 | tf_op jit(solution)/shard_map/ppermute | solution.py:116
  62.4 7.9 %collective-permute-start.10 = (f32[128,256]{1,0:T(8,128)S(1)}, f32[128,256]{1,0:T(8,128)S(1)}, u32[]{:S(2)}, u32[]{:S(2)}) collective-permute-start(f32[128,256]{1,0:T(8,128)S(1)} %constant_dynamic-slice_fusion.9), channel_id=1, source_target_pairs={{0,32},{32,0},{1,33},{33,1},{2,34},{34,2},{3,35},{35,3},{4,36},{36... | collective-permute-start | bytes 393224 | tf_op jit(solution)/shard_map/ppermute | solution.py:98
  71.5 7.8 %collective-permute-start.11 = (bf16[128,256]{1,0:T(8,128)(2,1)S(1)}, bf16[128,256]{1,0:T(8,128)(2,1)S(1)}, u32[]{:S(2)}, u32[]{:S(2)}) collective-permute-start(bf16[128,256]{1,0:T(8,128)(2,1)S(1)} %get-tuple-element.76), channel_id=1, source_target_pairs={{0,32},{32,0},{1,33},{33,1},{2,34},{34,2},{3,35},{35,3},{4,36},{36... | collective-permute-start | bytes 196616 | tf_op jit(solution)/shard_map/ppermute | solution.py:104
  79.4 6.4 %collective-permute-start.12 = (bf16[256,256]{1,0:T(8,128)(2,1)S(1)}, bf16[256,256]{1,0:T(8,128)(2,1)S(1)}, u32[]{:S(2)}, u32[]{:S(2)}) collective-permute-start(bf16[256,256]{1,0:T(8,128)(2,1)S(1)} %bitcast.116), channel_id=1, source_target_pairs={{0,192},{64,0},{128,64},{192,128},{1,193},{65,1},{129,65},{193,129... | collective-permute-start | bytes 393224 | tf_op jit(solution)/shard_map/ppermute | solution.py:104
  82.5 5.4 %collective-permute-start.13 = (bf16[256,256]{1,0:T(8,128)(2,1)S(1)}, bf16[256,256]{1,0:T(8,128)(2,1)S(1)}, u32[]{:S(2)}, u32[]{:S(2)}) collective-permute-start(bf16[256,256]{1,0:T(8,128)(2,1)S(1)} %bitcast.117), channel_id=1, source_target_pairs={{0,128},{64,192},{128,0},{192,64},{1,129},{65,193},{129,1},{193,65... | collective-permute-start | bytes 393224 | tf_op jit(solution)/shard_map/ppermute | solution.py:104
  82.6 6.4 %collective-permute-start.14 = (bf16[256,256]{1,0:T(8,128)(2,1)S(1)}, bf16[256,256]{1,0:T(8,128)(2,1)S(1)}, u32[]{:S(2)}, u32[]{:S(2)}) collective-permute-start(bf16[256,256]{1,0:T(8,128)(2,1)S(1)} %bitcast.118), channel_id=1, source_target_pairs={{0,64},{64,128},{128,192},{192,0},{1,65},{65,129},{129,193},{193,1... | collective-permute-start | bytes 393224 | tf_op jit(solution)/shard_map/ppermute | solution.py:104
  89.2 7.0 %copy-start.1 = (bf16[4,256,256]{2,1,0:T(8,128)(2,1)}, bf16[4,256,256]{2,1,0:T(8,128)(2,1)S(1)}, u32[]{:S(2)}) copy-start(bf16[4,256,256]{2,1,0:T(8,128)(2,1)S(1)} %constant_dynamic-slice_fusion.8) | copy-start | bytes 1572868
  89.2 7.0 %collective-permute-start.15 = (bf16[1024,256]{1,0:T(8,128)(2,1)S(1)}, bf16[1024,256]{1,0:T(8,128)(2,1)S(1)}, u32[]{:S(2)}, u32[]{:S(2)}) collective-permute-start(bf16[1024,256]{1,0:T(8,128)(2,1)S(1)} %bitcast.114), channel_id=1, source_target_pairs={{0,16},{16,0},{1,17},{17,1},{2,18},{18,2},{3,19},{19,3},{4,20},{20... | collective-permute-start | bytes 1572872 | tf_op jit(solution)/shard_map/ppermute | solution.py:98
  96.2 0.8 copy-start.2
  107.1 26.1 %collective-permute-start.16 = (f32[512,256]{0,1:T(8,128)S(1)}, f32[512,256]{0,1:T(8,128)S(1)}, u32[]{:S(2)}, u32[]{:S(2)}) collective-permute-start(f32[512,256]{0,1:T(8,128)S(1)} %get-tuple-element.59), channel_id=1, source_target_pairs={{0,4},{4,8},{8,12},{12,0},{1,5},{5,9},{9,13},{13,1},{2,6},{6,10},{... | collective-permute-start | bytes 1572872 | tf_op jit(solution)/shard_map/ppermute | solution.py:116
  107.2 26.0 %collective-permute-start.17 = (f32[512,256]{0,1:T(8,128)S(1)}, f32[512,256]{0,1:T(8,128)S(1)}, u32[]{:S(2)}, u32[]{:S(2)}) collective-permute-start(f32[512,256]{0,1:T(8,128)S(1)} %get-tuple-element.61), channel_id=1, source_target_pairs={{0,8},{4,12},{8,0},{12,4},{1,9},{5,13},{9,1},{13,5},{2,10},{6,14},... | collective-permute-start | bytes 1572872 | tf_op jit(solution)/shard_map/ppermute | solution.py:116
  107.3 26.8 %collective-permute-start.18 = (f32[512,256]{0,1:T(8,128)S(1)}, f32[512,256]{0,1:T(8,128)S(1)}, u32[]{:S(2)}, u32[]{:S(2)}) collective-permute-start(f32[512,256]{0,1:T(8,128)S(1)} %get-tuple-element.60), channel_id=1, source_target_pairs={{0,12},{4,0},{8,4},{12,8},{1,13},{5,1},{9,5},{13,9},{2,14},{6,2},{... | collective-permute-start | bytes 1572872 | tf_op jit(solution)/shard_map/ppermute | solution.py:116
  112.4 36.0 %copy-start.3 = (bf16[128,256]{1,0:T(8,128)(2,1)S(1)}, bf16[128,256]{1,0:T(8,128)(2,1)}, u32[]{:S(2)}) copy-start(bf16[128,256]{1,0:T(8,128)(2,1)} %param.13) | copy-start | bytes 196612
  135.4 6.5 %collective-permute-start.19 = (f32[128,256]{0,1:T(8,128)S(1)}, f32[128,256]{0,1:T(8,128)S(1)}, u32[]{:S(2)}, u32[]{:S(2)}) collective-permute-start(f32[128,256]{0,1:T(8,128)S(1)} %get-tuple-element.65), channel_id=1, source_target_pairs={{0,1},{1,2},{2,3},{3,0},{4,5},{5,6},{6,7},{7,4},{8,9},{9,10},{10,1... | collective-permute-start | bytes 393224 | tf_op jit(solution)/shard_map/ppermute | solution.py:116
  137.1 11.2 %collective-permute-start.20 = (f32[128,256]{0,1:T(8,128)S(1)}, f32[128,256]{0,1:T(8,128)S(1)}, u32[]{:S(2)}, u32[]{:S(2)}) collective-permute-start(f32[128,256]{0,1:T(8,128)S(1)} %get-tuple-element.67), channel_id=1, source_target_pairs={{0,2},{1,3},{2,0},{3,1},{4,6},{5,7},{6,4},{7,5},{8,10},{9,11},{10,... | collective-permute-start | bytes 393224 | tf_op jit(solution)/shard_map/ppermute | solution.py:116
  137.2 11.2 %collective-permute-start.21 = (f32[128,256]{0,1:T(8,128)S(1)}, f32[128,256]{0,1:T(8,128)S(1)}, u32[]{:S(2)}, u32[]{:S(2)}) collective-permute-start(f32[128,256]{0,1:T(8,128)S(1)} %get-tuple-element.66), channel_id=1, source_target_pairs={{0,3},{1,0},{2,1},{3,2},{4,7},{5,4},{6,5},{7,6},{8,11},{9,8},{10,9... | collective-permute-start | bytes 393224 | tf_op jit(solution)/shard_map/ppermute | solution.py:116
  148.6 1.8 collective-permute-start.22
  150.7 9.2 %collective-permute-start.23 = (f32[32,430]{0,1:T(8,128)S(1)}, f32[32,430]{0,1:T(8,128)S(1)}, u32[]{:S(2)}, u32[]{:S(2)}) collective-permute-start(f32[32,430]{0,1:T(8,128)S(1)} %get-tuple-element.68), channel_id=1, source_target_pairs={{0,1},{1,2},{2,3},{3,0},{4,5},{5,6},{6,7},{7,4},{8,9},{9,10},{10,1... | collective-permute-start | bytes 165128 | tf_op jit(solution)/shard_map/ppermute | solution.py:116
  153.8 16.1 %collective-permute-start.24 = (f32[32,430]{0,1:T(8,128)S(1)}, f32[32,430]{0,1:T(8,128)S(1)}, u32[]{:S(2)}, u32[]{:S(2)}) collective-permute-start(f32[32,430]{0,1:T(8,128)S(1)} %get-tuple-element.70), channel_id=1, source_target_pairs={{0,2},{1,3},{2,0},{3,1},{4,6},{5,7},{6,4},{7,5},{8,10},{9,11},{10,... | collective-permute-start | bytes 165128 | tf_op jit(solution)/shard_map/ppermute | solution.py:116
  154.7 15.1 %collective-permute-start.25 = (f32[32,430]{0,1:T(8,128)S(1)}, f32[32,430]{0,1:T(8,128)S(1)}, u32[]{:S(2)}, u32[]{:S(2)}) collective-permute-start(f32[32,430]{0,1:T(8,128)S(1)} %get-tuple-element.69), channel_id=1, source_target_pairs={{0,3},{1,0},{2,1},{3,2},{4,7},{5,4},{6,5},{7,6},{8,11},{9,8},{10,9... | collective-permute-start | bytes 165128 | tf_op jit(solution)/shard_map/ppermute | solution.py:116
  206.1 6.7 %collective-permute-start.26 = (f32[32,430]{1,0:T(8,128)S(1)}, f32[32,430]{1,0:T(8,128)S(1)}, u32[]{:S(2)}, u32[]{:S(2)}) collective-permute-start(f32[32,430]{1,0:T(8,128)S(1)} %bitcast.123), channel_id=1, source_target_pairs={{0,3},{1,0},{2,1},{3,2},{4,7},{5,4},{6,5},{7,6},{8,11},{9,8},{10,9... | collective-permute-start | bytes 165128 | tf_op jit(solution)/shard_map/ppermute | solution.py:104
  210.4 4.9 %collective-permute-start.27 = (f32[32,430]{1,0:T(8,128)S(1)}, f32[32,430]{1,0:T(8,128)S(1)}, u32[]{:S(2)}, u32[]{:S(2)}) collective-permute-start(f32[32,430]{1,0:T(8,128)S(1)} %bitcast.124), channel_id=1, source_target_pairs={{0,2},{1,3},{2,0},{3,1},{4,6},{5,7},{6,4},{7,5},{8,10},{9,11},{10,... | collective-permute-start | bytes 165128 | tf_op jit(solution)/shard_map/ppermute | solution.py:104
  212.3 4.9 %collective-permute-start.28 = (f32[32,430]{1,0:T(8,128)S(1)}, f32[32,430]{1,0:T(8,128)S(1)}, u32[]{:S(2)}, u32[]{:S(2)}) collective-permute-start(f32[32,430]{1,0:T(8,128)S(1)} %bitcast.125), channel_id=1, source_target_pairs={{0,1},{1,2},{2,3},{3,0},{4,5},{5,6},{6,7},{7,4},{8,9},{9,10},{10,1... | collective-permute-start | bytes 165128 | tf_op jit(solution)/shard_map/ppermute | solution.py:104
  217.3 6.1 %collective-permute-start.29 = (f32[128,430]{1,0:T(8,128)S(1)}, f32[128,430]{1,0:T(8,128)S(1)}, u32[]{:S(2)}, u32[]{:S(2)}) collective-permute-start(f32[128,430]{1,0:T(8,128)S(1)} %bitcast.121), channel_id=1, source_target_pairs={{0,16},{16,0},{1,17},{17,1},{2,18},{18,2},{3,19},{19,3},{4,20},{20... | collective-permute-start | bytes 660488 | tf_op jit(solution)/shard_map/ppermute | solution.py:98

commit v14 on v12

--- a/solution.py
+++ b/solution.py
@@ -183,7 +183,7 @@
     summed = mine + swap_core(other)
     agg = pair_scatter(ring_scatter(summed, "y"), "zh")
     loss_sum, out_term, bias_term, grad_z = head_block(agg, bias, w_out, labels)
-    gathered = ring_gather(ring_gather(grad_z, "zh"), "y")
+    gathered = gather_rows(grad_z, ("y", "zh"))
     sources = (gathered, swap_core(gathered))
     back_part = tile_product(tile_block, row_pos, col_ids, live_count, sources, col_tiles, True)
     grad_proj = ring_scatter(ring_scatter(back_part, "cx"), "cz").astype(jnp.bfloat16)

time: 206 us -> 210 us (1.019)
  blocking collectives: 46.7 us -> 66.1 us
  waiting for transfers between devices: 73.7 us -> 61.1 us
  Pallas kernels: 17.3 us -> 15.2 us
    all_to_all x1 -> x2, blocking collectives: 19.2 us -> 39.8 us  [gather_rows(): got = lax.all_to_all(spread, axis, 0, 0, tiled=False)]
    ppermute x10 -> x6, waiting for transfers between devices: 27 us -> 18.1 us  [ring_gather(): lax.ppermute(x, axis, [(i, (i + k) % n) for i in range(n)])]
    ppermute x10 -> x6, starting transfers between devices: 16.8 us -> 8.25 us  [ring_gather(): lax.ppermute(x, axis, [(i, (i + k) % n) for i in range(n)])]
    ppermute x5, starting transfers between devices: 13.8 us -> 18.1 us  [swap_core(): return lax.ppermute(x, axis, [(0, 1), (1, 0)])]
    ppermute x9, starting transfers between devices: 14.4 us -> 18.6 us  [ring_scatter(): lax.ppermute(piece, axis, [(i, (i + k) % n) for i in range(n)])]
    ppermute x9, waiting for transfers between devices: 38.2 us -> 34.6 us  [ring_scatter(): lax.ppermute(piece, axis, [(i, (i + k) % n) for i in range(n)])]
  transfers between devices with their start and end apart: 24 -> 20, of which waited for: 20 -> 17; matrix products, arithmetic and copies ran while one was open for 2% -> 2% of each run, Pallas kernels for 0% -> 0%
where the time goes in v14:
time: 210 us; the launch traced here: 209 us
  blocking collectives  66.1 us (31%)
  waiting for transfers between devices  61.1 us (29%)
  starting transfers between devices  44.9 us (21%)
  Pallas kernels  15.2 us (7%)
  local copies, waits for them, and re-layouts  9.59 us (5%)
  other arithmetic  6.28 us (3%)
  between operations  3.41 us (2%)
  matrix products  2.57 us (1%)
    all_to_all x2, blocking collectives, gather_rows(): got = lax.all_to_all(spread, axis, 0, 0, tiled=False)  39.8 us
    ppermute x9, waiting for transfers between devices, ring_scatter(): lax.ppermute(piece, axis, [(i, (i + k) % n) for i in range(n)])  34.6 us
    all_to_all x1, blocking collectives, scatter_rows(): got = lax.all_to_all(x.reshape(n, -1, x.shape[1]), axis, 0, 0, tiled=False)  26.3 us
    ppermute x9, starting transfers between devices, ring_scatter(): lax.ppermute(piece, axis, [(i, (i + k) % n) for i in range(n)])  18.6 us
    ppermute x6, waiting for transfers between devices, ring_gather(): lax.ppermute(x, axis, [(i, (i + k) % n) for i in range(n)])  18.1 us
    ppermute x5, starting transfers between devices, swap_core(): return lax.ppermute(x, axis, [(0, 1), (1, 0)])  18.1 us
    pallas_call x2, Pallas kernels, tile_product(): pl.pallas_call(lambda *refs: _dense_kernel(transpose, *refs), grid_spec=g...  15.2 us
    ppermute x5, waiting for transfers between devices, swap_core(): return lax.ppermute(x, axis, [(0, 1), (1, 0)])  8.42 us
  transfers between devices with their start and end apart: 20, of which 17 were waited for; matrix products, arithmetic and copies ran while one was open for 2% of the time, Pallas kernels for 0%

profile of v14, /device:TPU:1, one launch (start us, length us, event | category | flops | bytes accessed | tf_op | source)
XLA Modules:
  0.0 209.2 jit_solution(14496389276274437627)
XLA Ops:
  0.6 0.9 copy-done
  1.5 1.0 convolution_convert_fusion.1
  2.5 5.2 %collective-permute-start = (bf16[128,256]{1,0:T(8,128)(2,1)S(1)}, bf16[128,256]{1,0:T(8,128)(2,1)S(1)}, u32[]{:S(2)}, u32[]{:S(2)}) collective-permute-start(bf16[128,256]{1,0:T(8,128)(2,1)S(1)} %convolution_convert_fusion.1), channel_id=1, source_target_pairs={{0,3},{1,0},{2,1},{3,2},{4,7},{5,4},{6,5},{7,6},{8,11},{9,8},{10,9... | collective-permute-start | bytes 196616 | tf_op jit(solution)/shard_map/ppermute | solution.py:104
  7.8 0.4 collective-permute-start.2
  8.2 0.9 collective-permute-done
  9.1 5.5 %collective-permute-done.1 = bf16[128,256]{1,0:T(8,128)(2,1)S(1)} collective-permute-done((bf16[128,256]{1,0:T(8,128)(2,1)S(1)}, bf16[128,256]{1,0:T(8,128)(2,1)S(1)}, u32[]{:S(2)}, u32[]{:S(2)}) %collective-permute-start.1) | collective-permute-done | bytes 65568 | tf_op jit(solution)/shard_map/ppermute | solution.py:104
  14.8 1.4 collective-permute-start.3
  16.2 0.5 collective-permute-start.4
  16.7 1.2 compare_select_fusion.refs_0_
  18.5 0.7 collective-permute-start.5
  19.2 2.8 %collective-permute-done.3 = bf16[512,256]{1,0:T(8,128)(2,1)S(1)} collective-permute-done((bf16[512,256]{1,0:T(8,128)(2,1)S(1)}, bf16[512,256]{1,0:T(8,128)(2,1)S(1)}, u32[]{:S(2)}, u32[]{:S(2)}) %collective-permute-start.3) | collective-permute-done | bytes 262176 | tf_op jit(solution)/shard_map/ppermute | solution.py:104
  22.1 1.6 collective-permute-done.4
  23.7 7.2 %collective-permute-done.5 = bf16[512,256]{1,0:T(8,128)(2,1)S(1)} collective-permute-done((bf16[512,256]{1,0:T(8,128)(2,1)S(1)}, bf16[512,256]{1,0:T(8,128)(2,1)S(1)}, u32[]{:S(2)}, u32[]{:S(2)}) %collective-permute-start.5) | collective-permute-done | bytes 262176 | tf_op jit(solution)/shard_map/ppermute | solution.py:104
  31.1 1.1 constant_dynamic-slice_fusion.7
  32.2 0.6 broadcast_in_dim.6.refs_5_
  32.7 7.6 %shard_map.128 = (f32[1024,256]{1,0:T(8,128)}, f32[1024,256]{1,0:T(8,128)}) custom-call(s32[128]{0:T(128)} %compare_select_fusion.refs_0_, s32[128]{0:T(128)} %bitcast.87, s32[1]{0:T(128)} %bitcast.73.refs_2_, bf16[128,128,128]{2,1,0:T(8,128)(2,1)} %bitcast.75, bf16[2048,256]{1,0:T(8,128)(2,1)} %bitcast.77, bf16[8,128]{1,0:T(8,128)(2,1)} %broadcast_in_dim.6.refs_5_), custom_call_target="tpu_custom_call" | custom-call | tf_op jit(solution)/shard_map/pallas_call | solution.py:73
  40.3 2.1 %collective-permute-start.6 = (f32[1024,256]{1,0:T(8,128)}, f32[1024,256]{1,0:T(8,128)S(1)}, u32[]{:S(2)}, u32[]{:S(2)}) collective-permute-start(f32[1024,256]{1,0:T(8,128)} %get-tuple-element.33), channel_id=1, source_target_pairs={{0,16},{16,0},{1,17},{17,1},{2,18},{18,2},{3,19},{19,3},{4,20},{20... | collective-permute-start | bytes 3145736 | tf_op jit(solution)/shard_map/ppermute | solution.py:98
  42.4 2.5 %collective-permute-done.6 = f32[1024,256]{1,0:T(8,128)S(1)} collective-permute-done((f32[1024,256]{1,0:T(8,128)}, f32[1024,256]{1,0:T(8,128)S(1)}, u32[]{:S(2)}, u32[]{:S(2)}) %collective-permute-start.6) | collective-permute-done | bytes 1048608 | tf_op jit(solution)/shard_map/ppermute | solution.py:98
  44.9 1.4 add.199
  46.4 0.3 collective-permute-start.7
  46.7 3.9 %collective-permute-start.8 = (f32[256,256]{1,0:T(8,128)S(1)}, f32[256,256]{1,0:T(8,128)S(1)}, u32[]{:S(2)}, u32[]{:S(2)}) collective-permute-start(f32[256,256]{1,0:T(8,128)S(1)} %get-tuple-element.59), channel_id=1, source_target_pairs={{0,128},{64,192},{128,0},{192,64},{1,129},{65,193},{129,1},{193,65... | collective-permute-start | bytes 786440 | tf_op jit(solution)/shard_map/ppermute | solution.py:116
  50.6 0.3 collective-permute-start.9
  51.0 4.8 %collective-permute-done.7 = f32[256,256]{1,0:T(8,128)S(1)} collective-permute-done((f32[256,256]{1,0:T(8,128)S(1)}, f32[256,256]{1,0:T(8,128)S(1)}, u32[]{:S(2)}, u32[]{:S(2)}) %collective-permute-start.7) | collective-permute-done | bytes 262176 | tf_op jit(solution)/shard_map/ppermute | solution.py:116
  55.8 6.5 %collective-permute-done.8 = f32[256,256]{1,0:T(8,128)S(1)} collective-permute-done((f32[256,256]{1,0:T(8,128)S(1)}, f32[256,256]{1,0:T(8,128)S(1)}, u32[]{:S(2)}, u32[]{:S(2)}) %collective-permute-start.8) | collective-permute-done | bytes 262176 | tf_op jit(solution)/shard_map/ppermute | solution.py:116
  62.4 4.9 %collective-permute-start.10 = (f32[128,256]{1,0:T(8,128)S(1)}, f32[128,256]{1,0:T(8,128)S(1)}, u32[]{:S(2)}, u32[]{:S(2)}) collective-permute-start(f32[128,256]{1,0:T(8,128)S(1)} %constant_dynamic-slice_fusion.3), channel_id=1, source_target_pairs={{0,32},{32,0},{1,33},{33,1},{2,34},{34,2},{3,35},{35,3},{4,36},{36... | collective-permute-start | bytes 393224 | tf_op jit(solution)/shard_map/ppermute | solution.py:98
  67.3 3.0 %collective-permute-done.10 = f32[128,256]{1,0:T(8,128)S(1)} collective-permute-done((f32[128,256]{1,0:T(8,128)S(1)}, f32[128,256]{1,0:T(8,128)S(1)}, u32[]{:S(2)}, u32[]{:S(2)}) %collective-permute-start.10) | collective-permute-done | bytes 131104 | tf_op jit(solution)/shard_map/ppermute | solution.py:98
  70.4 0.2 fusion.4
  70.6 0.6 subtract_reduce_fusion
  71.2 0.2 convert_reduce_fusion
  71.5 20.6 %all_to_all.15 = bf16[8,128,256]{2,1,0:T(8,128)(2,1)S(1)} all-to-all(bf16[8,128,256]{2,1,0:T(8,128)(2,1)S(1)} %broadcast_in_dim.7), channel_id=1, replica_groups=mesh['y'=4,'zh'=2,'core'=2,'cx'=4,'cz'=4] {'y','zh'}, dimensions={0} | all-to-all | bytes 1048576 | tf_op jit(solution)/shard_map/all_to_all | solution.py:87
  92.1 4.9 %collective-permute-start.11 = (bf16[1024,256]{1,0:T(8,128)(2,1)S(1)}, bf16[1024,256]{1,0:T(8,128)(2,1)S(1)}, u32[]{:S(2)}, u32[]{:S(2)}) collective-permute-start(bf16[1024,256]{1,0:T(8,128)(2,1)S(1)} %bitcast.83), channel_id=1, source_target_pairs={{0,16},{16,0},{1,17},{17,1},{2,18},{18,2},{3,19},{19,3},{4,20},{20... | collective-permute-start | bytes 1572872 | tf_op jit(solution)/shard_map/ppermute | solution.py:98
  97.0 1.5 collective-permute-done.11.refs_5_
  98.5 0.8 copy-done.2
  99.3 7.6 %shard_map.129 = (f32[256,2048]{1,0:T(8,128)}, f32[8,128]{1,0:T(8,128)}) custom-call(s32[128]{0:T(128)} %compare_select_fusion.refs_0_, s32[128]{0:T(128)} %bitcast.88, s32[1]{0:T(128)} %bitcast.74.refs_2_, bf16[128,128,128]{2,1,0:T(8,128)(2,1)} %bitcast.76, bf16[1024,256]{1,0:T(8,128)(2,1)} %bitcast.84, bf16[1024,256]{1,0:T(8,128)(2,1)} %copy-done.2), custom_call_target="tpu_custom_call" | custom-call | tf_op jit(solution)/shard_map/pallas_call | solution.py:73
  107.0 1.5 dynamic-slice_bitcast_fusion.2
  108.5 2.5 %collective-permute-start.13 = (f32[512,256]{0,1:T(8,128)S(1)}, f32[512,256]{0,1:T(8,128)S(1)}, u32[]{:S(2)}, u32[]{:S(2)}) collective-permute-start(f32[512,256]{0,1:T(8,128)S(1)} %get-tuple-element.56), channel_id=1, source_target_pairs={{0,8},{4,12},{8,0},{12,4},{1,9},{5,13},{9,1},{13,5},{2,10},{6,14},... | collective-permute-start | bytes 1572872 | tf_op jit(solution)/shard_map/ppermute | solution.py:116
  111.0 0.2 collective-permute-start.14
  111.2 0.6 fusion.3
  111.8 2.0 scatter.9
  113.8 8.0 %collective-permute-done.12 = f32[512,256]{0,1:T(8,128)S(1)} collective-permute-done((f32[512,256]{0,1:T(8,128)S(1)}, f32[512,256]{0,1:T(8,128)S(1)}, u32[]{:S(2)}, u32[]{:S(2)}) %collective-permute-start.12) | collective-permute-done | bytes 524320 | tf_op jit(solution)/shard_map/ppermute | solution.py:116
  121.8 11.9 %collective-permute-done.13 = f32[512,256]{0,1:T(8,128)S(1)} collective-permute-done((f32[512,256]{0,1:T(8,128)S(1)}, f32[512,256]{0,1:T(8,128)S(1)}, u32[]{:S(2)}, u32[]{:S(2)}) %collective-permute-start.13) | collective-permute-done | bytes 524320 | tf_op jit(solution)/shard_map/ppermute | solution.py:116
  133.8 1.3 fusion.1
  135.1 6.5 %collective-permute-start.15 = (f32[128,256]{0,1:T(8,128)S(1)}, f32[128,256]{0,1:T(8,128)S(1)}, u32[]{:S(2)}, u32[]{:S(2)}) collective-permute-start(f32[128,256]{0,1:T(8,128)S(1)} %get-tuple-element.60), channel_id=1, source_target_pairs={{0,1},{1,2},{2,3},{3,0},{4,5},{5,6},{6,7},{7,4},{8,9},{9,10},{10,1... | collective-permute-start | bytes 393224 | tf_op jit(solution)/shard_map/ppermute | solution.py:116
  141.6 2.5 %collective-permute-start.16 = (f32[128,256]{0,1:T(8,128)S(1)}, f32[128,256]{0,1:T(8,128)S(1)}, u32[]{:S(2)}, u32[]{:S(2)}) collective-permute-start(f32[128,256]{0,1:T(8,128)S(1)} %get-tuple-element.62), channel_id=1, source_target_pairs={{0,2},{1,3},{2,0},{3,1},{4,6},{5,7},{6,4},{7,5},{8,10},{9,11},{10,... | collective-permute-start | bytes 393224 | tf_op jit(solution)/shard_map/ppermute | solution.py:116
  144.1 2.3 %collective-permute-start.17 = (f32[128,256]{0,1:T(8,128)S(1)}, f32[128,256]{0,1:T(8,128)S(1)}, u32[]{:S(2)}, u32[]{:S(2)}) collective-permute-start(f32[128,256]{0,1:T(8,128)S(1)} %get-tuple-element.61), channel_id=1, source_target_pairs={{0,3},{1,0},{2,1},{3,2},{4,7},{5,4},{6,5},{7,6},{8,11},{9,8},{10,9... | collective-permute-start | bytes 393224 | tf_op jit(solution)/shard_map/ppermute | solution.py:116
  146.4 0.2 fusion.2
  146.6 0.2 collective-permute-done.16
  146.8 3.0 %collective-permute-done.17 = f32[128,256]{0,1:T(8,128)S(1)} collective-permute-done((f32[128,256]{0,1:T(8,128)S(1)}, f32[128,256]{0,1:T(8,128)S(1)}, u32[]{:S(2)}, u32[]{:S(2)}) %collective-permute-start.17) | collective-permute-done | bytes 131104 | tf_op jit(solution)/shard_map/ppermute | solution.py:116
  149.9 0.2 convolution_bitcast_fusion
  150.1 3.1 %collective-permute-start.18 = (f32[128,430]{0,1:T(8,128)S(1)}, f32[128,430]{0,1:T(8,128)S(1)}, u32[]{:S(2)}, u32[]{:S(2)}) collective-permute-start(f32[128,430]{0,1:T(8,128)S(1)} %slice_select_fusion), channel_id=1, source_target_pairs={{0,16},{16,0},{1,17},{17,1},{2,18},{18,2},{3,19},{19,3},{4,20},{20... | collective-permute-start | bytes 660488 | tf_op jit(solution)/shard_map/ppermute | solution.py:98
  153.2 1.1 collective-permute-done.18
  154.3 0.1 copy.17
  154.5 26.3 %all_to_all.16 = f32[128,1,430]{2,1,0:T(1,128)S(1)} all-to-all(f32[128,1,430]{2,1,0:T(1,128)S(1)} %copy.17), channel_id=1, replica_groups=mesh['y'=4,'zh'=2,'core'=2,'cx'=4,'cz'=4] {'y','zh','cx','cz'}, dimensions={0} | all-to-all | bytes 440320 | tf_op jit(solution)/shard_map/all_to_all | solution.py:93
  180.8 0.2 reduce_sum.49
  181.1 0.1 broadcast_in_dim.8
  181.2 19.2 %all_to_all.17 = f32[128,1,430]{2,1,0:T(1,128)S(1)} all-to-all(f32[128,1,430]{2,1,0:T(1,128)S(1)} %broadcast_in_dim.8), channel_id=1, replica_groups=mesh['y'=4,'zh'=2,'core'=2,'cx'=4,'cz'=4] {'y','zh','cx','cz'}, dimensions={0} | all-to-all | bytes 440320 | tf_op jit(solution)/shard_map/all_to_all | solution.py:87
  200.4 0.1 copy.18
  200.5 3.2 %collective-permute-start.19 = (f32[128,430]{0,1:T(8,128)S(1)}, f32[128,430]{0,1:T(8,128)S(1)}, u32[]{:S(2)}, u32[]{:S(2)}) collective-permute-start(f32[128,430]{0,1:T(8,128)S(1)} %bitcast.85), channel_id=1, source_target_pairs={{0,16},{16,0},{1,17},{17,1},{2,18},{18,2},{3,19},{19,3},{4,20},{20... | collective-permute-start | bytes 660488 | tf_op jit(solution)/shard_map/ppermute | solution.py:98
  203.7 0.8 convolution_convert_fusion
  204.5 0.3 collective-permute-done.19
  204.8 0.7 slice_multiply_fusion.1
  205.5 0.5 slice.65
  206.0 0.6 slice_multiply_fusion.2
  206.6 0.8 copy.19
  (50 shorter events, 1.0 us)
Async XLA Ops:
  0.6 0.9 copy-start
  2.5 6.6 %collective-permute-start = (bf16[128,256]{1,0:T(8,128)(2,1)S(1)}, bf16[128,256]{1,0:T(8,128)(2,1)S(1)}, u32[]{:S(2)}, u32[]{:S(2)}) collective-permute-start(bf16[128,256]{1,0:T(8,128)(2,1)S(1)} %convolution_convert_fusion.1), channel_id=1, source_target_pairs={{0,3},{1,0},{2,1},{3,2},{4,7},{5,4},{6,5},{7,6},{8,11},{9,8},{10,9... | collective-permute-start | bytes 196616 | tf_op jit(solution)/shard_map/ppermute | solution.py:104
  7.8 6.8 %collective-permute-start.1 = (bf16[128,256]{1,0:T(8,128)(2,1)S(1)}, bf16[128,256]{1,0:T(8,128)(2,1)S(1)}, u32[]{:S(2)}, u32[]{:S(2)}) collective-permute-start(bf16[128,256]{1,0:T(8,128)(2,1)S(1)} %convolution_convert_fusion.1), channel_id=1, source_target_pairs={{0,2},{1,3},{2,0},{3,1},{4,6},{5,7},{6,4},{7,5},{8,10},{9,11},{10,... | collective-permute-start | bytes 196616 | tf_op jit(solution)/shard_map/ppermute | solution.py:104
  7.8 6.8 %collective-permute-start.2 = (bf16[128,256]{1,0:T(8,128)(2,1)S(1)}, bf16[128,256]{1,0:T(8,128)(2,1)S(1)}, u32[]{:S(2)}, u32[]{:S(2)}) collective-permute-start(bf16[128,256]{1,0:T(8,128)(2,1)S(1)} %convolution_convert_fusion.1), channel_id=1, source_target_pairs={{0,1},{1,2},{2,3},{3,0},{4,5},{5,6},{6,7},{7,4},{8,9},{9,10},{10,1... | collective-permute-start | bytes 196616 | tf_op jit(solution)/shard_map/ppermute | solution.py:104
  14.8 7.3 %collective-permute-start.3 = (bf16[512,256]{1,0:T(8,128)(2,1)S(1)}, bf16[512,256]{1,0:T(8,128)(2,1)S(1)}, u32[]{:S(2)}, u32[]{:S(2)}) collective-permute-start(bf16[512,256]{1,0:T(8,128)(2,1)S(1)} %bitcast.78), channel_id=1, source_target_pairs={{0,12},{4,0},{8,4},{12,8},{1,13},{5,1},{9,5},{13,9},{2,14},{6,2},{... | collective-permute-start | bytes 786440 | tf_op jit(solution)/shard_map/ppermute | solution.py:104
  16.2 7.5 %collective-permute-start.4 = (bf16[512,256]{1,0:T(8,128)(2,1)S(1)}, bf16[512,256]{1,0:T(8,128)(2,1)S(1)}, u32[]{:S(2)}, u32[]{:S(2)}) collective-permute-start(bf16[512,256]{1,0:T(8,128)(2,1)S(1)} %bitcast.79), channel_id=1, source_target_pairs={{0,8},{4,12},{8,0},{12,4},{1,9},{5,13},{9,1},{13,5},{2,10},{6,14},... | collective-permute-start | bytes 786440 | tf_op jit(solution)/shard_map/ppermute | solution.py:104
  18.5 12.4 %collective-permute-start.5 = (bf16[512,256]{1,0:T(8,128)(2,1)S(1)}, bf16[512,256]{1,0:T(8,128)(2,1)S(1)}, u32[]{:S(2)}, u32[]{:S(2)}) collective-permute-start(bf16[512,256]{1,0:T(8,128)(2,1)S(1)} %bitcast.80), channel_id=1, source_target_pairs={{0,4},{4,8},{8,12},{12,0},{1,5},{5,9},{9,13},{13,1},{2,6},{6,10},{... | collective-permute-start | bytes 786440 | tf_op jit(solution)/shard_map/ppermute | solution.py:104
  40.3 4.6 %collective-permute-start.6 = (f32[1024,256]{1,0:T(8,128)}, f32[1024,256]{1,0:T(8,128)S(1)}, u32[]{:S(2)}, u32[]{:S(2)}) collective-permute-start(f32[1024,256]{1,0:T(8,128)} %get-tuple-element.33), channel_id=1, source_target_pairs={{0,16},{16,0},{1,17},{17,1},{2,18},{18,2},{3,19},{19,3},{4,20},{20... | collective-permute-start | bytes 3145736 | tf_op jit(solution)/shard_map/ppermute | solution.py:98
  46.3 24.0 %copy-start.6 = (f32[256]{0:T(256)S(1)}, f32[256]{0:T(256)}, u32[]{:S(2)}) copy-start(f32[256]{0:T(256)} %param.15) | copy-start | bytes 3076
  46.3 24.1 %copy-start.4 = (bf16[256,172]{0,1:T(8,128)(2,1)S(1)}, bf16[256,172]{0,1:T(8,128)(2,1)}, u32[]{:S(2)}) copy-start(bf16[256,172]{0,1:T(8,128)(2,1)} %param.16) | copy-start | bytes 264196
  46.3 24.2 %copy-start.5 = (s32[128]{0:T(128)S(1)}, s32[128]{0:T(128)}, u32[]{:S(2)}) copy-start(s32[128]{0:T(128)} %param.21) | copy-start | bytes 1540
  46.4 9.4 %collective-permute-start.7 = (f32[256,256]{1,0:T(8,128)S(1)}, f32[256,256]{1,0:T(8,128)S(1)}, u32[]{:S(2)}, u32[]{:S(2)}) collective-permute-start(f32[256,256]{1,0:T(8,128)S(1)} %get-tuple-element.57), channel_id=1, source_target_pairs={{0,64},{64,128},{128,192},{192,0},{1,65},{65,129},{129,193},{193,1... | collective-permute-start | bytes 786440 | tf_op jit(solution)/shard_map/ppermute | solution.py:116
  46.7 15.6 %collective-permute-start.8 = (f32[256,256]{1,0:T(8,128)S(1)}, f32[256,256]{1,0:T(8,128)S(1)}, u32[]{:S(2)}, u32[]{:S(2)}) collective-permute-start(f32[256,256]{1,0:T(8,128)S(1)} %get-tuple-element.59), channel_id=1, source_target_pairs={{0,128},{64,192},{128,0},{192,64},{1,129},{65,193},{129,1},{193,65... | collective-permute-start | bytes 786440 | tf_op jit(solution)/shard_map/ppermute | solution.py:116
  50.6 11.6 %collective-permute-start.9 = (f32[256,256]{1,0:T(8,128)S(1)}, f32[256,256]{1,0:T(8,128)S(1)}, u32[]{:S(2)}, u32[]{:S(2)}) collective-permute-start(f32[256,256]{1,0:T(8,128)S(1)} %get-tuple-element.58), channel_id=1, source_target_pairs={{0,192},{64,0},{128,64},{192,128},{1,193},{65,1},{129,65},{193,129... | collective-permute-start | bytes 786440 | tf_op jit(solution)/shard_map/ppermute | solution.py:116
  62.4 7.9 %collective-permute-start.10 = (f32[128,256]{1,0:T(8,128)S(1)}, f32[128,256]{1,0:T(8,128)S(1)}, u32[]{:S(2)}, u32[]{:S(2)}) collective-permute-start(f32[128,256]{1,0:T(8,128)S(1)} %constant_dynamic-slice_fusion.3), channel_id=1, source_target_pairs={{0,32},{32,0},{1,33},{33,1},{2,34},{34,2},{3,35},{35,3},{4,36},{36... | collective-permute-start | bytes 393224 | tf_op jit(solution)/shard_map/ppermute | solution.py:98
  92.1 6.4 %copy-start.1 = (bf16[8,128,256]{2,1,0:T(8,128)(2,1)}, bf16[8,128,256]{2,1,0:T(8,128)(2,1)S(1)}, u32[]{:S(2)}) copy-start(bf16[8,128,256]{2,1,0:T(8,128)(2,1)S(1)} %all_to_all.15) | copy-start | bytes 1572868
  92.1 6.4 %collective-permute-start.11 = (bf16[1024,256]{1,0:T(8,128)(2,1)S(1)}, bf16[1024,256]{1,0:T(8,128)(2,1)S(1)}, u32[]{:S(2)}, u32[]{:S(2)}) collective-permute-start(bf16[1024,256]{1,0:T(8,128)(2,1)S(1)} %bitcast.83), channel_id=1, source_target_pairs={{0,16},{16,0},{1,17},{17,1},{2,18},{18,2},{3,19},{19,3},{4,20},{20... | collective-permute-start | bytes 1572872 | tf_op jit(solution)/shard_map/ppermute | solution.py:98
  98.5 0.8 copy-start.2
  108.4 13.4 %collective-permute-start.12 = (f32[512,256]{0,1:T(8,128)S(1)}, f32[512,256]{0,1:T(8,128)S(1)}, u32[]{:S(2)}, u32[]{:S(2)}) collective-permute-start(f32[512,256]{0,1:T(8,128)S(1)} %get-tuple-element.54), channel_id=1, source_target_pairs={{0,4},{4,8},{8,12},{12,0},{1,5},{5,9},{9,13},{13,1},{2,6},{6,10},{... | collective-permute-start | bytes 1572872 | tf_op jit(solution)/shard_map/ppermute | solution.py:116
  108.5 25.2 %collective-permute-start.13 = (f32[512,256]{0,1:T(8,128)S(1)}, f32[512,256]{0,1:T(8,128)S(1)}, u32[]{:S(2)}, u32[]{:S(2)}) collective-permute-start(f32[512,256]{0,1:T(8,128)S(1)} %get-tuple-element.56), channel_id=1, source_target_pairs={{0,8},{4,12},{8,0},{12,4},{1,9},{5,13},{9,1},{13,5},{2,10},{6,14},... | collective-permute-start | bytes 1572872 | tf_op jit(solution)/shard_map/ppermute | solution.py:116
  111.0 22.8 %collective-permute-start.14 = (f32[512,256]{0,1:T(8,128)S(1)}, f32[512,256]{0,1:T(8,128)S(1)}, u32[]{:S(2)}, u32[]{:S(2)}) collective-permute-start(f32[512,256]{0,1:T(8,128)S(1)} %get-tuple-element.55), channel_id=1, source_target_pairs={{0,12},{4,0},{8,4},{12,8},{1,13},{5,1},{9,5},{13,9},{2,14},{6,2},{... | collective-permute-start | bytes 1572872 | tf_op jit(solution)/shard_map/ppermute | solution.py:116
  113.8 36.1 %copy-start.3 = (bf16[128,256]{1,0:T(8,128)(2,1)S(1)}, bf16[128,256]{1,0:T(8,128)(2,1)}, u32[]{:S(2)}) copy-start(bf16[128,256]{1,0:T(8,128)(2,1)} %param.13) | copy-start | bytes 196612
  135.1 11.4 %collective-permute-start.15 = (f32[128,256]{0,1:T(8,128)S(1)}, f32[128,256]{0,1:T(8,128)S(1)}, u32[]{:S(2)}, u32[]{:S(2)}) collective-permute-start(f32[128,256]{0,1:T(8,128)S(1)} %get-tuple-element.60), channel_id=1, source_target_pairs={{0,1},{1,2},{2,3},{3,0},{4,5},{5,6},{6,7},{7,4},{8,9},{9,10},{10,1... | collective-permute-start | bytes 393224 | tf_op jit(solution)/shard_map/ppermute | solution.py:116
  141.6 5.2 %collective-permute-start.16 = (f32[128,256]{0,1:T(8,128)S(1)}, f32[128,256]{0,1:T(8,128)S(1)}, u32[]{:S(2)}, u32[]{:S(2)}) collective-permute-start(f32[128,256]{0,1:T(8,128)S(1)} %get-tuple-element.62), channel_id=1, source_target_pairs={{0,2},{1,3},{2,0},{3,1},{4,6},{5,7},{6,4},{7,5},{8,10},{9,11},{10,... | collective-permute-start | bytes 393224 | tf_op jit(solution)/shard_map/ppermute | solution.py:116
  144.1 5.7 %collective-permute-start.17 = (f32[128,256]{0,1:T(8,128)S(1)}, f32[128,256]{0,1:T(8,128)S(1)}, u32[]{:S(2)}, u32[]{:S(2)}) collective-permute-start(f32[128,256]{0,1:T(8,128)S(1)} %get-tuple-element.61), channel_id=1, source_target_pairs={{0,3},{1,0},{2,1},{3,2},{4,7},{5,4},{6,5},{7,6},{8,11},{9,8},{10,9... | collective-permute-start | bytes 393224 | tf_op jit(solution)/shard_map/ppermute | solution.py:116
  150.1 4.2 %collective-permute-start.18 = (f32[128,430]{0,1:T(8,128)S(1)}, f32[128,430]{0,1:T(8,128)S(1)}, u32[]{:S(2)}, u32[]{:S(2)}) collective-permute-start(f32[128,430]{0,1:T(8,128)S(1)} %slice_select_fusion), channel_id=1, source_target_pairs={{0,16},{16,0},{1,17},{17,1},{2,18},{18,2},{3,19},{19,3},{4,20},{20... | collective-permute-start | bytes 660488 | tf_op jit(solution)/shard_map/ppermute | solution.py:98
  200.5 4.3 %collective-permute-start.19 = (f32[128,430]{0,1:T(8,128)S(1)}, f32[128,430]{0,1:T(8,128)S(1)}, u32[]{:S(2)}, u32[]{:S(2)}) collective-permute-start(f32[128,430]{0,1:T(8,128)S(1)} %bitcast.85), channel_id=1, source_target_pairs={{0,16},{16,0},{1,17},{17,1},{2,18},{18,2},{3,19},{19,3},{4,20},{20... | collective-permute-start | bytes 660488 | tf_op jit(solution)/shard_map/ppermute | solution.py:98

commit v15 on v13

--- a/solution.py
+++ b/solution.py
@@ -8,7 +8,7 @@
 from jax.sharding import Mesh, PartitionSpec as P
 
 TILE = 128
-CHUNK = 32
+CHUNK = 64
 
 
 def _dense_kernel(transpose, rows_ref, cols_ref, count_ref, tiles_ref, src_a, src_b, out_a, out_b, dense_ref):
@@ -132,9 +132,9 @@
 
 
 def reduce_all(x, axes):
-    x = ring_scatter(pair_scatter(x, "core"), "cz")
-    x = gather_rows(scatter_rows(x, axes), axes)
-    return pair_gather(ring_gather(x, "cz"), "core")
+    summed = pair_scatter(x, "core")
+    summed = gather_rows(scatter_rows(summed, axes), axes)
+    return pair_gather(summed, "core")
 
 
 def head_block(agg, bias, w_out, node_labels):
@@ -187,7 +187,7 @@
     extra = jnp.zeros((feat, 2), jnp.float32)
     extra = extra.at[:, 0].set(bias_term).at[0, 1].set(loss_sum)
     packed = jnp.concatenate([in_term, out_term, extra], axis=1)
-    packed = reduce_all(packed, ("y", "zh", "cx"))
+    packed = reduce_all(packed, ("y", "zh", "cx", "cz"))
     grad_w_in = packed[:, :feat] * scale
     grad_w_out = packed[:, feat : feat + classes] * scale
     grad_bias = packed[:, feat + classes] * scale

time: 229 us -> 206 us (0.90)
  waiting for transfers between devices: 96.2 us -> 85.7 us
  blocking collectives: 35.8 us -> 28 us
  starting transfers between devices: 56.5 us -> 52.1 us
    ppermute x12 -> x9, waiting for transfers between devices: 54.9 us -> 37.4 us  [ring_scatter(): lax.ppermute(piece, axis, [(i, (i + k) % n) for i in range(n)])]
    all_to_all x1 -> x0, blocking collectives: 14.7 us -> none  [gather_rows(): got = lax.all_to_all(spread, axis, 0, 0, tiled=False)]
    all_to_all x0 -> x1, waiting for transfers between devices: none -> 12.8 us  [gather_rows(): got = lax.all_to_all(spread, axis, 0, 0, tiled=False)]
    all_to_all x1, blocking collectives: 21.2 us -> 28 us  [scatter_rows(): got = lax.all_to_all(x.reshape(n, -1, x.shape[1]), axis, 0, 0, tiled=False)]
    all_to_all x0 -> x1, starting transfers between devices: none -> 6.47 us  [gather_rows(): got = lax.all_to_all(spread, axis, 0, 0, tiled=False)]
    ppermute x13 -> x10, starting transfers between devices: 22.8 us -> 16.6 us  [ring_gather(): lax.ppermute(x, axis, [(i, (i + k) % n) for i in range(n)])]
    ppermute x13 -> x10, waiting for transfers between devices: 32.1 us -> 27 us  [ring_gather(): lax.ppermute(x, axis, [(i, (i + k) % n) for i in range(n)])]
    ppermute x12 -> x9, starting transfers between devices: 18.1 us -> 14.7 us  [ring_scatter(): lax.ppermute(piece, axis, [(i, (i + k) % n) for i in range(n)])]
  transfers between devices with their start and end apart: 30 -> 25, of which waited for: 25 -> 20; matrix products, arithmetic and copies ran while one was open for 2% -> 2% of each run, Pallas kernels for 0% -> 0%
where the time goes in v15:
time: 206 us; the launch traced here: 205 us
  waiting for transfers between devices  85.7 us (42%)
  starting transfers between devices  52.1 us (25%)
  blocking collectives  28 us (14%)
  Pallas kernels  16.3 us (8%)
  local copies, waits for them, and re-layouts  10.4 us (5%)
  other arithmetic  6.33 us (3%)
  between operations  3.48 us (2%)
  matrix products  2.57 us (1%)
    ppermute x9, waiting for transfers between devices, ring_scatter(): lax.ppermute(piece, axis, [(i, (i + k) % n) for i in range(n)])  37.4 us
    all_to_all x1, blocking collectives, scatter_rows(): got = lax.all_to_all(x.reshape(n, -1, x.shape[1]), axis, 0, 0, tiled=False)  28 us
    ppermute x10, waiting for transfers between devices, ring_gather(): lax.ppermute(x, axis, [(i, (i + k) % n) for i in range(n)])  27 us
    ppermute x10, starting transfers between devices, ring_gather(): lax.ppermute(x, axis, [(i, (i + k) % n) for i in range(n)])  16.6 us
    pallas_call x2, Pallas kernels, tile_product(): pl.pallas_call(lambda *refs: _dense_kernel(transpose, *refs), grid_spec=g...  16.3 us
    ppermute x9, starting transfers between devices, ring_scatter(): lax.ppermute(piece, axis, [(i, (i + k) % n) for i in range(n)])  14.7 us
    ppermute x5, starting transfers between devices, swap_core(): return lax.ppermute(x, axis, [(0, 1), (1, 0)])  14.3 us
    all_to_all x1, waiting for transfers between devices, gather_rows(): got = lax.all_to_all(spread, axis, 0, 0, tiled=False)  12.8 us
  transfers between devices with their start and end apart: 25, of which 20 were waited for; matrix products, arithmetic and copies ran while one was open for 2% of the time, Pallas kernels for 0%

profile of v15, /device:TPU:1, one launch (start us, length us, event | category | flops | bytes accessed | tf_op | source)
XLA Modules:
  0.0 204.9 jit_solution(13573062788314193461)
XLA Ops:
  0.6 0.9 copy-done
  1.5 1.0 convolution_convert_fusion.1
  2.5 5.2 %collective-permute-start = (bf16[128,256]{1,0:T(8,128)(2,1)S(1)}, bf16[128,256]{1,0:T(8,128)(2,1)S(1)}, u32[]{:S(2)}, u32[]{:S(2)}) collective-permute-start(bf16[128,256]{1,0:T(8,128)(2,1)S(1)} %convolution_convert_fusion.1), channel_id=1, source_target_pairs={{0,3},{1,0},{2,1},{3,2},{4,7},{5,4},{6,5},{7,6},{8,11},{9,8},{10,9... | collective-permute-start | bytes 196616 | tf_op jit(solution)/shard_map/ppermute | solution.py:104
  7.8 0.4 collective-permute-start.2
  8.2 0.9 collective-permute-done
  9.1 5.5 %collective-permute-done.1 = bf16[128,256]{1,0:T(8,128)(2,1)S(1)} collective-permute-done((bf16[128,256]{1,0:T(8,128)(2,1)S(1)}, bf16[128,256]{1,0:T(8,128)(2,1)S(1)}, u32[]{:S(2)}, u32[]{:S(2)}) %collective-permute-start.1) | collective-permute-done | bytes 65568 | tf_op jit(solution)/shard_map/ppermute | solution.py:104
  14.8 1.4 collective-permute-start.3
  16.2 0.5 collective-permute-start.4
  16.7 1.2 compare_select_fusion.refs_0_
  18.5 0.7 collective-permute-start.5
  19.2 2.8 %collective-permute-done.3 = bf16[512,256]{1,0:T(8,128)(2,1)S(1)} collective-permute-done((bf16[512,256]{1,0:T(8,128)(2,1)S(1)}, bf16[512,256]{1,0:T(8,128)(2,1)S(1)}, u32[]{:S(2)}, u32[]{:S(2)}) %collective-permute-start.3) | collective-permute-done | bytes 262176 | tf_op jit(solution)/shard_map/ppermute | solution.py:104
  22.1 1.6 collective-permute-done.4
  23.7 7.2 %collective-permute-done.5 = bf16[512,256]{1,0:T(8,128)(2,1)S(1)} collective-permute-done((bf16[512,256]{1,0:T(8,128)(2,1)S(1)}, bf16[512,256]{1,0:T(8,128)(2,1)S(1)}, u32[]{:S(2)}, u32[]{:S(2)}) %collective-permute-start.5) | collective-permute-done | bytes 262176 | tf_op jit(solution)/shard_map/ppermute | solution.py:104
  31.1 1.1 constant_dynamic-slice_fusion.9
  32.2 0.6 broadcast_in_dim.4.refs_5_
  32.8 8.1 %shard_map.128 = (f32[1024,256]{1,0:T(8,128)}, f32[1024,256]{1,0:T(8,128)}) custom-call(s32[128]{0:T(128)} %compare_select_fusion.refs_0_, s32[128]{0:T(128)} %bitcast.111, s32[1]{0:T(128)} %bitcast.90.refs_2_, bf16[128,128,128]{2,1,0:T(8,128)(2,1)} %bitcast.92, bf16[2048,256]{1,0:T(8,128)(2,1)} %bitcast.94, bf16[8,128]{1,0:T(8,128)(2,1)} %broadcast_in_dim.4.refs_5_), custom_call_target="tpu_custom_call" | custom-call | tf_op jit(solution)/shard_map/pallas_call | solution.py:73
  40.9 1.0 collective-permute-start.6
  41.9 2.5 %collective-permute-done.6 = f32[1024,256]{1,0:T(8,128)S(1)} collective-permute-done((f32[1024,256]{1,0:T(8,128)}, f32[1024,256]{1,0:T(8,128)S(1)}, u32[]{:S(2)}, u32[]{:S(2)}) %collective-permute-start.6) | collective-permute-done | bytes 1048608 | tf_op jit(solution)/shard_map/ppermute | solution.py:98
  44.4 1.4 add.225
  45.9 1.4 collective-permute-start.7
  47.3 2.5 %collective-permute-start.8 = (f32[256,256]{1,0:T(8,128)S(1)}, f32[256,256]{1,0:T(8,128)S(1)}, u32[]{:S(2)}, u32[]{:S(2)}) collective-permute-start(f32[256,256]{1,0:T(8,128)S(1)} %get-tuple-element.59), channel_id=1, source_target_pairs={{0,128},{64,192},{128,0},{192,64},{1,129},{65,193},{129,1},{193,65... | collective-permute-start | bytes 786440 | tf_op jit(solution)/shard_map/ppermute | solution.py:116
  49.8 1.1 collective-permute-start.9
  50.9 3.8 %collective-permute-done.7 = f32[256,256]{1,0:T(8,128)S(1)} collective-permute-done((f32[256,256]{1,0:T(8,128)S(1)}, f32[256,256]{1,0:T(8,128)S(1)}, u32[]{:S(2)}, u32[]{:S(2)}) %collective-permute-start.7) | collective-permute-done | bytes 262176 | tf_op jit(solution)/shard_map/ppermute | solution.py:116
  54.7 6.8 %collective-permute-done.8 = f32[256,256]{1,0:T(8,128)S(1)} collective-permute-done((f32[256,256]{1,0:T(8,128)S(1)}, f32[256,256]{1,0:T(8,128)S(1)}, u32[]{:S(2)}, u32[]{:S(2)}) %collective-permute-start.8) | collective-permute-done | bytes 262176 | tf_op jit(solution)/shard_map/ppermute | solution.py:116
  61.6 4.8 %collective-permute-start.10 = (f32[128,256]{1,0:T(8,128)S(1)}, f32[128,256]{1,0:T(8,128)S(1)}, u32[]{:S(2)}, u32[]{:S(2)}) collective-permute-start(f32[128,256]{1,0:T(8,128)S(1)} %constant_dynamic-slice_fusion.5), channel_id=1, source_target_pairs={{0,32},{32,0},{1,33},{33,1},{2,34},{34,2},{3,35},{35,3},{4,36},{36... | collective-permute-start | bytes 393224 | tf_op jit(solution)/shard_map/ppermute | solution.py:98
  66.4 3.1 %collective-permute-done.10 = f32[128,256]{1,0:T(8,128)S(1)} collective-permute-done((f32[128,256]{1,0:T(8,128)S(1)}, f32[128,256]{1,0:T(8,128)S(1)}, u32[]{:S(2)}, u32[]{:S(2)}) %collective-permute-start.10) | collective-permute-done | bytes 131104 | tf_op jit(solution)/shard_map/ppermute | solution.py:98
  69.8 0.6 subtract_reduce_fusion
  70.7 5.0 %collective-permute-start.11 = (bf16[128,256]{1,0:T(8,128)(2,1)S(1)}, bf16[128,256]{1,0:T(8,128)(2,1)S(1)}, u32[]{:S(2)}, u32[]{:S(2)}) collective-permute-start(bf16[128,256]{1,0:T(8,128)(2,1)S(1)} %get-tuple-element.68), channel_id=1, source_target_pairs={{0,32},{32,0},{1,33},{33,1},{2,34},{34,2},{3,35},{35,3},{4,36},{36... | collective-permute-start | bytes 196616 | tf_op jit(solution)/shard_map/ppermute | solution.py:104
  75.6 3.1 %collective-permute-done.11 = bf16[128,256]{1,0:T(8,128)(2,1)S(1)} collective-permute-done((bf16[128,256]{1,0:T(8,128)(2,1)S(1)}, bf16[128,256]{1,0:T(8,128)(2,1)S(1)}, u32[]{:S(2)}, u32[]{:S(2)}) %collective-permute-start.11) | collective-permute-done | bytes 65568 | tf_op jit(solution)/shard_map/ppermute | solution.py:104
  78.8 2.7 %collective-permute-start.12 = (bf16[256,256]{1,0:T(8,128)(2,1)S(1)}, bf16[256,256]{1,0:T(8,128)(2,1)S(1)}, u32[]{:S(2)}, u32[]{:S(2)}) collective-permute-start(bf16[256,256]{1,0:T(8,128)(2,1)S(1)} %bitcast.102), channel_id=1, source_target_pairs={{0,192},{64,0},{128,64},{192,128},{1,193},{65,1},{129,65},{193,129... | collective-permute-start | bytes 393224 | tf_op jit(solution)/shard_map/ppermute | solution.py:104
  81.6 0.7 collective-permute-start.14
  82.2 2.6 %collective-permute-done.12 = bf16[256,256]{1,0:T(8,128)(2,1)S(1)} collective-permute-done((bf16[256,256]{1,0:T(8,128)(2,1)S(1)}, bf16[256,256]{1,0:T(8,128)(2,1)S(1)}, u32[]{:S(2)}, u32[]{:S(2)}) %collective-permute-start.12) | collective-permute-done | bytes 131104 | tf_op jit(solution)/shard_map/ppermute | solution.py:104
  84.9 2.1 %collective-permute-done.13 = bf16[256,256]{1,0:T(8,128)(2,1)S(1)} collective-permute-done((bf16[256,256]{1,0:T(8,128)(2,1)S(1)}, bf16[256,256]{1,0:T(8,128)(2,1)S(1)}, u32[]{:S(2)}, u32[]{:S(2)}) %collective-permute-start.13) | collective-permute-done | bytes 131104 | tf_op jit(solution)/shard_map/ppermute | solution.py:104
  87.0 1.0 collective-permute-done.14
  88.2 4.3 %collective-permute-start.15 = (bf16[1024,256]{1,0:T(8,128)(2,1)S(1)}, bf16[1024,256]{1,0:T(8,128)(2,1)S(1)}, u32[]{:S(2)}, u32[]{:S(2)}) collective-permute-start(bf16[1024,256]{1,0:T(8,128)(2,1)S(1)} %bitcast.100), channel_id=1, source_target_pairs={{0,16},{16,0},{1,17},{17,1},{2,18},{18,2},{3,19},{19,3},{4,20},{20... | collective-permute-start | bytes 1572872 | tf_op jit(solution)/shard_map/ppermute | solution.py:98
  92.4 1.5 collective-permute-done.15.refs_5_
  94.0 0.8 copy-done.2
  94.8 8.2 %shard_map.129 = (f32[256,2048]{1,0:T(8,128)}, f32[8,128]{1,0:T(8,128)}) custom-call(s32[128]{0:T(128)} %compare_select_fusion.refs_0_, s32[128]{0:T(128)} %bitcast.112, s32[1]{0:T(128)} %bitcast.91.refs_2_, bf16[128,128,128]{2,1,0:T(8,128)(2,1)} %bitcast.93, bf16[1024,256]{1,0:T(8,128)(2,1)} %bitcast.101, bf16[1024,256]{1,0:T(8,128)(2,1)} %copy-done.2), custom_call_target="tpu_custom_call" | custom-call | tf_op jit(solution)/shard_map/pallas_call | solution.py:73
  102.9 1.5 dynamic-slice_bitcast_fusion.2
  104.5 1.3 collective-permute-start.17
  105.8 1.3 collective-permute-start.18
  107.2 0.6 fusion.6
  107.7 2.0 scatter.9
  109.7 20.3 %collective-permute-done.16 = f32[512,256]{0,1:T(8,128)S(1)} collective-permute-done((f32[512,256]{0,1:T(8,128)S(1)}, f32[512,256]{0,1:T(8,128)S(1)}, u32[]{:S(2)}, u32[]{:S(2)}) %collective-permute-start.16) | collective-permute-done | bytes 524320 | tf_op jit(solution)/shard_map/ppermute | solution.py:116
  130.1 0.4 collective-permute-done.18
  130.5 1.3 fusion.1
  131.8 3.6 %collective-permute-start.19 = (f32[128,256]{0,1:T(8,128)S(1)}, f32[128,256]{0,1:T(8,128)S(1)}, u32[]{:S(2)}, u32[]{:S(2)}) collective-permute-start(f32[128,256]{0,1:T(8,128)S(1)} %get-tuple-element.60), channel_id=1, source_target_pairs={{0,1},{1,2},{2,3},{3,0},{4,5},{5,6},{6,7},{7,4},{8,9},{9,10},{10,1... | collective-permute-start | bytes 393224 | tf_op jit(solution)/shard_map/ppermute | solution.py:116
  135.4 1.0 collective-permute-start.20
  136.4 2.3 %collective-permute-start.21 = (f32[128,256]{0,1:T(8,128)S(1)}, f32[128,256]{0,1:T(8,128)S(1)}, u32[]{:S(2)}, u32[]{:S(2)}) collective-permute-start(f32[128,256]{0,1:T(8,128)S(1)} %get-tuple-element.61), channel_id=1, source_target_pairs={{0,3},{1,0},{2,1},{3,2},{4,7},{5,4},{6,5},{7,6},{8,11},{9,8},{10,9... | collective-permute-start | bytes 393224 | tf_op jit(solution)/shard_map/ppermute | solution.py:116
  138.8 6.2 %collective-permute-done.20 = f32[128,256]{0,1:T(8,128)S(1)} collective-permute-done((f32[128,256]{0,1:T(8,128)S(1)}, f32[128,256]{0,1:T(8,128)S(1)}, u32[]{:S(2)}, u32[]{:S(2)}) %collective-permute-start.20) | collective-permute-done | bytes 131104 | tf_op jit(solution)/shard_map/ppermute | solution.py:116
  145.3 1.0 collective-permute-start.22
  146.3 1.1 collective-permute-done.22
  147.6 28.0 %all_to_all.10 = f32[128,1,430]{2,1,0:T(1,128)S(1)} all-to-all(f32[128,1,430]{2,1,0:T(1,128)S(1)} %copy.17), channel_id=1, replica_groups=mesh['y'=4,'zh'=2,'core'=2,'cx'=4,'cz'=4] {'y','zh','cx','cz'}, dimensions={0} | all-to-all | bytes 440320 | tf_op jit(solution)/shard_map/all_to_all | solution.py:93
  175.6 0.2 reduce_sum.49
  175.9 0.8 broadcast_in_dim.5
  176.7 6.5 %all-to-all-start.1 = ((f32[128,1,430]{2,1,0:T(1,128)}), f32[128,1,430]{2,1,0:T(1,128)S(1)}, u32[]{:S(2)}, u32[]{:S(2)}) async-start(f32[128,1,430]{2,1,0:T(1,128)} %broadcast_in_dim.5), calls=%async_computation.1 | async-start | bytes 524288 | tf_op jit(solution)/shard_map/all_to_all | solution.py:87
  183.2 12.8 %all-to-all-done.1 = f32[128,1,430]{2,1,0:T(1,128)S(1)} async-done(((f32[128,1,430]{2,1,0:T(1,128)}), f32[128,1,430]{2,1,0:T(1,128)S(1)}, u32[]{:S(2)}, u32[]{:S(2)}) %all-to-all-start.1) | async-done | bytes 220192 | tf_op jit(solution)/shard_map/all_to_all | solution.py:87
  196.1 3.3 %collective-permute-start.23 = (f32[128,430]{0,1:T(8,128)S(1)}, f32[128,430]{0,1:T(8,128)S(1)}, u32[]{:S(2)}, u32[]{:S(2)}) collective-permute-start(f32[128,430]{0,1:T(8,128)S(1)} %bitcast.107), channel_id=1, source_target_pairs={{0,16},{16,0},{1,17},{17,1},{2,18},{18,2},{3,19},{19,3},{4,20},{20... | collective-permute-start | bytes 660488 | tf_op jit(solution)/shard_map/ppermute | solution.py:98
  199.4 0.8 convolution_convert_fusion
  200.2 0.3 collective-permute-done.23
  200.5 0.7 slice_multiply_fusion.1
  201.2 0.5 slice.53
  201.7 0.6 slice_multiply_fusion.2
  202.3 0.8 copy.19
  (67 shorter events, 2.1 us)
Async XLA Ops:
  0.6 0.9 copy-start
  2.5 6.6 %collective-permute-start = (bf16[128,256]{1,0:T(8,128)(2,1)S(1)}, bf16[128,256]{1,0:T(8,128)(2,1)S(1)}, u32[]{:S(2)}, u32[]{:S(2)}) collective-permute-start(bf16[128,256]{1,0:T(8,128)(2,1)S(1)} %convolution_convert_fusion.1), channel_id=1, source_target_pairs={{0,3},{1,0},{2,1},{3,2},{4,7},{5,4},{6,5},{7,6},{8,11},{9,8},{10,9... | collective-permute-start | bytes 196616 | tf_op jit(solution)/shard_map/ppermute | solution.py:104
  7.8 6.8 %collective-permute-start.1 = (bf16[128,256]{1,0:T(8,128)(2,1)S(1)}, bf16[128,256]{1,0:T(8,128)(2,1)S(1)}, u32[]{:S(2)}, u32[]{:S(2)}) collective-permute-start(bf16[128,256]{1,0:T(8,128)(2,1)S(1)} %convolution_convert_fusion.1), channel_id=1, source_target_pairs={{0,2},{1,3},{2,0},{3,1},{4,6},{5,7},{6,4},{7,5},{8,10},{9,11},{10,... | collective-permute-start | bytes 196616 | tf_op jit(solution)/shard_map/ppermute | solution.py:104
  7.8 6.8 %collective-permute-start.2 = (bf16[128,256]{1,0:T(8,128)(2,1)S(1)}, bf16[128,256]{1,0:T(8,128)(2,1)S(1)}, u32[]{:S(2)}, u32[]{:S(2)}) collective-permute-start(bf16[128,256]{1,0:T(8,128)(2,1)S(1)} %convolution_convert_fusion.1), channel_id=1, source_target_pairs={{0,1},{1,2},{2,3},{3,0},{4,5},{5,6},{6,7},{7,4},{8,9},{9,10},{10,1... | collective-permute-start | bytes 196616 | tf_op jit(solution)/shard_map/ppermute | solution.py:104
  14.8 7.3 %collective-permute-start.3 = (bf16[512,256]{1,0:T(8,128)(2,1)S(1)}, bf16[512,256]{1,0:T(8,128)(2,1)S(1)}, u32[]{:S(2)}, u32[]{:S(2)}) collective-permute-start(bf16[512,256]{1,0:T(8,128)(2,1)S(1)} %bitcast.95), channel_id=1, source_target_pairs={{0,12},{4,0},{8,4},{12,8},{1,13},{5,1},{9,5},{13,9},{2,14},{6,2},{... | collective-permute-start | bytes 786440 | tf_op jit(solution)/shard_map/ppermute | solution.py:104
  16.2 7.5 %collective-permute-start.4 = (bf16[512,256]{1,0:T(8,128)(2,1)S(1)}, bf16[512,256]{1,0:T(8,128)(2,1)S(1)}, u32[]{:S(2)}, u32[]{:S(2)}) collective-permute-start(bf16[512,256]{1,0:T(8,128)(2,1)S(1)} %bitcast.96), channel_id=1, source_target_pairs={{0,8},{4,12},{8,0},{12,4},{1,9},{5,13},{9,1},{13,5},{2,10},{6,14},... | collective-permute-start | bytes 786440 | tf_op jit(solution)/shard_map/ppermute | solution.py:104
  18.5 12.4 %collective-permute-start.5 = (bf16[512,256]{1,0:T(8,128)(2,1)S(1)}, bf16[512,256]{1,0:T(8,128)(2,1)S(1)}, u32[]{:S(2)}, u32[]{:S(2)}) collective-permute-start(bf16[512,256]{1,0:T(8,128)(2,1)S(1)} %bitcast.97), channel_id=1, source_target_pairs={{0,4},{4,8},{8,12},{12,0},{1,5},{5,9},{9,13},{13,1},{2,6},{6,10},{... | collective-permute-start | bytes 786440 | tf_op jit(solution)/shard_map/ppermute | solution.py:104
  40.9 3.5 %collective-permute-start.6 = (f32[1024,256]{1,0:T(8,128)}, f32[1024,256]{1,0:T(8,128)S(1)}, u32[]{:S(2)}, u32[]{:S(2)}) collective-permute-start(f32[1024,256]{1,0:T(8,128)} %get-tuple-element.33), channel_id=1, source_target_pairs={{0,16},{16,0},{1,17},{17,1},{2,18},{18,2},{3,19},{19,3},{4,20},{20... | collective-permute-start | bytes 3145736 | tf_op jit(solution)/shard_map/ppermute | solution.py:98
  45.8 23.7 %copy-start.6 = (f32[256]{0:T(256)S(1)}, f32[256]{0:T(256)}, u32[]{:S(2)}) copy-start(f32[256]{0:T(256)} %param.15) | copy-start | bytes 3076
  45.8 23.8 %copy-start.4 = (bf16[256,172]{0,1:T(8,128)(2,1)S(1)}, bf16[256,172]{0,1:T(8,128)(2,1)}, u32[]{:S(2)}) copy-start(bf16[256,172]{0,1:T(8,128)(2,1)} %param.16) | copy-start | bytes 264196
  45.8 24.0 %copy-start.5 = (s32[128]{0:T(128)S(1)}, s32[128]{0:T(128)}, u32[]{:S(2)}) copy-start(s32[128]{0:T(128)} %param.21) | copy-start | bytes 1540
  45.9 8.8 %collective-permute-start.7 = (f32[256,256]{1,0:T(8,128)S(1)}, f32[256,256]{1,0:T(8,128)S(1)}, u32[]{:S(2)}, u32[]{:S(2)}) collective-permute-start(f32[256,256]{1,0:T(8,128)S(1)} %get-tuple-element.57), channel_id=1, source_target_pairs={{0,64},{64,128},{128,192},{192,0},{1,65},{65,129},{129,193},{193,1... | collective-permute-start | bytes 786440 | tf_op jit(solution)/shard_map/ppermute | solution.py:116
  47.3 14.2 %collective-permute-start.8 = (f32[256,256]{1,0:T(8,128)S(1)}, f32[256,256]{1,0:T(8,128)S(1)}, u32[]{:S(2)}, u32[]{:S(2)}) collective-permute-start(f32[256,256]{1,0:T(8,128)S(1)} %get-tuple-element.59), channel_id=1, source_target_pairs={{0,128},{64,192},{128,0},{192,64},{1,129},{65,193},{129,1},{193,65... | collective-permute-start | bytes 786440 | tf_op jit(solution)/shard_map/ppermute | solution.py:116
  49.8 11.6 %collective-permute-start.9 = (f32[256,256]{1,0:T(8,128)S(1)}, f32[256,256]{1,0:T(8,128)S(1)}, u32[]{:S(2)}, u32[]{:S(2)}) collective-permute-start(f32[256,256]{1,0:T(8,128)S(1)} %get-tuple-element.58), channel_id=1, source_target_pairs={{0,192},{64,0},{128,64},{192,128},{1,193},{65,1},{129,65},{193,129... | collective-permute-start | bytes 786440 | tf_op jit(solution)/shard_map/ppermute | solution.py:116
  61.6 7.9 %collective-permute-start.10 = (f32[128,256]{1,0:T(8,128)S(1)}, f32[128,256]{1,0:T(8,128)S(1)}, u32[]{:S(2)}, u32[]{:S(2)}) collective-permute-start(f32[128,256]{1,0:T(8,128)S(1)} %constant_dynamic-slice_fusion.5), channel_id=1, source_target_pairs={{0,32},{32,0},{1,33},{33,1},{2,34},{34,2},{3,35},{35,3},{4,36},{36... | collective-permute-start | bytes 393224 | tf_op jit(solution)/shard_map/ppermute | solution.py:98
  70.7 8.1 %collective-permute-start.11 = (bf16[128,256]{1,0:T(8,128)(2,1)S(1)}, bf16[128,256]{1,0:T(8,128)(2,1)S(1)}, u32[]{:S(2)}, u32[]{:S(2)}) collective-permute-start(bf16[128,256]{1,0:T(8,128)(2,1)S(1)} %get-tuple-element.68), channel_id=1, source_target_pairs={{0,32},{32,0},{1,33},{33,1},{2,34},{34,2},{3,35},{35,3},{4,36},{36... | collective-permute-start | bytes 196616 | tf_op jit(solution)/shard_map/ppermute | solution.py:104
  78.8 6.0 %collective-permute-start.12 = (bf16[256,256]{1,0:T(8,128)(2,1)S(1)}, bf16[256,256]{1,0:T(8,128)(2,1)S(1)}, u32[]{:S(2)}, u32[]{:S(2)}) collective-permute-start(bf16[256,256]{1,0:T(8,128)(2,1)S(1)} %bitcast.102), channel_id=1, source_target_pairs={{0,192},{64,0},{128,64},{192,128},{1,193},{65,1},{129,65},{193,129... | collective-permute-start | bytes 393224 | tf_op jit(solution)/shard_map/ppermute | solution.py:104
  81.5 5.4 %collective-permute-start.13 = (bf16[256,256]{1,0:T(8,128)(2,1)S(1)}, bf16[256,256]{1,0:T(8,128)(2,1)S(1)}, u32[]{:S(2)}, u32[]{:S(2)}) collective-permute-start(bf16[256,256]{1,0:T(8,128)(2,1)S(1)} %bitcast.103), channel_id=1, source_target_pairs={{0,128},{64,192},{128,0},{192,64},{1,129},{65,193},{129,1},{193,65... | collective-permute-start | bytes 393224 | tf_op jit(solution)/shard_map/ppermute | solution.py:104
  81.6 6.4 %collective-permute-start.14 = (bf16[256,256]{1,0:T(8,128)(2,1)S(1)}, bf16[256,256]{1,0:T(8,128)(2,1)S(1)}, u32[]{:S(2)}, u32[]{:S(2)}) collective-permute-start(bf16[256,256]{1,0:T(8,128)(2,1)S(1)} %bitcast.104), channel_id=1, source_target_pairs={{0,64},{64,128},{128,192},{192,0},{1,65},{65,129},{129,193},{193,1... | collective-permute-start | bytes 393224 | tf_op jit(solution)/shard_map/ppermute | solution.py:104
  88.2 5.8 %copy-start.1 = (bf16[4,256,256]{2,1,0:T(8,128)(2,1)}, bf16[4,256,256]{2,1,0:T(8,128)(2,1)S(1)}, u32[]{:S(2)}) copy-start(bf16[4,256,256]{2,1,0:T(8,128)(2,1)S(1)} %constant_dynamic-slice_fusion.4) | copy-start | bytes 1572868
  88.2 5.8 %collective-permute-start.15 = (bf16[1024,256]{1,0:T(8,128)(2,1)S(1)}, bf16[1024,256]{1,0:T(8,128)(2,1)S(1)}, u32[]{:S(2)}, u32[]{:S(2)}) collective-permute-start(bf16[1024,256]{1,0:T(8,128)(2,1)S(1)} %bitcast.100), channel_id=1, source_target_pairs={{0,16},{16,0},{1,17},{17,1},{2,18},{18,2},{3,19},{19,3},{4,20},{20... | collective-permute-start | bytes 1572872 | tf_op jit(solution)/shard_map/ppermute | solution.py:98
  94.0 0.8 copy-start.2
  104.4 25.7 %collective-permute-start.16 = (f32[512,256]{0,1:T(8,128)S(1)}, f32[512,256]{0,1:T(8,128)S(1)}, u32[]{:S(2)}, u32[]{:S(2)}) collective-permute-start(f32[512,256]{0,1:T(8,128)S(1)} %get-tuple-element.54), channel_id=1, source_target_pairs={{0,4},{4,8},{8,12},{12,0},{1,5},{5,9},{9,13},{13,1},{2,6},{6,10},{... | collective-permute-start | bytes 1572872 | tf_op jit(solution)/shard_map/ppermute | solution.py:116
  104.5 25.6 %collective-permute-start.17 = (f32[512,256]{0,1:T(8,128)S(1)}, f32[512,256]{0,1:T(8,128)S(1)}, u32[]{:S(2)}, u32[]{:S(2)}) collective-permute-start(f32[512,256]{0,1:T(8,128)S(1)} %get-tuple-element.56), channel_id=1, source_target_pairs={{0,8},{4,12},{8,0},{12,4},{1,9},{5,13},{9,1},{13,5},{2,10},{6,14},... | collective-permute-start | bytes 1572872 | tf_op jit(solution)/shard_map/ppermute | solution.py:116
  105.8 24.6 %collective-permute-start.18 = (f32[512,256]{0,1:T(8,128)S(1)}, f32[512,256]{0,1:T(8,128)S(1)}, u32[]{:S(2)}, u32[]{:S(2)}) collective-permute-start(f32[512,256]{0,1:T(8,128)S(1)} %get-tuple-element.55), channel_id=1, source_target_pairs={{0,12},{4,0},{8,4},{12,8},{1,13},{5,1},{9,5},{13,9},{2,14},{6,2},{... | collective-permute-start | bytes 1572872 | tf_op jit(solution)/shard_map/ppermute | solution.py:116
  109.7 35.3 %copy-start.3 = (bf16[128,256]{1,0:T(8,128)(2,1)S(1)}, bf16[128,256]{1,0:T(8,128)(2,1)}, u32[]{:S(2)}) copy-start(bf16[128,256]{1,0:T(8,128)(2,1)} %param.13) | copy-start | bytes 196612
  131.8 7.0 %collective-permute-start.19 = (f32[128,256]{0,1:T(8,128)S(1)}, f32[128,256]{0,1:T(8,128)S(1)}, u32[]{:S(2)}, u32[]{:S(2)}) collective-permute-start(f32[128,256]{0,1:T(8,128)S(1)} %get-tuple-element.60), channel_id=1, source_target_pairs={{0,1},{1,2},{2,3},{3,0},{4,5},{5,6},{6,7},{7,4},{8,9},{9,10},{10,1... | collective-permute-start | bytes 393224 | tf_op jit(solution)/shard_map/ppermute | solution.py:116
  135.4 9.6 %collective-permute-start.20 = (f32[128,256]{0,1:T(8,128)S(1)}, f32[128,256]{0,1:T(8,128)S(1)}, u32[]{:S(2)}, u32[]{:S(2)}) collective-permute-start(f32[128,256]{0,1:T(8,128)S(1)} %get-tuple-element.62), channel_id=1, source_target_pairs={{0,2},{1,3},{2,0},{3,1},{4,6},{5,7},{6,4},{7,5},{8,10},{9,11},{10,... | collective-permute-start | bytes 393224 | tf_op jit(solution)/shard_map/ppermute | solution.py:116
  136.4 8.6 %collective-permute-start.21 = (f32[128,256]{0,1:T(8,128)S(1)}, f32[128,256]{0,1:T(8,128)S(1)}, u32[]{:S(2)}, u32[]{:S(2)}) collective-permute-start(f32[128,256]{0,1:T(8,128)S(1)} %get-tuple-element.61), channel_id=1, source_target_pairs={{0,3},{1,0},{2,1},{3,2},{4,7},{5,4},{6,5},{7,6},{8,11},{9,8},{10,9... | collective-permute-start | bytes 393224 | tf_op jit(solution)/shard_map/ppermute | solution.py:116
  145.3 2.1 %collective-permute-start.22 = (f32[128,430]{0,1:T(8,128)S(1)}, f32[128,430]{0,1:T(8,128)S(1)}, u32[]{:S(2)}, u32[]{:S(2)}) collective-permute-start(f32[128,430]{0,1:T(8,128)S(1)} %constant_dynamic-slice_fusion), channel_id=1, source_target_pairs={{0,16},{16,0},{1,17},{17,1},{2,18},{18,2},{3,19},{19,3},{4,20},{20... | collective-permute-start | bytes 660488 | tf_op jit(solution)/shard_map/ppermute | solution.py:98
  176.7 19.3 %all-to-all-start.1 = ((f32[128,1,430]{2,1,0:T(1,128)}), f32[128,1,430]{2,1,0:T(1,128)S(1)}, u32[]{:S(2)}, u32[]{:S(2)}) async-start(f32[128,1,430]{2,1,0:T(1,128)} %broadcast_in_dim.5), calls=%async_computation.1 | async-start | bytes 524288 | tf_op jit(solution)/shard_map/all_to_all | solution.py:87
  196.1 4.4 %collective-permute-start.23 = (f32[128,430]{0,1:T(8,128)S(1)}, f32[128,430]{0,1:T(8,128)S(1)}, u32[]{:S(2)}, u32[]{:S(2)}) collective-permute-start(f32[128,430]{0,1:T(8,128)S(1)} %bitcast.107), channel_id=1, source_target_pairs={{0,16},{16,0},{1,17},{17,1},{2,18},{18,2},{3,19},{19,3},{4,20},{20... | collective-permute-start | bytes 660488 | tf_op jit(solution)/shard_map/ppermute | solution.py:98
